TPU v7x, 256 devices: a whole 4x4x8 slice. The times are simulated.
256 devices in a mesh: grp: 8 (over z), dev: 32 (over y, x, core).
Axes of the slice: x: 4, y: 4, z: 8, core: 2. Of those that a mesh axis runs over, the one named last changes fastest.
Arguments:
- pool: bfloat16 [786432, 1024], P(('grp', 'dev'))
- nearest: float32 [786432], P(('grp', 'dev')), may hold values from 0.5 to 2.2
- center_owner: int32 [8, 256], P('grp'), may hold values from 0 to 31, as said below
- center_offset: int32 [8, 256], P('grp'), may hold values from 0 to 3071
Outputs:
- nearest_after: float32 [786432], P(('grp', 'dev'))
Inputs may be any that keep to these rules, and one draw needn't show every extreme that they name: `center_owner`: in each group no more than 32 centers have the same owner, one owner has exactly 32, and the centers of a group are distinct rows.
All inputs are finite; a program needn't handle non-finite values.
Results may differ from a plain program's by a relative error of at most 0.0003.
Values may be sent and summed in bfloat16 or wider, within the bound.
No kernel may reach another device: no remote copies, remote signals or barrier semaphores. Data moves between devices by JAX's collectives and lax.ppermute only.
A program may use at most 64 MiB of HBM per device.

v0:
```python
import math

import jax
import jax.numpy as jnp
from jax import lax
from jax.sharding import PartitionSpec as P

MOST = 32


def nearest_fold(pool_rows, row_norm, running, fragment):
    center_norm = jnp.einsum("cd,cd->c", fragment, fragment, preferred_element_type=jnp.float32)
    total_rows = pool_rows.shape[0]
    block = math.gcd(total_rows, 512)
    blocks = total_rows // block

    def one_block(args):
        block_rows, block_norm, block_near = args
        inner = lax.dot_general(
            block_rows, fragment, (((1,), (1,)), ((), ())), preferred_element_type=jnp.float32
        )
        distance = jnp.maximum(block_norm[:, None] + center_norm[None, :] - 2.0 * inner, 0.0)
        return jnp.minimum(block_near, jnp.min(distance, axis=1))

    result = lax.map(
        one_block,
        (
            pool_rows.reshape(blocks, block, pool_rows.shape[1]),
            row_norm.reshape(blocks, block),
            running.reshape(blocks, block),
        ),
    )
    return result.reshape(total_rows)


def shards(pool, nearest, center_owner, center_offset):
    owners = center_owner[0]
    offsets = center_offset[0]
    dev_count = lax.axis_size("dev")
    my_index = lax.axis_index("dev")
    per_device = owners.shape[0] // dev_count
    owner_hot = (owners[:, None] == jnp.arange(dev_count, dtype=jnp.int32)[None, :]).astype(
        jnp.int32
    )
    slot_rank = jnp.sum((jnp.cumsum(owner_hot, axis=0) - 1) * owner_hot, axis=1)
    chosen = (
        (owners == my_index)[None, :]
        & (slot_rank[None, :] == jnp.arange(MOST, dtype=jnp.int32)[:, None])
    ).astype(jnp.int32)
    slot_offsets = jnp.sum(chosen * offsets[None, :], axis=1)
    slot_rows = jnp.take(pool, slot_offsets, axis=0)
    every_slot = lax.all_gather(slot_rows, "dev", axis=0, tiled=True)
    slot_index = owners * MOST + slot_rank
    mine = lax.dynamic_slice_in_dim(slot_index, my_index * per_device, per_device)
    local_centers = jnp.take(every_slot, mine, axis=0)
    row_norm = jnp.einsum("rd,rd->r", pool, pool, preferred_element_type=jnp.float32)
    return nearest_fold(
        pool, row_norm, nearest, lax.all_gather(local_centers, ("grp", "dev"), axis=0, tiled=True)
    )


def solution(mesh):
    in_specs = (P(("grp", "dev"), None), P(("grp", "dev")), P("grp", None), P("grp", None))
    out_specs = P(("grp", "dev"))
    return jax.shard_map(shards, mesh=mesh, in_specs=in_specs, out_specs=out_specs, check_vma=False)
```

profile of v0, /device:TPU:1, one launch (start us, length us, event | category | flops | bytes accessed | tf_op | source)
XLA Modules:
  0.0 228.6 jit_solution(5956748127939711534)
XLA Ops:
  6.5 0.7 fusion.7
  7.2 0.6 reduce-window.6
  7.8 0.2 slice_reduce_fusion
  8.0 0.7 compare_reduce_fusion
  8.7 0.8 fusion.6
  9.5 0.8 select_reduce_fusion
  10.3 4.3 %gather_fusion = bf16[32,1024]{1,0:T(8,128)(2,1)S(1)} fusion(bf16[3072,1024]{1,0:T(8,128)(2,1)} %param.6, s32[1024]{0:T(1024)S(1)} %pad_clamp_fusion.1), kind=kCustom, calls=%fused_computation | custom fusion | bytes 131200 | tf_op jit(solution)/shard_map/jit(_take)/gather | solution.py:51
  14.6 0.7 broadcast_select_fusion
  15.3 0.0 all-gather.3.cloned.1.call-update
  15.3 0.0 all-gather.5.cloned.1.call-start
  15.4 0.7 multiply_add_fusion
  16.1 0.1 compare_and_fusion.1
  16.2 52.4 %all-gather.3.cloned.1.call-done = bf16[1024,1024]{1,0:T(8,128)(2,1)} async-done(((bf16[32,1024]{1,0:T(8,128)(2,1)}), bf16[1024,1024]{1,0:T(8,128)(2,1)}) %all-gather.3.cloned.1.call-update) | async-done | bytes 2097168 | tf_op jit(solution)/shard_map/all_gather | solution.py:52
  68.6 2.4 %gather_fusion.1 = bf16[8,1024]{1,0:T(8,128)(2,1)S(1)} fusion(bf16[1024,1024]{1,0:T(8,128)(2,1)} %all-gather.3.cloned.1.call-done, s32[1024]{0:T(1024)S(1)} %pad_clamp_fusion), kind=kCustom, calls=%fused_computation.1 | custom fusion | bytes 32800 | tf_op jit(solution)/shard_map/jit(_take)/gather | solution.py:55
  71.0 0.7 broadcast_select_fusion.1
  71.7 4.1 %fusion.3 = f32[3072]{0:T(1024)S(1)} fusion(bf16[3072,1024]{1,0:T(8,128)(2,1)} %param.6), kind=kLoop, calls=%fused_computation.9 | loop fusion | flops 9434112 | bytes 6303744 | tf_op jit(solution)/shard_map/rd,rd->r/dot_general | solution.py:56
  75.9 110.8 %all-gather.5.cloned.1.call-done = bf16[2048,1024]{1,0:T(8,128)(2,1)} async-done(((bf16[8,1024]{1,0:T(8,128)(2,1)}), bf16[2048,1024]{1,0:T(8,128)(2,1)}) %all-gather.5.cloned.1.call-update) | async-done | bytes 4194320 | tf_op jit(solution)/shard_map/all_gather | solution.py:58
  186.6 3.1 %fusion.4 = f32[2048]{0:T(1024)S(1)} fusion(bf16[2048,1024]{1,0:T(8,128)(2,1)} %all-gather.5.cloned.1.call-done), kind=kLoop, calls=%fused_computation.11 | loop fusion | flops 6289408 | bytes 4202496 | tf_op jit(solution)/shard_map/cd,cd->c/dot_general | solution.py:12
  189.7 31.4 %while.10 = (s32[]{:T(128)}, f32[6,512]{1,0:T(8,128)S(1)}, f32[6,512]{1,0:T(8,128)S(1)}, f32[6,512]{1,0:T(8,128)S(1)}, f32[2048]{0:T(1024)S(1)}, /*index=5*/bf16...) while((s32[]{:T(128)}, f32[6,512]{1,0:T(8,128)S(1)}, f32[6,512]{1,0:T(8,128)S(1)}, ...), condition=%wide.region_6.7_spmd, body=%wide.region_4.6_spmd.sunk | while | flops 2152726528 | bytes 5270121 | solution.py:25
  189.7 5.1 %maximum_reduce_fusion.2 = f32[512]{0:T(512)S(1)} fusion(bf16[2048,1024]{1,0:T(8,128)(2,1)} %get-tuple-element.126, f32[2048]{0:T(1024)S(1)} %get-tuple-element.124, f32[512]{0:T(512)S(1)} %bitcast.39, bf16[6,512,1024]{2,1,0:T(8,128)(2,1)} %get-tuple-element.125, s32[]{:T(128)} %get-tuple-element.111), kind=kOutput, calls=%fused_computation.2.clone.1 | convolution fusion | flops 2152726016 | bytes 5255680 | tf_op jit(solution)/shard_map/while/body/eval_jaxpr/dot_general | solution.py:19
  194.9 0.1 dynamic_update_slice.5
  195.0 5.1 %maximum_reduce_fusion.2 = f32[512]{0:T(512)S(1)} fusion(bf16[2048,1024]{1,0:T(8,128)(2,1)} %get-tuple-element.126, f32[2048]{0:T(1024)S(1)} %get-tuple-element.124, f32[512]{0:T(512)S(1)} %bitcast.39, bf16[6,512,1024]{2,1,0:T(8,128)(2,1)} %get-tuple-element.125, s32[]{:T(128)} %get-tuple-element.111), kind=kOutput, calls=%fused_computation.2.clone.1 | convolution fusion | flops 2152726016 | bytes 5255680 | tf_op jit(solution)/shard_map/while/body/eval_jaxpr/dot_general | solution.py:19
  200.1 0.1 dynamic_update_slice.5
  200.2 5.1 %maximum_reduce_fusion.2 = f32[512]{0:T(512)S(1)} fusion(bf16[2048,1024]{1,0:T(8,128)(2,1)} %get-tuple-element.126, f32[2048]{0:T(1024)S(1)} %get-tuple-element.124, f32[512]{0:T(512)S(1)} %bitcast.39, bf16[6,512,1024]{2,1,0:T(8,128)(2,1)} %get-tuple-element.125, s32[]{:T(128)} %get-tuple-element.111), kind=kOutput, calls=%fused_computation.2.clone.1 | convolution fusion | flops 2152726016 | bytes 5255680 | tf_op jit(solution)/shard_map/while/body/eval_jaxpr/dot_general | solution.py:19
  205.3 0.1 dynamic_update_slice.5
  205.4 5.1 %maximum_reduce_fusion.2 = f32[512]{0:T(512)S(1)} fusion(bf16[2048,1024]{1,0:T(8,128)(2,1)} %get-tuple-element.126, f32[2048]{0:T(1024)S(1)} %get-tuple-element.124, f32[512]{0:T(512)S(1)} %bitcast.39, bf16[6,512,1024]{2,1,0:T(8,128)(2,1)} %get-tuple-element.125, s32[]{:T(128)} %get-tuple-element.111), kind=kOutput, calls=%fused_computation.2.clone.1 | convolution fusion | flops 2152726016 | bytes 5255680 | tf_op jit(solution)/shard_map/while/body/eval_jaxpr/dot_general | solution.py:19
  210.6 0.1 dynamic_update_slice.5
  210.7 5.1 %maximum_reduce_fusion.2 = f32[512]{0:T(512)S(1)} fusion(bf16[2048,1024]{1,0:T(8,128)(2,1)} %get-tuple-element.126, f32[2048]{0:T(1024)S(1)} %get-tuple-element.124, f32[512]{0:T(512)S(1)} %bitcast.39, bf16[6,512,1024]{2,1,0:T(8,128)(2,1)} %get-tuple-element.125, s32[]{:T(128)} %get-tuple-element.111), kind=kOutput, calls=%fused_computation.2.clone.1 | convolution fusion | flops 2152726016 | bytes 5255680 | tf_op jit(solution)/shard_map/while/body/eval_jaxpr/dot_general | solution.py:19
  215.8 0.1 dynamic_update_slice.5
  215.9 5.1 %maximum_reduce_fusion.2 = f32[512]{0:T(512)S(1)} fusion(bf16[2048,1024]{1,0:T(8,128)(2,1)} %get-tuple-element.126, f32[2048]{0:T(1024)S(1)} %get-tuple-element.124, f32[512]{0:T(512)S(1)} %bitcast.39, bf16[6,512,1024]{2,1,0:T(8,128)(2,1)} %get-tuple-element.125, s32[]{:T(128)} %get-tuple-element.111), kind=kOutput, calls=%fused_computation.2.clone.1 | convolution fusion | flops 2152726016 | bytes 5255680 | tf_op jit(solution)/shard_map/while/body/eval_jaxpr/dot_general | solution.py:19
  221.0 0.1 dynamic_update_slice.5
  221.1 0.6 reshape.63
  (25 shorter events, 0.2 us)
Async XLA Ops:
  6.5 69.3 %copy-start = (f32[3072]{0:T(1024)S(1)}, f32[3072]{0:T(1024)}, u32[]{:S(2)}) copy-start(f32[3072]{0:T(1024)} %param.7) | copy-start | bytes 36868
  6.5 62.0 %all-gather.3.cloned.1.call-start = ((), (), s32[]{:S(2)}) async-start(), calls=%async_computation | async-start | bytes 2162688 | tf_op jit(solution)/shard_map/all_gather | solution.py:52
  15.3 171.3 %all-gather.5.cloned.1.call-start = ((), (), s32[]{:S(2)}) async-start(), calls=%async_computation.1 | async-start | bytes 4210688 | tf_op jit(solution)/shard_map/all_gather | solution.py:58
Sparse Core Ops, SparseCore 0:
  15.5 53.0 all-gather.2
  72.2 114.3 all-gather.4
where the time goes:
time: 229 us
  waiting for transfers between devices  163 us (71%)
  matrix products  30.7 us (13%)
  between operations  13.5 us (6%)
  other arithmetic  13 us (6%)
  local copies, waits for them, and re-layouts  7.93 us (3%)
    all_gather x1, waiting for transfers between devices, shards(): lax.all_gather(local_centers, ('grp', 'dev'), axis=0, tiled=True)  111 us
    all_gather x1, waiting for transfers between devices, shards(): every_slot = lax.all_gather(slot_rows, 'dev', axis=0, tiled=True)  52.4 us
    dot_general x6, matrix products, one_block(): lax.dot_general(block_rows, fragment, (((1,), (1,)), ((), ())), preferred...  30.7 us
  transfers between devices with their start and end apart: 2, of which 2 were waited for; matrix products, arithmetic and copies ran while one was open for 2% of the time, Pallas kernels for 0%

commit v1 on v0

v1 whole, which is shorter than its diff:
```python
import math

import jax
import jax.numpy as jnp
from jax import lax
from jax.sharding import PartitionSpec as P

MOST = 32
X_CHIPS = 4
CORES = 2


def fold_chunk(pool_rows, row_norm, running, fragment):
    center_norm = jnp.einsum("cd,cd->c", fragment, fragment, preferred_element_type=jnp.float32)
    total_rows = pool_rows.shape[0]
    block = math.gcd(total_rows, 512)
    blocks = total_rows // block

    def one_block(args):
        block_rows, block_norm, block_near = args
        inner = lax.dot_general(
            block_rows, fragment, (((1,), (1,)), ((), ())), preferred_element_type=jnp.float32
        )
        distance = jnp.maximum(block_norm[:, None] + center_norm[None, :] - 2.0 * inner, 0.0)
        return jnp.minimum(block_near, jnp.min(distance, axis=1))

    result = lax.map(
        one_block,
        (
            pool_rows.reshape(blocks, block, pool_rows.shape[1]),
            row_norm.reshape(blocks, block),
            running.reshape(blocks, block),
        ),
    )
    return result.reshape(total_rows)


def x_step(d, s, dev_count):
    chips = dev_count // CORES
    y, rest = divmod(d, X_CHIPS * CORES)
    x, c = divmod(rest, CORES)
    del chips
    return (y * X_CHIPS + (x + s) % X_CHIPS) * CORES + c


def y_step(d, s, dev_count):
    ys = dev_count // (X_CHIPS * CORES)
    y, rest = divmod(d, X_CHIPS * CORES)
    return ((y + s) % ys) * X_CHIPS * CORES + rest


def ring_gather(block, send):
    n = send.size
    got = [block]
    fwd = block
    bwd = block
    steps = (n - 1) // 2
    for _ in range(steps):
        fwd = send(fwd, 1)
        bwd = send(bwd, -1)
        got += [fwd, bwd]
    if n % 2 == 0:
        fwd = send(fwd, 1)
        got.append(fwd)
    return got


class Ring:
    def __init__(self, size, fn):
        self.size = size
        self.fn = fn

    def __call__(self, x, s):
        return self.fn(x, s)


def shards(pool, nearest, center_owner, center_offset):
    owners = center_owner[0]
    offsets = center_offset[0]
    dev_count = lax.axis_size("dev")
    grp_count = lax.axis_size("grp")
    my_index = lax.axis_index("dev")
    per_device = owners.shape[0] // dev_count

    with jax.named_scope("compact_centers"):
        send_rows = jnp.take(pool, jnp.where(owners == my_index, offsets, 0), axis=0)
        landed = lax.all_to_all(send_rows, "dev", 0, 0, tiled=True)
        mine = lax.dynamic_slice_in_dim(owners, my_index * per_device, per_device)
        compact = jnp.take(
            landed, mine * per_device + jnp.arange(per_device, dtype=jnp.int32), axis=0
        )

    def z_send(x, s):
        return lax.ppermute(x, "grp", [(g, (g + s) % grp_count) for g in range(grp_count)])

    def x_send(x, s):
        return lax.ppermute(x, "dev", [(d, x_step(d, s, dev_count)) for d in range(dev_count)])

    def y_send(x, s):
        return lax.ppermute(x, "dev", [(d, y_step(d, s, dev_count)) for d in range(dev_count)])

    y_count = dev_count // (X_CHIPS * CORES)
    row_norm = jnp.einsum("rd,rd->r", pool, pool, preferred_element_type=jnp.float32)

    with jax.named_scope("spread_centers"):
        z_all = jnp.concatenate(ring_gather(compact, Ring(grp_count, z_send)), axis=0)
        x_all = jnp.concatenate(ring_gather(z_all, Ring(X_CHIPS, x_send)), axis=0)
        y_parts = ring_gather(x_all, Ring(y_count, y_send))
        half = jnp.concatenate(y_parts, axis=0)
        other = lax.ppermute(half, "dev", [(d, d ^ 1) for d in range(dev_count)])

    with jax.named_scope("distance_min"):
        running = nearest
        for part in y_parts:
            running = fold_chunk(pool, row_norm, running, part)
        running = fold_chunk(pool, row_norm, running, other)
    return running


def solution(mesh):
    in_specs = (P(("grp", "dev"), None), P(("grp", "dev")), P("grp", None), P("grp", None))
    out_specs = P(("grp", "dev"))
    return jax.shard_map(shards, mesh=mesh, in_specs=in_specs, out_specs=out_specs, check_vma=False)
```

time: 229 us -> 143 us (0.62)
  waiting for transfers between devices: 163 us -> 22.4 us
  starting transfers between devices: 0.04 us -> 31.2 us
  matrix products: 30.7 us -> 58.2 us
  between operations: 13.5 us -> 0.19 us
  local copies, waits for them, and re-layouts: 7.93 us -> 18.2 us
  other arithmetic: 13 us -> 9.85 us
    all_gather x2 -> x0, waiting for transfers between devices: 163 us -> none  [the longest x1 111 us: shards(): lax.all_gather(local_centers, ('grp', 'dev'), axis=0, tiled=True)]
    dot_general x6 -> x30, matrix products: 30.7 us -> 58.2 us  [one_block(): lax.dot_general(block_rows, fragment, (((1,), (1,)), ((), ())), preferred...]
    ppermute x0 -> x14, starting transfers between devices: none -> 22.6 us  [the longest x7 11.2 us: z_send(): lax.ppermute(x, 'grp', [(g, (g + s) % grp_count) for g in range(grp_count)])]
    all_to_all x0 -> x1, waiting for transfers between devices: none -> 11.4 us  [shards(): landed = lax.all_to_all(send_rows, 'dev', 0, 0, tiled=True)]
    ppermute x0 -> x14, waiting for transfers between devices: none -> 11 us  [the longest x3 5.61 us: x_send(): lax.ppermute(x, 'dev', [(d, x_step(d, s, dev_count)) for d in range(dev_c...]
    unnamed x2 -> x17, local copies, waits for them, and re-layouts: 0.01 us -> 8.8 us
    all_to_all x0 -> x1, starting transfers between devices: none -> 8.59 us  [shards(): landed = lax.all_to_all(send_rows, 'dev', 0, 0, tiled=True)]
  transfers between devices with their start and end apart: 2 -> 15, of which waited for: 2 -> 6; matrix products, arithmetic and copies ran while one was open for 2% -> 40% of each run, Pallas kernels for 0% -> 0%
where the time goes in v1:
time: 143 us; the launch traced here: 141 us
  matrix products  58.2 us (41%)
  starting transfers between devices  31.2 us (22%)
  waiting for transfers between devices  22.4 us (16%)
  local copies, waits for them, and re-layouts  18.2 us (13%)
  other arithmetic  9.85 us (7%)
    dot_general x30, matrix products, one_block(): lax.dot_general(block_rows, fragment, (((1,), (1,)), ((), ())), preferred...  58.2 us
    all_to_all x1, waiting for transfers between devices, shards(): landed = lax.all_to_all(send_rows, 'dev', 0, 0, tiled=True)  11.4 us
    ppermute x7, starting transfers between devices, z_send(): lax.ppermute(x, 'grp', [(g, (g + s) % grp_count) for g in range(grp_count)])  11.2 us
    unnamed x17, local copies, waits for them, and re-layouts  8.8 us
    all_to_all x1, starting transfers between devices, shards(): landed = lax.all_to_all(send_rows, 'dev', 0, 0, tiled=True)  8.59 us
    ppermute x1, starting transfers between devices, shards(): other = lax.ppermute(half, 'dev', [(d, d ^ 1) for d in range(dev_count)])  7.42 us
    ppermute x3, waiting for transfers between devices, x_send(): lax.ppermute(x, 'dev', [(d, x_step(d, s, dev_count)) for d in range(dev_c...  5.61 us
    ppermute x7, waiting for transfers between devices, z_send(): lax.ppermute(x, 'grp', [(g, (g + s) % grp_count) for g in range(grp_count)])  5.41 us
  transfers between devices with their start and end apart: 15, of which 6 were waited for; matrix products, arithmetic and copies ran while one was open for 40% of the time, Pallas kernels for 0%

profile of v1, /device:TPU:1, one launch (start us, length us, event | category | flops | bytes accessed | tf_op | source)
XLA Modules:
  0.0 141.2 jit_solution(2318074288935374381)
XLA Ops:
  1.5 5.2 %gather_fusion = bf16[256,1024]{1,0:T(8,128)(2,1)S(1)} fusion(bf16[3072,1024]{1,0:T(8,128)(2,1)} %param.14, s32[1024]{0:T(1024)S(1)} %pad_clamp_fusion.1), kind=kCustom, calls=%fused_computation | custom fusion | bytes 1049600 | tf_op jit(solution)/shard_map/compact_centers/jit(_take)/gather | solution.py:86
  7.6 8.6 %all-to-all-start = ((bf16[32,8,1024]{2,1,0:T(8,128)(2,1)}), bf16[32,8,1024]{2,1,0:T(8,128)(2,1)S(1)}, u32[]{:S(2)}, u32[]{:S(2)}) async-start(bf16[32,8,1024]{2,1,0:T(8,128)(2,1)} %bitcast_select_fusion), calls=%async_computation | async-start | bytes 1048576 | tf_op jit(solution)/shard_map/compact_centers/all_to_all | solution.py:87
  16.4 11.4 %all-to-all-done = bf16[32,8,1024]{2,1,0:T(8,128)(2,1)S(1)} async-done(((bf16[32,8,1024]{2,1,0:T(8,128)(2,1)}), bf16[32,8,1024]{2,1,0:T(8,128)(2,1)S(1)}, u32[]{:S(2)}, u32[]{:S(2)}) %all-to-all-start) | async-done | bytes 524320 | tf_op jit(solution)/shard_map/compact_centers/all_to_all | solution.py:87
  29.0 5.6 %collective-permute-start.1 = (bf16[8,1024]{1,0:T(8,128)(2,1)S(1)}, bf16[8,1024]{1,0:T(8,128)(2,1)S(1)}, u32[]{:S(2)}, u32[]{:S(2)}) collective-permute-start(bf16[8,1024]{1,0:T(8,128)(2,1)S(1)} %get-tuple-element.266), channel_id=1, source_target_pairs={{0,224},{32,0},{64,32},{96,64},{128,96},{160,128},{192,160},{224,1... | collective-permute-start | bytes 49160 | tf_op jit(solution)/shard_map/spread_centers/ppermute | solution.py:94
  35.4 2.9 %collective-permute-start.3 = (bf16[8,1024]{1,0:T(8,128)(2,1)S(1)}, bf16[8,1024]{1,0:T(8,128)(2,1)S(1)}, u32[]{:S(2)}, u32[]{:S(2)}) collective-permute-start(bf16[8,1024]{1,0:T(8,128)(2,1)S(1)} %collective-permute-done.1), channel_id=1, source_target_pairs={{0,224},{32,0},{64,32},{96,64},{128,96},{160,128},{192,160},{224,1... | collective-permute-start | bytes 49160 | tf_op jit(solution)/shard_map/spread_centers/ppermute | solution.py:94
  39.6 2.7 %collective-permute-start.5 = (bf16[8,1024]{1,0:T(8,128)(2,1)S(1)}, bf16[8,1024]{1,0:T(8,128)(2,1)S(1)}, u32[]{:S(2)}, u32[]{:S(2)}) collective-permute-start(bf16[8,1024]{1,0:T(8,128)(2,1)S(1)} %collective-permute-done.3), channel_id=1, source_target_pairs={{0,224},{32,0},{64,32},{96,64},{128,96},{160,128},{192,160},{224,1... | collective-permute-start | bytes 49160 | tf_op jit(solution)/shard_map/spread_centers/ppermute | solution.py:94
  43.5 2.6 %collective-permute-done.4 = bf16[8,1024]{1,0:T(8,128)(2,1)S(1)} collective-permute-done((bf16[8,1024]{1,0:T(8,128)(2,1)S(1)}, bf16[8,1024]{1,0:T(8,128)(2,1)S(1)}, u32[]{:S(2)}, u32[]{:S(2)}) %collective-permute-start.4) | collective-permute-done | bytes 16416 | tf_op jit(solution)/shard_map/spread_centers/ppermute | solution.py:94
  47.3 2.6 %collective-permute-done.6 = bf16[8,1024]{1,0:T(8,128)(2,1)S(1)} collective-permute-done((bf16[8,1024]{1,0:T(8,128)(2,1)S(1)}, bf16[8,1024]{1,0:T(8,128)(2,1)S(1)}, u32[]{:S(2)}, u32[]{:S(2)}) %collective-permute-start.6) | collective-permute-done | bytes 16416 | tf_op jit(solution)/shard_map/spread_centers/ppermute | solution.py:94
  52.1 4.1 %fusion.27 = f32[3072]{0:T(1024)S(1)} fusion(bf16[3072,1024]{1,0:T(8,128)(2,1)} %param.14), kind=kLoop, calls=%fused_computation.45 | loop fusion | flops 9434112 | bytes 6303744 | tf_op jit(solution)/shard_map/rd,rd->r/dot_general | solution.py:103
  58.6 4.7 %collective-permute-done.9 = bf16[64,1024]{1,0:T(8,128)(2,1)S(1)} collective-permute-done((bf16[64,1024]{1,0:T(8,128)(2,1)S(1)}, bf16[64,1024]{1,0:T(8,128)(2,1)S(1)}, u32[]{:S(2)}, u32[]{:S(2)}) %collective-permute-start.9) | collective-permute-done | bytes 131104 | tf_op jit(solution)/shard_map/spread_centers/ppermute | solution.py:97
  67.0 11.9 %while.50 = (s32[]{:T(128)}, f32[6,512]{1,0:T(8,128)S(1)}, f32[6,512]{1,0:T(8,128)S(1)}, f32[6,512]{1,0:T(8,128)S(1)}, f32[256]{0:T(256)S(1)}, /*index=5*/bf16[6...) while((s32[]{:T(128)}, f32[6,512]{1,0:T(8,128)S(1)}, f32[6,512]{1,0:T(8,128)S(1)}, ...), condition=%wide.region_2.3_spmd, body=%wide.region_0.2_spmd.sunk | while | flops 269090816 | bytes 1592437 | solution.py:27
  67.0 1.9 %fusion.56 = f32[512]{0:T(512)S(1)} fusion(bf16[256,1024]{1,0:T(8,128)(2,1)} %get-tuple-element.535, bf16[6,512,1024]{2,1,0:T(8,128)(2,1)} %get-tuple-element.534, s32[]{:T(128)S(6)} %copy.63, f32[256]{0:T(256)S(1)} %get-tuple-element.533, f32[512]{0:T(512)S(1)} %bitcast.94), kind=kOutput, calls=%fused_computation.5.clone.1 | convolution fusion | flops 269090304 | bytes 1577988 | tf_op jit(solution)/shard_map/distance_min/while/body/eval_jaxpr/dot_general | solution.py:21
  69.0 1.9 %fusion.56 = f32[512]{0:T(512)S(1)} fusion(bf16[256,1024]{1,0:T(8,128)(2,1)} %get-tuple-element.535, bf16[6,512,1024]{2,1,0:T(8,128)(2,1)} %get-tuple-element.534, s32[]{:T(128)S(6)} %copy.63, f32[256]{0:T(256)S(1)} %get-tuple-element.533, f32[512]{0:T(512)S(1)} %bitcast.94), kind=kOutput, calls=%fused_computation.5.clone.1 | convolution fusion | flops 269090304 | bytes 1577988 | tf_op jit(solution)/shard_map/distance_min/while/body/eval_jaxpr/dot_general | solution.py:21
  71.0 1.9 %fusion.56 = f32[512]{0:T(512)S(1)} fusion(bf16[256,1024]{1,0:T(8,128)(2,1)} %get-tuple-element.535, bf16[6,512,1024]{2,1,0:T(8,128)(2,1)} %get-tuple-element.534, s32[]{:T(128)S(6)} %copy.63, f32[256]{0:T(256)S(1)} %get-tuple-element.533, f32[512]{0:T(512)S(1)} %bitcast.94), kind=kOutput, calls=%fused_computation.5.clone.1 | convolution fusion | flops 269090304 | bytes 1577988 | tf_op jit(solution)/shard_map/distance_min/while/body/eval_jaxpr/dot_general | solution.py:21
  73.0 1.9 %fusion.56 = f32[512]{0:T(512)S(1)} fusion(bf16[256,1024]{1,0:T(8,128)(2,1)} %get-tuple-element.535, bf16[6,512,1024]{2,1,0:T(8,128)(2,1)} %get-tuple-element.534, s32[]{:T(128)S(6)} %copy.63, f32[256]{0:T(256)S(1)} %get-tuple-element.533, f32[512]{0:T(512)S(1)} %bitcast.94), kind=kOutput, calls=%fused_computation.5.clone.1 | convolution fusion | flops 269090304 | bytes 1577988 | tf_op jit(solution)/shard_map/distance_min/while/body/eval_jaxpr/dot_general | solution.py:21
  74.9 1.9 %fusion.56 = f32[512]{0:T(512)S(1)} fusion(bf16[256,1024]{1,0:T(8,128)(2,1)} %get-tuple-element.535, bf16[6,512,1024]{2,1,0:T(8,128)(2,1)} %get-tuple-element.534, s32[]{:T(128)S(6)} %copy.63, f32[256]{0:T(256)S(1)} %get-tuple-element.533, f32[512]{0:T(512)S(1)} %bitcast.94), kind=kOutput, calls=%fused_computation.5.clone.1 | convolution fusion | flops 269090304 | bytes 1577988 | tf_op jit(solution)/shard_map/distance_min/while/body/eval_jaxpr/dot_general | solution.py:21
  76.9 1.9 %fusion.56 = f32[512]{0:T(512)S(1)} fusion(bf16[256,1024]{1,0:T(8,128)(2,1)} %get-tuple-element.535, bf16[6,512,1024]{2,1,0:T(8,128)(2,1)} %get-tuple-element.534, s32[]{:T(128)S(6)} %copy.63, f32[256]{0:T(256)S(1)} %get-tuple-element.533, f32[512]{0:T(512)S(1)} %bitcast.94), kind=kOutput, calls=%fused_computation.5.clone.1 | convolution fusion | flops 269090304 | bytes 1577988 | tf_op jit(solution)/shard_map/distance_min/while/body/eval_jaxpr/dot_general | solution.py:21
  79.1 11.1 %while.51 = (s32[]{:T(128)}, f32[6,512]{1,0:T(8,128)S(1)}, f32[6,512]{1,0:T(8,128)S(1)}, f32[6,512]{1,0:T(8,128)S(1)}, f32[256]{0:T(256)S(1)}, /*index=5*/bf16[6...) while((s32[]{:T(128)}, f32[6,512]{1,0:T(8,128)S(1)}, f32[6,512]{1,0:T(8,128)S(1)}, ...), condition=%wide.region_5.6_spmd, body=%wide.region_3.5_spmd.sunk | while | flops 269090816 | bytes 1592437 | solution.py:27
  79.1 1.7 %fusion.59 = f32[512]{0:T(512)S(1)} fusion(bf16[256,1024]{1,0:T(8,128)(2,1)S(1)} %get-tuple-element.562, bf16[6,512,1024]{2,1,0:T(8,128)(2,1)} %get-tuple-element.561, s32[]{:T(128)S(6)} %copy.69, f32[256]{0:T(256)S(1)} %get-tuple-element.560, f32[512]{0:T(512)S(1)} %bitcast.95), kind=kOutput, calls=%fused_computation.14.clone.1 | convolution fusion | flops 269090304 | bytes 1577988 | tf_op jit(solution)/shard_map/distance_min/while/body/eval_jaxpr/dot_general | solution.py:21
  91.0 11.1 %while.52 = (s32[]{:T(128)}, f32[6,512]{1,0:T(8,128)S(1)}, f32[6,512]{1,0:T(8,128)S(1)}, f32[6,512]{1,0:T(8,128)S(1)}, f32[256]{0:T(256)S(1)}, /*index=5*/bf16[6...) while((s32[]{:T(128)}, f32[6,512]{1,0:T(8,128)S(1)}, f32[6,512]{1,0:T(8,128)S(1)}, ...), condition=%wide.region_8.9_spmd, body=%wide.region_6.8_spmd.sunk | while | flops 269090816 | bytes 1592437 | solution.py:27
  91.0 1.7 %fusion.62 = f32[512]{0:T(512)S(1)} fusion(bf16[256,1024]{1,0:T(8,128)(2,1)S(1)} %get-tuple-element.589, bf16[6,512,1024]{2,1,0:T(8,128)(2,1)} %get-tuple-element.588, s32[]{:T(128)S(6)} %copy.75, f32[256]{0:T(256)S(1)} %get-tuple-element.587, f32[512]{0:T(512)S(1)} %bitcast.96), kind=kOutput, calls=%fused_computation.23.clone.1 | convolution fusion | flops 269090304 | bytes 1577988 | tf_op jit(solution)/shard_map/distance_min/while/body/eval_jaxpr/dot_general | solution.py:21
  104.6 7.4 %collective-permute-start.13 = (bf16[1024,1024]{1,0:T(8,128)(2,1)}, bf16[1024,1024]{1,0:T(8,128)(2,1)S(1)}, u32[]{:S(2)}, u32[]{:S(2)}) collective-permute-start(bf16[1024,1024]{1,0:T(8,128)(2,1)} %constant_dynamic-update-slice_fusion.19), channel_id=1, source_target_pairs={{0,1},{1,0},{2,3},{3,2},{4,5},{5,4},{6,7},{7,6},{8,9},{9,8},{10,11... | collective-permute-start | bytes 6291464 | tf_op jit(solution)/shard_map/spread_centers/ppermute | solution.py:110
  112.2 11.1 %while.53 = (s32[]{:T(128)}, f32[6,512]{1,0:T(8,128)S(1)}, f32[6,512]{1,0:T(8,128)S(1)}, f32[6,512]{1,0:T(8,128)S(1)}, f32[256]{0:T(256)S(1)}, /*index=5*/bf16[6...) while((s32[]{:T(128)}, f32[6,512]{1,0:T(8,128)S(1)}, ...), condition=%wide.region_11.12_spmd, body=%wide.region_9.11_spmd.sunk | while | flops 269090816 | bytes 1592437 | solution.py:27
  112.2 1.7 %fusion.65 = f32[512]{0:T(512)S(1)} fusion(bf16[256,1024]{1,0:T(8,128)(2,1)S(1)} %get-tuple-element.616, bf16[6,512,1024]{2,1,0:T(8,128)(2,1)} %get-tuple-element.615, s32[]{:T(128)S(6)} %copy.81, f32[256]{0:T(256)S(1)} %get-tuple-element.614, f32[512]{0:T(512)S(1)} %bitcast.97), kind=kOutput, calls=%fused_computation.32.clone.1 | convolution fusion | flops 269090304 | bytes 1577988 | tf_op jit(solution)/shard_map/distance_min/while/body/eval_jaxpr/dot_general | solution.py:21
  115.9 1.7 %fusion.65 = f32[512]{0:T(512)S(1)} fusion(bf16[256,1024]{1,0:T(8,128)(2,1)S(1)} %get-tuple-element.616, bf16[6,512,1024]{2,1,0:T(8,128)(2,1)} %get-tuple-element.615, s32[]{:T(128)S(6)} %copy.81, f32[256]{0:T(256)S(1)} %get-tuple-element.614, f32[512]{0:T(512)S(1)} %bitcast.97), kind=kOutput, calls=%fused_computation.32.clone.1 | convolution fusion | flops 269090304 | bytes 1577988 | tf_op jit(solution)/shard_map/distance_min/while/body/eval_jaxpr/dot_general | solution.py:21
  123.8 16.8 %while.54 = (s32[]{:T(128)}, f32[6,512]{1,0:T(8,128)S(1)}, f32[6,512]{1,0:T(8,128)S(1)}, f32[6,512]{1,0:T(8,128)S(1)}, f32[1024]{0:T(1024)S(1)}, /*index=5*/bf16...) while((s32[]{:T(128)}, f32[6,512]{1,0:T(8,128)S(1)}, ...), condition=%wide.region_14.15_spmd, body=%wide.region_12.14_spmd.sunk | while | flops 1076363264 | bytes 3168373 | solution.py:27
  123.8 2.7 %maximum_reduce_fusion.2 = f32[512]{0:T(512)S(1)} fusion(bf16[1024,1024]{1,0:T(8,128)(2,1)S(1)} %get-tuple-element.643, bf16[6,512,1024]{2,1,0:T(8,128)(2,1)} %get-tuple-element.642, s32[]{:T(128)S(6)} %copy.90, f32[1024]{0:T(1024)S(1)} %get-tuple-element.641, f32[512]{0:T(512)S(1)} %bitcast.98), kind=kOutput, calls=%fused_computation.38.clone.1 | convolution fusion | flops 1076362752 | bytes 3153924 | tf_op jit(solution)/shard_map/distance_min/while/body/eval_jaxpr/dot_general | solution.py:21
  126.6 2.7 %maximum_reduce_fusion.2 = f32[512]{0:T(512)S(1)} fusion(bf16[1024,1024]{1,0:T(8,128)(2,1)S(1)} %get-tuple-element.643, bf16[6,512,1024]{2,1,0:T(8,128)(2,1)} %get-tuple-element.642, s32[]{:T(128)S(6)} %copy.90, f32[1024]{0:T(1024)S(1)} %get-tuple-element.641, f32[512]{0:T(512)S(1)} %bitcast.98), kind=kOutput, calls=%fused_computation.38.clone.1 | convolution fusion | flops 1076362752 | bytes 3153924 | tf_op jit(solution)/shard_map/distance_min/while/body/eval_jaxpr/dot_general | solution.py:21
  129.4 2.7 %maximum_reduce_fusion.2 = f32[512]{0:T(512)S(1)} fusion(bf16[1024,1024]{1,0:T(8,128)(2,1)S(1)} %get-tuple-element.643, bf16[6,512,1024]{2,1,0:T(8,128)(2,1)} %get-tuple-element.642, s32[]{:T(128)S(6)} %copy.90, f32[1024]{0:T(1024)S(1)} %get-tuple-element.641, f32[512]{0:T(512)S(1)} %bitcast.98), kind=kOutput, calls=%fused_computation.38.clone.1 | convolution fusion | flops 1076362752 | bytes 3153924 | tf_op jit(solution)/shard_map/distance_min/while/body/eval_jaxpr/dot_general | solution.py:21
  132.2 2.7 %maximum_reduce_fusion.2 = f32[512]{0:T(512)S(1)} fusion(bf16[1024,1024]{1,0:T(8,128)(2,1)S(1)} %get-tuple-element.643, bf16[6,512,1024]{2,1,0:T(8,128)(2,1)} %get-tuple-element.642, s32[]{:T(128)S(6)} %copy.90, f32[1024]{0:T(1024)S(1)} %get-tuple-element.641, f32[512]{0:T(512)S(1)} %bitcast.98), kind=kOutput, calls=%fused_computation.38.clone.1 | convolution fusion | flops 1076362752 | bytes 3153924 | tf_op jit(solution)/shard_map/distance_min/while/body/eval_jaxpr/dot_general | solution.py:21
  135.0 2.7 %maximum_reduce_fusion.2 = f32[512]{0:T(512)S(1)} fusion(bf16[1024,1024]{1,0:T(8,128)(2,1)S(1)} %get-tuple-element.643, bf16[6,512,1024]{2,1,0:T(8,128)(2,1)} %get-tuple-element.642, s32[]{:T(128)S(6)} %copy.90, f32[1024]{0:T(1024)S(1)} %get-tuple-element.641, f32[512]{0:T(512)S(1)} %bitcast.98), kind=kOutput, calls=%fused_computation.38.clone.1 | convolution fusion | flops 1076362752 | bytes 3153924 | tf_op jit(solution)/shard_map/distance_min/while/body/eval_jaxpr/dot_general | solution.py:21
  137.8 2.7 %maximum_reduce_fusion.2 = f32[512]{0:T(512)S(1)} fusion(bf16[1024,1024]{1,0:T(8,128)(2,1)S(1)} %get-tuple-element.643, bf16[6,512,1024]{2,1,0:T(8,128)(2,1)} %get-tuple-element.642, s32[]{:T(128)S(6)} %copy.90, f32[1024]{0:T(1024)S(1)} %get-tuple-element.641, f32[512]{0:T(512)S(1)} %bitcast.98), kind=kOutput, calls=%fused_computation.38.clone.1 | convolution fusion | flops 1076362752 | bytes 3153924 | tf_op jit(solution)/shard_map/distance_min/while/body/eval_jaxpr/dot_general | solution.py:21
  (167 shorter events, 48.1 us)
Async XLA Ops:
  6.7 9.5 %copy-start.1 = (s32[1,256]{1,0:T(1,128)S(1)}, s32[1,256]{1,0:T(1,128)}, u32[]{:S(2)}) copy-start(s32[1,256]{1,0:T(1,128)} %param.16) | copy-start | bytes 3076
  7.6 20.1 %all-to-all-start = ((bf16[32,8,1024]{2,1,0:T(8,128)(2,1)}), bf16[32,8,1024]{2,1,0:T(8,128)(2,1)S(1)}, u32[]{:S(2)}, u32[]{:S(2)}) async-start(bf16[32,8,1024]{2,1,0:T(8,128)(2,1)} %bitcast_select_fusion), calls=%async_computation | async-start | bytes 1048576 | tf_op jit(solution)/shard_map/compact_centers/all_to_all | solution.py:87
  29.0 6.4 %collective-permute-start.1 = (bf16[8,1024]{1,0:T(8,128)(2,1)S(1)}, bf16[8,1024]{1,0:T(8,128)(2,1)S(1)}, u32[]{:S(2)}, u32[]{:S(2)}) collective-permute-start(bf16[8,1024]{1,0:T(8,128)(2,1)S(1)} %get-tuple-element.266), channel_id=1, source_target_pairs={{0,224},{32,0},{64,32},{96,64},{128,96},{160,128},{192,160},{224,1... | collective-permute-start | bytes 49160 | tf_op jit(solution)/shard_map/spread_centers/ppermute | solution.py:94
  34.6 3.8 %collective-permute-start = (bf16[8,1024]{1,0:T(8,128)(2,1)S(1)}, bf16[8,1024]{1,0:T(8,128)(2,1)S(1)}, u32[]{:S(2)}, u32[]{:S(2)}) collective-permute-start(bf16[8,1024]{1,0:T(8,128)(2,1)S(1)} %get-tuple-element.266), channel_id=1, source_target_pairs={{0,32},{32,64},{64,96},{96,128},{128,160},{160,192},{192,224},{224... | collective-permute-start | bytes 49160 | tf_op jit(solution)/shard_map/spread_centers/ppermute | solution.py:94
  35.4 4.2 %collective-permute-start.3 = (bf16[8,1024]{1,0:T(8,128)(2,1)S(1)}, bf16[8,1024]{1,0:T(8,128)(2,1)S(1)}, u32[]{:S(2)}, u32[]{:S(2)}) collective-permute-start(bf16[8,1024]{1,0:T(8,128)(2,1)S(1)} %collective-permute-done.1), channel_id=1, source_target_pairs={{0,224},{32,0},{64,32},{96,64},{128,96},{160,128},{192,160},{224,1... | collective-permute-start | bytes 49160 | tf_op jit(solution)/shard_map/spread_centers/ppermute | solution.py:94
  38.4 3.9 %collective-permute-start.2 = (bf16[8,1024]{1,0:T(8,128)(2,1)S(1)}, bf16[8,1024]{1,0:T(8,128)(2,1)S(1)}, u32[]{:S(2)}, u32[]{:S(2)}) collective-permute-start(bf16[8,1024]{1,0:T(8,128)(2,1)S(1)} %collective-permute-done), channel_id=1, source_target_pairs={{0,32},{32,64},{64,96},{96,128},{128,160},{160,192},{192,224},{224... | collective-permute-start | bytes 49160 | tf_op jit(solution)/shard_map/spread_centers/ppermute | solution.py:94
  39.6 7.1 %collective-permute-start.5 = (bf16[8,1024]{1,0:T(8,128)(2,1)S(1)}, bf16[8,1024]{1,0:T(8,128)(2,1)S(1)}, u32[]{:S(2)}, u32[]{:S(2)}) collective-permute-start(bf16[8,1024]{1,0:T(8,128)(2,1)S(1)} %collective-permute-done.3), channel_id=1, source_target_pairs={{0,224},{32,0},{64,32},{96,64},{128,96},{160,128},{192,160},{224,1... | collective-permute-start | bytes 49160 | tf_op jit(solution)/shard_map/spread_centers/ppermute | solution.py:94
  42.3 3.8 %collective-permute-start.4 = (bf16[8,1024]{1,0:T(8,128)(2,1)S(1)}, bf16[8,1024]{1,0:T(8,128)(2,1)S(1)}, u32[]{:S(2)}, u32[]{:S(2)}) collective-permute-start(bf16[8,1024]{1,0:T(8,128)(2,1)S(1)} %collective-permute-done.2), channel_id=1, source_target_pairs={{0,32},{32,64},{64,96},{96,128},{128,160},{160,192},{192,224},{224... | collective-permute-start | bytes 49160 | tf_op jit(solution)/shard_map/spread_centers/ppermute | solution.py:94
  46.1 3.8 %collective-permute-start.6 = (bf16[8,1024]{1,0:T(8,128)(2,1)S(1)}, bf16[8,1024]{1,0:T(8,128)(2,1)S(1)}, u32[]{:S(2)}, u32[]{:S(2)}) collective-permute-start(bf16[8,1024]{1,0:T(8,128)(2,1)S(1)} %collective-permute-done.4), channel_id=1, source_target_pairs={{0,32},{32,64},{64,96},{96,128},{128,160},{160,192},{192,224},{224... | collective-permute-start | bytes 49160 | tf_op jit(solution)/shard_map/spread_centers/ppermute | solution.py:94
  50.5 5.7 %copy-start = (f32[3072]{0:T(1024)S(1)}, f32[3072]{0:T(1024)}, u32[]{:S(2)}) copy-start(f32[3072]{0:T(1024)} %param.15) | copy-start | bytes 36868
  50.5 7.4 %collective-permute-start.8 = (bf16[64,1024]{1,0:T(8,128)(2,1)S(1)}, bf16[64,1024]{1,0:T(8,128)(2,1)S(1)}, u32[]{:S(2)}, u32[]{:S(2)}) collective-permute-start(bf16[64,1024]{1,0:T(8,128)(2,1)S(1)} %get-tuple-element.275), channel_id=1, source_target_pairs={{0,6},{1,7},{2,0},{3,1},{4,2},{5,3},{6,4},{7,5},{8,14},{9,15},{10,... | collective-permute-start | bytes 393224 | tf_op jit(solution)/shard_map/spread_centers/ppermute | solution.py:97
  52.1 5.0 %collective-permute-start.7 = (bf16[64,1024]{1,0:T(8,128)(2,1)S(1)}, bf16[64,1024]{1,0:T(8,128)(2,1)S(1)}, u32[]{:S(2)}, u32[]{:S(2)}) collective-permute-start(bf16[64,1024]{1,0:T(8,128)(2,1)S(1)} %get-tuple-element.275), channel_id=1, source_target_pairs={{0,2},{1,3},{2,4},{3,5},{4,6},{5,7},{6,0},{7,1},{8,10},{9,11},{10,... | collective-permute-start | bytes 393224 | tf_op jit(solution)/shard_map/spread_centers/ppermute | solution.py:97
  57.2 6.2 %collective-permute-start.9 = (bf16[64,1024]{1,0:T(8,128)(2,1)S(1)}, bf16[64,1024]{1,0:T(8,128)(2,1)S(1)}, u32[]{:S(2)}, u32[]{:S(2)}) collective-permute-start(bf16[64,1024]{1,0:T(8,128)(2,1)S(1)} %collective-permute-done.7), channel_id=1, source_target_pairs={{0,2},{1,3},{2,4},{3,5},{4,6},{5,7},{6,0},{7,1},{8,10},{9,11},{10,... | collective-permute-start | bytes 393224 | tf_op jit(solution)/shard_map/spread_centers/ppermute | solution.py:97
  65.3 25.5 %collective-permute-start.11 = (bf16[256,1024]{1,0:T(8,128)(2,1)}, bf16[256,1024]{1,0:T(8,128)(2,1)S(1)}, u32[]{:S(2)}, u32[]{:S(2)}) collective-permute-start(bf16[256,1024]{1,0:T(8,128)(2,1)} %get-tuple-element.517), channel_id=1, source_target_pairs={{0,24},{1,25},{2,26},{3,27},{4,28},{5,29},{6,30},{7,31},{8,0},{9,1... | collective-permute-start | bytes 1572872 | tf_op jit(solution)/shard_map/spread_centers/ppermute | solution.py:100
  66.3 12.6 %collective-permute-start.10 = (bf16[256,1024]{1,0:T(8,128)(2,1)}, bf16[256,1024]{1,0:T(8,128)(2,1)S(1)}, u32[]{:S(2)}, u32[]{:S(2)}) collective-permute-start(bf16[256,1024]{1,0:T(8,128)(2,1)} %get-tuple-element.517), channel_id=1, source_target_pairs={{0,8},{1,9},{2,10},{3,11},{4,12},{5,13},{6,14},{7,15},{8,16},{9,17... | collective-permute-start | bytes 1572872 | tf_op jit(solution)/shard_map/spread_centers/ppermute | solution.py:100
  90.2 13.6 %collective-permute-start.12 = (bf16[256,1024]{1,0:T(8,128)(2,1)S(1)}, bf16[256,1024]{1,0:T(8,128)(2,1)S(1)}, u32[]{:S(2)}, u32[]{:S(2)}) collective-permute-start(bf16[256,1024]{1,0:T(8,128)(2,1)S(1)} %get-tuple-element.654), channel_id=1, source_target_pairs={{0,8},{1,9},{2,10},{3,11},{4,12},{5,13},{6,14},{7,15},{8,16},{9,17... | collective-permute-start | bytes 1572872 | tf_op jit(solution)/shard_map/spread_centers/ppermute | solution.py:100
  104.6 18.7 %collective-permute-start.13 = (bf16[1024,1024]{1,0:T(8,128)(2,1)}, bf16[1024,1024]{1,0:T(8,128)(2,1)S(1)}, u32[]{:S(2)}, u32[]{:S(2)}) collective-permute-start(bf16[1024,1024]{1,0:T(8,128)(2,1)} %constant_dynamic-update-slice_fusion.19), channel_id=1, source_target_pairs={{0,1},{1,0},{2,3},{3,2},{4,5},{5,4},{6,7},{7,6},{8,9},{9,8},{10,11... | collective-permute-start | bytes 6291464 | tf_op jit(solution)/shard_map/spread_centers/ppermute | solution.py:110

commit v2 on v1

--- a/solution.py
+++ b/solution.py
@@ -103,16 +103,17 @@
     row_norm = jnp.einsum("rd,rd->r", pool, pool, preferred_element_type=jnp.float32)
 
     with jax.named_scope("spread_centers"):
-        z_all = jnp.concatenate(ring_gather(compact, Ring(grp_count, z_send)), axis=0)
-        x_all = jnp.concatenate(ring_gather(z_all, Ring(X_CHIPS, x_send)), axis=0)
-        y_parts = ring_gather(x_all, Ring(y_count, y_send))
-        half = jnp.concatenate(y_parts, axis=0)
+        z_all = jnp.concatenate(
+            [compact] + [z_send(compact, s) for s in range(1, grp_count)], axis=0
+        )
+        x_all = jnp.concatenate(
+            [z_all] + [x_send(z_all, s) for s in range(1, X_CHIPS)], axis=0
+        )
+        half = jnp.concatenate(ring_gather(x_all, Ring(y_count, y_send)), axis=0)
         other = lax.ppermute(half, "dev", [(d, d ^ 1) for d in range(dev_count)])
 
     with jax.named_scope("distance_min"):
-        running = nearest
-        for part in y_parts:
-            running = fold_chunk(pool, row_norm, running, part)
+        running = fold_chunk(pool, row_norm, nearest, half)
         running = fold_chunk(pool, row_norm, running, other)
     return running
 

time: 143 us -> 127 us (0.89); the launches traced: 141 us -> 127 us
  matrix products: 58.2 us -> 36.4 us
  waiting for transfers between devices: 22.4 us -> 27.5 us
  starting transfers between devices: 31.2 us -> 36.3 us
  local copies, waits for them, and re-layouts: 18.2 us -> 16.6 us
    dot_general x30 -> x12, matrix products: 58.2 us -> 36.4 us  [one_block(): lax.dot_general(block_rows, fragment, (((1,), (1,)), ((), ())), preferred...]
    ppermute x3, waiting for transfers between devices: 0.01 us -> 12.6 us  [y_send(): lax.ppermute(x, 'dev', [(d, y_step(d, s, dev_count)) for d in range(dev_c...]
    ppermute x7, waiting for transfers between devices: 5.41 us -> 0.02 us  [z_send(): lax.ppermute(x, 'grp', [(g, (g + s) % grp_count) for g in range(grp_count)])]
    ppermute x7, starting transfers between devices: 11.2 us -> 16.4 us  [z_send(): lax.ppermute(x, 'grp', [(g, (g + s) % grp_count) for g in range(grp_count)])]
    ppermute x3, waiting for transfers between devices: 5.61 us -> 3.49 us  [x_send(): lax.ppermute(x, 'dev', [(d, x_step(d, s, dev_count)) for d in range(dev_c...]
    ppermute x1, starting transfers between devices: 7.42 us -> 5.65 us  [shards(): other = lax.ppermute(half, 'dev', [(d, d ^ 1) for d in range(dev_count)])]
    unnamed x17 -> x16, local copies, waits for them, and re-layouts: 8.8 us -> 7.88 us
  transfers between devices with their start and end apart: 15 -> 15, of which waited for: 6 -> 5; matrix products, arithmetic and copies ran while one was open for 40% -> 27% of each run, Pallas kernels for 0% -> 0%
where the time goes in v2:
time: 127 us
  matrix products  36.4 us (29%)
  starting transfers between devices  36.3 us (29%)
  waiting for transfers between devices  27.5 us (22%)
  local copies, waits for them, and re-layouts  16.6 us (13%)
  other arithmetic  9.35 us (7%)
    dot_general x12, matrix products, one_block(): lax.dot_general(block_rows, fragment, (((1,), (1,)), ((), ())), preferred...  36.4 us
    ppermute x7, starting transfers between devices, z_send(): lax.ppermute(x, 'grp', [(g, (g + s) % grp_count) for g in range(grp_count)])  16.4 us
    ppermute x3, waiting for transfers between devices, y_send(): lax.ppermute(x, 'dev', [(d, y_step(d, s, dev_count)) for d in range(dev_c...  12.6 us
    all_to_all x1, waiting for transfers between devices, shards(): landed = lax.all_to_all(send_rows, 'dev', 0, 0, tiled=True)  11.4 us
    all_to_all x1, starting transfers between devices, shards(): landed = lax.all_to_all(send_rows, 'dev', 0, 0, tiled=True)  8.59 us
    unnamed x16, local copies, waits for them, and re-layouts  7.88 us
    ppermute x1, starting transfers between devices, shards(): other = lax.ppermute(half, 'dev', [(d, d ^ 1) for d in range(dev_count)])  5.65 us
    gather x1, local copies, waits for them, and re-layouts, shards(): jnp.take(pool, jnp.where(owners == my_index, offsets, 0), axis=0)  5.15 us
  transfers between devices with their start and end apart: 15, of which 5 were waited for; matrix products, arithmetic and copies ran while one was open for 27% of the time, Pallas kernels for 0%

profile of v2, /device:TPU:1, one launch (start us, length us, event | category | flops | bytes accessed | tf_op | source)
XLA Modules:
  0.0 126.7 jit_solution(2527890117689532816)
XLA Ops:
  1.5 5.2 %gather_fusion = bf16[256,1024]{1,0:T(8,128)(2,1)S(1)} fusion(bf16[3072,1024]{1,0:T(8,128)(2,1)} %param.8, s32[1024]{0:T(1024)S(1)} %pad_clamp_fusion.1), kind=kCustom, calls=%fused_computation | custom fusion | bytes 1049600 | tf_op jit(solution)/shard_map/compact_centers/jit(_take)/gather | solution.py:86
  6.7 0.9 bitcast_select_fusion
  7.6 8.6 %all-to-all-start = ((bf16[32,8,1024]{2,1,0:T(8,128)(2,1)}), bf16[32,8,1024]{2,1,0:T(8,128)(2,1)S(1)}, u32[]{:S(2)}, u32[]{:S(2)}) async-start(bf16[32,8,1024]{2,1,0:T(8,128)(2,1)} %bitcast_select_fusion), calls=%async_computation | async-start | bytes 1048576 | tf_op jit(solution)/shard_map/compact_centers/all_to_all | solution.py:87
  16.4 11.4 %all-to-all-done = bf16[32,8,1024]{2,1,0:T(8,128)(2,1)S(1)} async-done(((bf16[32,8,1024]{2,1,0:T(8,128)(2,1)}), bf16[32,8,1024]{2,1,0:T(8,128)(2,1)S(1)}, u32[]{:S(2)}, u32[]{:S(2)}) %all-to-all-start) | async-done | bytes 524320 | tf_op jit(solution)/shard_map/compact_centers/all_to_all | solution.py:87
  28.4 1.7 %collective-permute-start = (bf16[8,1024]{1,0:T(8,128)(2,1)S(1)}, bf16[8,1024]{1,0:T(8,128)(2,1)S(1)}, u32[]{:S(2)}, u32[]{:S(2)}) collective-permute-start(bf16[8,1024]{1,0:T(8,128)(2,1)S(1)} %get-tuple-element.110), channel_id=1, source_target_pairs={{0,32},{32,64},{64,96},{96,128},{128,160},{160,192},{192,224},{224... | collective-permute-start | bytes 49160 | tf_op jit(solution)/shard_map/spread_centers/ppermute | solution.py:94
  30.7 3.0 %collective-permute-start.1 = (bf16[8,1024]{1,0:T(8,128)(2,1)S(1)}, bf16[8,1024]{1,0:T(8,128)(2,1)S(1)}, u32[]{:S(2)}, u32[]{:S(2)}) collective-permute-start(bf16[8,1024]{1,0:T(8,128)(2,1)S(1)} %get-tuple-element.110), channel_id=1, source_target_pairs={{0,64},{32,96},{64,128},{96,160},{128,192},{160,224},{192,0},{224,... | collective-permute-start | bytes 49160 | tf_op jit(solution)/shard_map/spread_centers/ppermute | solution.py:94
  33.7 3.8 %collective-permute-start.2 = (bf16[8,1024]{1,0:T(8,128)(2,1)S(1)}, bf16[8,1024]{1,0:T(8,128)(2,1)S(1)}, u32[]{:S(2)}, u32[]{:S(2)}) collective-permute-start(bf16[8,1024]{1,0:T(8,128)(2,1)S(1)} %get-tuple-element.110), channel_id=1, source_target_pairs={{0,96},{32,128},{64,160},{96,192},{128,224},{160,0},{192,32},{224,... | collective-permute-start | bytes 49160 | tf_op jit(solution)/shard_map/spread_centers/ppermute | solution.py:94
  37.9 4.5 %collective-permute-start.4 = (bf16[8,1024]{1,0:T(8,128)(2,1)S(1)}, bf16[8,1024]{1,0:T(8,128)(2,1)S(1)}, u32[]{:S(2)}, u32[]{:S(2)}) collective-permute-start(bf16[8,1024]{1,0:T(8,128)(2,1)S(1)} %get-tuple-element.110), channel_id=1, source_target_pairs={{0,160},{32,192},{64,224},{96,0},{128,32},{160,64},{192,96},{224,1... | collective-permute-start | bytes 49160 | tf_op jit(solution)/shard_map/spread_centers/ppermute | solution.py:94
  42.3 2.4 %collective-permute-start.5 = (bf16[8,1024]{1,0:T(8,128)(2,1)S(1)}, bf16[8,1024]{1,0:T(8,128)(2,1)S(1)}, u32[]{:S(2)}, u32[]{:S(2)}) collective-permute-start(bf16[8,1024]{1,0:T(8,128)(2,1)S(1)} %get-tuple-element.110), channel_id=1, source_target_pairs={{0,192},{32,224},{64,0},{96,32},{128,64},{160,96},{192,128},{224,1... | collective-permute-start | bytes 49160 | tf_op jit(solution)/shard_map/spread_centers/ppermute | solution.py:94
  50.2 1.9 %collective-permute-start.8 = (bf16[64,1024]{1,0:T(8,128)(2,1)S(1)}, bf16[64,1024]{1,0:T(8,128)(2,1)S(1)}, u32[]{:S(2)}, u32[]{:S(2)}) collective-permute-start(bf16[64,1024]{1,0:T(8,128)(2,1)S(1)} %get-tuple-element.119), channel_id=1, source_target_pairs={{0,4},{1,5},{2,6},{3,7},{4,0},{5,1},{6,2},{7,3},{8,12},{9,13},{10,... | collective-permute-start | bytes 393224 | tf_op jit(solution)/shard_map/spread_centers/ppermute | solution.py:97
  52.6 2.8 %collective-permute-done.7 = bf16[64,1024]{1,0:T(8,128)(2,1)S(1)} collective-permute-done((bf16[64,1024]{1,0:T(8,128)(2,1)S(1)}, bf16[64,1024]{1,0:T(8,128)(2,1)S(1)}, u32[]{:S(2)}, u32[]{:S(2)}) %collective-permute-start.7) | collective-permute-done | bytes 131104 | tf_op jit(solution)/shard_map/spread_centers/ppermute | solution.py:97
  58.3 2.5 %collective-permute-start.11 = (bf16[256,1024]{1,0:T(8,128)(2,1)S(1)}, bf16[256,1024]{1,0:T(8,128)(2,1)S(1)}, u32[]{:S(2)}, u32[]{:S(2)}) collective-permute-start(bf16[256,1024]{1,0:T(8,128)(2,1)S(1)} %get-tuple-element.111), channel_id=1, source_target_pairs={{0,24},{1,25},{2,26},{3,27},{4,28},{5,29},{6,30},{7,31},{8,0},{9,1... | collective-permute-start | bytes 1572872 | tf_op jit(solution)/shard_map/spread_centers/ppermute | solution.py:100
  60.8 8.1 %collective-permute-done.10 = bf16[256,1024]{1,0:T(8,128)(2,1)S(1)} collective-permute-done((bf16[256,1024]{1,0:T(8,128)(2,1)S(1)}, bf16[256,1024]{1,0:T(8,128)(2,1)S(1)}, u32[]{:S(2)}, u32[]{:S(2)}) %collective-permute-start.10) | collective-permute-done | bytes 524320 | tf_op jit(solution)/shard_map/spread_centers/ppermute | solution.py:100
  68.9 4.1 %fusion.6 = f32[3072]{0:T(1024)S(1)} fusion(bf16[3072,1024]{1,0:T(8,128)(2,1)} %param.8), kind=kLoop, calls=%fused_computation.15 | loop fusion | flops 9434112 | bytes 6303744 | tf_op jit(solution)/shard_map/rd,rd->r/dot_general | solution.py:103
  73.9 0.9 constant_dynamic-update-slice_fusion.20
  74.7 4.5 %collective-permute-done.12 = bf16[256,1024]{1,0:T(8,128)(2,1)S(1)} collective-permute-done((bf16[256,1024]{1,0:T(8,128)(2,1)S(1)}, bf16[256,1024]{1,0:T(8,128)(2,1)S(1)}, u32[]{:S(2)}, u32[]{:S(2)}) %collective-permute-start.12) | collective-permute-done | bytes 524320 | tf_op jit(solution)/shard_map/spread_centers/ppermute | solution.py:100
  80.1 5.7 %collective-permute-start.13 = (bf16[1024,1024]{1,0:T(8,128)(2,1)}, bf16[1024,1024]{1,0:T(8,128)(2,1)S(1)}, u32[]{:S(2)}, u32[]{:S(2)}) collective-permute-start(bf16[1024,1024]{1,0:T(8,128)(2,1)} %constant_dynamic-update-slice_fusion.19), channel_id=1, source_target_pairs={{0,1},{1,0},{2,3},{3,2},{4,5},{5,4},{6,7},{7,6},{8,9},{9,8},{10,11... | collective-permute-start | bytes 6291464 | tf_op jit(solution)/shard_map/spread_centers/ppermute | solution.py:113
  85.8 2.1 %fusion.8 = f32[1024]{0:T(1024)S(1)} fusion(bf16[1024,1024]{1,0:T(8,128)(2,1)} %constant_dynamic-update-slice_fusion.19), kind=kLoop, calls=%fused_computation.19 | loop fusion | flops 3144704 | bytes 2101248 | tf_op jit(solution)/shard_map/distance_min/cd,cd->c/dot_general | solution.py:14
  87.8 21.0 %while.20 = (s32[]{:T(128)}, f32[6,512]{1,0:T(8,128)S(1)}, f32[6,512]{1,0:T(8,128)S(1)}, f32[6,512]{1,0:T(8,128)S(1)}, f32[1024]{0:T(1024)S(1)}, /*index=5*/bf16...) while((s32[]{:T(128)}, f32[6,512]{1,0:T(8,128)S(1)}, f32[6,512]{1,0:T(8,128)S(1)}, ...), condition=%wide.region_2.3_spmd, body=%wide.region_0.2_spmd.sunk | while | flops 1076363264 | bytes 3168873 | solution.py:27
  87.9 3.4 %maximum_reduce_fusion.4 = f32[512]{0:T(512)S(1)} fusion(bf16[1024,1024]{1,0:T(8,128)(2,1)} %get-tuple-element.250, bf16[6,512,1024]{2,1,0:T(8,128)(2,1)} %get-tuple-element.249, s32[]{:T(128)} %get-tuple-element.235, f32[1024]{0:T(1024)S(1)} %get-tuple-element.248, f32[512]{0:T(512)S(1)} %bitcast.49), kind=kOutput, calls=%fused_computation.2.clone.1 | convolution fusion | flops 1076362752 | bytes 3154432 | tf_op jit(solution)/shard_map/distance_min/while/body/eval_jaxpr/dot_general | solution.py:21
  91.4 3.4 %maximum_reduce_fusion.4 = f32[512]{0:T(512)S(1)} fusion(bf16[1024,1024]{1,0:T(8,128)(2,1)} %get-tuple-element.250, bf16[6,512,1024]{2,1,0:T(8,128)(2,1)} %get-tuple-element.249, s32[]{:T(128)} %get-tuple-element.235, f32[1024]{0:T(1024)S(1)} %get-tuple-element.248, f32[512]{0:T(512)S(1)} %bitcast.49), kind=kOutput, calls=%fused_computation.2.clone.1 | convolution fusion | flops 1076362752 | bytes 3154432 | tf_op jit(solution)/shard_map/distance_min/while/body/eval_jaxpr/dot_general | solution.py:21
  94.8 3.4 %maximum_reduce_fusion.4 = f32[512]{0:T(512)S(1)} fusion(bf16[1024,1024]{1,0:T(8,128)(2,1)} %get-tuple-element.250, bf16[6,512,1024]{2,1,0:T(8,128)(2,1)} %get-tuple-element.249, s32[]{:T(128)} %get-tuple-element.235, f32[1024]{0:T(1024)S(1)} %get-tuple-element.248, f32[512]{0:T(512)S(1)} %bitcast.49), kind=kOutput, calls=%fused_computation.2.clone.1 | convolution fusion | flops 1076362752 | bytes 3154432 | tf_op jit(solution)/shard_map/distance_min/while/body/eval_jaxpr/dot_general | solution.py:21
  98.3 3.4 %maximum_reduce_fusion.4 = f32[512]{0:T(512)S(1)} fusion(bf16[1024,1024]{1,0:T(8,128)(2,1)} %get-tuple-element.250, bf16[6,512,1024]{2,1,0:T(8,128)(2,1)} %get-tuple-element.249, s32[]{:T(128)} %get-tuple-element.235, f32[1024]{0:T(1024)S(1)} %get-tuple-element.248, f32[512]{0:T(512)S(1)} %bitcast.49), kind=kOutput, calls=%fused_computation.2.clone.1 | convolution fusion | flops 1076362752 | bytes 3154432 | tf_op jit(solution)/shard_map/distance_min/while/body/eval_jaxpr/dot_general | solution.py:21
  101.8 3.4 %maximum_reduce_fusion.4 = f32[512]{0:T(512)S(1)} fusion(bf16[1024,1024]{1,0:T(8,128)(2,1)} %get-tuple-element.250, bf16[6,512,1024]{2,1,0:T(8,128)(2,1)} %get-tuple-element.249, s32[]{:T(128)} %get-tuple-element.235, f32[1024]{0:T(1024)S(1)} %get-tuple-element.248, f32[512]{0:T(512)S(1)} %bitcast.49), kind=kOutput, calls=%fused_computation.2.clone.1 | convolution fusion | flops 1076362752 | bytes 3154432 | tf_op jit(solution)/shard_map/distance_min/while/body/eval_jaxpr/dot_general | solution.py:21
  105.3 3.4 %maximum_reduce_fusion.4 = f32[512]{0:T(512)S(1)} fusion(bf16[1024,1024]{1,0:T(8,128)(2,1)} %get-tuple-element.250, bf16[6,512,1024]{2,1,0:T(8,128)(2,1)} %get-tuple-element.249, s32[]{:T(128)} %get-tuple-element.235, f32[1024]{0:T(1024)S(1)} %get-tuple-element.248, f32[512]{0:T(512)S(1)} %bitcast.49), kind=kOutput, calls=%fused_computation.2.clone.1 | convolution fusion | flops 1076362752 | bytes 3154432 | tf_op jit(solution)/shard_map/distance_min/while/body/eval_jaxpr/dot_general | solution.py:21
  109.3 16.8 %while.21 = (s32[]{:T(128)}, f32[6,512]{1,0:T(8,128)S(1)}, f32[6,512]{1,0:T(8,128)S(1)}, f32[6,512]{1,0:T(8,128)S(1)}, f32[1024]{0:T(1024)S(1)}, /*index=5*/bf16...) while((s32[]{:T(128)}, f32[6,512]{1,0:T(8,128)S(1)}, ...), condition=%wide.region_5.6_spmd, body=%wide.region_3.5_spmd.sunk | while | flops 1076363264 | bytes 3168873 | solution.py:27
  109.4 2.7 %maximum_reduce_fusion.5 = f32[512]{0:T(512)S(1)} fusion(bf16[1024,1024]{1,0:T(8,128)(2,1)S(1)} %get-tuple-element.277, bf16[6,512,1024]{2,1,0:T(8,128)(2,1)} %get-tuple-element.276, s32[]{:T(128)} %get-tuple-element.262, f32[1024]{0:T(1024)S(1)} %get-tuple-element.275, f32[512]{0:T(512)S(1)} %bitcast.50), kind=kOutput, calls=%fused_computation.8.clone.1 | convolution fusion | flops 1076362752 | bytes 3154432 | tf_op jit(solution)/shard_map/distance_min/while/body/eval_jaxpr/dot_general | solution.py:21
  112.2 2.7 %maximum_reduce_fusion.5 = f32[512]{0:T(512)S(1)} fusion(bf16[1024,1024]{1,0:T(8,128)(2,1)S(1)} %get-tuple-element.277, bf16[6,512,1024]{2,1,0:T(8,128)(2,1)} %get-tuple-element.276, s32[]{:T(128)} %get-tuple-element.262, f32[1024]{0:T(1024)S(1)} %get-tuple-element.275, f32[512]{0:T(512)S(1)} %bitcast.50), kind=kOutput, calls=%fused_computation.8.clone.1 | convolution fusion | flops 1076362752 | bytes 3154432 | tf_op jit(solution)/shard_map/distance_min/while/body/eval_jaxpr/dot_general | solution.py:21
  115.0 2.7 %maximum_reduce_fusion.5 = f32[512]{0:T(512)S(1)} fusion(bf16[1024,1024]{1,0:T(8,128)(2,1)S(1)} %get-tuple-element.277, bf16[6,512,1024]{2,1,0:T(8,128)(2,1)} %get-tuple-element.276, s32[]{:T(128)} %get-tuple-element.262, f32[1024]{0:T(1024)S(1)} %get-tuple-element.275, f32[512]{0:T(512)S(1)} %bitcast.50), kind=kOutput, calls=%fused_computation.8.clone.1 | convolution fusion | flops 1076362752 | bytes 3154432 | tf_op jit(solution)/shard_map/distance_min/while/body/eval_jaxpr/dot_general | solution.py:21
  117.8 2.7 %maximum_reduce_fusion.5 = f32[512]{0:T(512)S(1)} fusion(bf16[1024,1024]{1,0:T(8,128)(2,1)S(1)} %get-tuple-element.277, bf16[6,512,1024]{2,1,0:T(8,128)(2,1)} %get-tuple-element.276, s32[]{:T(128)} %get-tuple-element.262, f32[1024]{0:T(1024)S(1)} %get-tuple-element.275, f32[512]{0:T(512)S(1)} %bitcast.50), kind=kOutput, calls=%fused_computation.8.clone.1 | convolution fusion | flops 1076362752 | bytes 3154432 | tf_op jit(solution)/shard_map/distance_min/while/body/eval_jaxpr/dot_general | solution.py:21
  120.6 2.7 %maximum_reduce_fusion.5 = f32[512]{0:T(512)S(1)} fusion(bf16[1024,1024]{1,0:T(8,128)(2,1)S(1)} %get-tuple-element.277, bf16[6,512,1024]{2,1,0:T(8,128)(2,1)} %get-tuple-element.276, s32[]{:T(128)} %get-tuple-element.262, f32[1024]{0:T(1024)S(1)} %get-tuple-element.275, f32[512]{0:T(512)S(1)} %bitcast.50), kind=kOutput, calls=%fused_computation.8.clone.1 | convolution fusion | flops 1076362752 | bytes 3154432 | tf_op jit(solution)/shard_map/distance_min/while/body/eval_jaxpr/dot_general | solution.py:21
  123.3 2.7 %maximum_reduce_fusion.5 = f32[512]{0:T(512)S(1)} fusion(bf16[1024,1024]{1,0:T(8,128)(2,1)S(1)} %get-tuple-element.277, bf16[6,512,1024]{2,1,0:T(8,128)(2,1)} %get-tuple-element.276, s32[]{:T(128)} %get-tuple-element.262, f32[1024]{0:T(1024)S(1)} %get-tuple-element.275, f32[512]{0:T(512)S(1)} %bitcast.50), kind=kOutput, calls=%fused_computation.8.clone.1 | convolution fusion | flops 1076362752 | bytes 3154432 | tf_op jit(solution)/shard_map/distance_min/while/body/eval_jaxpr/dot_general | solution.py:21
  (86 shorter events, 16.0 us)
Async XLA Ops:
  6.7 9.5 %copy-start.1 = (s32[1,256]{1,0:T(1,128)S(1)}, s32[1,256]{1,0:T(1,128)}, u32[]{:S(2)}) copy-start(s32[1,256]{1,0:T(1,128)} %param.10) | copy-start | bytes 3076
  7.6 20.1 %all-to-all-start = ((bf16[32,8,1024]{2,1,0:T(8,128)(2,1)}), bf16[32,8,1024]{2,1,0:T(8,128)(2,1)S(1)}, u32[]{:S(2)}, u32[]{:S(2)}) async-start(bf16[32,8,1024]{2,1,0:T(8,128)(2,1)} %bitcast_select_fusion), calls=%async_computation | async-start | bytes 1048576 | tf_op jit(solution)/shard_map/compact_centers/all_to_all | solution.py:87
  28.4 13.9 %collective-permute-start = (bf16[8,1024]{1,0:T(8,128)(2,1)S(1)}, bf16[8,1024]{1,0:T(8,128)(2,1)S(1)}, u32[]{:S(2)}, u32[]{:S(2)}) collective-permute-start(bf16[8,1024]{1,0:T(8,128)(2,1)S(1)} %get-tuple-element.110), channel_id=1, source_target_pairs={{0,32},{32,64},{64,96},{96,128},{128,160},{160,192},{192,224},{224... | collective-permute-start | bytes 49160 | tf_op jit(solution)/shard_map/spread_centers/ppermute | solution.py:94
  30.7 14.7 %collective-permute-start.1 = (bf16[8,1024]{1,0:T(8,128)(2,1)S(1)}, bf16[8,1024]{1,0:T(8,128)(2,1)S(1)}, u32[]{:S(2)}, u32[]{:S(2)}) collective-permute-start(bf16[8,1024]{1,0:T(8,128)(2,1)S(1)} %get-tuple-element.110), channel_id=1, source_target_pairs={{0,64},{32,96},{64,128},{96,160},{128,192},{160,224},{192,0},{224,... | collective-permute-start | bytes 49160 | tf_op jit(solution)/shard_map/spread_centers/ppermute | solution.py:94
  33.7 13.0 %collective-permute-start.2 = (bf16[8,1024]{1,0:T(8,128)(2,1)S(1)}, bf16[8,1024]{1,0:T(8,128)(2,1)S(1)}, u32[]{:S(2)}, u32[]{:S(2)}) collective-permute-start(bf16[8,1024]{1,0:T(8,128)(2,1)S(1)} %get-tuple-element.110), channel_id=1, source_target_pairs={{0,96},{32,128},{64,160},{96,192},{128,224},{160,0},{192,32},{224,... | collective-permute-start | bytes 49160 | tf_op jit(solution)/shard_map/spread_centers/ppermute | solution.py:94
  37.4 9.9 %collective-permute-start.3 = (bf16[8,1024]{1,0:T(8,128)(2,1)S(1)}, bf16[8,1024]{1,0:T(8,128)(2,1)S(1)}, u32[]{:S(2)}, u32[]{:S(2)}) collective-permute-start(bf16[8,1024]{1,0:T(8,128)(2,1)S(1)} %get-tuple-element.110), channel_id=1, source_target_pairs={{0,128},{32,160},{64,192},{96,224},{128,0},{160,32},{192,64},{224,... | collective-permute-start | bytes 49160 | tf_op jit(solution)/shard_map/spread_centers/ppermute | solution.py:94
  37.9 10.0 %collective-permute-start.4 = (bf16[8,1024]{1,0:T(8,128)(2,1)S(1)}, bf16[8,1024]{1,0:T(8,128)(2,1)S(1)}, u32[]{:S(2)}, u32[]{:S(2)}) collective-permute-start(bf16[8,1024]{1,0:T(8,128)(2,1)S(1)} %get-tuple-element.110), channel_id=1, source_target_pairs={{0,160},{32,192},{64,224},{96,0},{128,32},{160,64},{192,96},{224,1... | collective-permute-start | bytes 49160 | tf_op jit(solution)/shard_map/spread_centers/ppermute | solution.py:94
  42.3 6.1 %collective-permute-start.5 = (bf16[8,1024]{1,0:T(8,128)(2,1)S(1)}, bf16[8,1024]{1,0:T(8,128)(2,1)S(1)}, u32[]{:S(2)}, u32[]{:S(2)}) collective-permute-start(bf16[8,1024]{1,0:T(8,128)(2,1)S(1)} %get-tuple-element.110), channel_id=1, source_target_pairs={{0,192},{32,224},{64,0},{96,32},{128,64},{160,96},{192,128},{224,1... | collective-permute-start | bytes 49160 | tf_op jit(solution)/shard_map/spread_centers/ppermute | solution.py:94
  45.3 3.8 %collective-permute-start.6 = (bf16[8,1024]{1,0:T(8,128)(2,1)S(1)}, bf16[8,1024]{1,0:T(8,128)(2,1)S(1)}, u32[]{:S(2)}, u32[]{:S(2)}) collective-permute-start(bf16[8,1024]{1,0:T(8,128)(2,1)S(1)} %get-tuple-element.110), channel_id=1, source_target_pairs={{0,224},{32,0},{64,32},{96,64},{128,96},{160,128},{192,160},{224,1... | collective-permute-start | bytes 49160 | tf_op jit(solution)/shard_map/spread_centers/ppermute | solution.py:94
  49.7 5.8 %collective-permute-start.7 = (bf16[64,1024]{1,0:T(8,128)(2,1)S(1)}, bf16[64,1024]{1,0:T(8,128)(2,1)S(1)}, u32[]{:S(2)}, u32[]{:S(2)}) collective-permute-start(bf16[64,1024]{1,0:T(8,128)(2,1)S(1)} %get-tuple-element.119), channel_id=1, source_target_pairs={{0,2},{1,3},{2,4},{3,5},{4,6},{5,7},{6,0},{7,1},{8,10},{9,11},{10,... | collective-permute-start | bytes 393224 | tf_op jit(solution)/shard_map/spread_centers/ppermute | solution.py:97
  50.2 6.6 %collective-permute-start.8 = (bf16[64,1024]{1,0:T(8,128)(2,1)S(1)}, bf16[64,1024]{1,0:T(8,128)(2,1)S(1)}, u32[]{:S(2)}, u32[]{:S(2)}) collective-permute-start(bf16[64,1024]{1,0:T(8,128)(2,1)S(1)} %get-tuple-element.119), channel_id=1, source_target_pairs={{0,4},{1,5},{2,6},{3,7},{4,0},{5,1},{6,2},{7,3},{8,12},{9,13},{10,... | collective-permute-start | bytes 393224 | tf_op jit(solution)/shard_map/spread_centers/ppermute | solution.py:97
  52.2 5.3 %collective-permute-start.9 = (bf16[64,1024]{1,0:T(8,128)(2,1)S(1)}, bf16[64,1024]{1,0:T(8,128)(2,1)S(1)}, u32[]{:S(2)}, u32[]{:S(2)}) collective-permute-start(bf16[64,1024]{1,0:T(8,128)(2,1)S(1)} %get-tuple-element.119), channel_id=1, source_target_pairs={{0,6},{1,7},{2,0},{3,1},{4,2},{5,3},{6,4},{7,5},{8,14},{9,15},{10,... | collective-permute-start | bytes 393224 | tf_op jit(solution)/shard_map/spread_centers/ppermute | solution.py:97
  58.1 10.8 %collective-permute-start.10 = (bf16[256,1024]{1,0:T(8,128)(2,1)S(1)}, bf16[256,1024]{1,0:T(8,128)(2,1)S(1)}, u32[]{:S(2)}, u32[]{:S(2)}) collective-permute-start(bf16[256,1024]{1,0:T(8,128)(2,1)S(1)} %get-tuple-element.111), channel_id=1, source_target_pairs={{0,8},{1,9},{2,10},{3,11},{4,12},{5,13},{6,14},{7,15},{8,16},{9,17... | collective-permute-start | bytes 1572872 | tf_op jit(solution)/shard_map/spread_centers/ppermute | solution.py:100
  58.3 14.7 %copy-start = (f32[3072]{0:T(1024)S(1)}, f32[3072]{0:T(1024)}, u32[]{:S(2)}) copy-start(f32[3072]{0:T(1024)} %param.9) | copy-start | bytes 36868
  58.3 15.5 %collective-permute-start.11 = (bf16[256,1024]{1,0:T(8,128)(2,1)S(1)}, bf16[256,1024]{1,0:T(8,128)(2,1)S(1)}, u32[]{:S(2)}, u32[]{:S(2)}) collective-permute-start(bf16[256,1024]{1,0:T(8,128)(2,1)S(1)} %get-tuple-element.111), channel_id=1, source_target_pairs={{0,24},{1,25},{2,26},{3,27},{4,28},{5,29},{6,30},{7,31},{8,0},{9,1... | collective-permute-start | bytes 1572872 | tf_op jit(solution)/shard_map/spread_centers/ppermute | solution.py:100
  68.9 10.4 %collective-permute-start.12 = (bf16[256,1024]{1,0:T(8,128)(2,1)S(1)}, bf16[256,1024]{1,0:T(8,128)(2,1)S(1)}, u32[]{:S(2)}, u32[]{:S(2)}) collective-permute-start(bf16[256,1024]{1,0:T(8,128)(2,1)S(1)} %collective-permute-done.10), channel_id=1, source_target_pairs={{0,8},{1,9},{2,10},{3,11},{4,12},{5,13},{6,14},{7,15},{8,16},{9,17... | collective-permute-start | bytes 1572872 | tf_op jit(solution)/shard_map/spread_centers/ppermute | solution.py:100
  80.1 28.7 %collective-permute-start.13 = (bf16[1024,1024]{1,0:T(8,128)(2,1)}, bf16[1024,1024]{1,0:T(8,128)(2,1)S(1)}, u32[]{:S(2)}, u32[]{:S(2)}) collective-permute-start(bf16[1024,1024]{1,0:T(8,128)(2,1)} %constant_dynamic-update-slice_fusion.19), channel_id=1, source_target_pairs={{0,1},{1,0},{2,3},{3,2},{4,5},{5,4},{6,7},{7,6},{8,9},{9,8},{10,11... | collective-permute-start | bytes 6291464 | tf_op jit(solution)/shard_map/spread_centers/ppermute | solution.py:113

commit v3 on v2

v3 whole, which is shorter than its diff:
```python
import math

import jax
import jax.numpy as jnp
from jax import lax
from jax.sharding import Mesh, PartitionSpec as P

MOST = 32
X_CHIPS = 4
CORES = 2


def fold_chunk(pool_rows, row_norm, running, fragment):
    center_norm = jnp.einsum("cd,cd->c", fragment, fragment, preferred_element_type=jnp.float32)
    total_rows = pool_rows.shape[0]
    block = total_rows
    blocks = total_rows // block

    def one_block(args):
        block_rows, block_norm, block_near = args
        inner = lax.dot_general(
            block_rows, fragment, (((1,), (1,)), ((), ())), preferred_element_type=jnp.float32
        )
        distance = jnp.maximum(block_norm[:, None] + center_norm[None, :] - 2.0 * inner, 0.0)
        return jnp.minimum(block_near, jnp.min(distance, axis=1))

    result = lax.map(
        one_block,
        (
            pool_rows.reshape(blocks, block, pool_rows.shape[1]),
            row_norm.reshape(blocks, block),
            running.reshape(blocks, block),
        ),
    )
    return result.reshape(total_rows)


def ring_gather(block, send, size):
    got = [block]
    fwd = block
    bwd = block
    for _ in range((size - 1) // 2):
        fwd = send(fwd, 1)
        bwd = send(bwd, -1)
        got += [fwd, bwd]
    if size % 2 == 0:
        fwd = send(fwd, 1)
        got.append(fwd)
    return got


def replicate_gather(x, axes, count):
    copies = jnp.broadcast_to(x[None], (count,) + x.shape)
    got = lax.all_to_all(copies, axes, 0, 0, tiled=True)
    return got.reshape((count * x.shape[0],) + x.shape[1:])


DEV_AXES = ("y", "x", "c")


def shards(pool, nearest, center_owner, center_offset):
    owners = center_owner[0]
    offsets = center_offset[0]
    dev_count = lax.axis_size(DEV_AXES)
    z_count = lax.axis_size("z")
    x_count = lax.axis_size("x")
    y_count = lax.axis_size("y")
    my_index = lax.axis_index(DEV_AXES)
    per_device = owners.shape[0] // dev_count

    with jax.named_scope("compact_centers"):
        send_rows = jnp.take(pool, jnp.where(owners == my_index, offsets, 0), axis=0)
        landed = lax.all_to_all(send_rows, DEV_AXES, 0, 0, tiled=True)
        mine = lax.dynamic_slice_in_dim(owners, my_index * per_device, per_device)
        compact = jnp.take(
            landed, mine * per_device + jnp.arange(per_device, dtype=jnp.int32), axis=0
        )

    def y_send(x, s):
        return lax.ppermute(x, "y", [(i, (i + s) % y_count) for i in range(y_count)])

    row_norm = jnp.einsum("rd,rd->r", pool, pool, preferred_element_type=jnp.float32)

    with jax.named_scope("spread_centers"):
        z_all = replicate_gather(compact, "z", z_count)
        x_all = replicate_gather(z_all, "x", x_count)
        half = jnp.concatenate(ring_gather(x_all, y_send, y_count), axis=0)
        other = lax.ppermute(half, "c", [(0, 1), (1, 0)])

    with jax.named_scope("distance_min"):
        running = fold_chunk(pool, row_norm, nearest, half)
        running = fold_chunk(pool, row_norm, running, other)
    return running


def solution(mesh):
    grp_count = mesh.shape["grp"]
    dev_count = mesh.shape["dev"]
    y_count = dev_count // (X_CHIPS * CORES)
    torus = Mesh(mesh.devices.reshape(grp_count, y_count, X_CHIPS, CORES), ("z",) + DEV_AXES)
    rows = ("z",) + DEV_AXES
    in_specs = (P(rows, None), P(rows), P("z", None), P("z", None))
    out_specs = P(rows)
    return jax.shard_map(shards, mesh=torus, in_specs=in_specs, out_specs=out_specs, check_vma=False)
```

time: 127 us -> 103 us (0.81)
  blocking collectives: 0 us -> 28.8 us
  matrix products: 36.4 us -> 15.1 us
  starting transfers between devices: 36.3 us -> 15.2 us
  local copies, waits for them, and re-layouts: 16.6 us -> 5.88 us
  waiting for transfers between devices: 27.5 us -> 29.2 us
    all_to_all x0 -> x2, blocking collectives: none -> 28.8 us  [replicate_gather(): got = lax.all_to_all(copies, axes, 0, 0, tiled=True)]
    dot_general x12 -> x2, matrix products: 36.4 us -> 15.1 us  [one_block(): lax.dot_general(block_rows, fragment, (((1,), (1,)), ((), ())), preferred...]
    ppermute x14 -> x4, starting transfers between devices: 27.7 us -> 6.64 us  [the longest x1 3.96 us: shards(): other = lax.ppermute(half, 'c', [(0, 1), (1, 0)])]
    unnamed x16 -> x8, local copies, waits for them, and re-layouts: 7.88 us -> 0.02 us
    ppermute x14 -> x4, waiting for transfers between devices: 16.1 us -> 17.9 us  [the longest x3 17.9 us: y_send(): lax.ppermute(x, 'y', [(i, (i + s) % y_count) for i in range(y_count)])]
    concatenate x2 -> x0, local copies, waits for them, and re-layouts: 1.5 us -> none  [the longest x1 0.83 us: shards(): half = jnp.concatenate(ring_gather(x_all, Ring(y_count, y_send)), axis=0)]
    dot_general x2, other arithmetic: 2.54 us -> 1.09 us  [fold_chunk(): jnp.einsum('cd,cd->c', fragment, fragment, preferred_element_type=jnp.flo...]
  transfers between devices with their start and end apart: 15 -> 5, of which waited for: 5 -> 3; matrix products, arithmetic and copies ran while one was open for 27% -> 11% of each run, Pallas kernels for 0% -> 0%
where the time goes in v3:
time: 103 us
  waiting for transfers between devices  29.2 us (28%)
  blocking collectives  28.8 us (28%)
  starting transfers between devices  15.2 us (15%)
  matrix products  15.1 us (15%)
  other arithmetic  8.41 us (8%)
  local copies, waits for them, and re-layouts  5.88 us (6%)
    all_to_all x2, blocking collectives, replicate_gather(): got = lax.all_to_all(copies, axes, 0, 0, tiled=True)  28.8 us
    ppermute x3, waiting for transfers between devices, y_send(): lax.ppermute(x, 'y', [(i, (i + s) % y_count) for i in range(y_count)])  17.9 us
    dot_general x2, matrix products, one_block(): lax.dot_general(block_rows, fragment, (((1,), (1,)), ((), ())), preferred...  15.1 us
    all_to_all x1, waiting for transfers between devices, shards(): landed = lax.all_to_all(send_rows, DEV_AXES, 0, 0, tiled=True)  11.4 us
    all_to_all x1, starting transfers between devices, shards(): landed = lax.all_to_all(send_rows, DEV_AXES, 0, 0, tiled=True)  8.59 us
    gather x1, local copies, waits for them, and re-layouts, shards(): jnp.take(pool, jnp.where(owners == my_index, offsets, 0), axis=0)  5.15 us
    dot_general x1, other arithmetic, shards(): jnp.einsum('rd,rd->r', pool, pool, preferred_element_type=jnp.float32)  4.08 us
    ppermute x1, starting transfers between devices, shards(): other = lax.ppermute(half, 'c', [(0, 1), (1, 0)])  3.96 us
  transfers between devices with their start and end apart: 5, of which 3 were waited for; matrix products, arithmetic and copies ran while one was open for 11% of the time, Pallas kernels for 0%

profile of v3, /device:TPU:1, one launch (start us, length us, event | category | flops | bytes accessed | tf_op | source)
XLA Modules:
  0.0 102.8 jit_solution(7486223503998027290)
XLA Ops:
  0.0 0.8 compare_select_fusion.1
  0.8 0.7 fusion.8
  1.5 0.1 select_n.72
  1.6 5.2 %gather_fusion = bf16[256,1024]{1,0:T(8,128)(2,1)S(1)} fusion(bf16[3072,1024]{1,0:T(8,128)(2,1)} %param.4, s32[1024]{0:T(1024)S(1)} %pad_clamp_fusion.1), kind=kCustom, calls=%fused_computation | custom fusion | bytes 1049600 | tf_op jit(solution)/shard_map/compact_centers/jit(_take)/gather | solution.py:72
  6.7 0.9 bitcast_select_fusion
  7.7 8.6 %all-to-all-start = ((bf16[32,8,1024]{2,1,0:T(8,128)(2,1)}), bf16[32,8,1024]{2,1,0:T(8,128)(2,1)S(1)}, u32[]{:S(2)}, u32[]{:S(2)}) async-start(bf16[32,8,1024]{2,1,0:T(8,128)(2,1)} %bitcast_select_fusion), calls=%async_computation | async-start | bytes 1048576 | tf_op jit(solution)/shard_map/compact_centers/all_to_all | solution.py:73
  16.2 0.0 copy-done.1
  16.3 0.1 fusion.7
  16.3 0.1 compare_and_fusion.1
  16.4 11.4 %all-to-all-done = bf16[32,8,1024]{2,1,0:T(8,128)(2,1)S(1)} async-done(((bf16[32,8,1024]{2,1,0:T(8,128)(2,1)}), bf16[32,8,1024]{2,1,0:T(8,128)(2,1)S(1)}, u32[]{:S(2)}, u32[]{:S(2)}) %all-to-all-start) | async-done | bytes 524320 | tf_op jit(solution)/shard_map/compact_centers/all_to_all | solution.py:73
  27.8 0.6 gather_fusion.1
  28.4 0.1 broadcast_select_fusion
  28.5 16.0 %all_to_all.19 = bf16[8,8,1024]{2,1,0:T(8,128)(2,1)S(1)} all-to-all(bf16[8,8,1024]{2,1,0:T(8,128)(2,1)S(1)} %broadcast_in_dim.61), channel_id=1, replica_groups=mesh['z'=8,'y'=4,'x'=4,'c'=2] {'z'}, dimensions={0} | all-to-all | bytes 262144 | tf_op jit(solution)/shard_map/spread_centers/all_to_all | solution.py:54
  44.6 12.8 %all_to_all.20 = bf16[4,64,1024]{2,1,0:T(8,128)(2,1)S(1)} all-to-all(bf16[4,64,1024]{2,1,0:T(8,128)(2,1)S(1)} %broadcast_in_dim.63), channel_id=1, replica_groups=mesh['z'=8,'y'=4,'x'=4,'c'=2] {'x'}, dimensions={0} | all-to-all | bytes 1048576 | tf_op jit(solution)/shard_map/spread_centers/all_to_all | solution.py:54
  57.3 0.3 collective-permute-start
  57.6 2.4 %collective-permute-start.1 = (bf16[256,1024]{1,0:T(8,128)(2,1)S(1)}, bf16[256,1024]{1,0:T(8,128)(2,1)S(1)}, u32[]{:S(2)}, u32[]{:S(2)}) collective-permute-start(bf16[256,1024]{1,0:T(8,128)(2,1)S(1)} %bitcast.37), channel_id=1, source_target_pairs={{0,24},{8,0},{16,8},{24,16},{1,25},{9,1},{17,9},{25,17},{2,26},{10... | collective-permute-start | bytes 1572872 | tf_op jit(solution)/shard_map/spread_centers/ppermute | solution.py:80
  60.0 10.1 %collective-permute-done = bf16[256,1024]{1,0:T(8,128)(2,1)S(1)} collective-permute-done((bf16[256,1024]{1,0:T(8,128)(2,1)S(1)}, bf16[256,1024]{1,0:T(8,128)(2,1)S(1)}, u32[]{:S(2)}, u32[]{:S(2)}) %collective-permute-start) | collective-permute-done | bytes 524320 | tf_op jit(solution)/shard_map/spread_centers/ppermute | solution.py:80
  70.1 0.0 collective-permute-start.2
  70.1 4.1 %fusion.4 = f32[3072]{0:T(1024)S(1)} fusion(bf16[3072,1024]{1,0:T(8,128)(2,1)} %param.4), kind=kLoop, calls=%fused_computation.9 | loop fusion | flops 9434112 | bytes 6303744 | tf_op jit(solution)/shard_map/rd,rd->r/dot_general | solution.py:82
  74.2 0.0 collective-permute-done.1
  74.2 7.8 %collective-permute-done.2 = bf16[256,1024]{1,0:T(8,128)(2,1)S(1)} collective-permute-done((bf16[256,1024]{1,0:T(8,128)(2,1)S(1)}, bf16[256,1024]{1,0:T(8,128)(2,1)S(1)}, u32[]{:S(2)}, u32[]{:S(2)}) %collective-permute-start.2) | collective-permute-done | bytes 524320 | tf_op jit(solution)/shard_map/spread_centers/ppermute | solution.py:80
  82.0 0.6 fusion.6
  82.6 4.0 %collective-permute-start.3 = (bf16[1024,1024]{1,0:T(8,128)(2,1)S(1)}, bf16[1024,1024]{1,0:T(8,128)(2,1)S(1)}, u32[]{:S(2)}, u32[]{:S(2)}) collective-permute-start(bf16[1024,1024]{1,0:T(8,128)(2,1)S(1)} %get-tuple-element.32), channel_id=1, source_target_pairs={{0,1},{1,0},{2,3},{3,2},{4,5},{5,4},{6,7},{7,6},{8,9},{9,8},{10,11... | collective-permute-start | bytes 6291464 | tf_op jit(solution)/shard_map/spread_centers/ppermute | solution.py:88
  86.5 0.0 slice-done
  86.5 0.0 slice-done.1
  86.5 7.6 %fusion.3 = f32[3072]{0:T(1024)S(1)} fusion(bf16[1024,1024]{1,0:T(8,128)(2,1)S(1)} %get-tuple-element.32, bf16[3072,1024]{1,0:T(8,128)(2,1)S(1)} %bitcast.35, f32[1024]{0:T(1024)S(1)} %get-tuple-element.31, f32[3072]{0:T(1024)S(1)} %fusion.4), kind=kOutput, calls=%fused_computation.7 | convolution fusion | flops 6458176512 | bytes 8417280 | tf_op jit(solution)/shard_map/distance_min/while/body/eval_jaxpr/dot_general | solution.py:21
  94.1 0.0 collective-permute-done.3
  94.1 0.5 fusion.5
  94.6 0.0 copy-start
  94.6 7.6 %fusion.1 = f32[3072]{0:T(1024)S(1)} fusion(bf16[1024,1024]{1,0:T(8,128)(2,1)S(1)} %collective-permute-done.3, bf16[3072,1024]{1,0:T(8,128)(2,1)S(1)} %bitcast.35, f32[1024]{0:T(1024)S(1)} %fusion.5, f32[3072]{0:T(1024)S(1)} %fusion.4), kind=kOutput, calls=%fused_computation.4 | convolution fusion | flops 6458176512 | bytes 8417280 | tf_op jit(solution)/shard_map/distance_min/while/body/eval_jaxpr/dot_general | solution.py:21
  102.2 0.0 copy-done
  102.2 0.6 minimum_minimum_fusion
  (9 shorter events, 0.1 us)
Async XLA Ops:
  0.0 16.3 %copy-start.1 = (s32[1,256]{1,0:T(1,128)S(1)}, s32[1,256]{1,0:T(1,128)}, u32[]{:S(2)}) copy-start(s32[1,256]{1,0:T(1,128)} %param.6) | copy-start | bytes 3076
  7.7 20.1 %all-to-all-start = ((bf16[32,8,1024]{2,1,0:T(8,128)(2,1)}), bf16[32,8,1024]{2,1,0:T(8,128)(2,1)S(1)}, u32[]{:S(2)}, u32[]{:S(2)}) async-start(bf16[32,8,1024]{2,1,0:T(8,128)(2,1)} %bitcast_select_fusion), calls=%async_computation | async-start | bytes 1048576 | tf_op jit(solution)/shard_map/compact_centers/all_to_all | solution.py:73
  28.4 58.1 %slice-start = ((s8[6291456]{0:T(1024)(128)(4,1)}), s8[4194304]{0:T(1024)(128)(4,1)S(1)}, s32[]{:S(2)}) async-start(s8[6291456]{0:T(1024)(128)(4,1)} %bitcast.34), calls=%async_computation.3 | async-start | bytes 8388608
  57.3 29.2 %slice-start.1 = ((s8[6291456]{0:T(1024)(128)(4,1)}), s8[2097152]{0:T(1024)(128)(4,1)S(1)}, s32[]{:S(2)}) async-start(s8[6291456]{0:T(1024)(128)(4,1)} %bitcast.34), calls=%async_computation.4 | async-start | bytes 4194304
  57.3 12.8 %collective-permute-start = (bf16[256,1024]{1,0:T(8,128)(2,1)S(1)}, bf16[256,1024]{1,0:T(8,128)(2,1)S(1)}, u32[]{:S(2)}, u32[]{:S(2)}) collective-permute-start(bf16[256,1024]{1,0:T(8,128)(2,1)S(1)} %bitcast.36), channel_id=1, source_target_pairs={{0,8},{8,16},{16,24},{24,0},{1,9},{9,17},{17,25},{25,1},{2,10},{10... | collective-permute-start | bytes 1572872 | tf_op jit(solution)/shard_map/spread_centers/ppermute | solution.py:80
  57.6 16.6 %collective-permute-start.1 = (bf16[256,1024]{1,0:T(8,128)(2,1)S(1)}, bf16[256,1024]{1,0:T(8,128)(2,1)S(1)}, u32[]{:S(2)}, u32[]{:S(2)}) collective-permute-start(bf16[256,1024]{1,0:T(8,128)(2,1)S(1)} %bitcast.37), channel_id=1, source_target_pairs={{0,24},{8,0},{16,8},{24,16},{1,25},{9,1},{17,9},{25,17},{2,26},{10... | collective-permute-start | bytes 1572872 | tf_op jit(solution)/shard_map/spread_centers/ppermute | solution.py:80
  70.1 11.9 %collective-permute-start.2 = (bf16[256,1024]{1,0:T(8,128)(2,1)S(1)}, bf16[256,1024]{1,0:T(8,128)(2,1)S(1)}, u32[]{:S(2)}, u32[]{:S(2)}) collective-permute-start(bf16[256,1024]{1,0:T(8,128)(2,1)S(1)} %collective-permute-done), channel_id=1, source_target_pairs={{0,8},{8,16},{16,24},{24,0},{1,9},{9,17},{17,25},{25,1},{2,10},{10... | collective-permute-start | bytes 1572872 | tf_op jit(solution)/shard_map/spread_centers/ppermute | solution.py:80
  82.6 11.6 %collective-permute-start.3 = (bf16[1024,1024]{1,0:T(8,128)(2,1)S(1)}, bf16[1024,1024]{1,0:T(8,128)(2,1)S(1)}, u32[]{:S(2)}, u32[]{:S(2)}) collective-permute-start(bf16[1024,1024]{1,0:T(8,128)(2,1)S(1)} %get-tuple-element.32), channel_id=1, source_target_pairs={{0,1},{1,0},{2,3},{3,2},{4,5},{5,4},{6,7},{7,6},{8,9},{9,8},{10,11... | collective-permute-start | bytes 6291464 | tf_op jit(solution)/shard_map/spread_centers/ppermute | solution.py:88
  94.6 7.6 %copy-start = (f32[3072]{0:T(1024)S(1)}, f32[3072]{0:T(1024)}, u32[]{:S(2)}) copy-start(f32[3072]{0:T(1024)} %param.5) | copy-start | bytes 36868

commit v4 on v3

--- a/solution.py
+++ b/solution.py
@@ -81,15 +81,20 @@
 
     row_norm = jnp.einsum("rd,rd->r", pool, pool, preferred_element_type=jnp.float32)
 
+    def core_swap(x):
+        return lax.ppermute(x, "c", [(0, 1), (1, 0)])
+
     with jax.named_scope("spread_centers"):
-        z_all = replicate_gather(compact, "z", z_count)
-        x_all = replicate_gather(z_all, "x", x_count)
-        half = jnp.concatenate(ring_gather(x_all, y_send, y_count), axis=0)
-        other = lax.ppermute(half, "c", [(0, 1), (1, 0)])
+        plane = replicate_gather(compact, ("z", "x"), z_count * x_count)
+        y_near = y_send(plane, 1), y_send(plane, -1)
+        y_far = y_send(y_near[0], 1)
+        near = jnp.concatenate(y_near, axis=0)
+        pieces = [plane, core_swap(plane), near, core_swap(near), y_far, core_swap(y_far)]
 
     with jax.named_scope("distance_min"):
-        running = fold_chunk(pool, row_norm, nearest, half)
-        running = fold_chunk(pool, row_norm, running, other)
+        running = nearest
+        for piece in pieces:
+            running = fold_chunk(pool, row_norm, running, piece)
     return running
 
 

time: 103 us -> 99.3 us (0.964)
  blocking collectives: 28.8 us -> 0 us
  waiting for transfers between devices: 29.2 us -> 40.1 us
  starting transfers between devices: 15.2 us -> 23.8 us
  matrix products: 15.1 us -> 19.5 us
    all_to_all x2 -> x0, blocking collectives: 28.8 us -> none  [replicate_gather(): got = lax.all_to_all(copies, axes, 0, 0, tiled=True)]
    all_to_all x0 -> x1, waiting for transfers between devices: none -> 12.7 us  [replicate_gather(): got = lax.all_to_all(copies, axes, 0, 0, tiled=True)]
    all_to_all x0 -> x1, starting transfers between devices: none -> 9.59 us  [replicate_gather(): got = lax.all_to_all(copies, axes, 0, 0, tiled=True)]
    dot_general x2 -> x6, matrix products: 15.1 us -> 19.5 us  [one_block(): lax.dot_general(block_rows, fragment, (((1,), (1,)), ((), ())), preferred...]
    ppermute x3, waiting for transfers between devices: 17.9 us -> 16 us  [y_send(): lax.ppermute(x, 'y', [(i, (i + s) % y_count) for i in range(y_count)])]
    ppermute x3, starting transfers between devices: 2.68 us -> 1.5 us  [y_send(): lax.ppermute(x, 'y', [(i, (i + s) % y_count) for i in range(y_count)])]
    ppermute x1 -> x3, starting transfers between devices: 3.96 us -> 4.15 us  [core_swap(): return lax.ppermute(x, 'c', [(0, 1), (1, 0)])]
  transfers between devices with their start and end apart: 5 -> 8, of which waited for: 3 -> 4; matrix products, arithmetic and copies ran while one was open for 11% -> 23% of each run, Pallas kernels for 0% -> 0%
where the time goes in v4:
time: 99.3 us; the launch traced here: 98.9 us
  waiting for transfers between devices  40.1 us (40%)
  starting transfers between devices  23.8 us (24%)
  matrix products  19.5 us (20%)
  other arithmetic  8.62 us (9%)
  local copies, waits for them, and re-layouts  6.74 us (7%)
    dot_general x6, matrix products, one_block(): lax.dot_general(block_rows, fragment, (((1,), (1,)), ((), ())), preferred...  19.5 us
    ppermute x3, waiting for transfers between devices, y_send(): lax.ppermute(x, 'y', [(i, (i + s) % y_count) for i in range(y_count)])  16 us
    all_to_all x1, waiting for transfers between devices, replicate_gather(): got = lax.all_to_all(copies, axes, 0, 0, tiled=True)  12.7 us
    all_to_all x1, waiting for transfers between devices, shards(): landed = lax.all_to_all(send_rows, DEV_AXES, 0, 0, tiled=True)  11.4 us
    all_to_all x1, starting transfers between devices, replicate_gather(): got = lax.all_to_all(copies, axes, 0, 0, tiled=True)  9.59 us
    all_to_all x1, starting transfers between devices, shards(): landed = lax.all_to_all(send_rows, DEV_AXES, 0, 0, tiled=True)  8.59 us
    gather x1, local copies, waits for them, and re-layouts, shards(): jnp.take(pool, jnp.where(owners == my_index, offsets, 0), axis=0)  5.15 us
    ppermute x3, starting transfers between devices, core_swap(): return lax.ppermute(x, 'c', [(0, 1), (1, 0)])  4.15 us
  transfers between devices with their start and end apart: 8, of which 4 were waited for; matrix products, arithmetic and copies ran while one was open for 23% of the time, Pallas kernels for 0%

profile of v4, /device:TPU:1, one launch (start us, length us, event | category | flops | bytes accessed | tf_op | source)
XLA Modules:
  0.0 98.9 jit_solution(16543988072423335912)
XLA Ops:
  0.0 0.8 compare_select_fusion.1
  0.8 0.7 fusion.20
  1.6 5.2 %gather_fusion = bf16[256,1024]{1,0:T(8,128)(2,1)S(1)} fusion(bf16[3072,1024]{1,0:T(8,128)(2,1)} %param.4, s32[1024]{0:T(1024)S(1)} %pad_clamp_fusion.1), kind=kCustom, calls=%fused_computation | custom fusion | bytes 1049600 | tf_op jit(solution)/shard_map/compact_centers/jit(_take)/gather | solution.py:72
  6.7 0.9 bitcast_select_fusion
  7.7 8.6 %all-to-all-start = ((bf16[32,8,1024]{2,1,0:T(8,128)(2,1)}), bf16[32,8,1024]{2,1,0:T(8,128)(2,1)S(1)}, u32[]{:S(2)}, u32[]{:S(2)}) async-start(bf16[32,8,1024]{2,1,0:T(8,128)(2,1)} %bitcast_select_fusion), calls=%async_computation | async-start | bytes 1048576 | tf_op jit(solution)/shard_map/compact_centers/all_to_all | solution.py:73
  16.3 0.1 fusion.18
  16.4 11.4 %all-to-all-done = bf16[32,8,1024]{2,1,0:T(8,128)(2,1)S(1)} async-done(((bf16[32,8,1024]{2,1,0:T(8,128)(2,1)}), bf16[32,8,1024]{2,1,0:T(8,128)(2,1)S(1)}, u32[]{:S(2)}, u32[]{:S(2)}) %all-to-all-start) | async-done | bytes 524320 | tf_op jit(solution)/shard_map/compact_centers/all_to_all | solution.py:73
  27.8 0.6 gather_fusion.1
  28.4 0.9 broadcast_in_dim.78
  29.3 9.6 %all-to-all-start.1 = ((bf16[32,8,1024]{2,1,0:T(8,128)(2,1)}), bf16[32,8,1024]{2,1,0:T(8,128)(2,1)S(1)}, u32[]{:S(2)}, u32[]{:S(2)}) async-start(bf16[32,8,1024]{2,1,0:T(8,128)(2,1)} %broadcast_in_dim.78), calls=%async_computation.1 | async-start | bytes 1048576 | tf_op jit(solution)/shard_map/spread_centers/all_to_all | solution.py:54
  38.9 4.1 %fusion = f32[3072]{0:T(1024)S(1)} fusion(bf16[3072,1024]{1,0:T(8,128)(2,1)} %param.4), kind=kLoop, calls=%fused_computation.3 | loop fusion | flops 9434112 | bytes 6303744 | tf_op jit(solution)/shard_map/rd,rd->r/dot_general | solution.py:82
  43.0 12.7 %all-to-all-done.1 = bf16[32,8,1024]{2,1,0:T(8,128)(2,1)S(1)} async-done(((bf16[32,8,1024]{2,1,0:T(8,128)(2,1)}), bf16[32,8,1024]{2,1,0:T(8,128)(2,1)S(1)}, u32[]{:S(2)}, u32[]{:S(2)}) %all-to-all-start.1) | async-done | bytes 524320 | tf_op jit(solution)/shard_map/spread_centers/all_to_all | solution.py:54
  55.7 1.9 %collective-permute-start = (bf16[256,1024]{1,0:T(8,128)(2,1)S(1)}, bf16[256,1024]{1,0:T(8,128)(2,1)S(1)}, u32[]{:S(2)}, u32[]{:S(2)}) collective-permute-start(bf16[256,1024]{1,0:T(8,128)(2,1)S(1)} %bitcast.65), channel_id=1, source_target_pairs={{0,1},{1,0},{2,3},{3,2},{4,5},{5,4},{6,7},{7,6},{8,9},{9,8},{10,11... | collective-permute-start | bytes 1572872 | tf_op jit(solution)/shard_map/spread_centers/ppermute | solution.py:85
  57.5 0.2 collective-permute-start.2
  57.8 1.2 %collective-permute-start.1 = (bf16[256,1024]{1,0:T(8,128)(2,1)S(1)}, bf16[256,1024]{1,0:T(8,128)(2,1)S(1)}, u32[]{:S(2)}, u32[]{:S(2)}) collective-permute-start(bf16[256,1024]{1,0:T(8,128)(2,1)S(1)} %bitcast.67), channel_id=1, source_target_pairs={{0,8},{8,16},{16,24},{24,0},{1,9},{9,17},{17,25},{25,1},{2,10},{10... | collective-permute-start | bytes 1572872 | tf_op jit(solution)/shard_map/spread_centers/ppermute | solution.py:80
  59.0 0.2 fusion.17
  59.2 5.0 %fusion.13 = f32[3072]{0:T(1024)S(1)} fusion(bf16[3072,1024]{1,0:T(8,128)(2,1)} %param.4, f32[256]{0:T(256)S(1)} %fusion.17, f32[3072]{0:T(1024)S(1)} %fusion, bf16[32,8,1024]{2,1,0:T(8,128)(2,1)S(1)} %all-to-all-done.1), kind=kOutput, calls=%fused_computation.27 | convolution fusion | flops 1614541824 | bytes 6841344 | tf_op jit(solution)/shard_map/distance_min/while/body/eval_jaxpr/dot_general | solution.py:21
  64.2 8.0 %collective-permute-done.1 = bf16[256,1024]{1,0:T(8,128)(2,1)S(1)} collective-permute-done((bf16[256,1024]{1,0:T(8,128)(2,1)S(1)}, bf16[256,1024]{1,0:T(8,128)(2,1)S(1)}, u32[]{:S(2)}, u32[]{:S(2)}) %collective-permute-start.1) | collective-permute-done | bytes 524320 | tf_op jit(solution)/shard_map/spread_centers/ppermute | solution.py:80
  72.3 0.3 fusion.12
  72.6 1.2 %collective-permute-start.3 = (bf16[512,1024]{1,0:T(8,128)(2,1)S(1)}, bf16[512,1024]{1,0:T(8,128)(2,1)S(1)}, u32[]{:S(2)}, u32[]{:S(2)}) collective-permute-start(bf16[512,1024]{1,0:T(8,128)(2,1)S(1)} %constant_dynamic-update-slice_fusion), channel_id=1, source_target_pairs={{0,1},{1,0},{2,3},{3,2},{4,5},{5,4},{6,7},{7,6},{8,9},{9,8},{10,11... | collective-permute-start | bytes 3145736 | tf_op jit(solution)/shard_map/spread_centers/ppermute | solution.py:85
  73.8 4.0 %fusion.4 = f32[3072]{0:T(1024)S(1)} fusion(bf16[512,1024]{1,0:T(8,128)(2,1)S(1)} %constant_dynamic-update-slice_fusion, bf16[3072,1024]{1,0:T(8,128)(2,1)S(1)} %bitcast.64, f32[512]{0:T(512)S(1)} %fusion.12, f32[3072]{0:T(1024)S(1)} %fusion), kind=kOutput, calls=%fused_computation.9 | convolution fusion | flops 3229086720 | bytes 7366656 | tf_op jit(solution)/shard_map/distance_min/while/body/eval_jaxpr/dot_general | solution.py:21
  77.9 0.2 fusion.16
  78.0 2.2 %maximum_reduce_fusion.2 = f32[3072]{0:T(1024)S(1)} fusion(f32[256]{0:T(256)S(1)} %fusion.16, f32[3072]{0:T(1024)S(1)} %fusion, bf16[256,1024]{1,0:T(8,128)(2,1)S(1)} %collective-permute-done, bf16[3072,1024]{1,0:T(8,128)(2,1)S(1)} %bitcast.64), kind=kOutput, calls=%fused_computation.22 | convolution fusion | flops 1614541824 | bytes 6841344 | tf_op jit(solution)/shard_map/distance_min/while/body/eval_jaxpr/dot_general | solution.py:21
  80.2 8.0 %collective-permute-done.4 = bf16[256,1024]{1,0:T(8,128)(2,1)S(1)} collective-permute-done((bf16[256,1024]{1,0:T(8,128)(2,1)S(1)}, bf16[256,1024]{1,0:T(8,128)(2,1)S(1)}, u32[]{:S(2)}, u32[]{:S(2)}) %collective-permute-start.4) | collective-permute-done | bytes 524320 | tf_op jit(solution)/shard_map/spread_centers/ppermute | solution.py:80
  88.2 1.1 %collective-permute-start.5 = (bf16[256,1024]{1,0:T(8,128)(2,1)S(1)}, bf16[256,1024]{1,0:T(8,128)(2,1)S(1)}, u32[]{:S(2)}, u32[]{:S(2)}) collective-permute-start(bf16[256,1024]{1,0:T(8,128)(2,1)S(1)} %collective-permute-done.4), channel_id=1, source_target_pairs={{0,1},{1,0},{2,3},{3,2},{4,5},{5,4},{6,7},{7,6},{8,9},{9,8},{10,11... | collective-permute-start | bytes 1572872 | tf_op jit(solution)/shard_map/spread_centers/ppermute | solution.py:85
  89.3 0.2 fusion.15
  89.5 2.1 %maximum_reduce_fusion.1 = f32[3072]{0:T(1024)S(1)} fusion(f32[256]{0:T(256)S(1)} %fusion.15, f32[3072]{0:T(1024)S(1)} %fusion, bf16[256,1024]{1,0:T(8,128)(2,1)S(1)} %collective-permute-done.4, bf16[3072,1024]{1,0:T(8,128)(2,1)S(1)} %bitcast.64), kind=kOutput, calls=%fused_computation.21 | convolution fusion | flops 1614541824 | bytes 6841344 | tf_op jit(solution)/shard_map/distance_min/while/body/eval_jaxpr/dot_general | solution.py:21
  91.7 0.3 fusion.11
  91.9 4.0 %fusion.2 = f32[3072]{0:T(1024)S(1)} fusion(bf16[512,1024]{1,0:T(8,128)(2,1)S(1)} %collective-permute-done.3, bf16[3072,1024]{1,0:T(8,128)(2,1)S(1)} %bitcast.64, f32[512]{0:T(512)S(1)} %fusion.11, f32[3072]{0:T(1024)S(1)} %fusion), kind=kOutput, calls=%fused_computation.6 | convolution fusion | flops 3229086720 | bytes 7366656 | tf_op jit(solution)/shard_map/distance_min/while/body/eval_jaxpr/dot_general | solution.py:21
  96.0 0.2 fusion.14
  96.2 2.1 %maximum_reduce_fusion = f32[3072]{0:T(1024)S(1)} fusion(f32[256]{0:T(256)S(1)} %fusion.14, f32[3072]{0:T(1024)S(1)} %fusion, bf16[256,1024]{1,0:T(8,128)(2,1)S(1)} %collective-permute-done.5, bf16[3072,1024]{1,0:T(8,128)(2,1)S(1)} %bitcast.64), kind=kOutput, calls=%fused_computation.20 | convolution fusion | flops 1614541824 | bytes 6841344 | tf_op jit(solution)/shard_map/distance_min/while/body/eval_jaxpr/dot_general | solution.py:21
  98.3 0.6 minimum_minimum_fusion
  (22 shorter events, 0.4 us)
Async XLA Ops:
  0.0 16.3 %copy-start.1 = (s32[1,256]{1,0:T(1,128)S(1)}, s32[1,256]{1,0:T(1,128)}, u32[]{:S(2)}) copy-start(s32[1,256]{1,0:T(1,128)} %param.6) | copy-start | bytes 3076
  7.7 20.1 %all-to-all-start = ((bf16[32,8,1024]{2,1,0:T(8,128)(2,1)}), bf16[32,8,1024]{2,1,0:T(8,128)(2,1)S(1)}, u32[]{:S(2)}, u32[]{:S(2)}) async-start(bf16[32,8,1024]{2,1,0:T(8,128)(2,1)} %bitcast_select_fusion), calls=%async_computation | async-start | bytes 1048576 | tf_op jit(solution)/shard_map/compact_centers/all_to_all | solution.py:73
  29.3 26.4 %all-to-all-start.1 = ((bf16[32,8,1024]{2,1,0:T(8,128)(2,1)}), bf16[32,8,1024]{2,1,0:T(8,128)(2,1)S(1)}, u32[]{:S(2)}, u32[]{:S(2)}) async-start(bf16[32,8,1024]{2,1,0:T(8,128)(2,1)} %broadcast_in_dim.78), calls=%async_computation.1 | async-start | bytes 1048576 | tf_op jit(solution)/shard_map/spread_centers/all_to_all | solution.py:54
  55.7 22.2 %collective-permute-start = (bf16[256,1024]{1,0:T(8,128)(2,1)S(1)}, bf16[256,1024]{1,0:T(8,128)(2,1)S(1)}, u32[]{:S(2)}, u32[]{:S(2)}) collective-permute-start(bf16[256,1024]{1,0:T(8,128)(2,1)S(1)} %bitcast.65), channel_id=1, source_target_pairs={{0,1},{1,0},{2,3},{3,2},{4,5},{5,4},{6,7},{7,6},{8,9},{9,8},{10,11... | collective-permute-start | bytes 1572872 | tf_op jit(solution)/shard_map/spread_centers/ppermute | solution.py:85
  57.5 14.7 %collective-permute-start.2 = (bf16[256,1024]{1,0:T(8,128)(2,1)S(1)}, bf16[256,1024]{1,0:T(8,128)(2,1)S(1)}, u32[]{:S(2)}, u32[]{:S(2)}) collective-permute-start(bf16[256,1024]{1,0:T(8,128)(2,1)S(1)} %bitcast.66), channel_id=1, source_target_pairs={{0,24},{8,0},{16,8},{24,16},{1,25},{9,1},{17,9},{25,17},{2,26},{10... | collective-permute-start | bytes 1572872 | tf_op jit(solution)/shard_map/spread_centers/ppermute | solution.py:80
  57.8 14.4 %collective-permute-start.1 = (bf16[256,1024]{1,0:T(8,128)(2,1)S(1)}, bf16[256,1024]{1,0:T(8,128)(2,1)S(1)}, u32[]{:S(2)}, u32[]{:S(2)}) collective-permute-start(bf16[256,1024]{1,0:T(8,128)(2,1)S(1)} %bitcast.67), channel_id=1, source_target_pairs={{0,8},{8,16},{16,24},{24,0},{1,9},{9,17},{17,25},{25,1},{2,10},{10... | collective-permute-start | bytes 1572872 | tf_op jit(solution)/shard_map/spread_centers/ppermute | solution.py:80
  59.0 14.8 %slice-start = ((s8[6291456]{0:T(1024)(128)(4,1)}), s8[4194304]{0:T(1024)(128)(4,1)S(1)}, s32[]{:S(2)}) async-start(s8[6291456]{0:T(1024)(128)(4,1)} %bitcast.63), calls=%async_computation.2 | async-start | bytes 8388608
  59.2 14.6 %slice-start.1 = ((s8[6291456]{0:T(1024)(128)(4,1)}), s8[2097152]{0:T(1024)(128)(4,1)S(1)}, s32[]{:S(2)}) async-start(s8[6291456]{0:T(1024)(128)(4,1)} %bitcast.63), calls=%async_computation.3 | async-start | bytes 4194304
  72.6 19.1 %collective-permute-start.3 = (bf16[512,1024]{1,0:T(8,128)(2,1)S(1)}, bf16[512,1024]{1,0:T(8,128)(2,1)S(1)}, u32[]{:S(2)}, u32[]{:S(2)}) collective-permute-start(bf16[512,1024]{1,0:T(8,128)(2,1)S(1)} %constant_dynamic-update-slice_fusion), channel_id=1, source_target_pairs={{0,1},{1,0},{2,3},{3,2},{4,5},{5,4},{6,7},{7,6},{8,9},{9,8},{10,11... | collective-permute-start | bytes 3145736 | tf_op jit(solution)/shard_map/spread_centers/ppermute | solution.py:85
  73.8 14.5 %collective-permute-start.4 = (bf16[256,1024]{1,0:T(8,128)(2,1)S(1)}, bf16[256,1024]{1,0:T(8,128)(2,1)S(1)}, u32[]{:S(2)}, u32[]{:S(2)}) collective-permute-start(bf16[256,1024]{1,0:T(8,128)(2,1)S(1)} %collective-permute-done.1), channel_id=1, source_target_pairs={{0,8},{8,16},{16,24},{24,0},{1,9},{9,17},{17,25},{25,1},{2,10},{10... | collective-permute-start | bytes 1572872 | tf_op jit(solution)/shard_map/spread_centers/ppermute | solution.py:80
  88.2 7.7 %collective-permute-start.5 = (bf16[256,1024]{1,0:T(8,128)(2,1)S(1)}, bf16[256,1024]{1,0:T(8,128)(2,1)S(1)}, u32[]{:S(2)}, u32[]{:S(2)}) collective-permute-start(bf16[256,1024]{1,0:T(8,128)(2,1)S(1)} %collective-permute-done.4), channel_id=1, source_target_pairs={{0,1},{1,0},{2,3},{3,2},{4,5},{5,4},{6,7},{7,6},{8,9},{9,8},{10,11... | collective-permute-start | bytes 1572872 | tf_op jit(solution)/shard_map/spread_centers/ppermute | solution.py:85
  96.2 2.2 %copy-start = (f32[3072]{0:T(1024)S(1)}, f32[3072]{0:T(1024)}, u32[]{:S(2)}) copy-start(f32[3072]{0:T(1024)} %param.5) | copy-start | bytes 36868

commit v5 on v4

--- a/solution.py
+++ b/solution.py
@@ -69,12 +69,24 @@
     per_device = owners.shape[0] // dev_count
 
     with jax.named_scope("compact_centers"):
-        send_rows = jnp.take(pool, jnp.where(owners == my_index, offsets, 0), axis=0)
+        devices = jnp.arange(dev_count, dtype=jnp.int32)
+        owner_hot = (owners[:, None] == devices[None, :]).astype(jnp.int32)
+        counts = jnp.sum(owner_hot, axis=0)
+        ends = jnp.cumsum(counts)
+        rank = jnp.sum((jnp.cumsum(owner_hot, axis=0) - 1) * owner_hot, axis=1)
+        position = ends[owners] - counts[owners] + rank
+        to_peer = ((owners == my_index)[None, :]) & (
+            (position % dev_count)[None, :] == devices[:, None]
+        )
+        peer_offset = jnp.sum(jnp.where(to_peer, offsets[None, :], 0), axis=1)
+        peer_valid = jnp.any(to_peer, axis=1)
+        rows_iota = lax.broadcasted_iota(jnp.int32, (dev_count, pool.shape[0]), 1)
+        pick = ((rows_iota == peer_offset[:, None]) & peer_valid[:, None]).astype(pool.dtype)
+        send_rows = jnp.dot(pick, pool, preferred_element_type=jnp.float32).astype(pool.dtype)
         landed = lax.all_to_all(send_rows, DEV_AXES, 0, 0, tiled=True)
-        mine = lax.dynamic_slice_in_dim(owners, my_index * per_device, per_device)
-        compact = jnp.take(
-            landed, mine * per_device + jnp.arange(per_device, dtype=jnp.int32), axis=0
-        )
+        wanted = my_index + dev_count * jnp.arange(per_device, dtype=jnp.int32)
+        source = jnp.sum((ends[None, :] <= wanted[:, None]).astype(jnp.int32), axis=1)
+        compact = jnp.take(landed, source, axis=0)
 
     def y_send(x, s):
         return lax.ppermute(x, "y", [(i, (i + s) % y_count) for i in range(y_count)])

time: 99.3 us -> 142 us (1.43)
  other arithmetic: 8.62 us -> 51.5 us
  matrix products: 19.5 us -> 23.5 us
  waiting for transfers between devices: 40.1 us -> 36.2 us
    select_n x5 -> x3, other arithmetic: 2.53 us -> 31.3 us  [the longest x1 31.2 us: shards(): position % dev_count]
    gather x2 -> x4, other arithmetic: 0.01 us -> 9.42 us  [the longest x3 9.42 us: shards(): position = ends[owners] - counts[owners] + rank]
    all_to_all x1, waiting for transfers between devices: 11.4 us -> 6.97 us  [shards(): landed = lax.all_to_all(send_rows, DEV_AXES, 0, 0, tiled=True)]
    dot_general x0 -> x1, matrix products: none -> 3.98 us  [shards(): jnp.dot(pick, pool, preferred_element_type=jnp.float32).astype(pool.dtype)]
    gather x2 -> x5, local copies, waits for them, and re-layouts: 5.72 us -> 3.31 us  [the longest x4 2.73 us: shards(): position = ends[owners] - counts[owners] + rank]
    reduce_sum x0 -> x3, other arithmetic: none -> 1.87 us  [the longest x1 0.89 us: shards(): counts = jnp.sum(owner_hot, axis=0)]
  transfers between devices with their start and end apart: 8 -> 8, of which waited for: 4 -> 4; matrix products, arithmetic and copies ran while one was open for 23% -> 15% of each run, Pallas kernels for 0% -> 0%
where the time goes in v5:
time: 142 us; the launch traced here: 141 us
  other arithmetic  51.5 us (36%)
  waiting for transfers between devices  36.2 us (25%)
  starting transfers between devices  23.8 us (17%)
  matrix products  23.5 us (17%)
  local copies, waits for them, and re-layouts  5.76 us (4%)
    select_n x1, other arithmetic, shards(): position % dev_count  31.2 us
    dot_general x6, matrix products, one_block(): lax.dot_general(block_rows, fragment, (((1,), (1,)), ((), ())), preferred...  19.5 us
    ppermute x3, waiting for transfers between devices, y_send(): lax.ppermute(x, 'y', [(i, (i + s) % y_count) for i in range(y_count)])  16.7 us
    all_to_all x1, waiting for transfers between devices, replicate_gather(): got = lax.all_to_all(copies, axes, 0, 0, tiled=True)  12.5 us
    gather x3, other arithmetic, shards(): position = ends[owners] - counts[owners] + rank  9.42 us
    all_to_all x1, starting transfers between devices, replicate_gather(): got = lax.all_to_all(copies, axes, 0, 0, tiled=True)  9.24 us
    all_to_all x1, starting transfers between devices, shards(): landed = lax.all_to_all(send_rows, DEV_AXES, 0, 0, tiled=True)  8.59 us
    all_to_all x1, waiting for transfers between devices, shards(): landed = lax.all_to_all(send_rows, DEV_AXES, 0, 0, tiled=True)  6.97 us
  transfers between devices with their start and end apart: 8, of which 4 were waited for; matrix products, arithmetic and copies ran while one was open for 15% of the time, Pallas kernels for 0%

profile of v5, /device:TPU:1, one launch (start us, length us, event | category | flops | bytes accessed | tf_op | source)
XLA Modules:
  0.0 141.0 jit_solution(1134108657046141064)
XLA Ops:
  0.0 0.7 fusion.25
  1.5 0.9 convert_reduce_fusion
  2.4 0.7 fusion.35
  3.1 0.7 fusion.34
  4.0 0.6 fusion.33
  4.6 0.7 fusion.32
  5.3 0.7 compare_reduce_fusion.25
  6.0 5.0 %compare_select_fusion.3 = (s32[256,1]{0,1:T(1,128)S(1)}, s32[256,1]{0,1:T(1,128)S(1)}) fusion(s32[]{:T(128)} %bitcast.28, s32[]{:T(128)} %bitcast.29, s32[]{:T(128)} %bitcast.30, s32[]{:T(128)} %bitcast.31, s32[]{:T(128)} %bitcast.32, s32[]{:T(128)} %bitcast.34, s32[]{:T(128)} %bitcast.33, s32[1,256]{1,0:T(1,128)} %param.6), kind=kLoop, calls=%fused_computation.90 | loop fusion | flops 3840 | bytes 3100 | tf_op jit(solution)/shard_map/compact_centers/gather | solution.py:77
  11.0 4.3 %compare_select_fusion.4 = s32[256,1]{0,1:T(1,128)S(1)} fusion(s32[256,1]{0,1:T(1,128)S(1)} %get-tuple-element.143, s32[]{:T(128)} %bitcast.61, s32[]{:T(128)} %bitcast.62, s32[]{:T(128)} %bitcast.63, s32[]{:T(128)} %bitcast.64, s32[]{:T(128)} %bitcast.65, s32[]{:T(128)} %bitcast.67, s32[]{:T(128)} %bitcast.66), kind=kLoop, calls=%fused_computation.91 | loop fusion | flops 3072 | bytes 2076 | tf_op jit(solution)/shard_map/compact_centers/gather | solution.py:77
  15.4 31.2 %and_select_fusion = s32[256]{0:T(256)S(1)} fusion(s32[256]{0:T(256)S(1)} %get-tuple-element.88, pred[256]{0:T(512)(128)(4,1)S(1)} %get-tuple-element.141, pred[256]{0:T(512)(128)(4,1)S(1)} %get-tuple-element.140, pred[256]{0:T(512)(128)(4,1)S(1)} %get-tuple-element.132, pred[256]{0:T(512)(128)(4,1)S(1)} %get-tuple-element.131, ...), kind=kLoop, calls=%fused_computation.104 | loop fusion | flops 16128 | bytes 10696 | tf_op jit(solution)/shard_map/compact_centers/jit(remainder)/select_n | solution.py:79
  46.7 0.8 select_reduce_fusion
  47.5 4.0 %fusion.14 = bf16[32,1,1024]{2,0,1:T(8,128)(2,1)S(1)} fusion(bf16[3072,1024]{1,0:T(8,128)(2,1)} %param.4, s32[32]{0:T(128)S(1)} %select_reduce_fusion, pred[32]{0:T(512)(128)(4,1)S(1)} %fusion.27), kind=kOutput, calls=%fused_computation.28 | convolution fusion | flops 201555968 | bytes 6357152 | tf_op jit(solution)/shard_map/compact_centers/dot_general | solution.py:85
  52.0 0.7 reduce.69
  52.7 0.7 reshape.459
  53.3 8.6 %all-to-all-start = ((bf16[32,2,512]{2,1,0:T(2,128)(2,1)}), bf16[32,2,512]{2,1,0:T(2,128)(2,1)S(1)}, u32[]{:S(2)}, u32[]{:S(2)}) async-start(bf16[32,2,512]{2,1,0:T(2,128)(2,1)} %reshape.459), calls=%async_computation | async-start | bytes 131072 | tf_op jit(solution)/shard_map/compact_centers/all_to_all | solution.py:86
  62.3 7.0 %all-to-all-done = bf16[32,2,512]{2,1,0:T(2,128)(2,1)S(1)} async-done(((bf16[32,2,512]{2,1,0:T(2,128)(2,1)}), bf16[32,2,512]{2,1,0:T(2,128)(2,1)S(1)}, u32[]{:S(2)}, u32[]{:S(2)}) %all-to-all-start) | async-done | bytes 65568 | tf_op jit(solution)/shard_map/compact_centers/all_to_all | solution.py:86
  70.0 0.9 broadcast_in_dim.82
  70.8 9.2 %all-to-all-start.1 = ((bf16[32,8,1024]{2,1,0:T(8,128)(2,1)}), bf16[32,8,1024]{2,1,0:T(8,128)(2,1)S(1)}, u32[]{:S(2)}, u32[]{:S(2)}) async-start(bf16[32,8,1024]{2,1,0:T(8,128)(2,1)} %broadcast_in_dim.82), calls=%async_computation.1 | async-start | bytes 1048576 | tf_op jit(solution)/shard_map/spread_centers/all_to_all | solution.py:54
  80.1 4.1 %fusion = f32[3072]{0:T(1024)S(1)} fusion(bf16[3072,1024]{1,0:T(8,128)(2,1)} %param.4), kind=kLoop, calls=%fused_computation.2 | loop fusion | flops 9434112 | bytes 6303744 | tf_op jit(solution)/shard_map/rd,rd->r/dot_general | solution.py:94
  84.2 12.5 %all-to-all-done.1 = bf16[32,8,1024]{2,1,0:T(8,128)(2,1)S(1)} async-done(((bf16[32,8,1024]{2,1,0:T(8,128)(2,1)}), bf16[32,8,1024]{2,1,0:T(8,128)(2,1)S(1)}, u32[]{:S(2)}, u32[]{:S(2)}) %all-to-all-start.1) | async-done | bytes 524320 | tf_op jit(solution)/shard_map/spread_centers/all_to_all | solution.py:54
  96.6 2.2 %collective-permute-start = (bf16[256,1024]{1,0:T(8,128)(2,1)S(1)}, bf16[256,1024]{1,0:T(8,128)(2,1)S(1)}, u32[]{:S(2)}, u32[]{:S(2)}) collective-permute-start(bf16[256,1024]{1,0:T(8,128)(2,1)S(1)} %bitcast.147), channel_id=1, source_target_pairs={{0,1},{1,0},{2,3},{3,2},{4,5},{5,4},{6,7},{7,6},{8,9},{9,8},{10,11... | collective-permute-start | bytes 1572872 | tf_op jit(solution)/shard_map/spread_centers/ppermute | solution.py:97
  98.8 0.9 collective-permute-start.2
  100.5 5.0 %fusion.13 = f32[3072]{0:T(1024)S(1)} fusion(bf16[3072,1024]{1,0:T(8,128)(2,1)} %param.4, f32[256]{0:T(256)S(1)} %fusion.18, f32[3072]{0:T(1024)S(1)} %fusion, bf16[32,8,1024]{2,1,0:T(8,128)(2,1)S(1)} %all-to-all-done.1), kind=kOutput, calls=%fused_computation.26 | convolution fusion | flops 1614541824 | bytes 6841344 | tf_op jit(solution)/shard_map/distance_min/while/body/eval_jaxpr/dot_general | solution.py:21
  105.5 8.6 %collective-permute-done.1 = bf16[256,1024]{1,0:T(8,128)(2,1)S(1)} collective-permute-done((bf16[256,1024]{1,0:T(8,128)(2,1)S(1)}, bf16[256,1024]{1,0:T(8,128)(2,1)S(1)}, u32[]{:S(2)}, u32[]{:S(2)}) %collective-permute-start.1) | collective-permute-done | bytes 524320 | tf_op jit(solution)/shard_map/spread_centers/ppermute | solution.py:92
  114.5 1.2 collective-permute-start.3
  115.7 4.0 %fusion.4 = f32[3072]{0:T(1024)S(1)} fusion(bf16[512,1024]{1,0:T(8,128)(2,1)S(1)} %constant_dynamic-update-slice_fusion, bf16[3072,1024]{1,0:T(8,128)(2,1)S(1)} %bitcast.146, f32[512]{0:T(512)S(1)} %fusion.12, f32[3072]{0:T(1024)S(1)} %fusion), kind=kOutput, calls=%fused_computation.8 | convolution fusion | flops 3229086720 | bytes 7366656 | tf_op jit(solution)/shard_map/distance_min/while/body/eval_jaxpr/dot_general | solution.py:21
  119.9 2.1 %maximum_reduce_fusion.2 = f32[3072]{0:T(1024)S(1)} fusion(f32[256]{0:T(256)S(1)} %fusion.17, f32[3072]{0:T(1024)S(1)} %fusion, bf16[256,1024]{1,0:T(8,128)(2,1)S(1)} %collective-permute-done, bf16[3072,1024]{1,0:T(8,128)(2,1)S(1)} %bitcast.146), kind=kOutput, calls=%fused_computation.21 | convolution fusion | flops 1614541824 | bytes 6841344 | tf_op jit(solution)/shard_map/distance_min/while/body/eval_jaxpr/dot_general | solution.py:21
  122.1 8.1 %collective-permute-done.4 = bf16[256,1024]{1,0:T(8,128)(2,1)S(1)} collective-permute-done((bf16[256,1024]{1,0:T(8,128)(2,1)S(1)}, bf16[256,1024]{1,0:T(8,128)(2,1)S(1)}, u32[]{:S(2)}, u32[]{:S(2)}) %collective-permute-start.4) | collective-permute-done | bytes 524320 | tf_op jit(solution)/shard_map/spread_centers/ppermute | solution.py:92
  130.3 1.2 collective-permute-start.5
  131.5 2.1 %maximum_reduce_fusion.1 = f32[3072]{0:T(1024)S(1)} fusion(f32[256]{0:T(256)S(1)} %fusion.16, f32[3072]{0:T(1024)S(1)} %fusion, bf16[256,1024]{1,0:T(8,128)(2,1)S(1)} %collective-permute-done.4, bf16[3072,1024]{1,0:T(8,128)(2,1)S(1)} %bitcast.146), kind=kOutput, calls=%fused_computation.20 | convolution fusion | flops 1614541824 | bytes 6841344 | tf_op jit(solution)/shard_map/distance_min/while/body/eval_jaxpr/dot_general | solution.py:21
  133.9 2.1 %maximum_reduce_fusion = f32[3072]{0:T(1024)S(1)} fusion(f32[256]{0:T(256)S(1)} %fusion.15, f32[3072]{0:T(1024)S(1)} %fusion, bf16[256,1024]{1,0:T(8,128)(2,1)S(1)} %collective-permute-done.5, bf16[3072,1024]{1,0:T(8,128)(2,1)S(1)} %bitcast.146), kind=kOutput, calls=%fused_computation.19 | convolution fusion | flops 1614541824 | bytes 6841344 | tf_op jit(solution)/shard_map/distance_min/while/body/eval_jaxpr/dot_general | solution.py:21
  136.3 4.0 %fusion.2 = f32[3072]{0:T(1024)S(1)} fusion(bf16[512,1024]{1,0:T(8,128)(2,1)S(1)} %collective-permute-done.3, bf16[3072,1024]{1,0:T(8,128)(2,1)S(1)} %bitcast.146, f32[512]{0:T(512)S(1)} %fusion.11, f32[3072]{0:T(1024)S(1)} %fusion), kind=kOutput, calls=%fused_computation.5 | convolution fusion | flops 3229086720 | bytes 7366656 | tf_op jit(solution)/shard_map/distance_min/while/body/eval_jaxpr/dot_general | solution.py:21
  (41 shorter events, 5.3 us)
Async XLA Ops:
  53.3 15.9 %all-to-all-start = ((bf16[32,2,512]{2,1,0:T(2,128)(2,1)}), bf16[32,2,512]{2,1,0:T(2,128)(2,1)S(1)}, u32[]{:S(2)}, u32[]{:S(2)}) async-start(bf16[32,2,512]{2,1,0:T(2,128)(2,1)} %reshape.459), calls=%async_computation | async-start | bytes 131072 | tf_op jit(solution)/shard_map/compact_centers/all_to_all | solution.py:86
  70.8 25.8 %all-to-all-start.1 = ((bf16[32,8,1024]{2,1,0:T(8,128)(2,1)}), bf16[32,8,1024]{2,1,0:T(8,128)(2,1)S(1)}, u32[]{:S(2)}, u32[]{:S(2)}) async-start(bf16[32,8,1024]{2,1,0:T(8,128)(2,1)} %broadcast_in_dim.82), calls=%async_computation.1 | async-start | bytes 1048576 | tf_op jit(solution)/shard_map/spread_centers/all_to_all | solution.py:54
  96.6 23.1 %collective-permute-start = (bf16[256,1024]{1,0:T(8,128)(2,1)S(1)}, bf16[256,1024]{1,0:T(8,128)(2,1)S(1)}, u32[]{:S(2)}, u32[]{:S(2)}) collective-permute-start(bf16[256,1024]{1,0:T(8,128)(2,1)S(1)} %bitcast.147), channel_id=1, source_target_pairs={{0,1},{1,0},{2,3},{3,2},{4,5},{5,4},{6,7},{7,6},{8,9},{9,8},{10,11... | collective-permute-start | bytes 1572872 | tf_op jit(solution)/shard_map/spread_centers/ppermute | solution.py:97
  98.8 15.4 %collective-permute-start.2 = (bf16[256,1024]{1,0:T(8,128)(2,1)S(1)}, bf16[256,1024]{1,0:T(8,128)(2,1)S(1)}, u32[]{:S(2)}, u32[]{:S(2)}) collective-permute-start(bf16[256,1024]{1,0:T(8,128)(2,1)S(1)} %bitcast.148), channel_id=1, source_target_pairs={{0,24},{8,0},{16,8},{24,16},{1,25},{9,1},{17,9},{25,17},{2,26},{10... | collective-permute-start | bytes 1572872 | tf_op jit(solution)/shard_map/spread_centers/ppermute | solution.py:92
  99.7 14.4 %collective-permute-start.1 = (bf16[256,1024]{1,0:T(8,128)(2,1)S(1)}, bf16[256,1024]{1,0:T(8,128)(2,1)S(1)}, u32[]{:S(2)}, u32[]{:S(2)}) collective-permute-start(bf16[256,1024]{1,0:T(8,128)(2,1)S(1)} %bitcast.149), channel_id=1, source_target_pairs={{0,8},{8,16},{16,24},{24,0},{1,9},{9,17},{17,25},{25,1},{2,10},{10... | collective-permute-start | bytes 1572872 | tf_op jit(solution)/shard_map/spread_centers/ppermute | solution.py:92
  100.3 15.4 %slice-start = ((s8[6291456]{0:T(1024)(128)(4,1)}), s8[4194304]{0:T(1024)(128)(4,1)S(1)}, s32[]{:S(2)}) async-start(s8[6291456]{0:T(1024)(128)(4,1)} %bitcast.145), calls=%async_computation.2 | async-start | bytes 8388608
  100.5 15.2 %slice-start.1 = ((s8[6291456]{0:T(1024)(128)(4,1)}), s8[2097152]{0:T(1024)(128)(4,1)S(1)}, s32[]{:S(2)}) async-start(s8[6291456]{0:T(1024)(128)(4,1)} %bitcast.145), calls=%async_computation.3 | async-start | bytes 4194304
  114.5 21.5 %collective-permute-start.3 = (bf16[512,1024]{1,0:T(8,128)(2,1)S(1)}, bf16[512,1024]{1,0:T(8,128)(2,1)S(1)}, u32[]{:S(2)}, u32[]{:S(2)}) collective-permute-start(bf16[512,1024]{1,0:T(8,128)(2,1)S(1)} %constant_dynamic-update-slice_fusion), channel_id=1, source_target_pairs={{0,1},{1,0},{2,3},{3,2},{4,5},{5,4},{6,7},{7,6},{8,9},{9,8},{10,11... | collective-permute-start | bytes 3145736 | tf_op jit(solution)/shard_map/spread_centers/ppermute | solution.py:97
  115.7 14.5 %collective-permute-start.4 = (bf16[256,1024]{1,0:T(8,128)(2,1)S(1)}, bf16[256,1024]{1,0:T(8,128)(2,1)S(1)}, u32[]{:S(2)}, u32[]{:S(2)}) collective-permute-start(bf16[256,1024]{1,0:T(8,128)(2,1)S(1)} %collective-permute-done.1), channel_id=1, source_target_pairs={{0,8},{8,16},{16,24},{24,0},{1,9},{9,17},{17,25},{25,1},{2,10},{10... | collective-permute-start | bytes 1572872 | tf_op jit(solution)/shard_map/spread_centers/ppermute | solution.py:92
  130.3 3.3 %collective-permute-start.5 = (bf16[256,1024]{1,0:T(8,128)(2,1)S(1)}, bf16[256,1024]{1,0:T(8,128)(2,1)S(1)}, u32[]{:S(2)}, u32[]{:S(2)}) collective-permute-start(bf16[256,1024]{1,0:T(8,128)(2,1)S(1)} %collective-permute-done.4), channel_id=1, source_target_pairs={{0,1},{1,0},{2,3},{3,2},{4,5},{5,4},{6,7},{7,6},{8,9},{9,8},{10,11... | collective-permute-start | bytes 1572872 | tf_op jit(solution)/shard_map/spread_centers/ppermute | solution.py:97
  136.3 4.1 %copy-start = (f32[3072]{0:T(1024)S(1)}, f32[3072]{0:T(1024)}, u32[]{:S(2)}) copy-start(f32[3072]{0:T(1024)} %param.5) | copy-start | bytes 36868

commit v6 on v5

--- a/solution.py
+++ b/solution.py
@@ -74,15 +74,13 @@
         counts = jnp.sum(owner_hot, axis=0)
         ends = jnp.cumsum(counts)
         rank = jnp.sum((jnp.cumsum(owner_hot, axis=0) - 1) * owner_hot, axis=1)
-        position = ends[owners] - counts[owners] + rank
+        starts = jnp.sum(owner_hot * (ends - counts)[None, :], axis=1)
+        position = starts + rank
         to_peer = ((owners == my_index)[None, :]) & (
             (position % dev_count)[None, :] == devices[:, None]
         )
         peer_offset = jnp.sum(jnp.where(to_peer, offsets[None, :], 0), axis=1)
-        peer_valid = jnp.any(to_peer, axis=1)
-        rows_iota = lax.broadcasted_iota(jnp.int32, (dev_count, pool.shape[0]), 1)
-        pick = ((rows_iota == peer_offset[:, None]) & peer_valid[:, None]).astype(pool.dtype)
-        send_rows = jnp.dot(pick, pool, preferred_element_type=jnp.float32).astype(pool.dtype)
+        send_rows = jnp.take(pool, peer_offset, axis=0)
         landed = lax.all_to_all(send_rows, DEV_AXES, 0, 0, tiled=True)
         wanted = my_index + dev_count * jnp.arange(per_device, dtype=jnp.int32)
         source = jnp.sum((ends[None, :] <= wanted[:, None]).astype(jnp.int32), axis=1)

time: 142 us -> 99.1 us (0.70)
  other arithmetic: 51.5 us -> 11.6 us
  matrix products: 23.5 us -> 19.5 us
  local copies, waits for them, and re-layouts: 5.76 us -> 7.29 us
    select_n x1, other arithmetic: 31.2 us -> 0.01 us  [shards(): position % dev_count]
    gather x3 -> x1, other arithmetic: 9.42 us -> 0.01 us  [shards(): send_rows = jnp.take(pool, peer_offset, axis=0)]
    dot_general x1 -> x0, matrix products: 3.98 us -> none  [shards(): jnp.dot(pick, pool, preferred_element_type=jnp.float32).astype(pool.dtype)]
    gather x4 -> x1, local copies, waits for them, and re-layouts: 2.73 us -> 4.27 us  [shards(): send_rows = jnp.take(pool, peer_offset, axis=0)]
  transfers between devices with their start and end apart: 8 -> 8, of which waited for: 4 -> 4; matrix products, arithmetic and copies ran while one was open for 15% -> 21% of each run, Pallas kernels for 0% -> 0%
where the time goes in v6:
time: 99.1 us; the launch traced here: 98.7 us
  waiting for transfers between devices  36.3 us (37%)
  starting transfers between devices  23.8 us (24%)
  matrix products  19.5 us (20%)
  other arithmetic  11.6 us (12%)
  local copies, waits for them, and re-layouts  7.29 us (7%)
    dot_general x6, matrix products, one_block(): lax.dot_general(block_rows, fragment, (((1,), (1,)), ((), ())), preferred...  19.5 us
    ppermute x3, waiting for transfers between devices, y_send(): lax.ppermute(x, 'y', [(i, (i + s) % y_count) for i in range(y_count)])  16.7 us
    all_to_all x1, waiting for transfers between devices, replicate_gather(): got = lax.all_to_all(copies, axes, 0, 0, tiled=True)  12.5 us
    all_to_all x1, starting transfers between devices, replicate_gather(): got = lax.all_to_all(copies, axes, 0, 0, tiled=True)  9.24 us
    all_to_all x1, starting transfers between devices, shards(): landed = lax.all_to_all(send_rows, DEV_AXES, 0, 0, tiled=True)  8.59 us
    all_to_all x1, waiting for transfers between devices, shards(): landed = lax.all_to_all(send_rows, DEV_AXES, 0, 0, tiled=True)  7.1 us
    ppermute x3, starting transfers between devices, core_swap(): return lax.ppermute(x, 'c', [(0, 1), (1, 0)])  4.54 us
    gather x1, local copies, waits for them, and re-layouts, shards(): send_rows = jnp.take(pool, peer_offset, axis=0)  4.27 us
  transfers between devices with their start and end apart: 8, of which 4 were waited for; matrix products, arithmetic and copies ran while one was open for 21% of the time, Pallas kernels for 0%

profile of v6, /device:TPU:1, one launch (start us, length us, event | category | flops | bytes accessed | tf_op | source)
XLA Modules:
  0.0 98.7 jit_solution(6130957164245006650)
XLA Ops:
  0.0 0.8 convert_reduce_fusion
  0.8 0.7 compare_reduce_fusion
  1.8 0.7 fusion.20
  2.5 0.6 reduce-window.18
  3.3 0.8 fusion.19
  4.1 0.8 select_reduce_fusion
  4.9 4.3 %gather_fusion = bf16[32,1024]{1,0:T(8,128)(2,1)S(1)} fusion(bf16[3072,1024]{1,0:T(8,128)(2,1)} %param.4, s32[1024]{0:T(1024)S(1)} %pad_clamp_fusion.1), kind=kCustom, calls=%fused_computation | custom fusion | bytes 131200 | tf_op jit(solution)/shard_map/compact_centers/jit(_take)/gather | solution.py:83
  9.2 0.5 broadcast.251
  9.8 0.7 reduce.19
  10.4 0.7 reshape.218
  11.1 8.6 %all-to-all-start = ((bf16[32,2,512]{2,1,0:T(2,128)(2,1)}), bf16[32,2,512]{2,1,0:T(2,128)(2,1)S(1)}, u32[]{:S(2)}, u32[]{:S(2)}) async-start(bf16[32,2,512]{2,1,0:T(2,128)(2,1)} %reshape.218), calls=%async_computation | async-start | bytes 131072 | tf_op jit(solution)/shard_map/compact_centers/all_to_all | solution.py:84
  19.9 7.1 %all-to-all-done = bf16[32,2,512]{2,1,0:T(2,128)(2,1)S(1)} async-done(((bf16[32,2,512]{2,1,0:T(2,128)(2,1)}), bf16[32,2,512]{2,1,0:T(2,128)(2,1)S(1)}, u32[]{:S(2)}, u32[]{:S(2)}) %all-to-all-start) | async-done | bytes 65568 | tf_op jit(solution)/shard_map/compact_centers/all_to_all | solution.py:84
  27.1 0.6 gather_fusion.1
  27.7 0.9 broadcast_in_dim.91
  28.6 9.2 %all-to-all-start.1 = ((bf16[32,8,1024]{2,1,0:T(8,128)(2,1)}), bf16[32,8,1024]{2,1,0:T(8,128)(2,1)S(1)}, u32[]{:S(2)}, u32[]{:S(2)}) async-start(bf16[32,8,1024]{2,1,0:T(8,128)(2,1)} %broadcast_in_dim.91), calls=%async_computation.1 | async-start | bytes 1048576 | tf_op jit(solution)/shard_map/spread_centers/all_to_all | solution.py:54
  37.8 4.1 %fusion = f32[3072]{0:T(1024)S(1)} fusion(bf16[3072,1024]{1,0:T(8,128)(2,1)} %param.4), kind=kLoop, calls=%fused_computation.3 | loop fusion | flops 9434112 | bytes 6303744 | tf_op jit(solution)/shard_map/rd,rd->r/dot_general | solution.py:92
  41.9 12.5 %all-to-all-done.1 = bf16[32,8,1024]{2,1,0:T(8,128)(2,1)S(1)} async-done(((bf16[32,8,1024]{2,1,0:T(8,128)(2,1)}), bf16[32,8,1024]{2,1,0:T(8,128)(2,1)S(1)}, u32[]{:S(2)}, u32[]{:S(2)}) %all-to-all-start.1) | async-done | bytes 524320 | tf_op jit(solution)/shard_map/spread_centers/all_to_all | solution.py:54
  54.4 2.2 %collective-permute-start = (bf16[256,1024]{1,0:T(8,128)(2,1)S(1)}, bf16[256,1024]{1,0:T(8,128)(2,1)S(1)}, u32[]{:S(2)}, u32[]{:S(2)}) collective-permute-start(bf16[256,1024]{1,0:T(8,128)(2,1)S(1)} %bitcast.81), channel_id=1, source_target_pairs={{0,1},{1,0},{2,3},{3,2},{4,5},{5,4},{6,7},{7,6},{8,9},{9,8},{10,11... | collective-permute-start | bytes 1572872 | tf_op jit(solution)/shard_map/spread_centers/ppermute | solution.py:95
  56.6 0.9 collective-permute-start.2
  57.5 0.6 collective-permute-start.1
  58.2 5.0 %fusion.13 = f32[3072]{0:T(1024)S(1)} fusion(bf16[3072,1024]{1,0:T(8,128)(2,1)} %param.4, f32[256]{0:T(256)S(1)} %fusion.17, f32[3072]{0:T(1024)S(1)} %fusion, bf16[32,8,1024]{2,1,0:T(8,128)(2,1)S(1)} %all-to-all-done.1), kind=kOutput, calls=%fused_computation.27 | convolution fusion | flops 1614541824 | bytes 6841344 | tf_op jit(solution)/shard_map/distance_min/while/body/eval_jaxpr/dot_general | solution.py:21
  63.3 8.7 %collective-permute-done.1 = bf16[256,1024]{1,0:T(8,128)(2,1)S(1)} collective-permute-done((bf16[256,1024]{1,0:T(8,128)(2,1)S(1)}, bf16[256,1024]{1,0:T(8,128)(2,1)S(1)}, u32[]{:S(2)}, u32[]{:S(2)}) %collective-permute-start.1) | collective-permute-done | bytes 524320 | tf_op jit(solution)/shard_map/spread_centers/ppermute | solution.py:90
  72.3 1.2 %collective-permute-start.3 = (bf16[512,1024]{1,0:T(8,128)(2,1)S(1)}, bf16[512,1024]{1,0:T(8,128)(2,1)S(1)}, u32[]{:S(2)}, u32[]{:S(2)}) collective-permute-start(bf16[512,1024]{1,0:T(8,128)(2,1)S(1)} %constant_dynamic-update-slice_fusion), channel_id=1, source_target_pairs={{0,1},{1,0},{2,3},{3,2},{4,5},{5,4},{6,7},{7,6},{8,9},{9,8},{10,11... | collective-permute-start | bytes 3145736 | tf_op jit(solution)/shard_map/spread_centers/ppermute | solution.py:95
  73.5 4.0 %fusion.4 = f32[3072]{0:T(1024)S(1)} fusion(bf16[512,1024]{1,0:T(8,128)(2,1)S(1)} %constant_dynamic-update-slice_fusion, bf16[3072,1024]{1,0:T(8,128)(2,1)S(1)} %bitcast.80, f32[512]{0:T(512)S(1)} %fusion.12, f32[3072]{0:T(1024)S(1)} %fusion), kind=kOutput, calls=%fused_computation.9 | convolution fusion | flops 3229086720 | bytes 7366656 | tf_op jit(solution)/shard_map/distance_min/while/body/eval_jaxpr/dot_general | solution.py:21
  77.7 2.2 %maximum_reduce_fusion.2 = f32[3072]{0:T(1024)S(1)} fusion(f32[256]{0:T(256)S(1)} %fusion.16, f32[3072]{0:T(1024)S(1)} %fusion, bf16[256,1024]{1,0:T(8,128)(2,1)S(1)} %collective-permute-done, bf16[3072,1024]{1,0:T(8,128)(2,1)S(1)} %bitcast.80), kind=kOutput, calls=%fused_computation.22 | convolution fusion | flops 1614541824 | bytes 6841344 | tf_op jit(solution)/shard_map/distance_min/while/body/eval_jaxpr/dot_general | solution.py:21
  79.9 8.0 %collective-permute-done.4 = bf16[256,1024]{1,0:T(8,128)(2,1)S(1)} collective-permute-done((bf16[256,1024]{1,0:T(8,128)(2,1)S(1)}, bf16[256,1024]{1,0:T(8,128)(2,1)S(1)}, u32[]{:S(2)}, u32[]{:S(2)}) %collective-permute-start.4) | collective-permute-done | bytes 524320 | tf_op jit(solution)/shard_map/spread_centers/ppermute | solution.py:90
  88.1 1.2 %collective-permute-start.5 = (bf16[256,1024]{1,0:T(8,128)(2,1)S(1)}, bf16[256,1024]{1,0:T(8,128)(2,1)S(1)}, u32[]{:S(2)}, u32[]{:S(2)}) collective-permute-start(bf16[256,1024]{1,0:T(8,128)(2,1)S(1)} %collective-permute-done.4), channel_id=1, source_target_pairs={{0,1},{1,0},{2,3},{3,2},{4,5},{5,4},{6,7},{7,6},{8,9},{9,8},{10,11... | collective-permute-start | bytes 1572872 | tf_op jit(solution)/shard_map/spread_centers/ppermute | solution.py:95
  89.3 2.1 %maximum_reduce_fusion.1 = f32[3072]{0:T(1024)S(1)} fusion(f32[256]{0:T(256)S(1)} %fusion.15, f32[3072]{0:T(1024)S(1)} %fusion, bf16[256,1024]{1,0:T(8,128)(2,1)S(1)} %collective-permute-done.4, bf16[3072,1024]{1,0:T(8,128)(2,1)S(1)} %bitcast.80), kind=kOutput, calls=%fused_computation.21 | convolution fusion | flops 1614541824 | bytes 6841344 | tf_op jit(solution)/shard_map/distance_min/while/body/eval_jaxpr/dot_general | solution.py:21
  91.6 2.1 %maximum_reduce_fusion = f32[3072]{0:T(1024)S(1)} fusion(f32[256]{0:T(256)S(1)} %fusion.14, f32[3072]{0:T(1024)S(1)} %fusion, bf16[256,1024]{1,0:T(8,128)(2,1)S(1)} %collective-permute-done.5, bf16[3072,1024]{1,0:T(8,128)(2,1)S(1)} %bitcast.80), kind=kOutput, calls=%fused_computation.20 | convolution fusion | flops 1614541824 | bytes 6841344 | tf_op jit(solution)/shard_map/distance_min/while/body/eval_jaxpr/dot_general | solution.py:21
  93.8 0.3 fusion.11
  94.1 4.0 %fusion.2 = f32[3072]{0:T(1024)S(1)} fusion(bf16[512,1024]{1,0:T(8,128)(2,1)S(1)} %collective-permute-done.3, bf16[3072,1024]{1,0:T(8,128)(2,1)S(1)} %bitcast.80, f32[512]{0:T(512)S(1)} %fusion.11, f32[3072]{0:T(1024)S(1)} %fusion), kind=kOutput, calls=%fused_computation.6 | convolution fusion | flops 3229086720 | bytes 7366656 | tf_op jit(solution)/shard_map/distance_min/while/body/eval_jaxpr/dot_general | solution.py:21
  98.1 0.6 minimum_minimum_fusion
  (39 shorter events, 2.1 us)
Async XLA Ops:
  11.1 15.9 %all-to-all-start = ((bf16[32,2,512]{2,1,0:T(2,128)(2,1)}), bf16[32,2,512]{2,1,0:T(2,128)(2,1)S(1)}, u32[]{:S(2)}, u32[]{:S(2)}) async-start(bf16[32,2,512]{2,1,0:T(2,128)(2,1)} %reshape.218), calls=%async_computation | async-start | bytes 131072 | tf_op jit(solution)/shard_map/compact_centers/all_to_all | solution.py:84
  28.6 25.8 %all-to-all-start.1 = ((bf16[32,8,1024]{2,1,0:T(8,128)(2,1)}), bf16[32,8,1024]{2,1,0:T(8,128)(2,1)S(1)}, u32[]{:S(2)}, u32[]{:S(2)}) async-start(bf16[32,8,1024]{2,1,0:T(8,128)(2,1)} %broadcast_in_dim.91), calls=%async_computation.1 | async-start | bytes 1048576 | tf_op jit(solution)/shard_map/spread_centers/all_to_all | solution.py:54
  54.4 23.1 %collective-permute-start = (bf16[256,1024]{1,0:T(8,128)(2,1)S(1)}, bf16[256,1024]{1,0:T(8,128)(2,1)S(1)}, u32[]{:S(2)}, u32[]{:S(2)}) collective-permute-start(bf16[256,1024]{1,0:T(8,128)(2,1)S(1)} %bitcast.81), channel_id=1, source_target_pairs={{0,1},{1,0},{2,3},{3,2},{4,5},{5,4},{6,7},{7,6},{8,9},{9,8},{10,11... | collective-permute-start | bytes 1572872 | tf_op jit(solution)/shard_map/spread_centers/ppermute | solution.py:95
  56.6 15.4 %collective-permute-start.2 = (bf16[256,1024]{1,0:T(8,128)(2,1)S(1)}, bf16[256,1024]{1,0:T(8,128)(2,1)S(1)}, u32[]{:S(2)}, u32[]{:S(2)}) collective-permute-start(bf16[256,1024]{1,0:T(8,128)(2,1)S(1)} %bitcast.82), channel_id=1, source_target_pairs={{0,24},{8,0},{16,8},{24,16},{1,25},{9,1},{17,9},{25,17},{2,26},{10... | collective-permute-start | bytes 1572872 | tf_op jit(solution)/shard_map/spread_centers/ppermute | solution.py:90
  57.5 14.4 %collective-permute-start.1 = (bf16[256,1024]{1,0:T(8,128)(2,1)S(1)}, bf16[256,1024]{1,0:T(8,128)(2,1)S(1)}, u32[]{:S(2)}, u32[]{:S(2)}) collective-permute-start(bf16[256,1024]{1,0:T(8,128)(2,1)S(1)} %bitcast.83), channel_id=1, source_target_pairs={{0,8},{8,16},{16,24},{24,0},{1,9},{9,17},{17,25},{25,1},{2,10},{10... | collective-permute-start | bytes 1572872 | tf_op jit(solution)/shard_map/spread_centers/ppermute | solution.py:90
  58.1 15.4 %slice-start = ((s8[6291456]{0:T(1024)(128)(4,1)}), s8[4194304]{0:T(1024)(128)(4,1)S(1)}, s32[]{:S(2)}) async-start(s8[6291456]{0:T(1024)(128)(4,1)} %bitcast.79), calls=%async_computation.2 | async-start | bytes 8388608
  58.2 15.2 %slice-start.1 = ((s8[6291456]{0:T(1024)(128)(4,1)}), s8[2097152]{0:T(1024)(128)(4,1)S(1)}, s32[]{:S(2)}) async-start(s8[6291456]{0:T(1024)(128)(4,1)} %bitcast.79), calls=%async_computation.3 | async-start | bytes 4194304
  72.3 21.5 %collective-permute-start.3 = (bf16[512,1024]{1,0:T(8,128)(2,1)S(1)}, bf16[512,1024]{1,0:T(8,128)(2,1)S(1)}, u32[]{:S(2)}, u32[]{:S(2)}) collective-permute-start(bf16[512,1024]{1,0:T(8,128)(2,1)S(1)} %constant_dynamic-update-slice_fusion), channel_id=1, source_target_pairs={{0,1},{1,0},{2,3},{3,2},{4,5},{5,4},{6,7},{7,6},{8,9},{9,8},{10,11... | collective-permute-start | bytes 3145736 | tf_op jit(solution)/shard_map/spread_centers/ppermute | solution.py:95
  73.5 14.5 %collective-permute-start.4 = (bf16[256,1024]{1,0:T(8,128)(2,1)S(1)}, bf16[256,1024]{1,0:T(8,128)(2,1)S(1)}, u32[]{:S(2)}, u32[]{:S(2)}) collective-permute-start(bf16[256,1024]{1,0:T(8,128)(2,1)S(1)} %collective-permute-done.1), channel_id=1, source_target_pairs={{0,8},{8,16},{16,24},{24,0},{1,9},{9,17},{17,25},{25,1},{2,10},{10... | collective-permute-start | bytes 1572872 | tf_op jit(solution)/shard_map/spread_centers/ppermute | solution.py:90
  88.1 3.3 %collective-permute-start.5 = (bf16[256,1024]{1,0:T(8,128)(2,1)S(1)}, bf16[256,1024]{1,0:T(8,128)(2,1)S(1)}, u32[]{:S(2)}, u32[]{:S(2)}) collective-permute-start(bf16[256,1024]{1,0:T(8,128)(2,1)S(1)} %collective-permute-done.4), channel_id=1, source_target_pairs={{0,1},{1,0},{2,3},{3,2},{4,5},{5,4},{6,7},{7,6},{8,9},{9,8},{10,11... | collective-permute-start | bytes 1572872 | tf_op jit(solution)/shard_map/spread_centers/ppermute | solution.py:95
  94.1 4.1 %copy-start = (f32[3072]{0:T(1024)S(1)}, f32[3072]{0:T(1024)}, u32[]{:S(2)}) copy-start(f32[3072]{0:T(1024)} %param.5) | copy-start | bytes 36868

commit v7 on v6

--- a/solution.py
+++ b/solution.py
@@ -70,12 +70,9 @@
 
     with jax.named_scope("compact_centers"):
         devices = jnp.arange(dev_count, dtype=jnp.int32)
-        owner_hot = (owners[:, None] == devices[None, :]).astype(jnp.int32)
-        counts = jnp.sum(owner_hot, axis=0)
-        ends = jnp.cumsum(counts)
-        rank = jnp.sum((jnp.cumsum(owner_hot, axis=0) - 1) * owner_hot, axis=1)
-        starts = jnp.sum(owner_hot * (ends - counts)[None, :], axis=1)
-        position = starts + rank
+        center_count = owners.shape[0]
+        key = owners * center_count + jnp.arange(center_count, dtype=jnp.int32)
+        position = jnp.sum((key[None, :] < key[:, None]).astype(jnp.int32), axis=1)
         to_peer = ((owners == my_index)[None, :]) & (
             (position % dev_count)[None, :] == devices[:, None]
         )
@@ -83,7 +80,9 @@
         send_rows = jnp.take(pool, peer_offset, axis=0)
         landed = lax.all_to_all(send_rows, DEV_AXES, 0, 0, tiled=True)
         wanted = my_index + dev_count * jnp.arange(per_device, dtype=jnp.int32)
-        source = jnp.sum((ends[None, :] <= wanted[:, None]).astype(jnp.int32), axis=1)
+        source = jnp.sum(
+            jnp.where(position[None, :] == wanted[:, None], owners[None, :], 0), axis=1
+        )
         compact = jnp.take(landed, source, axis=0)
 
     def y_send(x, s):
@@ -97,7 +96,10 @@
     with jax.named_scope("spread_centers"):
         plane = replicate_gather(compact, ("z", "x"), z_count * x_count)
         y_near = y_send(plane, 1), y_send(plane, -1)
-        y_far = y_send(y_near[0], 1)
+        split = plane.shape[0] // 2
+        y_far = jnp.concatenate(
+            [y_send(y_near[0][:split], 1), y_send(y_near[1][split:], -1)], axis=0
+        )
         near = jnp.concatenate(y_near, axis=0)
         pieces = [plane, core_swap(plane), near, core_swap(near), y_far, core_swap(y_far)]
 

time: 99.1 us -> 88.9 us (0.90)
  waiting for transfers between devices: 36.3 us -> 20.8 us
  starting transfers between devices: 23.8 us -> 30.1 us
    ppermute x3 -> x4, waiting for transfers between devices: 16.7 us -> 1.84 us  [y_send(): lax.ppermute(x, 'y', [(i, (i + s) % y_count) for i in range(y_count)])]
    ppermute x3 -> x4, starting transfers between devices: 1.47 us -> 5.67 us  [y_send(): lax.ppermute(x, 'y', [(i, (i + s) % y_count) for i in range(y_count)])]
    ppermute x3, starting transfers between devices: 4.54 us -> 6.62 us  [core_swap(): return lax.ppermute(x, 'c', [(0, 1), (1, 0)])]
    add x0 -> x2, other arithmetic: none -> 1.36 us  [shards(): key = owners * center_count + jnp.arange(center_count, dtype=jnp.int32)]
  transfers between devices with their start and end apart: 8 -> 9, of which waited for: 4 -> 3; matrix products, arithmetic and copies ran while one was open for 21% -> 24% of each run, Pallas kernels for 0% -> 0%
where the time goes in v7:
time: 88.9 us; the launch traced here: 88.5 us
  starting transfers between devices  30.1 us (34%)
  waiting for transfers between devices  20.8 us (23%)
  matrix products  19.6 us (22%)
  other arithmetic  10.7 us (12%)
  local copies, waits for them, and re-layouts  7.09 us (8%)
    dot_general x6, matrix products, one_block(): lax.dot_general(block_rows, fragment, (((1,), (1,)), ((), ())), preferred...  19.6 us
    all_to_all x1, waiting for transfers between devices, replicate_gather(): got = lax.all_to_all(copies, axes, 0, 0, tiled=True)  12.5 us
    all_to_all x1, starting transfers between devices, replicate_gather(): got = lax.all_to_all(copies, axes, 0, 0, tiled=True)  9.24 us
    all_to_all x1, starting transfers between devices, shards(): landed = lax.all_to_all(send_rows, DEV_AXES, 0, 0, tiled=True)  8.59 us
    ppermute x3, starting transfers between devices, core_swap(): return lax.ppermute(x, 'c', [(0, 1), (1, 0)])  6.62 us
    all_to_all x1, waiting for transfers between devices, shards(): landed = lax.all_to_all(send_rows, DEV_AXES, 0, 0, tiled=True)  6.42 us
    ppermute x4, starting transfers between devices, y_send(): lax.ppermute(x, 'y', [(i, (i + s) % y_count) for i in range(y_count)])  5.67 us
    gather x1, local copies, waits for them, and re-layouts, shards(): send_rows = jnp.take(pool, peer_offset, axis=0)  4.27 us
  transfers between devices with their start and end apart: 9, of which 3 were waited for; matrix products, arithmetic and copies ran while one was open for 24% of the time, Pallas kernels for 0%

profile of v7, /device:TPU:1, one launch (start us, length us, event | category | flops | bytes accessed | tf_op | source)
XLA Modules:
  0.0 88.5 jit_solution(16204632996872507702)
XLA Ops:
  0.0 0.7 iota_add_fusion.1
  0.7 0.7 iota_add_fusion
  1.6 0.7 compare_reduce_fusion
  2.3 0.8 select_reduce_fusion
  3.1 4.3 %gather_fusion = bf16[32,1024]{1,0:T(8,128)(2,1)S(1)} fusion(bf16[3072,1024]{1,0:T(8,128)(2,1)} %param.4, s32[1024]{0:T(1024)S(1)} %pad_clamp_fusion.1), kind=kCustom, calls=%fused_computation | custom fusion | bytes 131200 | tf_op jit(solution)/shard_map/compact_centers/jit(_take)/gather | solution.py:80
  7.5 0.5 broadcast.226
  8.0 0.7 reduce.16
  8.6 0.7 reshape.177
  9.3 8.6 %all-to-all-start = ((bf16[32,2,512]{2,1,0:T(2,128)(2,1)}), bf16[32,2,512]{2,1,0:T(2,128)(2,1)S(1)}, u32[]{:S(2)}, u32[]{:S(2)}) async-start(bf16[32,2,512]{2,1,0:T(2,128)(2,1)} %reshape.177), calls=%async_computation | async-start | bytes 131072 | tf_op jit(solution)/shard_map/compact_centers/all_to_all | solution.py:81
  17.9 0.9 select_reduce_fusion.1
  18.8 6.4 %all-to-all-done = bf16[32,2,512]{2,1,0:T(2,128)(2,1)S(1)} async-done(((bf16[32,2,512]{2,1,0:T(2,128)(2,1)}), bf16[32,2,512]{2,1,0:T(2,128)(2,1)S(1)}, u32[]{:S(2)}, u32[]{:S(2)}) %all-to-all-start) | async-done | bytes 65568 | tf_op jit(solution)/shard_map/compact_centers/all_to_all | solution.py:81
  25.3 0.6 gather_fusion.1
  25.9 0.9 broadcast_in_dim.105
  26.8 9.2 %all-to-all-start.1 = ((bf16[32,8,1024]{2,1,0:T(8,128)(2,1)}), bf16[32,8,1024]{2,1,0:T(8,128)(2,1)S(1)}, u32[]{:S(2)}, u32[]{:S(2)}) async-start(bf16[32,8,1024]{2,1,0:T(8,128)(2,1)} %broadcast_in_dim.105), calls=%async_computation.1 | async-start | bytes 1048576 | tf_op jit(solution)/shard_map/spread_centers/all_to_all | solution.py:54
  36.0 4.1 %fusion = f32[3072]{0:T(1024)S(1)} fusion(bf16[3072,1024]{1,0:T(8,128)(2,1)} %param.4), kind=kLoop, calls=%fused_computation.3 | loop fusion | flops 9434112 | bytes 6303744 | tf_op jit(solution)/shard_map/rd,rd->r/dot_general | solution.py:91
  40.1 12.5 %all-to-all-done.1 = bf16[32,8,1024]{2,1,0:T(8,128)(2,1)S(1)} async-done(((bf16[32,8,1024]{2,1,0:T(8,128)(2,1)}), bf16[32,8,1024]{2,1,0:T(8,128)(2,1)S(1)}, u32[]{:S(2)}, u32[]{:S(2)}) %all-to-all-start.1) | async-done | bytes 524320 | tf_op jit(solution)/shard_map/spread_centers/all_to_all | solution.py:54
  52.6 0.3 collective-permute-start.1
  52.9 2.3 %collective-permute-start.2 = (bf16[256,1024]{1,0:T(8,128)(2,1)S(1)}, bf16[256,1024]{1,0:T(8,128)(2,1)S(1)}, u32[]{:S(2)}, u32[]{:S(2)}) collective-permute-start(bf16[256,1024]{1,0:T(8,128)(2,1)S(1)} %bitcast.70), channel_id=1, source_target_pairs={{0,24},{8,0},{16,8},{24,16},{1,25},{9,1},{17,9},{25,17},{2,26},{10... | collective-permute-start | bytes 1572872 | tf_op jit(solution)/shard_map/spread_centers/ppermute | solution.py:89
  55.3 2.7 %collective-permute-start = (bf16[256,1024]{1,0:T(8,128)(2,1)S(1)}, bf16[256,1024]{1,0:T(8,128)(2,1)S(1)}, u32[]{:S(2)}, u32[]{:S(2)}) collective-permute-start(bf16[256,1024]{1,0:T(8,128)(2,1)S(1)} %bitcast.71), channel_id=1, source_target_pairs={{0,1},{1,0},{2,3},{3,2},{4,5},{5,4},{6,7},{7,6},{8,9},{9,8},{10,11... | collective-permute-start | bytes 1572872 | tf_op jit(solution)/shard_map/spread_centers/ppermute | solution.py:94
  58.2 5.0 %fusion.16 = f32[3072]{0:T(1024)S(1)} fusion(bf16[3072,1024]{1,0:T(8,128)(2,1)} %param.4, f32[256]{0:T(256)S(1)} %fusion.20, f32[3072]{0:T(1024)S(1)} %fusion, bf16[32,8,1024]{2,1,0:T(8,128)(2,1)S(1)} %all-to-all-done.1), kind=kOutput, calls=%fused_computation.29 | convolution fusion | flops 1614541824 | bytes 6841344 | tf_op jit(solution)/shard_map/distance_min/while/body/eval_jaxpr/dot_general | solution.py:21
  63.2 1.8 %collective-permute-done.1 = bf16[256,1024]{1,0:T(8,128)(2,1)S(1)} collective-permute-done((bf16[256,1024]{1,0:T(8,128)(2,1)S(1)}, bf16[256,1024]{1,0:T(8,128)(2,1)S(1)}, u32[]{:S(2)}, u32[]{:S(2)}) %collective-permute-start.1) | collective-permute-done | bytes 524320 | tf_op jit(solution)/shard_map/spread_centers/ppermute | solution.py:89
  65.2 3.2 %collective-permute-start.3 = (bf16[512,1024]{1,0:T(8,128)(2,1)S(1)}, bf16[512,1024]{1,0:T(8,128)(2,1)S(1)}, u32[]{:S(2)}, u32[]{:S(2)}) collective-permute-start(bf16[512,1024]{1,0:T(8,128)(2,1)S(1)} %constant_dynamic-update-slice_fusion), channel_id=1, source_target_pairs={{0,1},{1,0},{2,3},{3,2},{4,5},{5,4},{6,7},{7,6},{8,9},{9,8},{10,11... | collective-permute-start | bytes 3145736 | tf_op jit(solution)/shard_map/spread_centers/ppermute | solution.py:94
  68.3 0.3 fusion.14
  68.8 2.9 %collective-permute-start.5 = (bf16[128,1024]{1,0:T(8,128)(2,1)S(1)}, bf16[128,1024]{1,0:T(8,128)(2,1)S(1)}, u32[]{:S(2)}, u32[]{:S(2)}) collective-permute-start(bf16[128,1024]{1,0:T(8,128)(2,1)S(1)} %slice.13), channel_id=1, source_target_pairs={{0,24},{8,0},{16,8},{24,16},{1,25},{9,1},{17,9},{25,17},{2,26},{10... | collective-permute-start | bytes 786440 | tf_op jit(solution)/shard_map/spread_centers/ppermute | solution.py:89
  71.7 4.0 %fusion.4 = f32[3072]{0:T(1024)S(1)} fusion(bf16[512,1024]{1,0:T(8,128)(2,1)S(1)} %constant_dynamic-update-slice_fusion, bf16[3072,1024]{1,0:T(8,128)(2,1)S(1)} %bitcast.68, f32[512]{0:T(512)S(1)} %fusion.14, f32[3072]{0:T(1024)S(1)} %fusion), kind=kOutput, calls=%fused_computation.9 | convolution fusion | flops 3229086720 | bytes 7366656 | tf_op jit(solution)/shard_map/distance_min/while/body/eval_jaxpr/dot_general | solution.py:21
  75.9 2.1 %maximum_reduce_fusion.1 = f32[3072]{0:T(1024)S(1)} fusion(f32[256]{0:T(256)S(1)} %fusion.19, f32[3072]{0:T(1024)S(1)} %fusion, bf16[256,1024]{1,0:T(8,128)(2,1)S(1)} %collective-permute-done, bf16[3072,1024]{1,0:T(8,128)(2,1)S(1)} %bitcast.68), kind=kOutput, calls=%fused_computation.23 | convolution fusion | flops 1614541824 | bytes 6841344 | tf_op jit(solution)/shard_map/distance_min/while/body/eval_jaxpr/dot_general | solution.py:21
  78.1 0.7 collective-permute-start.6
  79.0 2.2 %fusion.15 = f32[3072]{0:T(1024)S(1)} fusion(bf16[256,1024]{1,0:T(8,128)(2,1)S(1)} %constant_dynamic-update-slice_fusion.2, bf16[3072,1024]{1,0:T(8,128)(2,1)S(1)} %bitcast.68, f32[256]{0:T(256)S(1)} %fusion.18, f32[3072]{0:T(1024)S(1)} %fusion), kind=kOutput, calls=%fused_computation.28 | convolution fusion | flops 1614541824 | bytes 6841344 | tf_op jit(solution)/shard_map/distance_min/while/body/eval_jaxpr/dot_general | solution.py:21
  81.4 2.2 %maximum_reduce_fusion = f32[3072]{0:T(1024)S(1)} fusion(f32[256]{0:T(256)S(1)} %fusion.17, f32[3072]{0:T(1024)S(1)} %fusion, bf16[256,1024]{1,0:T(8,128)(2,1)S(1)} %collective-permute-done.6, bf16[3072,1024]{1,0:T(8,128)(2,1)S(1)} %bitcast.68), kind=kOutput, calls=%fused_computation.22 | convolution fusion | flops 1614541824 | bytes 6841344 | tf_op jit(solution)/shard_map/distance_min/while/body/eval_jaxpr/dot_general | solution.py:21
  83.6 0.3 fusion.13
  83.9 4.0 %fusion.2 = f32[3072]{0:T(1024)S(1)} fusion(bf16[512,1024]{1,0:T(8,128)(2,1)S(1)} %collective-permute-done.3, bf16[3072,1024]{1,0:T(8,128)(2,1)S(1)} %bitcast.68, f32[512]{0:T(512)S(1)} %fusion.13, f32[3072]{0:T(1024)S(1)} %fusion), kind=kOutput, calls=%fused_computation.6 | convolution fusion | flops 3229086720 | bytes 7366656 | tf_op jit(solution)/shard_map/distance_min/while/body/eval_jaxpr/dot_general | solution.py:21
  87.9 0.6 minimum_minimum_fusion
  (37 shorter events, 1.5 us)
Async XLA Ops:
  9.3 15.9 %all-to-all-start = ((bf16[32,2,512]{2,1,0:T(2,128)(2,1)}), bf16[32,2,512]{2,1,0:T(2,128)(2,1)S(1)}, u32[]{:S(2)}, u32[]{:S(2)}) async-start(bf16[32,2,512]{2,1,0:T(2,128)(2,1)} %reshape.177), calls=%async_computation | async-start | bytes 131072 | tf_op jit(solution)/shard_map/compact_centers/all_to_all | solution.py:81
  26.8 25.8 %all-to-all-start.1 = ((bf16[32,8,1024]{2,1,0:T(8,128)(2,1)}), bf16[32,8,1024]{2,1,0:T(8,128)(2,1)S(1)}, u32[]{:S(2)}, u32[]{:S(2)}) async-start(bf16[32,8,1024]{2,1,0:T(8,128)(2,1)} %broadcast_in_dim.105), calls=%async_computation.1 | async-start | bytes 1048576 | tf_op jit(solution)/shard_map/spread_centers/all_to_all | solution.py:54
  52.6 12.4 %collective-permute-start.1 = (bf16[256,1024]{1,0:T(8,128)(2,1)S(1)}, bf16[256,1024]{1,0:T(8,128)(2,1)S(1)}, u32[]{:S(2)}, u32[]{:S(2)}) collective-permute-start(bf16[256,1024]{1,0:T(8,128)(2,1)S(1)} %bitcast.69), channel_id=1, source_target_pairs={{0,8},{8,16},{16,24},{24,0},{1,9},{9,17},{17,25},{25,1},{2,10},{10... | collective-permute-start | bytes 1572872 | tf_op jit(solution)/shard_map/spread_centers/ppermute | solution.py:89
  52.9 12.2 %collective-permute-start.2 = (bf16[256,1024]{1,0:T(8,128)(2,1)S(1)}, bf16[256,1024]{1,0:T(8,128)(2,1)S(1)}, u32[]{:S(2)}, u32[]{:S(2)}) collective-permute-start(bf16[256,1024]{1,0:T(8,128)(2,1)S(1)} %bitcast.70), channel_id=1, source_target_pairs={{0,24},{8,0},{16,8},{24,16},{1,25},{9,1},{17,9},{25,17},{2,26},{10... | collective-permute-start | bytes 1572872 | tf_op jit(solution)/shard_map/spread_centers/ppermute | solution.py:89
  55.3 20.4 %collective-permute-start = (bf16[256,1024]{1,0:T(8,128)(2,1)S(1)}, bf16[256,1024]{1,0:T(8,128)(2,1)S(1)}, u32[]{:S(2)}, u32[]{:S(2)}) collective-permute-start(bf16[256,1024]{1,0:T(8,128)(2,1)S(1)} %bitcast.71), channel_id=1, source_target_pairs={{0,1},{1,0},{2,3},{3,2},{4,5},{5,4},{6,7},{7,6},{8,9},{9,8},{10,11... | collective-permute-start | bytes 1572872 | tf_op jit(solution)/shard_map/spread_centers/ppermute | solution.py:94
  58.0 13.7 %slice-start = ((s8[6291456]{0:T(1024)(128)(4,1)}), s8[4194304]{0:T(1024)(128)(4,1)S(1)}, s32[]{:S(2)}) async-start(s8[6291456]{0:T(1024)(128)(4,1)} %bitcast.67), calls=%async_computation.2 | async-start | bytes 8388608
  58.2 13.5 %slice-start.1 = ((s8[6291456]{0:T(1024)(128)(4,1)}), s8[2097152]{0:T(1024)(128)(4,1)S(1)}, s32[]{:S(2)}) async-start(s8[6291456]{0:T(1024)(128)(4,1)} %bitcast.67), calls=%async_computation.3 | async-start | bytes 4194304
  65.2 18.4 %collective-permute-start.3 = (bf16[512,1024]{1,0:T(8,128)(2,1)S(1)}, bf16[512,1024]{1,0:T(8,128)(2,1)S(1)}, u32[]{:S(2)}, u32[]{:S(2)}) collective-permute-start(bf16[512,1024]{1,0:T(8,128)(2,1)S(1)} %constant_dynamic-update-slice_fusion), channel_id=1, source_target_pairs={{0,1},{1,0},{2,3},{3,2},{4,5},{5,4},{6,7},{7,6},{8,9},{9,8},{10,11... | collective-permute-start | bytes 3145736 | tf_op jit(solution)/shard_map/spread_centers/ppermute | solution.py:94
  68.6 9.4 %collective-permute-start.4 = (bf16[128,1024]{1,0:T(8,128)(2,1)S(1)}, bf16[128,1024]{1,0:T(8,128)(2,1)S(1)}, u32[]{:S(2)}, u32[]{:S(2)}) collective-permute-start(bf16[128,1024]{1,0:T(8,128)(2,1)S(1)} %slice.12), channel_id=1, source_target_pairs={{0,8},{8,16},{16,24},{24,0},{1,9},{9,17},{17,25},{25,1},{2,10},{10... | collective-permute-start | bytes 786440 | tf_op jit(solution)/shard_map/spread_centers/ppermute | solution.py:89
  68.8 9.3 %collective-permute-start.5 = (bf16[128,1024]{1,0:T(8,128)(2,1)S(1)}, bf16[128,1024]{1,0:T(8,128)(2,1)S(1)}, u32[]{:S(2)}, u32[]{:S(2)}) collective-permute-start(bf16[128,1024]{1,0:T(8,128)(2,1)S(1)} %slice.13), channel_id=1, source_target_pairs={{0,24},{8,0},{16,8},{24,16},{1,25},{9,1},{17,9},{25,17},{2,26},{10... | collective-permute-start | bytes 786440 | tf_op jit(solution)/shard_map/spread_centers/ppermute | solution.py:89
  78.1 3.1 %collective-permute-start.6 = (bf16[256,1024]{1,0:T(8,128)(2,1)S(1)}, bf16[256,1024]{1,0:T(8,128)(2,1)S(1)}, u32[]{:S(2)}, u32[]{:S(2)}) collective-permute-start(bf16[256,1024]{1,0:T(8,128)(2,1)S(1)} %constant_dynamic-update-slice_fusion.2), channel_id=1, source_target_pairs={{0,1},{1,0},{2,3},{3,2},{4,5},{5,4},{6,7},{7,6},{8,9},{9,8},{10,11... | collective-permute-start | bytes 1572872 | tf_op jit(solution)/shard_map/spread_centers/ppermute | solution.py:94
  83.9 4.0 %copy-start = (f32[3072]{0:T(1024)S(1)}, f32[3072]{0:T(1024)}, u32[]{:S(2)}) copy-start(f32[3072]{0:T(1024)} %param.5) | copy-start | bytes 36868

commit v8 on v7

--- a/solution.py
+++ b/solution.py
@@ -93,15 +93,20 @@
     def core_swap(x):
         return lax.ppermute(x, "c", [(0, 1), (1, 0)])
 
+    def y_ring(block):
+        near = y_send(block, 1), y_send(block, -1)
+        split = block.shape[0] // 2
+        far = y_send(near[0][:split], 1), y_send(near[1][split:], -1)
+        return jnp.concatenate(near, axis=0), jnp.concatenate(far, axis=0)
+
     with jax.named_scope("spread_centers"):
         plane = replicate_gather(compact, ("z", "x"), z_count * x_count)
-        y_near = y_send(plane, 1), y_send(plane, -1)
         split = plane.shape[0] // 2
-        y_far = jnp.concatenate(
-            [y_send(y_near[0][:split], 1), y_send(y_near[1][split:], -1)], axis=0
-        )
-        near = jnp.concatenate(y_near, axis=0)
-        pieces = [plane, core_swap(plane), near, core_swap(near), y_far, core_swap(y_far)]
+        near_a, far_a = y_ring(plane[:split])
+        near_b, far_b = y_ring(plane[split:])
+        far = jnp.concatenate([far_a, far_b], axis=0)
+        pieces = [plane, core_swap(plane), near_a, core_swap(near_a), near_b, core_swap(near_b)]
+        pieces += [far, core_swap(far)]
 
     with jax.named_scope("distance_min"):
         running = nearest

time: 88.9 us -> 97.7 us (1.099)
  starting transfers between devices: 30.1 us -> 36 us
  waiting for transfers between devices: 20.8 us -> 22.9 us
    ppermute x4 -> x8, starting transfers between devices: 5.67 us -> 11 us  [y_send(): lax.ppermute(x, 'y', [(i, (i + s) % y_count) for i in range(y_count)])]
    ppermute x4 -> x8, waiting for transfers between devices: 1.84 us -> 4 us  [y_send(): lax.ppermute(x, 'y', [(i, (i + s) % y_count) for i in range(y_count)])]
    ppermute x3 -> x4, starting transfers between devices: 6.62 us -> 7.17 us  [core_swap(): return lax.ppermute(x, 'c', [(0, 1), (1, 0)])]
    dot_general x6 -> x8, matrix products: 19.6 us -> 19.9 us  [one_block(): lax.dot_general(block_rows, fragment, (((1,), (1,)), ((), ())), preferred...]
  transfers between devices with their start and end apart: 9 -> 14, of which waited for: 3 -> 4; matrix products, arithmetic and copies ran while one was open for 24% -> 25% of each run, Pallas kernels for 0% -> 0%
where the time goes in v8:
time: 97.7 us; the launch traced here: 97.3 us
  starting transfers between devices  36 us (37%)
  waiting for transfers between devices  22.9 us (23%)
  matrix products  19.9 us (20%)
  other arithmetic  10.9 us (11%)
  local copies, waits for them, and re-layouts  7.14 us (7%)
    dot_general x8, matrix products, one_block(): lax.dot_general(block_rows, fragment, (((1,), (1,)), ((), ())), preferred...  19.9 us
    all_to_all x1, waiting for transfers between devices, replicate_gather(): got = lax.all_to_all(copies, axes, 0, 0, tiled=True)  12.5 us
    ppermute x8, starting transfers between devices, y_send(): lax.ppermute(x, 'y', [(i, (i + s) % y_count) for i in range(y_count)])  11 us
    all_to_all x1, starting transfers between devices, replicate_gather(): got = lax.all_to_all(copies, axes, 0, 0, tiled=True)  9.24 us
    all_to_all x1, starting transfers between devices, shards(): landed = lax.all_to_all(send_rows, DEV_AXES, 0, 0, tiled=True)  8.59 us
    ppermute x4, starting transfers between devices, core_swap(): return lax.ppermute(x, 'c', [(0, 1), (1, 0)])  7.17 us
    all_to_all x1, waiting for transfers between devices, shards(): landed = lax.all_to_all(send_rows, DEV_AXES, 0, 0, tiled=True)  6.42 us
    gather x1, local copies, waits for them, and re-layouts, shards(): send_rows = jnp.take(pool, peer_offset, axis=0)  4.27 us
  transfers between devices with their start and end apart: 14, of which 4 were waited for; matrix products, arithmetic and copies ran while one was open for 25% of the time, Pallas kernels for 0%

profile of v8, /device:TPU:1, one launch (start us, length us, event | category | flops | bytes accessed | tf_op | source)
XLA Modules:
  0.0 97.3 jit_solution(10662829084510829219)
XLA Ops:
  0.0 0.7 iota_add_fusion.1
  0.7 0.7 compare_reduce_fusion
  1.4 0.7 iota_add_fusion
  2.3 0.8 select_reduce_fusion
  3.1 4.3 %gather_fusion = bf16[32,1024]{1,0:T(8,128)(2,1)S(1)} fusion(bf16[3072,1024]{1,0:T(8,128)(2,1)} %param.4, s32[1024]{0:T(1024)S(1)} %pad_clamp_fusion.1), kind=kCustom, calls=%fused_computation | custom fusion | bytes 131200 | tf_op jit(solution)/shard_map/compact_centers/jit(_take)/gather | solution.py:80
  8.0 0.7 reduce.20
  8.6 0.7 reshape.193
  9.3 8.6 %all-to-all-start = ((bf16[32,2,512]{2,1,0:T(2,128)(2,1)}), bf16[32,2,512]{2,1,0:T(2,128)(2,1)S(1)}, u32[]{:S(2)}, u32[]{:S(2)}) async-start(bf16[32,2,512]{2,1,0:T(2,128)(2,1)} %reshape.193), calls=%async_computation | async-start | bytes 131072 | tf_op jit(solution)/shard_map/compact_centers/all_to_all | solution.py:81
  17.9 0.9 select_reduce_fusion.1
  18.8 6.4 %all-to-all-done = bf16[32,2,512]{2,1,0:T(2,128)(2,1)S(1)} async-done(((bf16[32,2,512]{2,1,0:T(2,128)(2,1)}), bf16[32,2,512]{2,1,0:T(2,128)(2,1)S(1)}, u32[]{:S(2)}, u32[]{:S(2)}) %all-to-all-start) | async-done | bytes 65568 | tf_op jit(solution)/shard_map/compact_centers/all_to_all | solution.py:81
  25.9 0.9 broadcast_in_dim.117
  26.8 9.2 %all-to-all-start.1 = ((bf16[32,8,1024]{2,1,0:T(8,128)(2,1)}), bf16[32,8,1024]{2,1,0:T(8,128)(2,1)S(1)}, u32[]{:S(2)}, u32[]{:S(2)}) async-start(bf16[32,8,1024]{2,1,0:T(8,128)(2,1)} %broadcast_in_dim.117), calls=%async_computation.1 | async-start | bytes 1048576 | tf_op jit(solution)/shard_map/spread_centers/all_to_all | solution.py:54
  36.0 4.1 %fusion = f32[3072]{0:T(1024)S(1)} fusion(bf16[3072,1024]{1,0:T(8,128)(2,1)} %param.4), kind=kLoop, calls=%fused_computation.3 | loop fusion | flops 9434112 | bytes 6303744 | tf_op jit(solution)/shard_map/rd,rd->r/dot_general | solution.py:91
  40.1 12.5 %all-to-all-done.1 = bf16[32,8,1024]{2,1,0:T(8,128)(2,1)S(1)} async-done(((bf16[32,8,1024]{2,1,0:T(8,128)(2,1)}), bf16[32,8,1024]{2,1,0:T(8,128)(2,1)S(1)}, u32[]{:S(2)}, u32[]{:S(2)}) %all-to-all-start.1) | async-done | bytes 524320 | tf_op jit(solution)/shard_map/spread_centers/all_to_all | solution.py:54
  53.1 2.3 %collective-permute-start.2 = (bf16[128,1024]{1,0:T(8,128)(2,1)S(1)}, bf16[128,1024]{1,0:T(8,128)(2,1)S(1)}, u32[]{:S(2)}, u32[]{:S(2)}) collective-permute-start(bf16[128,1024]{1,0:T(8,128)(2,1)S(1)} %get-tuple-element.116), channel_id=1, source_target_pairs={{0,24},{8,0},{16,8},{24,16},{1,25},{9,1},{17,9},{25,17},{2,26},{10... | collective-permute-start | bytes 786440 | tf_op jit(solution)/shard_map/spread_centers/ppermute | solution.py:89
  55.4 2.7 %collective-permute-start.5 = (bf16[128,1024]{1,0:T(8,128)(2,1)S(1)}, bf16[128,1024]{1,0:T(8,128)(2,1)S(1)}, u32[]{:S(2)}, u32[]{:S(2)}) collective-permute-start(bf16[128,1024]{1,0:T(8,128)(2,1)S(1)} %get-tuple-element.115), channel_id=1, source_target_pairs={{0,24},{8,0},{16,8},{24,16},{1,25},{9,1},{17,9},{25,17},{2,26},{10... | collective-permute-start | bytes 786440 | tf_op jit(solution)/shard_map/spread_centers/ppermute | solution.py:89
  58.1 3.3 %collective-permute-start = (bf16[256,1024]{1,0:T(8,128)(2,1)S(1)}, bf16[256,1024]{1,0:T(8,128)(2,1)S(1)}, u32[]{:S(2)}, u32[]{:S(2)}) collective-permute-start(bf16[256,1024]{1,0:T(8,128)(2,1)S(1)} %bitcast.89), channel_id=1, source_target_pairs={{0,1},{1,0},{2,3},{3,2},{4,5},{5,4},{6,7},{7,6},{8,9},{9,8},{10,11... | collective-permute-start | bytes 1572872 | tf_op jit(solution)/shard_map/spread_centers/ppermute | solution.py:94
  61.6 5.0 %fusion.20 = f32[3072]{0:T(1024)S(1)} fusion(bf16[3072,1024]{1,0:T(8,128)(2,1)} %param.4, f32[256]{0:T(256)S(1)} %fusion.28, f32[3072]{0:T(1024)S(1)} %fusion, bf16[32,8,1024]{2,1,0:T(8,128)(2,1)S(1)} %all-to-all-done.1), kind=kOutput, calls=%fused_computation.35 | convolution fusion | flops 1614541824 | bytes 6841344 | tf_op jit(solution)/shard_map/distance_min/while/body/eval_jaxpr/dot_general | solution.py:21
  67.2 1.8 %collective-permute-start.6 = (bf16[256,1024]{1,0:T(8,128)(2,1)S(1)}, bf16[256,1024]{1,0:T(8,128)(2,1)S(1)}, u32[]{:S(2)}, u32[]{:S(2)}) collective-permute-start(bf16[256,1024]{1,0:T(8,128)(2,1)S(1)} %constant_dynamic-update-slice_fusion.2), channel_id=1, source_target_pairs={{0,1},{1,0},{2,3},{3,2},{4,5},{5,4},{6,7},{7,6},{8,9},{9,8},{10,11... | collective-permute-start | bytes 1572872 | tf_op jit(solution)/shard_map/spread_centers/ppermute | solution.py:94
  69.0 2.1 %fusion.19 = f32[3072]{0:T(1024)S(1)} fusion(bf16[256,1024]{1,0:T(8,128)(2,1)S(1)} %constant_dynamic-update-slice_fusion, bf16[3072,1024]{1,0:T(8,128)(2,1)S(1)} %bitcast.88, f32[256]{0:T(256)S(1)} %fusion.26, f32[3072]{0:T(1024)S(1)} %fusion), kind=kOutput, calls=%fused_computation.34 | convolution fusion | flops 1614541824 | bytes 6841344 | tf_op jit(solution)/shard_map/distance_min/while/body/eval_jaxpr/dot_general | solution.py:21
  71.2 2.7 %collective-permute-start.8 = (bf16[64,1024]{1,0:T(8,128)(2,1)S(1)}, bf16[64,1024]{1,0:T(8,128)(2,1)S(1)}, u32[]{:S(2)}, u32[]{:S(2)}) collective-permute-start(bf16[64,1024]{1,0:T(8,128)(2,1)S(1)} %slice.39), channel_id=1, source_target_pairs={{0,24},{8,0},{16,8},{24,16},{1,25},{9,1},{17,9},{25,17},{2,26},{10... | collective-permute-start | bytes 393224 | tf_op jit(solution)/shard_map/spread_centers/ppermute | solution.py:89
  74.0 2.1 %fusion.18 = f32[3072]{0:T(1024)S(1)} fusion(bf16[256,1024]{1,0:T(8,128)(2,1)S(1)} %constant_dynamic-update-slice_fusion.2, bf16[3072,1024]{1,0:T(8,128)(2,1)S(1)} %bitcast.88, f32[256]{0:T(256)S(1)} %fusion.24, f32[3072]{0:T(1024)S(1)} %fusion), kind=kOutput, calls=%fused_computation.33 | convolution fusion | flops 1614541824 | bytes 6841344 | tf_op jit(solution)/shard_map/distance_min/while/body/eval_jaxpr/dot_general | solution.py:21
  76.1 1.4 %collective-permute-done.7 = bf16[64,1024]{1,0:T(8,128)(2,1)S(1)} collective-permute-done((bf16[64,1024]{1,0:T(8,128)(2,1)S(1)}, bf16[64,1024]{1,0:T(8,128)(2,1)S(1)}, u32[]{:S(2)}, u32[]{:S(2)}) %collective-permute-start.7) | collective-permute-done | bytes 131104 | tf_op jit(solution)/shard_map/spread_centers/ppermute | solution.py:89
  77.5 2.8 %collective-permute-start.10 = (bf16[64,1024]{1,0:T(8,128)(2,1)S(1)}, bf16[64,1024]{1,0:T(8,128)(2,1)S(1)}, u32[]{:S(2)}, u32[]{:S(2)}) collective-permute-start(bf16[64,1024]{1,0:T(8,128)(2,1)S(1)} %slice.41), channel_id=1, source_target_pairs={{0,24},{8,0},{16,8},{24,16},{1,25},{9,1},{17,9},{25,17},{2,26},{10... | collective-permute-start | bytes 393224 | tf_op jit(solution)/shard_map/spread_centers/ppermute | solution.py:89
  80.3 2.6 %collective-permute-done.9 = bf16[64,1024]{1,0:T(8,128)(2,1)S(1)} collective-permute-done((bf16[64,1024]{1,0:T(8,128)(2,1)S(1)}, bf16[64,1024]{1,0:T(8,128)(2,1)S(1)}, u32[]{:S(2)}, u32[]{:S(2)}) %collective-permute-start.9) | collective-permute-done | bytes 131104 | tf_op jit(solution)/shard_map/spread_centers/ppermute | solution.py:89
  83.1 2.0 %collective-permute-start.11 = (bf16[256,1024]{1,0:T(8,128)(2,1)S(1)}, bf16[256,1024]{1,0:T(8,128)(2,1)S(1)}, u32[]{:S(2)}, u32[]{:S(2)}) collective-permute-start(bf16[256,1024]{1,0:T(8,128)(2,1)S(1)} %constant_dynamic-update-slice_fusion.4), channel_id=1, source_target_pairs={{0,1},{1,0},{2,3},{3,2},{4,5},{5,4},{6,7},{7,6},{8,9},{9,8},{10,11... | collective-permute-start | bytes 1572872 | tf_op jit(solution)/shard_map/spread_centers/ppermute | solution.py:94
  85.2 2.1 %fusion.17 = f32[3072]{0:T(1024)S(1)} fusion(bf16[256,1024]{1,0:T(8,128)(2,1)S(1)} %constant_dynamic-update-slice_fusion.4, bf16[3072,1024]{1,0:T(8,128)(2,1)S(1)} %bitcast.88, f32[256]{0:T(256)S(1)} %fusion.22, f32[3072]{0:T(1024)S(1)} %fusion), kind=kOutput, calls=%fused_computation.32 | convolution fusion | flops 1614541824 | bytes 6841344 | tf_op jit(solution)/shard_map/distance_min/while/body/eval_jaxpr/dot_general | solution.py:21
  87.5 2.1 %maximum_reduce_fusion.3 = f32[3072]{0:T(1024)S(1)} fusion(f32[256]{0:T(256)S(1)} %fusion.27, f32[3072]{0:T(1024)S(1)} %fusion, bf16[256,1024]{1,0:T(8,128)(2,1)S(1)} %collective-permute-done, bf16[3072,1024]{1,0:T(8,128)(2,1)S(1)} %bitcast.88), kind=kOutput, calls=%fused_computation.31 | convolution fusion | flops 1614541824 | bytes 6841344 | tf_op jit(solution)/shard_map/distance_min/while/body/eval_jaxpr/dot_general | solution.py:21
  89.8 2.1 %maximum_reduce_fusion.2 = f32[3072]{0:T(1024)S(1)} fusion(f32[256]{0:T(256)S(1)} %fusion.25, f32[3072]{0:T(1024)S(1)} %fusion, bf16[256,1024]{1,0:T(8,128)(2,1)S(1)} %collective-permute-done.3, bf16[3072,1024]{1,0:T(8,128)(2,1)S(1)} %bitcast.88), kind=kOutput, calls=%fused_computation.30 | convolution fusion | flops 1614541824 | bytes 6841344 | tf_op jit(solution)/shard_map/distance_min/while/body/eval_jaxpr/dot_general | solution.py:21
  92.2 2.1 %maximum_reduce_fusion.1 = f32[3072]{0:T(1024)S(1)} fusion(f32[256]{0:T(256)S(1)} %fusion.23, f32[3072]{0:T(1024)S(1)} %fusion, bf16[256,1024]{1,0:T(8,128)(2,1)S(1)} %collective-permute-done.6, bf16[3072,1024]{1,0:T(8,128)(2,1)S(1)} %bitcast.88), kind=kOutput, calls=%fused_computation.29 | convolution fusion | flops 1614541824 | bytes 6841344 | tf_op jit(solution)/shard_map/distance_min/while/body/eval_jaxpr/dot_general | solution.py:21
  94.5 2.1 %maximum_reduce_fusion = f32[3072]{0:T(1024)S(1)} fusion(f32[256]{0:T(256)S(1)} %fusion.21, f32[3072]{0:T(1024)S(1)} %fusion, bf16[256,1024]{1,0:T(8,128)(2,1)S(1)} %collective-permute-done.11, bf16[3072,1024]{1,0:T(8,128)(2,1)S(1)} %bitcast.88), kind=kOutput, calls=%fused_computation.28 | convolution fusion | flops 1614541824 | bytes 6841344 | tf_op jit(solution)/shard_map/distance_min/while/body/eval_jaxpr/dot_general | solution.py:21
  96.6 0.6 minimum_minimum_fusion
  (58 shorter events, 3.8 us)
Async XLA Ops:
  9.3 15.9 %all-to-all-start = ((bf16[32,2,512]{2,1,0:T(2,128)(2,1)}), bf16[32,2,512]{2,1,0:T(2,128)(2,1)S(1)}, u32[]{:S(2)}, u32[]{:S(2)}) async-start(bf16[32,2,512]{2,1,0:T(2,128)(2,1)} %reshape.193), calls=%async_computation | async-start | bytes 131072 | tf_op jit(solution)/shard_map/compact_centers/all_to_all | solution.py:81
  26.8 25.8 %all-to-all-start.1 = ((bf16[32,8,1024]{2,1,0:T(8,128)(2,1)}), bf16[32,8,1024]{2,1,0:T(8,128)(2,1)S(1)}, u32[]{:S(2)}, u32[]{:S(2)}) async-start(bf16[32,8,1024]{2,1,0:T(8,128)(2,1)} %broadcast_in_dim.117), calls=%async_computation.1 | async-start | bytes 1048576 | tf_op jit(solution)/shard_map/spread_centers/all_to_all | solution.py:54
  52.6 13.9 %collective-permute-start.1 = (bf16[128,1024]{1,0:T(8,128)(2,1)S(1)}, bf16[128,1024]{1,0:T(8,128)(2,1)S(1)}, u32[]{:S(2)}, u32[]{:S(2)}) collective-permute-start(bf16[128,1024]{1,0:T(8,128)(2,1)S(1)} %get-tuple-element.116), channel_id=1, source_target_pairs={{0,8},{8,16},{16,24},{24,0},{1,9},{9,17},{17,25},{25,1},{2,10},{10... | collective-permute-start | bytes 786440 | tf_op jit(solution)/shard_map/spread_centers/ppermute | solution.py:89
  53.1 13.6 %collective-permute-start.2 = (bf16[128,1024]{1,0:T(8,128)(2,1)S(1)}, bf16[128,1024]{1,0:T(8,128)(2,1)S(1)}, u32[]{:S(2)}, u32[]{:S(2)}) collective-permute-start(bf16[128,1024]{1,0:T(8,128)(2,1)S(1)} %get-tuple-element.116), channel_id=1, source_target_pairs={{0,24},{8,0},{16,8},{24,16},{1,25},{9,1},{17,9},{25,17},{2,26},{10... | collective-permute-start | bytes 786440 | tf_op jit(solution)/shard_map/spread_centers/ppermute | solution.py:89
  55.4 11.4 %collective-permute-start.4 = (bf16[128,1024]{1,0:T(8,128)(2,1)S(1)}, bf16[128,1024]{1,0:T(8,128)(2,1)S(1)}, u32[]{:S(2)}, u32[]{:S(2)}) collective-permute-start(bf16[128,1024]{1,0:T(8,128)(2,1)S(1)} %get-tuple-element.115), channel_id=1, source_target_pairs={{0,8},{8,16},{16,24},{24,0},{1,9},{9,17},{17,25},{25,1},{2,10},{10... | collective-permute-start | bytes 786440 | tf_op jit(solution)/shard_map/spread_centers/ppermute | solution.py:89
  55.4 11.6 %collective-permute-start.5 = (bf16[128,1024]{1,0:T(8,128)(2,1)S(1)}, bf16[128,1024]{1,0:T(8,128)(2,1)S(1)}, u32[]{:S(2)}, u32[]{:S(2)}) collective-permute-start(bf16[128,1024]{1,0:T(8,128)(2,1)S(1)} %get-tuple-element.115), channel_id=1, source_target_pairs={{0,24},{8,0},{16,8},{24,16},{1,25},{9,1},{17,9},{25,17},{2,26},{10... | collective-permute-start | bytes 786440 | tf_op jit(solution)/shard_map/spread_centers/ppermute | solution.py:89
  58.1 29.2 %collective-permute-start = (bf16[256,1024]{1,0:T(8,128)(2,1)S(1)}, bf16[256,1024]{1,0:T(8,128)(2,1)S(1)}, u32[]{:S(2)}, u32[]{:S(2)}) collective-permute-start(bf16[256,1024]{1,0:T(8,128)(2,1)S(1)} %bitcast.89), channel_id=1, source_target_pairs={{0,1},{1,0},{2,3},{3,2},{4,5},{5,4},{6,7},{7,6},{8,9},{9,8},{10,11... | collective-permute-start | bytes 1572872 | tf_op jit(solution)/shard_map/spread_centers/ppermute | solution.py:94
  61.4 7.6 %slice-start = ((s8[6291456]{0:T(1024)(128)(4,1)}), s8[4194304]{0:T(1024)(128)(4,1)S(1)}, s32[]{:S(2)}) async-start(s8[6291456]{0:T(1024)(128)(4,1)} %bitcast.87), calls=%async_computation.2 | async-start | bytes 8388608
  61.6 7.4 %slice-start.1 = ((s8[6291456]{0:T(1024)(128)(4,1)}), s8[2097152]{0:T(1024)(128)(4,1)S(1)}, s32[]{:S(2)}) async-start(s8[6291456]{0:T(1024)(128)(4,1)} %bitcast.87), calls=%async_computation.3 | async-start | bytes 4194304
  66.7 23.0 %collective-permute-start.3 = (bf16[256,1024]{1,0:T(8,128)(2,1)S(1)}, bf16[256,1024]{1,0:T(8,128)(2,1)S(1)}, u32[]{:S(2)}, u32[]{:S(2)}) collective-permute-start(bf16[256,1024]{1,0:T(8,128)(2,1)S(1)} %constant_dynamic-update-slice_fusion), channel_id=1, source_target_pairs={{0,1},{1,0},{2,3},{3,2},{4,5},{5,4},{6,7},{7,6},{8,9},{9,8},{10,11... | collective-permute-start | bytes 1572872 | tf_op jit(solution)/shard_map/spread_centers/ppermute | solution.py:94
  67.2 24.8 %collective-permute-start.6 = (bf16[256,1024]{1,0:T(8,128)(2,1)S(1)}, bf16[256,1024]{1,0:T(8,128)(2,1)S(1)}, u32[]{:S(2)}, u32[]{:S(2)}) collective-permute-start(bf16[256,1024]{1,0:T(8,128)(2,1)S(1)} %constant_dynamic-update-slice_fusion.2), channel_id=1, source_target_pairs={{0,1},{1,0},{2,3},{3,2},{4,5},{5,4},{6,7},{7,6},{8,9},{9,8},{10,11... | collective-permute-start | bytes 1572872 | tf_op jit(solution)/shard_map/spread_centers/ppermute | solution.py:94
  71.1 6.4 %collective-permute-start.7 = (bf16[64,1024]{1,0:T(8,128)(2,1)S(1)}, bf16[64,1024]{1,0:T(8,128)(2,1)S(1)}, u32[]{:S(2)}, u32[]{:S(2)}) collective-permute-start(bf16[64,1024]{1,0:T(8,128)(2,1)S(1)} %slice.38), channel_id=1, source_target_pairs={{0,8},{8,16},{16,24},{24,0},{1,9},{9,17},{17,25},{25,1},{2,10},{10... | collective-permute-start | bytes 393224 | tf_op jit(solution)/shard_map/spread_centers/ppermute | solution.py:89
  71.2 6.3 %collective-permute-start.8 = (bf16[64,1024]{1,0:T(8,128)(2,1)S(1)}, bf16[64,1024]{1,0:T(8,128)(2,1)S(1)}, u32[]{:S(2)}, u32[]{:S(2)}) collective-permute-start(bf16[64,1024]{1,0:T(8,128)(2,1)S(1)} %slice.39), channel_id=1, source_target_pairs={{0,24},{8,0},{16,8},{24,16},{1,25},{9,1},{17,9},{25,17},{2,26},{10... | collective-permute-start | bytes 393224 | tf_op jit(solution)/shard_map/spread_centers/ppermute | solution.py:89
  77.5 5.4 %collective-permute-start.9 = (bf16[64,1024]{1,0:T(8,128)(2,1)S(1)}, bf16[64,1024]{1,0:T(8,128)(2,1)S(1)}, u32[]{:S(2)}, u32[]{:S(2)}) collective-permute-start(bf16[64,1024]{1,0:T(8,128)(2,1)S(1)} %slice.40), channel_id=1, source_target_pairs={{0,8},{8,16},{16,24},{24,0},{1,9},{9,17},{17,25},{25,1},{2,10},{10... | collective-permute-start | bytes 393224 | tf_op jit(solution)/shard_map/spread_centers/ppermute | solution.py:89
  77.5 5.4 %collective-permute-start.10 = (bf16[64,1024]{1,0:T(8,128)(2,1)S(1)}, bf16[64,1024]{1,0:T(8,128)(2,1)S(1)}, u32[]{:S(2)}, u32[]{:S(2)}) collective-permute-start(bf16[64,1024]{1,0:T(8,128)(2,1)S(1)} %slice.41), channel_id=1, source_target_pairs={{0,24},{8,0},{16,8},{24,16},{1,25},{9,1},{17,9},{25,17},{2,26},{10... | collective-permute-start | bytes 393224 | tf_op jit(solution)/shard_map/spread_centers/ppermute | solution.py:89
  83.1 11.2 %collective-permute-start.11 = (bf16[256,1024]{1,0:T(8,128)(2,1)S(1)}, bf16[256,1024]{1,0:T(8,128)(2,1)S(1)}, u32[]{:S(2)}, u32[]{:S(2)}) collective-permute-start(bf16[256,1024]{1,0:T(8,128)(2,1)S(1)} %constant_dynamic-update-slice_fusion.4), channel_id=1, source_target_pairs={{0,1},{1,0},{2,3},{3,2},{4,5},{5,4},{6,7},{7,6},{8,9},{9,8},{10,11... | collective-permute-start | bytes 1572872 | tf_op jit(solution)/shard_map/spread_centers/ppermute | solution.py:94
  94.5 2.1 %copy-start = (f32[3072]{0:T(1024)S(1)}, f32[3072]{0:T(1024)}, u32[]{:S(2)}) copy-start(f32[3072]{0:T(1024)} %param.5) | copy-start | bytes 36868

commit v9 on v7

--- a/solution.py
+++ b/solution.py
@@ -3,6 +3,8 @@
 import jax
 import jax.numpy as jnp
 from jax import lax
+from jax.experimental import pallas as pl
+from jax.experimental.pallas import tpu as pltpu
 from jax.sharding import Mesh, PartitionSpec as P
 
 MOST = 32
@@ -49,6 +51,36 @@
     return got
 
 
+def _gather_rows_kernel(index_ref, table_ref, out_ref, sems):
+    count = out_ref.shape[0]
+
+    def copy(r):
+        return pltpu.make_async_copy(
+            table_ref.at[pl.ds(pl.multiple_of(index_ref[r] * 2, 2), 2)], out_ref.at[r], sems.at[r]
+        )
+
+    for r in range(count):
+        copy(r).start()
+    for r in range(count):
+        copy(r).wait()
+
+
+def gather_rows(table, index):
+    count = index.shape[0]
+    width = table.shape[1]
+    index = jnp.clip(index // 2, 0, table.shape[0] // 2 - 1).astype(jnp.int32)
+    return pl.pallas_call(
+        _gather_rows_kernel,
+        out_shape=jax.ShapeDtypeStruct((count, 2, width), table.dtype),
+        in_specs=[pl.BlockSpec(memory_space=pltpu.SMEM), pl.BlockSpec(memory_space=pl.ANY)],
+        out_specs=pl.BlockSpec(memory_space=pltpu.VMEM),
+        scratch_shapes=[pltpu.SemaphoreType.DMA((count,))],
+        cost_estimate=pl.CostEstimate(
+            flops=0, bytes_accessed=2 * count * width * table.dtype.itemsize, transcendentals=0
+        ),
+    )(index, table)
+
+
 def replicate_gather(x, axes, count):
     copies = jnp.broadcast_to(x[None], (count,) + x.shape)
     got = lax.all_to_all(copies, axes, 0, 0, tiled=True)
@@ -77,13 +109,13 @@
             (position % dev_count)[None, :] == devices[:, None]
         )
         peer_offset = jnp.sum(jnp.where(to_peer, offsets[None, :], 0), axis=1)
-        send_rows = jnp.take(pool, peer_offset, axis=0)
+        send_rows = gather_rows(pool, peer_offset)
         landed = lax.all_to_all(send_rows, DEV_AXES, 0, 0, tiled=True)
         wanted = my_index + dev_count * jnp.arange(per_device, dtype=jnp.int32)
-        source = jnp.sum(
-            jnp.where(position[None, :] == wanted[:, None], owners[None, :], 0), axis=1
-        )
-        compact = jnp.take(landed, source, axis=0)
+        is_wanted = position[None, :] == wanted[:, None]
+        source = jnp.sum(jnp.where(is_wanted, owners[None, :], 0), axis=1)
+        parity = jnp.sum(jnp.where(is_wanted, offsets[None, :], 0), axis=1) % 2
+        compact = jnp.take(landed.reshape(-1, landed.shape[-1]), source * 2 + parity, axis=0)
 
     def y_send(x, s):
         return lax.ppermute(x, "y", [(i, (i + s) % y_count) for i in range(y_count)])

time: 88.9 us -> 86.9 us (0.978)
  local copies, waits for them, and re-layouts: 7.09 us -> 1.64 us
  Pallas kernels: 0 us -> 3.06 us
  waiting for transfers between devices: 20.8 us -> 21.7 us
    gather x2 -> x1, local copies, waits for them, and re-layouts: 4.84 us -> 0.57 us  [shards(): jnp.take(landed.reshape(-1, landed.shape[-1]), source * 2 + parity, axis=0)]
    pallas_call x0 -> x1, Pallas kernels: none -> 3.06 us  [gather_rows(): pl.pallas_call(_gather_rows_kernel, out_shape=jax.ShapeDtypeStruct((count...]
    all_to_all x1, waiting for transfers between devices: 6.42 us -> 7.37 us  [shards(): landed = lax.all_to_all(send_rows, DEV_AXES, 0, 0, tiled=True)]
where the time goes in v9:
time: 86.9 us; the launch traced here: 86.5 us
  starting transfers between devices  30.3 us (35%)
  waiting for transfers between devices  21.7 us (25%)
  matrix products  19.6 us (23%)
  other arithmetic  9.93 us (11%)
  Pallas kernels  3.06 us (4%)
  local copies, waits for them, and re-layouts  1.64 us (2%)
    dot_general x6, matrix products, one_block(): lax.dot_general(block_rows, fragment, (((1,), (1,)), ((), ())), preferred...  19.6 us
    all_to_all x1, waiting for transfers between devices, replicate_gather(): got = lax.all_to_all(copies, axes, 0, 0, tiled=True)  12.5 us
    all_to_all x1, starting transfers between devices, replicate_gather(): got = lax.all_to_all(copies, axes, 0, 0, tiled=True)  9.41 us
    all_to_all x1, starting transfers between devices, shards(): landed = lax.all_to_all(send_rows, DEV_AXES, 0, 0, tiled=True)  8.66 us
    all_to_all x1, waiting for transfers between devices, shards(): landed = lax.all_to_all(send_rows, DEV_AXES, 0, 0, tiled=True)  7.37 us
    ppermute x3, starting transfers between devices, core_swap(): return lax.ppermute(x, 'c', [(0, 1), (1, 0)])  6.58 us
    ppermute x4, starting transfers between devices, y_send(): lax.ppermute(x, 'y', [(i, (i + s) % y_count) for i in range(y_count)])  5.67 us
    dot_general x1, other arithmetic, shards(): jnp.einsum('rd,rd->r', pool, pool, preferred_element_type=jnp.float32)  4.08 us
  transfers between devices with their start and end apart: 9, of which 3 were waited for; matrix products, arithmetic and copies ran while one was open for 24% of the time, Pallas kernels for 0%

profile of v9, /device:TPU:1, one launch (start us, length us, event | category | flops | bytes accessed | tf_op | source)
XLA Modules:
  0.0 86.5 jit_solution(1452718579699768568)
XLA Ops:
  0.0 0.8 iota_add_fusion.1
  0.8 0.7 iota_add_fusion
  1.6 0.7 compare_reduce_fusion
  2.3 0.8 select_reduce_fusion
  3.1 0.5 fusion.30.index_ref
  3.7 3.1 %compact_centers.1 = bf16[32,2,1024]{2,1,0:T(2,128)(2,1)} custom-call(s32[32]{0:T(128)} %fusion.30.index_ref, bf16[3072,1024]{1,0:T(8,128)(2,1)} %table_ref.1), custom_call_target="tpu_custom_call" | custom-call | bytes 131072 | tf_op jit(solution)/shard_map/compact_centers/pallas_call | solution.py:72
  6.7 8.7 %all-to-all-start = ((bf16[32,2,1024]{2,1,0:T(2,128)(2,1)}), bf16[32,2,1024]{2,1,0:T(2,128)(2,1)S(1)}, u32[]{:S(2)}, u32[]{:S(2)}) async-start(bf16[32,2,1024]{2,1,0:T(2,128)(2,1)} %compact_centers.1), calls=%async_computation | async-start | bytes 262144 | tf_op jit(solution)/shard_map/compact_centers/all_to_all | solution.py:113
  15.4 0.2 fusion.22
  15.7 7.4 %all-to-all-done = bf16[32,2,1024]{2,1,0:T(2,128)(2,1)S(1)} async-done(((bf16[32,2,1024]{2,1,0:T(2,128)(2,1)}), bf16[32,2,1024]{2,1,0:T(2,128)(2,1)S(1)}, u32[]{:S(2)}, u32[]{:S(2)}) %all-to-all-start) | async-done | bytes 131104 | tf_op jit(solution)/shard_map/compact_centers/all_to_all | solution.py:113
  23.1 0.6 gather_fusion
  23.7 0.9 broadcast_in_dim.100
  24.6 9.4 %all-to-all-start.1 = ((bf16[32,8,1024]{2,1,0:T(8,128)(2,1)}), bf16[32,8,1024]{2,1,0:T(8,128)(2,1)S(1)}, u32[]{:S(2)}, u32[]{:S(2)}) async-start(bf16[32,8,1024]{2,1,0:T(8,128)(2,1)} %broadcast_in_dim.100), calls=%async_computation.1 | async-start | bytes 1048576 | tf_op jit(solution)/shard_map/spread_centers/all_to_all | solution.py:86
  34.0 4.1 %fusion = f32[3072]{0:T(1024)S(1)} fusion(bf16[3072,1024]{1,0:T(8,128)(2,1)} %table_ref.1), kind=kLoop, calls=%fused_computation.2 | loop fusion | flops 9434112 | bytes 6303744 | tf_op jit(solution)/shard_map/rd,rd->r/dot_general | solution.py:123
  38.1 12.5 %all-to-all-done.1 = bf16[32,8,1024]{2,1,0:T(8,128)(2,1)S(1)} async-done(((bf16[32,8,1024]{2,1,0:T(8,128)(2,1)}), bf16[32,8,1024]{2,1,0:T(8,128)(2,1)S(1)}, u32[]{:S(2)}, u32[]{:S(2)}) %all-to-all-start.1) | async-done | bytes 524320 | tf_op jit(solution)/shard_map/spread_centers/all_to_all | solution.py:86
  50.6 0.3 collective-permute-start.1
  50.9 2.3 %collective-permute-start.2 = (bf16[256,1024]{1,0:T(8,128)(2,1)S(1)}, bf16[256,1024]{1,0:T(8,128)(2,1)S(1)}, u32[]{:S(2)}, u32[]{:S(2)}) collective-permute-start(bf16[256,1024]{1,0:T(8,128)(2,1)S(1)} %bitcast.67), channel_id=1, source_target_pairs={{0,24},{8,0},{16,8},{24,16},{1,25},{9,1},{17,9},{25,17},{2,26},{10... | collective-permute-start | bytes 1572872 | tf_op jit(solution)/shard_map/spread_centers/ppermute | solution.py:121
  53.3 2.7 %collective-permute-start = (bf16[256,1024]{1,0:T(8,128)(2,1)S(1)}, bf16[256,1024]{1,0:T(8,128)(2,1)S(1)}, u32[]{:S(2)}, u32[]{:S(2)}) collective-permute-start(bf16[256,1024]{1,0:T(8,128)(2,1)S(1)} %bitcast.68), channel_id=1, source_target_pairs={{0,1},{1,0},{2,3},{3,2},{4,5},{5,4},{6,7},{7,6},{8,9},{9,8},{10,11... | collective-permute-start | bytes 1572872 | tf_op jit(solution)/shard_map/spread_centers/ppermute | solution.py:126
  56.2 5.0 %fusion.16 = f32[3072]{0:T(1024)S(1)} fusion(bf16[3072,1024]{1,0:T(8,128)(2,1)} %table_ref.1, f32[256]{0:T(256)S(1)} %fusion.20, f32[3072]{0:T(1024)S(1)} %fusion, bf16[32,8,1024]{2,1,0:T(8,128)(2,1)S(1)} %all-to-all-done.1), kind=kOutput, calls=%fused_computation.28 | convolution fusion | flops 1614541824 | bytes 6841344 | tf_op jit(solution)/shard_map/distance_min/while/body/eval_jaxpr/dot_general | solution.py:23
  61.2 1.8 %collective-permute-done.1 = bf16[256,1024]{1,0:T(8,128)(2,1)S(1)} collective-permute-done((bf16[256,1024]{1,0:T(8,128)(2,1)S(1)}, bf16[256,1024]{1,0:T(8,128)(2,1)S(1)}, u32[]{:S(2)}, u32[]{:S(2)}) %collective-permute-start.1) | collective-permute-done | bytes 524320 | tf_op jit(solution)/shard_map/spread_centers/ppermute | solution.py:121
  63.1 3.2 %collective-permute-start.3 = (bf16[512,1024]{1,0:T(8,128)(2,1)S(1)}, bf16[512,1024]{1,0:T(8,128)(2,1)S(1)}, u32[]{:S(2)}, u32[]{:S(2)}) collective-permute-start(bf16[512,1024]{1,0:T(8,128)(2,1)S(1)} %constant_dynamic-update-slice_fusion), channel_id=1, source_target_pairs={{0,1},{1,0},{2,3},{3,2},{4,5},{5,4},{6,7},{7,6},{8,9},{9,8},{10,11... | collective-permute-start | bytes 3145736 | tf_op jit(solution)/shard_map/spread_centers/ppermute | solution.py:126
  66.3 0.3 fusion.14
  66.7 2.9 %collective-permute-start.5 = (bf16[128,1024]{1,0:T(8,128)(2,1)S(1)}, bf16[128,1024]{1,0:T(8,128)(2,1)S(1)}, u32[]{:S(2)}, u32[]{:S(2)}) collective-permute-start(bf16[128,1024]{1,0:T(8,128)(2,1)S(1)} %slice.11), channel_id=1, source_target_pairs={{0,24},{8,0},{16,8},{24,16},{1,25},{9,1},{17,9},{25,17},{2,26},{10... | collective-permute-start | bytes 786440 | tf_op jit(solution)/shard_map/spread_centers/ppermute | solution.py:121
  69.7 4.0 %fusion.4 = f32[3072]{0:T(1024)S(1)} fusion(bf16[512,1024]{1,0:T(8,128)(2,1)S(1)} %constant_dynamic-update-slice_fusion, bf16[3072,1024]{1,0:T(8,128)(2,1)S(1)} %bitcast.65, f32[512]{0:T(512)S(1)} %fusion.14, f32[3072]{0:T(1024)S(1)} %fusion), kind=kOutput, calls=%fused_computation.8 | convolution fusion | flops 3229086720 | bytes 7366656 | tf_op jit(solution)/shard_map/distance_min/while/body/eval_jaxpr/dot_general | solution.py:23
  73.7 0.2 fusion.19
  73.9 2.2 %maximum_reduce_fusion.1 = f32[3072]{0:T(1024)S(1)} fusion(f32[256]{0:T(256)S(1)} %fusion.19, f32[3072]{0:T(1024)S(1)} %fusion, bf16[256,1024]{1,0:T(8,128)(2,1)S(1)} %collective-permute-done, bf16[3072,1024]{1,0:T(8,128)(2,1)S(1)} %bitcast.65), kind=kOutput, calls=%fused_computation.22 | convolution fusion | flops 1614541824 | bytes 6841344 | tf_op jit(solution)/shard_map/distance_min/while/body/eval_jaxpr/dot_general | solution.py:23
  76.1 0.7 collective-permute-start.6
  77.0 2.2 %fusion.15 = f32[3072]{0:T(1024)S(1)} fusion(bf16[256,1024]{1,0:T(8,128)(2,1)S(1)} %constant_dynamic-update-slice_fusion.2, bf16[3072,1024]{1,0:T(8,128)(2,1)S(1)} %bitcast.65, f32[256]{0:T(256)S(1)} %fusion.18, f32[3072]{0:T(1024)S(1)} %fusion), kind=kOutput, calls=%fused_computation.27 | convolution fusion | flops 1614541824 | bytes 6841344 | tf_op jit(solution)/shard_map/distance_min/while/body/eval_jaxpr/dot_general | solution.py:23
  79.2 0.2 fusion.17
  79.4 2.2 %maximum_reduce_fusion = f32[3072]{0:T(1024)S(1)} fusion(f32[256]{0:T(256)S(1)} %fusion.17, f32[3072]{0:T(1024)S(1)} %fusion, bf16[256,1024]{1,0:T(8,128)(2,1)S(1)} %collective-permute-done.6, bf16[3072,1024]{1,0:T(8,128)(2,1)S(1)} %bitcast.65), kind=kOutput, calls=%fused_computation.21 | convolution fusion | flops 1614541824 | bytes 6841344 | tf_op jit(solution)/shard_map/distance_min/while/body/eval_jaxpr/dot_general | solution.py:23
  81.6 0.3 fusion.13
  81.9 4.0 %fusion.2 = f32[3072]{0:T(1024)S(1)} fusion(bf16[512,1024]{1,0:T(8,128)(2,1)S(1)} %collective-permute-done.3, bf16[3072,1024]{1,0:T(8,128)(2,1)S(1)} %bitcast.65, f32[512]{0:T(512)S(1)} %fusion.13, f32[3072]{0:T(1024)S(1)} %fusion), kind=kOutput, calls=%fused_computation.5 | convolution fusion | flops 3229086720 | bytes 7366656 | tf_op jit(solution)/shard_map/distance_min/while/body/eval_jaxpr/dot_general | solution.py:23
  85.9 0.6 minimum_minimum_fusion
  (34 shorter events, 1.0 us)
Async XLA Ops:
  0.0 15.4 %copy-start = (s32[1,256]{1,0:T(1,128)S(1)}, s32[1,256]{1,0:T(1,128)}, u32[]{:S(2)}) copy-start(s32[1,256]{1,0:T(1,128)} %param.6) | copy-start | bytes 3076
  0.0 15.4 %copy-start.2 = (s32[1,256]{1,0:T(1,128)S(1)}, s32[1,256]{1,0:T(1,128)}, u32[]{:S(2)}) copy-start(s32[1,256]{1,0:T(1,128)} %param.7) | copy-start | bytes 3076
  6.7 16.3 %all-to-all-start = ((bf16[32,2,1024]{2,1,0:T(2,128)(2,1)}), bf16[32,2,1024]{2,1,0:T(2,128)(2,1)S(1)}, u32[]{:S(2)}, u32[]{:S(2)}) async-start(bf16[32,2,1024]{2,1,0:T(2,128)(2,1)} %compact_centers.1), calls=%async_computation | async-start | bytes 262144 | tf_op jit(solution)/shard_map/compact_centers/all_to_all | solution.py:113
  24.6 26.0 %all-to-all-start.1 = ((bf16[32,8,1024]{2,1,0:T(8,128)(2,1)}), bf16[32,8,1024]{2,1,0:T(8,128)(2,1)S(1)}, u32[]{:S(2)}, u32[]{:S(2)}) async-start(bf16[32,8,1024]{2,1,0:T(8,128)(2,1)} %broadcast_in_dim.100), calls=%async_computation.1 | async-start | bytes 1048576 | tf_op jit(solution)/shard_map/spread_centers/all_to_all | solution.py:86
  50.6 12.4 %collective-permute-start.1 = (bf16[256,1024]{1,0:T(8,128)(2,1)S(1)}, bf16[256,1024]{1,0:T(8,128)(2,1)S(1)}, u32[]{:S(2)}, u32[]{:S(2)}) collective-permute-start(bf16[256,1024]{1,0:T(8,128)(2,1)S(1)} %bitcast.66), channel_id=1, source_target_pairs={{0,8},{8,16},{16,24},{24,0},{1,9},{9,17},{17,25},{25,1},{2,10},{10... | collective-permute-start | bytes 1572872 | tf_op jit(solution)/shard_map/spread_centers/ppermute | solution.py:121
  50.9 12.2 %collective-permute-start.2 = (bf16[256,1024]{1,0:T(8,128)(2,1)S(1)}, bf16[256,1024]{1,0:T(8,128)(2,1)S(1)}, u32[]{:S(2)}, u32[]{:S(2)}) collective-permute-start(bf16[256,1024]{1,0:T(8,128)(2,1)S(1)} %bitcast.67), channel_id=1, source_target_pairs={{0,24},{8,0},{16,8},{24,16},{1,25},{9,1},{17,9},{25,17},{2,26},{10... | collective-permute-start | bytes 1572872 | tf_op jit(solution)/shard_map/spread_centers/ppermute | solution.py:121
  53.3 20.4 %collective-permute-start = (bf16[256,1024]{1,0:T(8,128)(2,1)S(1)}, bf16[256,1024]{1,0:T(8,128)(2,1)S(1)}, u32[]{:S(2)}, u32[]{:S(2)}) collective-permute-start(bf16[256,1024]{1,0:T(8,128)(2,1)S(1)} %bitcast.68), channel_id=1, source_target_pairs={{0,1},{1,0},{2,3},{3,2},{4,5},{5,4},{6,7},{7,6},{8,9},{9,8},{10,11... | collective-permute-start | bytes 1572872 | tf_op jit(solution)/shard_map/spread_centers/ppermute | solution.py:126
  56.0 13.7 %slice-start = ((s8[6291456]{0:T(1024)(128)(4,1)}), s8[4194304]{0:T(1024)(128)(4,1)S(1)}, s32[]{:S(2)}) async-start(s8[6291456]{0:T(1024)(128)(4,1)} %bitcast.64), calls=%async_computation.2 | async-start | bytes 8388608
  56.2 13.5 %slice-start.1 = ((s8[6291456]{0:T(1024)(128)(4,1)}), s8[2097152]{0:T(1024)(128)(4,1)S(1)}, s32[]{:S(2)}) async-start(s8[6291456]{0:T(1024)(128)(4,1)} %bitcast.64), calls=%async_computation.3 | async-start | bytes 4194304
  63.1 18.4 %collective-permute-start.3 = (bf16[512,1024]{1,0:T(8,128)(2,1)S(1)}, bf16[512,1024]{1,0:T(8,128)(2,1)S(1)}, u32[]{:S(2)}, u32[]{:S(2)}) collective-permute-start(bf16[512,1024]{1,0:T(8,128)(2,1)S(1)} %constant_dynamic-update-slice_fusion), channel_id=1, source_target_pairs={{0,1},{1,0},{2,3},{3,2},{4,5},{5,4},{6,7},{7,6},{8,9},{9,8},{10,11... | collective-permute-start | bytes 3145736 | tf_op jit(solution)/shard_map/spread_centers/ppermute | solution.py:126
  66.6 9.4 %collective-permute-start.4 = (bf16[128,1024]{1,0:T(8,128)(2,1)S(1)}, bf16[128,1024]{1,0:T(8,128)(2,1)S(1)}, u32[]{:S(2)}, u32[]{:S(2)}) collective-permute-start(bf16[128,1024]{1,0:T(8,128)(2,1)S(1)} %slice.10), channel_id=1, source_target_pairs={{0,8},{8,16},{16,24},{24,0},{1,9},{9,17},{17,25},{25,1},{2,10},{10... | collective-permute-start | bytes 786440 | tf_op jit(solution)/shard_map/spread_centers/ppermute | solution.py:121
  66.7 9.3 %collective-permute-start.5 = (bf16[128,1024]{1,0:T(8,128)(2,1)S(1)}, bf16[128,1024]{1,0:T(8,128)(2,1)S(1)}, u32[]{:S(2)}, u32[]{:S(2)}) collective-permute-start(bf16[128,1024]{1,0:T(8,128)(2,1)S(1)} %slice.11), channel_id=1, source_target_pairs={{0,24},{8,0},{16,8},{24,16},{1,25},{9,1},{17,9},{25,17},{2,26},{10... | collective-permute-start | bytes 786440 | tf_op jit(solution)/shard_map/spread_centers/ppermute | solution.py:121
  76.1 3.1 %collective-permute-start.6 = (bf16[256,1024]{1,0:T(8,128)(2,1)S(1)}, bf16[256,1024]{1,0:T(8,128)(2,1)S(1)}, u32[]{:S(2)}, u32[]{:S(2)}) collective-permute-start(bf16[256,1024]{1,0:T(8,128)(2,1)S(1)} %constant_dynamic-update-slice_fusion.2), channel_id=1, source_target_pairs={{0,1},{1,0},{2,3},{3,2},{4,5},{5,4},{6,7},{7,6},{8,9},{9,8},{10,11... | collective-permute-start | bytes 1572872 | tf_op jit(solution)/shard_map/spread_centers/ppermute | solution.py:126
  81.8 4.0 %copy-start.1 = (f32[3072]{0:T(1024)S(1)}, f32[3072]{0:T(1024)}, u32[]{:S(2)}) copy-start(f32[3072]{0:T(1024)} %param.5) | copy-start | bytes 36868

commit v10 on v9

--- a/solution.py
+++ b/solution.py
@@ -133,7 +133,9 @@
             [y_send(y_near[0][:split], 1), y_send(y_near[1][split:], -1)], axis=0
         )
         near = jnp.concatenate(y_near, axis=0)
-        pieces = [plane, core_swap(plane), near, core_swap(near), y_far, core_swap(y_far)]
+        both_planes = jnp.concatenate([plane, core_swap(plane)], axis=0)
+        both_far = jnp.concatenate([y_far, core_swap(y_far)], axis=0)
+        pieces = [both_planes, near, core_swap(near), both_far]
 
     with jax.named_scope("distance_min"):
         running = nearest

time: 86.9 us -> 89.9 us (1.035)
  blocking collectives: 0 us -> 25.7 us
  waiting for transfers between devices: 21.7 us -> 12.2 us
  starting transfers between devices: 30.3 us -> 21.3 us
  matrix products: 19.6 us -> 16.3 us
    all_to_all x0 -> x1, blocking collectives: none -> 25.7 us  [replicate_gather(): got = lax.all_to_all(copies, axes, 0, 0, tiled=True)]
    all_to_all x1 -> x0, waiting for transfers between devices: 12.5 us -> none  [replicate_gather(): got = lax.all_to_all(copies, axes, 0, 0, tiled=True)]
    all_to_all x1 -> x0, starting transfers between devices: 9.41 us -> none  [replicate_gather(): got = lax.all_to_all(copies, axes, 0, 0, tiled=True)]
    dot_general x6 -> x4, matrix products: 19.6 us -> 16.3 us  [one_block(): lax.dot_general(block_rows, fragment, (((1,), (1,)), ((), ())), preferred...]
    ppermute x4, waiting for transfers between devices: 1.83 us -> 4.84 us  [y_send(): lax.ppermute(x, 'y', [(i, (i + s) % y_count) for i in range(y_count)])]
  transfers between devices with their start and end apart: 9 -> 8, of which waited for: 3 -> 3; matrix products, arithmetic and copies ran while one was open for 24% -> 20% of each run, Pallas kernels for 0% -> 0%
where the time goes in v10:
time: 89.9 us; the launch traced here: 89.6 us
  blocking collectives  25.7 us (29%)
  starting transfers between devices  21.3 us (24%)
  matrix products  16.3 us (18%)
  waiting for transfers between devices  12.2 us (14%)
  other arithmetic  9.79 us (11%)
  Pallas kernels  3.13 us (3%)
    all_to_all x1, blocking collectives, replicate_gather(): got = lax.all_to_all(copies, axes, 0, 0, tiled=True)  25.7 us
    dot_general x4, matrix products, one_block(): lax.dot_general(block_rows, fragment, (((1,), (1,)), ((), ())), preferred...  16.3 us
    all_to_all x1, starting transfers between devices, shards(): landed = lax.all_to_all(send_rows, DEV_AXES, 0, 0, tiled=True)  8.74 us
    all_to_all x1, waiting for transfers between devices, shards(): landed = lax.all_to_all(send_rows, DEV_AXES, 0, 0, tiled=True)  7.35 us
    ppermute x3, starting transfers between devices, core_swap(): return lax.ppermute(x, 'c', [(0, 1), (1, 0)])  7.07 us
    ppermute x4, starting transfers between devices, y_send(): lax.ppermute(x, 'y', [(i, (i + s) % y_count) for i in range(y_count)])  5.49 us
    ppermute x4, waiting for transfers between devices, y_send(): lax.ppermute(x, 'y', [(i, (i + s) % y_count) for i in range(y_count)])  4.84 us
    dot_general x1, other arithmetic, shards(): jnp.einsum('rd,rd->r', pool, pool, preferred_element_type=jnp.float32)  4.08 us
  transfers between devices with their start and end apart: 8, of which 3 were waited for; matrix products, arithmetic and copies ran while one was open for 20% of the time, Pallas kernels for 0%

profile of v10, /device:TPU:1, one launch (start us, length us, event | category | flops | bytes accessed | tf_op | source)
XLA Modules:
  0.0 89.6 jit_solution(16023000195085743570)
XLA Ops:
  0.0 0.8 iota_add_fusion.1
  0.8 0.7 iota_add_fusion
  1.4 0.7 compare_reduce_fusion
  2.1 0.2 convert_reduce_fusion
  2.3 0.8 select_reduce_fusion
  3.1 0.5 fusion.22.index_ref
  3.7 3.1 %compact_centers.1 = bf16[32,2,1024]{2,1,0:T(2,128)(2,1)} custom-call(s32[32]{0:T(128)} %fusion.22.index_ref, bf16[3072,1024]{1,0:T(8,128)(2,1)} %table_ref.1), custom_call_target="tpu_custom_call" | custom-call | bytes 131072 | tf_op jit(solution)/shard_map/compact_centers/pallas_call | solution.py:72
  6.8 8.7 %all-to-all-start = ((bf16[32,2,1024]{2,1,0:T(2,128)(2,1)}), bf16[32,2,1024]{2,1,0:T(2,128)(2,1)S(1)}, u32[]{:S(2)}, u32[]{:S(2)}) async-start(bf16[32,2,1024]{2,1,0:T(2,128)(2,1)} %compact_centers.1), calls=%async_computation | async-start | bytes 262144 | tf_op jit(solution)/shard_map/compact_centers/all_to_all | solution.py:113
  15.6 0.2 fusion.14
  15.8 7.4 %all-to-all-done = bf16[32,2,1024]{2,1,0:T(2,128)(2,1)S(1)} async-done(((bf16[32,2,1024]{2,1,0:T(2,128)(2,1)}), bf16[32,2,1024]{2,1,0:T(2,128)(2,1)S(1)}, u32[]{:S(2)}, u32[]{:S(2)}) %all-to-all-start) | async-done | bytes 131104 | tf_op jit(solution)/shard_map/compact_centers/all_to_all | solution.py:113
  23.2 0.6 gather_fusion
  23.8 0.1 broadcast_select_fusion
  23.9 25.7 %all_to_all.10 = bf16[32,8,1024]{2,1,0:T(8,128)(2,1)S(1)} all-to-all(bf16[32,8,1024]{2,1,0:T(8,128)(2,1)S(1)} %broadcast_in_dim.88), channel_id=1, replica_groups=mesh['z'=8,'y'=4,'x'=4,'c'=2] {'z','x'}, dimensions={0} | all-to-all | bytes 1048576 | tf_op jit(solution)/shard_map/spread_centers/all_to_all | solution.py:86
  49.7 0.3 collective-permute-start.1
  50.0 2.3 %collective-permute-start.2 = (bf16[256,1024]{1,0:T(8,128)(2,1)S(1)}, bf16[256,1024]{1,0:T(8,128)(2,1)S(1)}, u32[]{:S(2)}, u32[]{:S(2)}) collective-permute-start(bf16[256,1024]{1,0:T(8,128)(2,1)S(1)} %bitcast.48), channel_id=1, source_target_pairs={{0,24},{8,0},{16,8},{24,16},{1,25},{9,1},{17,9},{25,17},{2,26},{10... | collective-permute-start | bytes 1572872 | tf_op jit(solution)/shard_map/spread_centers/ppermute | solution.py:121
  52.4 4.1 %fusion = f32[3072]{0:T(1024)S(1)} fusion(bf16[3072,1024]{1,0:T(8,128)(2,1)} %table_ref.1), kind=kLoop, calls=%fused_computation.2 | loop fusion | flops 9434112 | bytes 6303744 | tf_op jit(solution)/shard_map/rd,rd->r/dot_general | solution.py:123
  56.5 2.8 %collective-permute-start = (bf16[256,1024]{1,0:T(8,128)(2,1)S(1)}, bf16[256,1024]{1,0:T(8,128)(2,1)S(1)}, u32[]{:S(2)}, u32[]{:S(2)}) collective-permute-start(bf16[256,1024]{1,0:T(8,128)(2,1)S(1)} %bitcast.49), channel_id=1, source_target_pairs={{0,1},{1,0},{2,3},{3,2},{4,5},{5,4},{6,7},{7,6},{8,9},{9,8},{10,11... | collective-permute-start | bytes 1572872 | tf_op jit(solution)/shard_map/spread_centers/ppermute | solution.py:126
  59.3 2.9 %collective-permute-done.1 = bf16[256,1024]{1,0:T(8,128)(2,1)S(1)} collective-permute-done((bf16[256,1024]{1,0:T(8,128)(2,1)S(1)}, bf16[256,1024]{1,0:T(8,128)(2,1)S(1)}, u32[]{:S(2)}, u32[]{:S(2)}) %collective-permute-start.1) | collective-permute-done | bytes 524320 | tf_op jit(solution)/shard_map/spread_centers/ppermute | solution.py:121
  62.2 3.2 %collective-permute-start.3 = (bf16[512,1024]{1,0:T(8,128)(2,1)S(1)}, bf16[512,1024]{1,0:T(8,128)(2,1)S(1)}, u32[]{:S(2)}, u32[]{:S(2)}) collective-permute-start(bf16[512,1024]{1,0:T(8,128)(2,1)S(1)} %constant_dynamic-update-slice_fusion), channel_id=1, source_target_pairs={{0,1},{1,0},{2,3},{3,2},{4,5},{5,4},{6,7},{7,6},{8,9},{9,8},{10,11... | collective-permute-start | bytes 3145736 | tf_op jit(solution)/shard_map/spread_centers/ppermute | solution.py:126
  65.4 0.3 fusion.11
  65.7 0.1 collective-permute-start.4
  65.8 2.7 %collective-permute-start.5 = (bf16[128,1024]{1,0:T(8,128)(2,1)S(1)}, bf16[128,1024]{1,0:T(8,128)(2,1)S(1)}, u32[]{:S(2)}, u32[]{:S(2)}) collective-permute-start(bf16[128,1024]{1,0:T(8,128)(2,1)S(1)} %slice.11), channel_id=1, source_target_pairs={{0,24},{8,0},{16,8},{24,16},{1,25},{9,1},{17,9},{25,17},{2,26},{10... | collective-permute-start | bytes 786440 | tf_op jit(solution)/shard_map/spread_centers/ppermute | solution.py:121
  68.6 4.1 %fusion.6 = f32[3072]{0:T(1024)S(1)} fusion(bf16[512,1024]{1,0:T(8,128)(2,1)S(1)} %constant_dynamic-update-slice_fusion, bf16[3072,1024]{1,0:T(8,128)(2,1)S(1)} %bitcast.46, f32[512]{0:T(512)S(1)} %fusion.11, f32[3072]{0:T(1024)S(1)} %fusion), kind=kOutput, calls=%fused_computation.11 | convolution fusion | flops 3229086720 | bytes 7366656 | tf_op jit(solution)/shard_map/distance_min/while/body/eval_jaxpr/dot_general | solution.py:23
  72.7 0.3 fusion.12
  73.0 2.0 %collective-permute-done.4 = bf16[128,1024]{1,0:T(8,128)(2,1)S(1)} collective-permute-done((bf16[128,1024]{1,0:T(8,128)(2,1)S(1)}, bf16[128,1024]{1,0:T(8,128)(2,1)S(1)}, u32[]{:S(2)}, u32[]{:S(2)}) %collective-permute-start.4) | collective-permute-done | bytes 262176 | tf_op jit(solution)/shard_map/spread_centers/ppermute | solution.py:121
  75.0 1.1 %collective-permute-start.6 = (bf16[256,1024]{1,0:T(8,128)(2,1)S(1)}, bf16[256,1024]{1,0:T(8,128)(2,1)S(1)}, u32[]{:S(2)}, u32[]{:S(2)}) collective-permute-start(bf16[256,1024]{1,0:T(8,128)(2,1)S(1)} %pad_maximum_fusion.2), channel_id=1, source_target_pairs={{0,1},{1,0},{2,3},{3,2},{4,5},{5,4},{6,7},{7,6},{8,9},{9,8},{10,11... | collective-permute-start | bytes 1572872 | tf_op jit(solution)/shard_map/spread_centers/ppermute | solution.py:126
  76.0 4.1 %fusion.8 = f32[3072]{0:T(1024)S(1)} fusion(bf16[3072,1024]{1,0:T(8,128)(2,1)S(1)} %bitcast.46, f32[512]{0:T(512)S(1)} %fusion.12, f32[3072]{0:T(1024)S(1)} %fusion, bf16[256,1024]{1,0:T(8,128)(2,1)S(1)} %collective-permute-done, bf16[256,1024]{1,0:T(8,128)(2,1)S(1)} %bitcast.51), kind=kOutput, calls=%fused_computation.14 | convolution fusion | flops 3231183872 | bytes 7366656 | tf_op jit(solution)/shard_map/distance_min/while/body/eval_jaxpr/dot_general | solution.py:23
  80.2 0.3 fusion.9
  80.5 4.1 %fusion.2 = f32[3072]{0:T(1024)S(1)} fusion(bf16[512,1024]{1,0:T(8,128)(2,1)S(1)} %constant_dynamic-update-slice_fusion.2, bf16[3072,1024]{1,0:T(8,128)(2,1)S(1)} %bitcast.46, f32[512]{0:T(512)S(1)} %fusion.9, f32[3072]{0:T(1024)S(1)} %fusion), kind=kOutput, calls=%fused_computation.5 | convolution fusion | flops 3229086720 | bytes 7366656 | tf_op jit(solution)/shard_map/distance_min/while/body/eval_jaxpr/dot_general | solution.py:23
  84.6 0.3 fusion.10
  84.9 4.1 %fusion.4 = f32[3072]{0:T(1024)S(1)} fusion(bf16[512,1024]{1,0:T(8,128)(2,1)S(1)} %collective-permute-done.3, bf16[3072,1024]{1,0:T(8,128)(2,1)S(1)} %bitcast.46, f32[512]{0:T(512)S(1)} %fusion.10, f32[3072]{0:T(1024)S(1)} %fusion), kind=kOutput, calls=%fused_computation.8 | convolution fusion | flops 3229086720 | bytes 7366656 | tf_op jit(solution)/shard_map/distance_min/while/body/eval_jaxpr/dot_general | solution.py:23
  89.0 0.6 minimum_minimum_fusion
  (31 shorter events, 0.4 us)
Async XLA Ops:
  0.0 15.6 %copy-start = (s32[1,256]{1,0:T(1,128)S(1)}, s32[1,256]{1,0:T(1,128)}, u32[]{:S(2)}) copy-start(s32[1,256]{1,0:T(1,128)} %param.6) | copy-start | bytes 3076
  0.0 15.6 %copy-start.2 = (s32[1,256]{1,0:T(1,128)S(1)}, s32[1,256]{1,0:T(1,128)}, u32[]{:S(2)}) copy-start(s32[1,256]{1,0:T(1,128)} %param.7) | copy-start | bytes 3076
  6.8 16.4 %all-to-all-start = ((bf16[32,2,1024]{2,1,0:T(2,128)(2,1)}), bf16[32,2,1024]{2,1,0:T(2,128)(2,1)S(1)}, u32[]{:S(2)}, u32[]{:S(2)}) async-start(bf16[32,2,1024]{2,1,0:T(2,128)(2,1)} %compact_centers.1), calls=%async_computation | async-start | bytes 262144 | tf_op jit(solution)/shard_map/compact_centers/all_to_all | solution.py:113
  15.6 53.0 %slice-start = ((s8[6291456]{0:T(1024)(128)(4,1)}), s8[2097152]{0:T(1024)(128)(4,1)S(1)}, s32[]{:S(2)}) async-start(s8[6291456]{0:T(1024)(128)(4,1)} %bitcast.45), calls=%async_computation.2 | async-start | bytes 4194304
  49.7 18.9 %slice-start.1 = ((s8[6291456]{0:T(1024)(128)(4,1)}), s8[4194304]{0:T(1024)(128)(4,1)S(1)}, s32[]{:S(2)}) async-start(s8[6291456]{0:T(1024)(128)(4,1)} %bitcast.45), calls=%async_computation.3 | async-start | bytes 8388608
  49.7 12.4 %collective-permute-start.1 = (bf16[256,1024]{1,0:T(8,128)(2,1)S(1)}, bf16[256,1024]{1,0:T(8,128)(2,1)S(1)}, u32[]{:S(2)}, u32[]{:S(2)}) collective-permute-start(bf16[256,1024]{1,0:T(8,128)(2,1)S(1)} %bitcast.47), channel_id=1, source_target_pairs={{0,8},{8,16},{16,24},{24,0},{1,9},{9,17},{17,25},{25,1},{2,10},{10... | collective-permute-start | bytes 1572872 | tf_op jit(solution)/shard_map/spread_centers/ppermute | solution.py:121
  50.0 12.2 %collective-permute-start.2 = (bf16[256,1024]{1,0:T(8,128)(2,1)S(1)}, bf16[256,1024]{1,0:T(8,128)(2,1)S(1)}, u32[]{:S(2)}, u32[]{:S(2)}) collective-permute-start(bf16[256,1024]{1,0:T(8,128)(2,1)S(1)} %bitcast.48), channel_id=1, source_target_pairs={{0,24},{8,0},{16,8},{24,16},{1,25},{9,1},{17,9},{25,17},{2,26},{10... | collective-permute-start | bytes 1572872 | tf_op jit(solution)/shard_map/spread_centers/ppermute | solution.py:121
  56.5 16.2 %collective-permute-start = (bf16[256,1024]{1,0:T(8,128)(2,1)S(1)}, bf16[256,1024]{1,0:T(8,128)(2,1)S(1)}, u32[]{:S(2)}, u32[]{:S(2)}) collective-permute-start(bf16[256,1024]{1,0:T(8,128)(2,1)S(1)} %bitcast.49), channel_id=1, source_target_pairs={{0,1},{1,0},{2,3},{3,2},{4,5},{5,4},{6,7},{7,6},{8,9},{9,8},{10,11... | collective-permute-start | bytes 1572872 | tf_op jit(solution)/shard_map/spread_centers/ppermute | solution.py:126
  62.2 22.4 %collective-permute-start.3 = (bf16[512,1024]{1,0:T(8,128)(2,1)S(1)}, bf16[512,1024]{1,0:T(8,128)(2,1)S(1)}, u32[]{:S(2)}, u32[]{:S(2)}) collective-permute-start(bf16[512,1024]{1,0:T(8,128)(2,1)S(1)} %constant_dynamic-update-slice_fusion), channel_id=1, source_target_pairs={{0,1},{1,0},{2,3},{3,2},{4,5},{5,4},{6,7},{7,6},{8,9},{9,8},{10,11... | collective-permute-start | bytes 3145736 | tf_op jit(solution)/shard_map/spread_centers/ppermute | solution.py:126
  65.7 9.2 %collective-permute-start.4 = (bf16[128,1024]{1,0:T(8,128)(2,1)S(1)}, bf16[128,1024]{1,0:T(8,128)(2,1)S(1)}, u32[]{:S(2)}, u32[]{:S(2)}) collective-permute-start(bf16[128,1024]{1,0:T(8,128)(2,1)S(1)} %slice.10), channel_id=1, source_target_pairs={{0,8},{8,16},{16,24},{24,0},{1,9},{9,17},{17,25},{25,1},{2,10},{10... | collective-permute-start | bytes 786440 | tf_op jit(solution)/shard_map/spread_centers/ppermute | solution.py:121
  65.8 9.1 %collective-permute-start.5 = (bf16[128,1024]{1,0:T(8,128)(2,1)S(1)}, bf16[128,1024]{1,0:T(8,128)(2,1)S(1)}, u32[]{:S(2)}, u32[]{:S(2)}) collective-permute-start(bf16[128,1024]{1,0:T(8,128)(2,1)S(1)} %slice.11), channel_id=1, source_target_pairs={{0,24},{8,0},{16,8},{24,16},{1,25},{9,1},{17,9},{25,17},{2,26},{10... | collective-permute-start | bytes 786440 | tf_op jit(solution)/shard_map/spread_centers/ppermute | solution.py:121
  75.0 5.2 %collective-permute-start.6 = (bf16[256,1024]{1,0:T(8,128)(2,1)S(1)}, bf16[256,1024]{1,0:T(8,128)(2,1)S(1)}, u32[]{:S(2)}, u32[]{:S(2)}) collective-permute-start(bf16[256,1024]{1,0:T(8,128)(2,1)S(1)} %pad_maximum_fusion.2), channel_id=1, source_target_pairs={{0,1},{1,0},{2,3},{3,2},{4,5},{5,4},{6,7},{7,6},{8,9},{9,8},{10,11... | collective-permute-start | bytes 1572872 | tf_op jit(solution)/shard_map/spread_centers/ppermute | solution.py:126
  84.9 4.1 %copy-start.1 = (f32[3072]{0:T(1024)S(1)}, f32[3072]{0:T(1024)}, u32[]{:S(2)}) copy-start(f32[3072]{0:T(1024)} %param.5) | copy-start | bytes 36868

commit v11 on v9

--- a/solution.py
+++ b/solution.py
@@ -98,24 +98,44 @@
     x_count = lax.axis_size("x")
     y_count = lax.axis_size("y")
     my_index = lax.axis_index(DEV_AXES)
-    per_device = owners.shape[0] // dev_count
+    devices = jnp.arange(dev_count, dtype=jnp.int32)
 
     with jax.named_scope("compact_centers"):
-        devices = jnp.arange(dev_count, dtype=jnp.int32)
+        columns = y_count * lax.axis_size("c")
+        slots = -(-MOST // columns)
         center_count = owners.shape[0]
         key = owners * center_count + jnp.arange(center_count, dtype=jnp.int32)
         position = jnp.sum((key[None, :] < key[:, None]).astype(jnp.int32), axis=1)
-        to_peer = ((owners == my_index)[None, :]) & (
-            (position % dev_count)[None, :] == devices[:, None]
+        owner_start = jnp.sum((owners[None, :] < owners[:, None]).astype(jnp.int32), axis=1)
+        rank = position - owner_start
+        mine_mask = owners == my_index
+        my_start = jnp.sum((owners < my_index).astype(jnp.int32))
+        ranks = jnp.arange(MOST, dtype=jnp.int32)
+        rank_offset = jnp.sum(
+            jnp.where(mine_mask[None, :] & (rank[None, :] == ranks[:, None]), offsets[None, :], 0),
+            axis=1,
         )
-        peer_offset = jnp.sum(jnp.where(to_peer, offsets[None, :], 0), axis=1)
-        send_rows = gather_rows(pool, peer_offset)
+        pairs = gather_rows(pool, rank_offset)
+        peer_column = (devices // (x_count * 2)) * 2 + devices % 2
+        send_rank = ((peer_column[:, None] - my_start) % columns) + columns * jnp.arange(
+            slots, dtype=jnp.int32
+        )[None, :]
+        send_rank = jnp.minimum(send_rank, MOST - 1).reshape(-1)
+        send_parity = jnp.sum(
+            jnp.where(send_rank[:, None] == ranks[None, :], rank_offset[None, :] % 2, 0), axis=1
+        )
+        send_rows = jnp.take(pairs.reshape(-1, pairs.shape[-1]), send_rank * 2 + send_parity, axis=0)
+        send_rows = send_rows.reshape(dev_count, slots, send_rows.shape[-1])
         landed = lax.all_to_all(send_rows, DEV_AXES, 0, 0, tiled=True)
-        wanted = my_index + dev_count * jnp.arange(per_device, dtype=jnp.int32)
+        my_column = lax.axis_index("y") * 2 + lax.axis_index("c")
+        wanted = my_column + columns * jnp.arange(center_count // columns, dtype=jnp.int32)
         is_wanted = position[None, :] == wanted[:, None]
         source = jnp.sum(jnp.where(is_wanted, owners[None, :], 0), axis=1)
-        parity = jnp.sum(jnp.where(is_wanted, offsets[None, :], 0), axis=1) % 2
-        compact = jnp.take(landed.reshape(-1, landed.shape[-1]), source * 2 + parity, axis=0)
+        source_start = jnp.sum(jnp.where(is_wanted, owner_start[None, :], 0), axis=1)
+        slot = (wanted - source_start) // columns
+        column_rows = jnp.take(
+            landed.reshape(-1, landed.shape[-1]), source * slots + slot, axis=0
+        )
 
     def y_send(x, s):
         return lax.ppermute(x, "y", [(i, (i + s) % y_count) for i in range(y_count)])
@@ -126,7 +146,7 @@
         return lax.ppermute(x, "c", [(0, 1), (1, 0)])
 
     with jax.named_scope("spread_centers"):
-        plane = replicate_gather(compact, ("z", "x"), z_count * x_count)
+        plane = replicate_gather(column_rows, "z", z_count)
         y_near = y_send(plane, 1), y_send(plane, -1)
         split = plane.shape[0] // 2
         y_far = jnp.concatenate(

time: 86.9 us -> 95.2 us (1.096)
  waiting for transfers between devices: 21.7 us -> 28.6 us
  starting transfers between devices: 30.3 us -> 25.5 us
  other arithmetic: 9.93 us -> 13.2 us
  local copies, waits for them, and re-layouts: 1.64 us -> 4.31 us
    ppermute x3, starting transfers between devices: 6.58 us -> 2.28 us  [core_swap(): return lax.ppermute(x, 'c', [(0, 1), (1, 0)])]
    ppermute x4, waiting for transfers between devices: 1.83 us -> 6.12 us  [y_send(): lax.ppermute(x, 'y', [(i, (i + s) % y_count) for i in range(y_count)])]
    reduce_sum x2 -> x4, other arithmetic: 0.97 us -> 3.2 us  [the longest x1 1.32 us: shards(): my_start = jnp.sum((owners < my_index).astype(jnp.int32))]
    select_n x3 -> x6, other arithmetic: 0.1 us -> 2.19 us  [the longest x2 0.9 us: shards(): jnp.take(pairs.reshape(-1, pairs.shape[-1]), send_rank * 2 + send_parity,...]
    all_to_all x1, waiting for transfers between devices: 12.5 us -> 13.9 us  [replicate_gather(): got = lax.all_to_all(copies, axes, 0, 0, tiled=True)]
    all_to_all x1, waiting for transfers between devices: 7.37 us -> 8.63 us  [shards(): landed = lax.all_to_all(send_rows, DEV_AXES, 0, 0, tiled=True)]
    all_to_all x1, starting transfers between devices: 9.41 us -> 8.16 us  [replicate_gather(): got = lax.all_to_all(copies, axes, 0, 0, tiled=True)]
    gather x1 -> x3, local copies, waits for them, and re-layouts: 0.57 us -> 1.6 us  [the longest x2 0.97 us: shards(): jnp.take(pairs.reshape(-1, pairs.shape[-1]), send_rank * 2 + send_parity,...]
  transfers between devices with their start and end apart: 9 -> 9, of which waited for: 3 -> 4; matrix products, arithmetic and copies ran while one was open for 24% -> 22% of each run, Pallas kernels for 0% -> 0%
where the time goes in v11:
time: 95.2 us; the launch traced here: 94.7 us
  waiting for transfers between devices  28.6 us (30%)
  starting transfers between devices  25.5 us (27%)
  matrix products  19.6 us (21%)
  other arithmetic  13.2 us (14%)
  local copies, waits for them, and re-layouts  4.31 us (5%)
  Pallas kernels  3.26 us (3%)
    dot_general x6, matrix products, one_block(): lax.dot_general(block_rows, fragment, (((1,), (1,)), ((), ())), preferred...  19.6 us
    all_to_all x1, waiting for transfers between devices, replicate_gather(): got = lax.all_to_all(copies, axes, 0, 0, tiled=True)  13.9 us
    all_to_all x1, waiting for transfers between devices, shards(): landed = lax.all_to_all(send_rows, DEV_AXES, 0, 0, tiled=True)  8.63 us
    all_to_all x1, starting transfers between devices, shards(): landed = lax.all_to_all(send_rows, DEV_AXES, 0, 0, tiled=True)  8.59 us
    all_to_all x1, starting transfers between devices, replicate_gather(): got = lax.all_to_all(copies, axes, 0, 0, tiled=True)  8.16 us
    ppermute x4, starting transfers between devices, y_send(): lax.ppermute(x, 'y', [(i, (i + s) % y_count) for i in range(y_count)])  6.45 us
    ppermute x4, waiting for transfers between devices, y_send(): lax.ppermute(x, 'y', [(i, (i + s) % y_count) for i in range(y_count)])  6.12 us
    dot_general x1, other arithmetic, shards(): jnp.einsum('rd,rd->r', pool, pool, preferred_element_type=jnp.float32)  4.08 us
  transfers between devices with their start and end apart: 9, of which 4 were waited for; matrix products, arithmetic and copies ran while one was open for 22% of the time, Pallas kernels for 0%

profile of v11, /device:TPU:1, one launch (start us, length us, event | category | flops | bytes accessed | tf_op | source)
XLA Modules:
  0.0 94.7 jit_solution(9894126489275959350)
XLA Ops:
  0.0 0.8 iota_add_fusion.1
  0.8 0.7 compare_reduce_fusion
  1.5 1.3 %fusion.24 = (s32[]{:T(128)}, s32[256]{0:T(256)S(1)}) fusion(s32[256]{0:T(256)} %bitcast.75, s32[]{:T(128)S(6)} %add.333), kind=kLoop, calls=%fused_computation.89 | loop fusion | flops 1279 | bytes 2056 | tf_op jit(solution)/shard_map/compact_centers/reduce_sum | solution.py:112
  2.8 0.7 and_select_fusion.3
  3.4 1.0 %convert_reduce_fusion = (s32[256]{0:T(256)S(1)}, s32[256]{0:T(256)S(1)}) fusion(s32[256]{0:T(256)} %bitcast.76, s32[256]{0:T(256)S(1)} %get-tuple-element.99, s32[256]{0:T(256)S(1)} %bitcast.78), kind=kLoop, calls=%fused_computation.38 | loop fusion | flops 392704 | bytes 5120 | tf_op jit(solution)/shard_map/compact_centers/reduce_sum | solution.py:109
  4.4 0.8 select_reduce_fusion
  5.2 0.5 and_select_fusion.2
  6.7 3.3 %compact_centers.1 = bf16[32,2,1024]{2,1,0:T(2,128)(2,1)} custom-call(s32[32]{0:T(128)} %get-tuple-element.101.index_ref, bf16[3072,1024]{1,0:T(8,128)(2,1)} %table_ref.1), custom_call_target="tpu_custom_call" | custom-call | bytes 131072 | tf_op jit(solution)/shard_map/compact_centers/pallas_call | solution.py:72
  10.0 1.0 %reshape.313 = bf16[64,1024]{1,0:T(8,128)(2,1)S(1)} reshape(bf16[32,2,1024]{2,1,0:T(2,128)(2,1)} %compact_centers.1) | data formatting | bytes 262144 | tf_op jit(solution)/shard_map/compact_centers/reshape | solution.py:127
  11.0 0.9 gather_fusion
  11.9 0.9 broadcast_select_fusion
  12.8 8.6 %all-to-all-start = ((bf16[32,4,1024]{2,1,0:T(4,128)(2,1)}), bf16[32,4,1024]{2,1,0:T(4,128)(2,1)S(1)}, u32[]{:S(2)}, u32[]{:S(2)}) async-start(bf16[32,4,1024]{2,1,0:T(4,128)(2,1)} %broadcast_select_fusion), calls=%async_computation | async-start | bytes 524288 | tf_op jit(solution)/shard_map/compact_centers/all_to_all | solution.py:129
  21.7 8.6 %all-to-all-done = bf16[32,4,1024]{2,1,0:T(4,128)(2,1)S(1)} async-done(((bf16[32,4,1024]{2,1,0:T(4,128)(2,1)}), bf16[32,4,1024]{2,1,0:T(4,128)(2,1)S(1)}, u32[]{:S(2)}, u32[]{:S(2)}) %all-to-all-start) | async-done | bytes 262176 | tf_op jit(solution)/shard_map/compact_centers/all_to_all | solution.py:129
  30.4 0.6 gather_fusion.1
  31.1 0.9 broadcast_in_dim.124
  32.0 8.2 %all-to-all-start.1 = ((bf16[8,32,1024]{2,1,0:T(8,128)(2,1)}), bf16[8,32,1024]{2,1,0:T(8,128)(2,1)S(1)}, u32[]{:S(2)}, u32[]{:S(2)}) async-start(bf16[8,32,1024]{2,1,0:T(8,128)(2,1)} %broadcast_in_dim.124), calls=%async_computation.1 | async-start | bytes 1048576 | tf_op jit(solution)/shard_map/spread_centers/all_to_all | solution.py:86
  40.1 4.1 %fusion = f32[3072]{0:T(1024)S(1)} fusion(bf16[3072,1024]{1,0:T(8,128)(2,1)} %table_ref.1), kind=kLoop, calls=%fused_computation.3 | loop fusion | flops 9434112 | bytes 6303744 | tf_op jit(solution)/shard_map/rd,rd->r/dot_general | solution.py:143
  44.2 13.9 %all-to-all-done.1 = bf16[8,32,1024]{2,1,0:T(8,128)(2,1)S(1)} async-done(((bf16[8,32,1024]{2,1,0:T(8,128)(2,1)}), bf16[8,32,1024]{2,1,0:T(8,128)(2,1)S(1)}, u32[]{:S(2)}, u32[]{:S(2)}) %all-to-all-start.1) | async-done | bytes 524320 | tf_op jit(solution)/shard_map/spread_centers/all_to_all | solution.py:86
  58.5 0.7 collective-permute-start
  59.2 2.3 %collective-permute-start.2 = (bf16[256,1024]{1,0:T(8,128)(2,1)S(1)}, bf16[256,1024]{1,0:T(8,128)(2,1)S(1)}, u32[]{:S(2)}, u32[]{:S(2)}) collective-permute-start(bf16[256,1024]{1,0:T(8,128)(2,1)S(1)} %bitcast.73), channel_id=1, source_target_pairs={{0,24},{8,0},{16,8},{24,16},{1,25},{9,1},{17,9},{25,17},{2,26},{10... | collective-permute-start | bytes 1572872 | tf_op jit(solution)/shard_map/spread_centers/ppermute | solution.py:141
  61.7 5.0 %fusion.16 = f32[3072]{0:T(1024)S(1)} fusion(bf16[256,1024]{1,0:T(8,128)(2,1)S(1)} %bitcast.74, bf16[3072,1024]{1,0:T(8,128)(2,1)} %table_ref.1, f32[256]{0:T(256)S(1)} %fusion.20, f32[3072]{0:T(1024)S(1)} %fusion), kind=kOutput, calls=%fused_computation.29 | convolution fusion | flops 1614541824 | bytes 6841344 | tf_op jit(solution)/shard_map/distance_min/while/body/eval_jaxpr/dot_general | solution.py:23
  66.7 5.6 %collective-permute-done.1 = bf16[256,1024]{1,0:T(8,128)(2,1)S(1)} collective-permute-done((bf16[256,1024]{1,0:T(8,128)(2,1)S(1)}, bf16[256,1024]{1,0:T(8,128)(2,1)S(1)}, u32[]{:S(2)}, u32[]{:S(2)}) %collective-permute-start.1) | collective-permute-done | bytes 524320 | tf_op jit(solution)/shard_map/spread_centers/ppermute | solution.py:141
  72.3 0.5 collective-permute-done.2
  73.2 0.9 collective-permute-start.3
  74.6 3.3 %collective-permute-start.5 = (bf16[128,1024]{1,0:T(8,128)(2,1)S(1)}, bf16[128,1024]{1,0:T(8,128)(2,1)S(1)}, u32[]{:S(2)}, u32[]{:S(2)}) collective-permute-start(bf16[128,1024]{1,0:T(8,128)(2,1)S(1)} %slice.13), channel_id=1, source_target_pairs={{0,24},{8,0},{16,8},{24,16},{1,25},{9,1},{17,9},{25,17},{2,26},{10... | collective-permute-start | bytes 786440 | tf_op jit(solution)/shard_map/spread_centers/ppermute | solution.py:141
  77.9 4.0 %fusion.4 = f32[3072]{0:T(1024)S(1)} fusion(bf16[512,1024]{1,0:T(8,128)(2,1)S(1)} %constant_dynamic-update-slice_fusion, bf16[3072,1024]{1,0:T(8,128)(2,1)S(1)} %bitcast.70, f32[512]{0:T(512)S(1)} %fusion.14, f32[3072]{0:T(1024)S(1)} %fusion), kind=kOutput, calls=%fused_computation.9 | convolution fusion | flops 3229086720 | bytes 7366656 | tf_op jit(solution)/shard_map/distance_min/while/body/eval_jaxpr/dot_general | solution.py:23
  82.1 2.1 %maximum_reduce_fusion.1 = f32[3072]{0:T(1024)S(1)} fusion(f32[256]{0:T(256)S(1)} %fusion.19, f32[3072]{0:T(1024)S(1)} %fusion, bf16[256,1024]{1,0:T(8,128)(2,1)S(1)} %collective-permute-done, bf16[3072,1024]{1,0:T(8,128)(2,1)S(1)} %bitcast.70), kind=kOutput, calls=%fused_computation.23 | convolution fusion | flops 1614541824 | bytes 6841344 | tf_op jit(solution)/shard_map/distance_min/while/body/eval_jaxpr/dot_general | solution.py:23
  84.5 0.7 collective-permute-start.6
  85.2 2.2 %fusion.15 = f32[3072]{0:T(1024)S(1)} fusion(bf16[256,1024]{1,0:T(8,128)(2,1)S(1)} %constant_dynamic-update-slice_fusion.2, bf16[3072,1024]{1,0:T(8,128)(2,1)S(1)} %bitcast.70, f32[256]{0:T(256)S(1)} %fusion.18, f32[3072]{0:T(1024)S(1)} %fusion), kind=kOutput, calls=%fused_computation.28 | convolution fusion | flops 1614541824 | bytes 6841344 | tf_op jit(solution)/shard_map/distance_min/while/body/eval_jaxpr/dot_general | solution.py:23
  87.6 2.2 %maximum_reduce_fusion = f32[3072]{0:T(1024)S(1)} fusion(f32[256]{0:T(256)S(1)} %fusion.17, f32[3072]{0:T(1024)S(1)} %fusion, bf16[256,1024]{1,0:T(8,128)(2,1)S(1)} %collective-permute-done.6, bf16[3072,1024]{1,0:T(8,128)(2,1)S(1)} %bitcast.70), kind=kOutput, calls=%fused_computation.22 | convolution fusion | flops 1614541824 | bytes 6841344 | tf_op jit(solution)/shard_map/distance_min/while/body/eval_jaxpr/dot_general | solution.py:23
  90.1 4.0 %fusion.2 = f32[3072]{0:T(1024)S(1)} fusion(bf16[512,1024]{1,0:T(8,128)(2,1)S(1)} %collective-permute-done.3, bf16[3072,1024]{1,0:T(8,128)(2,1)S(1)} %bitcast.70, f32[512]{0:T(512)S(1)} %fusion.13, f32[3072]{0:T(1024)S(1)} %fusion), kind=kOutput, calls=%fused_computation.6 | convolution fusion | flops 3229086720 | bytes 7366656 | tf_op jit(solution)/shard_map/distance_min/while/body/eval_jaxpr/dot_general | solution.py:23
  94.1 0.6 minimum_minimum_fusion
  (50 shorter events, 3.7 us)
Async XLA Ops:
  0.0 21.5 %copy-start = (s32[1,256]{1,0:T(1,128)S(1)}, s32[1,256]{1,0:T(1,128)}, u32[]{:S(2)}) copy-start(s32[1,256]{1,0:T(1,128)} %param.6) | copy-start | bytes 3076
  12.8 17.5 %all-to-all-start = ((bf16[32,4,1024]{2,1,0:T(4,128)(2,1)}), bf16[32,4,1024]{2,1,0:T(4,128)(2,1)S(1)}, u32[]{:S(2)}, u32[]{:S(2)}) async-start(bf16[32,4,1024]{2,1,0:T(4,128)(2,1)} %broadcast_select_fusion), calls=%async_computation | async-start | bytes 524288 | tf_op jit(solution)/shard_map/compact_centers/all_to_all | solution.py:129
  32.0 26.1 %all-to-all-start.1 = ((bf16[8,32,1024]{2,1,0:T(8,128)(2,1)}), bf16[8,32,1024]{2,1,0:T(8,128)(2,1)S(1)}, u32[]{:S(2)}, u32[]{:S(2)}) async-start(bf16[8,32,1024]{2,1,0:T(8,128)(2,1)} %broadcast_in_dim.124), calls=%async_computation.1 | async-start | bytes 1048576 | tf_op jit(solution)/shard_map/spread_centers/all_to_all | solution.py:86
  58.1 14.2 %collective-permute-start.1 = (bf16[256,1024]{1,0:T(8,128)(2,1)S(1)}, bf16[256,1024]{1,0:T(8,128)(2,1)S(1)}, u32[]{:S(2)}, u32[]{:S(2)}) collective-permute-start(bf16[256,1024]{1,0:T(8,128)(2,1)S(1)} %bitcast.71), channel_id=1, source_target_pairs={{0,8},{8,16},{16,24},{24,0},{1,9},{9,17},{17,25},{25,1},{2,10},{10... | collective-permute-start | bytes 1572872 | tf_op jit(solution)/shard_map/spread_centers/ppermute | solution.py:141
  58.5 23.4 %collective-permute-start = (bf16[256,1024]{1,0:T(8,128)(2,1)S(1)}, bf16[256,1024]{1,0:T(8,128)(2,1)S(1)}, u32[]{:S(2)}, u32[]{:S(2)}) collective-permute-start(bf16[256,1024]{1,0:T(8,128)(2,1)S(1)} %bitcast.72), channel_id=1, source_target_pairs={{0,1},{1,0},{2,3},{3,2},{4,5},{5,4},{6,7},{7,6},{8,9},{9,8},{10,11... | collective-permute-start | bytes 1572872 | tf_op jit(solution)/shard_map/spread_centers/ppermute | solution.py:146
  59.2 13.6 %collective-permute-start.2 = (bf16[256,1024]{1,0:T(8,128)(2,1)S(1)}, bf16[256,1024]{1,0:T(8,128)(2,1)S(1)}, u32[]{:S(2)}, u32[]{:S(2)}) collective-permute-start(bf16[256,1024]{1,0:T(8,128)(2,1)S(1)} %bitcast.73), channel_id=1, source_target_pairs={{0,24},{8,0},{16,8},{24,16},{1,25},{9,1},{17,9},{25,17},{2,26},{10... | collective-permute-start | bytes 1572872 | tf_op jit(solution)/shard_map/spread_centers/ppermute | solution.py:141
  61.5 16.4 %slice-start = ((s8[6291456]{0:T(1024)(128)(4,1)}), s8[4194304]{0:T(1024)(128)(4,1)S(1)}, s32[]{:S(2)}) async-start(s8[6291456]{0:T(1024)(128)(4,1)} %bitcast.69), calls=%async_computation.2 | async-start | bytes 8388608
  61.7 16.2 %slice-start.1 = ((s8[6291456]{0:T(1024)(128)(4,1)}), s8[2097152]{0:T(1024)(128)(4,1)S(1)}, s32[]{:S(2)}) async-start(s8[6291456]{0:T(1024)(128)(4,1)} %bitcast.69), calls=%async_computation.3 | async-start | bytes 4194304
  73.2 16.6 %collective-permute-start.3 = (bf16[512,1024]{1,0:T(8,128)(2,1)S(1)}, bf16[512,1024]{1,0:T(8,128)(2,1)S(1)}, u32[]{:S(2)}, u32[]{:S(2)}) collective-permute-start(bf16[512,1024]{1,0:T(8,128)(2,1)S(1)} %constant_dynamic-update-slice_fusion), channel_id=1, source_target_pairs={{0,1},{1,0},{2,3},{3,2},{4,5},{5,4},{6,7},{7,6},{8,9},{9,8},{10,11... | collective-permute-start | bytes 3145736 | tf_op jit(solution)/shard_map/spread_centers/ppermute | solution.py:146
  74.1 10.1 %collective-permute-start.4 = (bf16[128,1024]{1,0:T(8,128)(2,1)S(1)}, bf16[128,1024]{1,0:T(8,128)(2,1)S(1)}, u32[]{:S(2)}, u32[]{:S(2)}) collective-permute-start(bf16[128,1024]{1,0:T(8,128)(2,1)S(1)} %slice.12), channel_id=1, source_target_pairs={{0,8},{8,16},{16,24},{24,0},{1,9},{9,17},{17,25},{25,1},{2,10},{10... | collective-permute-start | bytes 786440 | tf_op jit(solution)/shard_map/spread_centers/ppermute | solution.py:141
  74.6 9.7 %collective-permute-start.5 = (bf16[128,1024]{1,0:T(8,128)(2,1)S(1)}, bf16[128,1024]{1,0:T(8,128)(2,1)S(1)}, u32[]{:S(2)}, u32[]{:S(2)}) collective-permute-start(bf16[128,1024]{1,0:T(8,128)(2,1)S(1)} %slice.13), channel_id=1, source_target_pairs={{0,24},{8,0},{16,8},{24,16},{1,25},{9,1},{17,9},{25,17},{2,26},{10... | collective-permute-start | bytes 786440 | tf_op jit(solution)/shard_map/spread_centers/ppermute | solution.py:141
  84.5 2.9 %collective-permute-start.6 = (bf16[256,1024]{1,0:T(8,128)(2,1)S(1)}, bf16[256,1024]{1,0:T(8,128)(2,1)S(1)}, u32[]{:S(2)}, u32[]{:S(2)}) collective-permute-start(bf16[256,1024]{1,0:T(8,128)(2,1)S(1)} %constant_dynamic-update-slice_fusion.2), channel_id=1, source_target_pairs={{0,1},{1,0},{2,3},{3,2},{4,5},{5,4},{6,7},{7,6},{8,9},{9,8},{10,11... | collective-permute-start | bytes 1572872 | tf_op jit(solution)/shard_map/spread_centers/ppermute | solution.py:146
  90.1 4.0 %copy-start.1 = (f32[3072]{0:T(1024)S(1)}, f32[3072]{0:T(1024)}, u32[]{:S(2)}) copy-start(f32[3072]{0:T(1024)} %param.5) | copy-start | bytes 36868

commit v12 on v9

--- a/solution.py
+++ b/solution.py
@@ -24,7 +24,7 @@
             block_rows, fragment, (((1,), (1,)), ((), ())), preferred_element_type=jnp.float32
         )
         distance = jnp.maximum(block_norm[:, None] + center_norm[None, :] - 2.0 * inner, 0.0)
-        return jnp.minimum(block_near, jnp.min(distance, axis=1))
+        return jnp.min(jnp.minimum(distance, block_near[:, None]), axis=1)
 
     result = lax.map(
         one_block,

time: 86.9 us -> 93.7 us (1.078)
  waiting for transfers between devices: 21.7 us -> 30.2 us
  starting transfers between devices: 30.3 us -> 27.1 us
  matrix products: 19.6 us -> 21.4 us
    ppermute x4, waiting for transfers between devices: 1.83 us -> 10.4 us  [y_send(): lax.ppermute(x, 'y', [(i, (i + s) % y_count) for i in range(y_count)])]
    ppermute x4, starting transfers between devices: 5.67 us -> 3.73 us  [y_send(): lax.ppermute(x, 'y', [(i, (i + s) % y_count) for i in range(y_count)])]
    dot_general x6, matrix products: 19.6 us -> 21.4 us  [one_block(): lax.dot_general(block_rows, fragment, (((1,), (1,)), ((), ())), preferred...]
    ppermute x3, starting transfers between devices: 6.58 us -> 5.58 us  [core_swap(): return lax.ppermute(x, 'c', [(0, 1), (1, 0)])]
  transfers between devices with their start and end apart: 9 -> 9, of which waited for: 3 -> 4; matrix products, arithmetic and copies ran while one was open for 24% -> 19% of each run, Pallas kernels for 0% -> 0%
where the time goes in v12:
time: 93.7 us; the launch traced here: 93.2 us
  waiting for transfers between devices  30.2 us (32%)
  starting transfers between devices  27.1 us (29%)
  matrix products  21.4 us (23%)
  other arithmetic  9.26 us (10%)
  Pallas kernels  3.34 us (4%)
  local copies, waits for them, and re-layouts  1.65 us (2%)
    dot_general x6, matrix products, one_block(): lax.dot_general(block_rows, fragment, (((1,), (1,)), ((), ())), preferred...  21.4 us
    all_to_all x1, waiting for transfers between devices, replicate_gather(): got = lax.all_to_all(copies, axes, 0, 0, tiled=True)  12.5 us
    ppermute x4, waiting for transfers between devices, y_send(): lax.ppermute(x, 'y', [(i, (i + s) % y_count) for i in range(y_count)])  10.4 us
    all_to_all x1, starting transfers between devices, replicate_gather(): got = lax.all_to_all(copies, axes, 0, 0, tiled=True)  9.3 us
    all_to_all x1, starting transfers between devices, shards(): landed = lax.all_to_all(send_rows, DEV_AXES, 0, 0, tiled=True)  8.53 us
    all_to_all x1, waiting for transfers between devices, shards(): landed = lax.all_to_all(send_rows, DEV_AXES, 0, 0, tiled=True)  7.37 us
    ppermute x3, starting transfers between devices, core_swap(): return lax.ppermute(x, 'c', [(0, 1), (1, 0)])  5.58 us
    dot_general x1, other arithmetic, shards(): jnp.einsum('rd,rd->r', pool, pool, preferred_element_type=jnp.float32)  4.09 us
  transfers between devices with their start and end apart: 9, of which 4 were waited for; matrix products, arithmetic and copies ran while one was open for 19% of the time, Pallas kernels for 0%

profile of v12, /device:TPU:1, one launch (start us, length us, event | category | flops | bytes accessed | tf_op | source)
XLA Modules:
  0.0 93.2 jit_solution(15882797496739042062)
XLA Ops:
  0.0 0.7 iota_add_fusion.1
  0.7 0.7 compare_reduce_fusion
  1.4 0.7 iota_add_fusion
  2.3 0.8 select_reduce_fusion
  3.1 0.5 fusion.34.index_ref
  3.6 3.3 %compact_centers.1 = bf16[32,2,1024]{2,1,0:T(2,128)(2,1)} custom-call(s32[32]{0:T(128)} %fusion.34.index_ref, bf16[3072,1024]{1,0:T(8,128)(2,1)} %table_ref.1), custom_call_target="tpu_custom_call" | custom-call | bytes 131072 | tf_op jit(solution)/shard_map/compact_centers/pallas_call | solution.py:72
  6.9 8.5 %all-to-all-start = ((bf16[32,2,1024]{2,1,0:T(2,128)(2,1)}), bf16[32,2,1024]{2,1,0:T(2,128)(2,1)S(1)}, u32[]{:S(2)}, u32[]{:S(2)}) async-start(bf16[32,2,1024]{2,1,0:T(2,128)(2,1)} %compact_centers.1), calls=%async_computation | async-start | bytes 262144 | tf_op jit(solution)/shard_map/compact_centers/all_to_all | solution.py:113
  15.5 0.2 fusion.26
  15.7 7.4 %all-to-all-done = bf16[32,2,1024]{2,1,0:T(2,128)(2,1)S(1)} async-done(((bf16[32,2,1024]{2,1,0:T(2,128)(2,1)}), bf16[32,2,1024]{2,1,0:T(2,128)(2,1)S(1)}, u32[]{:S(2)}, u32[]{:S(2)}) %all-to-all-start) | async-done | bytes 131104 | tf_op jit(solution)/shard_map/compact_centers/all_to_all | solution.py:113
  23.2 0.6 gather_fusion
  23.8 0.9 broadcast_in_dim.112
  24.7 9.3 %all-to-all-start.1 = ((bf16[32,8,1024]{2,1,0:T(8,128)(2,1)}), bf16[32,8,1024]{2,1,0:T(8,128)(2,1)S(1)}, u32[]{:S(2)}, u32[]{:S(2)}) async-start(bf16[32,8,1024]{2,1,0:T(8,128)(2,1)} %broadcast_in_dim.112), calls=%async_computation.1 | async-start | bytes 1048576 | tf_op jit(solution)/shard_map/spread_centers/all_to_all | solution.py:86
  34.0 4.1 %fusion = f32[3072]{0:T(1024)S(1)} fusion(bf16[3072,1024]{1,0:T(8,128)(2,1)} %table_ref.1), kind=kLoop, calls=%fused_computation.2 | loop fusion | flops 9434112 | bytes 6303744 | tf_op jit(solution)/shard_map/rd,rd->r/dot_general | solution.py:123
  38.1 12.5 %all-to-all-done.1 = bf16[32,8,1024]{2,1,0:T(8,128)(2,1)S(1)} async-done(((bf16[32,8,1024]{2,1,0:T(8,128)(2,1)}), bf16[32,8,1024]{2,1,0:T(8,128)(2,1)S(1)}, u32[]{:S(2)}, u32[]{:S(2)}) %all-to-all-start.1) | async-done | bytes 524320 | tf_op jit(solution)/shard_map/spread_centers/all_to_all | solution.py:86
  50.5 2.2 %collective-permute-start.6 = (bf16[256,1024]{1,0:T(8,128)(2,1)S(1)}, bf16[256,1024]{1,0:T(8,128)(2,1)S(1)}, u32[]{:S(2)}, u32[]{:S(2)}) collective-permute-start(bf16[256,1024]{1,0:T(8,128)(2,1)S(1)} %bitcast.74), channel_id=1, source_target_pairs={{0,1},{1,0},{2,3},{3,2},{4,5},{5,4},{6,7},{7,6},{8,9},{9,8},{10,11... | collective-permute-start | bytes 1572872 | tf_op jit(solution)/shard_map/spread_centers/ppermute | solution.py:126
  52.7 0.9 collective-permute-start.2
  53.6 0.6 collective-permute-start
  54.4 5.3 %fusion.19 = f32[3072]{0:T(1024)S(1)} fusion(f32[3072]{0:T(1024)S(1)} %copy-done.2, bf16[3072,1024]{1,0:T(8,128)(2,1)} %table_ref.1, f32[256]{0:T(256)S(1)} %fusion.21, f32[3072]{0:T(1024)S(1)} %fusion, bf16[32,8,1024]{2,1,0:T(8,128)(2,1)S(1)} %all-to-all-done.1), kind=kOutput, calls=%fused_computation.31 | convolution fusion | flops 1615328256 | bytes 6853632 | tf_op jit(solution)/shard_map/distance_min/while/body/eval_jaxpr/dot_general | solution.py:23
  59.7 6.6 %collective-permute-done.2 = bf16[256,1024]{1,0:T(8,128)(2,1)S(1)} collective-permute-done((bf16[256,1024]{1,0:T(8,128)(2,1)S(1)}, bf16[256,1024]{1,0:T(8,128)(2,1)S(1)}, u32[]{:S(2)}, u32[]{:S(2)}) %collective-permute-start.2) | collective-permute-done | bytes 524320 | tf_op jit(solution)/shard_map/spread_centers/ppermute | solution.py:121
  66.3 2.2 %collective-permute-start.3 = (bf16[128,1024]{1,0:T(8,128)(2,1)S(1)}, bf16[128,1024]{1,0:T(8,128)(2,1)S(1)}, u32[]{:S(2)}, u32[]{:S(2)}) collective-permute-start(bf16[128,1024]{1,0:T(8,128)(2,1)S(1)} %slice.11), channel_id=1, source_target_pairs={{0,24},{8,0},{16,8},{24,16},{1,25},{9,1},{17,9},{25,17},{2,26},{10... | collective-permute-start | bytes 786440 | tf_op jit(solution)/shard_map/spread_centers/ppermute | solution.py:121
  68.7 1.2 %collective-permute-start.5 = (bf16[512,1024]{1,0:T(8,128)(2,1)S(1)}, bf16[512,1024]{1,0:T(8,128)(2,1)S(1)}, u32[]{:S(2)}, u32[]{:S(2)}) collective-permute-start(bf16[512,1024]{1,0:T(8,128)(2,1)S(1)} %constant_dynamic-update-slice_fusion.2), channel_id=1, source_target_pairs={{0,1},{1,0},{2,3},{3,2},{4,5},{5,4},{6,7},{7,6},{8,9},{9,8},{10,11... | collective-permute-start | bytes 3145736 | tf_op jit(solution)/shard_map/spread_centers/ppermute | solution.py:126
  70.0 2.4 %minimum_reduce_fusion.1 = f32[3072]{0:T(1024)S(1)} fusion(f32[3072]{0:T(1024)S(1)} %fusion.19, f32[256]{0:T(256)S(1)} %fusion.22, f32[3072]{0:T(1024)S(1)} %fusion, bf16[256,1024]{1,0:T(8,128)(2,1)S(1)} %collective-permute-done.6, bf16[3072,1024]{1,0:T(8,128)(2,1)S(1)} %bitcast.73), kind=kOutput, calls=%fused_computation.26 | convolution fusion | flops 1615328256 | bytes 6853632 | tf_op jit(solution)/shard_map/distance_min/while/body/eval_jaxpr/dot_general | solution.py:23
  72.5 0.3 fusion.17
  72.8 3.8 %collective-permute-done.1 = bf16[128,1024]{1,0:T(8,128)(2,1)S(1)} collective-permute-done((bf16[128,1024]{1,0:T(8,128)(2,1)S(1)}, bf16[128,1024]{1,0:T(8,128)(2,1)S(1)}, u32[]{:S(2)}, u32[]{:S(2)}) %collective-permute-start.1) | collective-permute-done | bytes 262176 | tf_op jit(solution)/shard_map/spread_centers/ppermute | solution.py:121
  76.6 2.3 %collective-permute-start.4 = (bf16[256,1024]{1,0:T(8,128)(2,1)S(1)}, bf16[256,1024]{1,0:T(8,128)(2,1)S(1)}, u32[]{:S(2)}, u32[]{:S(2)}) collective-permute-start(bf16[256,1024]{1,0:T(8,128)(2,1)S(1)} %constant_dynamic-update-slice_fusion), channel_id=1, source_target_pairs={{0,1},{1,0},{2,3},{3,2},{4,5},{5,4},{6,7},{7,6},{8,9},{9,8},{10,11... | collective-permute-start | bytes 1572872 | tf_op jit(solution)/shard_map/spread_centers/ppermute | solution.py:126
  78.8 4.2 %fusion.3 = f32[3072]{0:T(1024)S(1)} fusion(bf16[512,1024]{1,0:T(8,128)(2,1)S(1)} %constant_dynamic-update-slice_fusion.2, bf16[3072,1024]{1,0:T(8,128)(2,1)S(1)} %bitcast.73, f32[3072]{0:T(1024)S(1)} %minimum_reduce_fusion.1, f32[512]{0:T(512)S(1)} %fusion.17, f32[3072]{0:T(1024)S(1)} %fusion), kind=kOutput, calls=%fused_computation.6 | convolution fusion | flops 3230659584 | bytes 7378944 | tf_op jit(solution)/shard_map/distance_min/while/body/eval_jaxpr/dot_general | solution.py:23
  83.0 0.2 fusion.23
  83.2 0.2 fusion.24
  83.4 0.3 fusion.18
  83.7 4.2 %fusion.6 = f32[3072]{0:T(1024)S(1)} fusion(f32[3072]{0:T(1024)S(1)} %fusion.3, f32[512]{0:T(512)S(1)} %fusion.18, f32[3072]{0:T(1024)S(1)} %fusion, bf16[512,1024]{1,0:T(8,128)(2,1)S(1)} %collective-permute-done.5, bf16[3072,1024]{1,0:T(8,128)(2,1)S(1)} %bitcast.73), kind=kOutput, calls=%fused_computation.10 | convolution fusion | flops 3230659584 | bytes 7378944 | tf_op jit(solution)/shard_map/distance_min/while/body/eval_jaxpr/dot_general | solution.py:23
  87.9 2.3 %fusion.20 = f32[3072]{0:T(1024)S(1)} fusion(f32[3072]{0:T(1024)S(1)} %fusion.6, bf16[256,1024]{1,0:T(8,128)(2,1)S(1)} %constant_dynamic-update-slice_fusion, bf16[3072,1024]{1,0:T(8,128)(2,1)S(1)} %bitcast.73, f32[256]{0:T(256)S(1)} %fusion.23, f32[3072]{0:T(1024)S(1)} %fusion), kind=kOutput, calls=%fused_computation.32 | convolution fusion | flops 1615328256 | bytes 6853632 | tf_op jit(solution)/shard_map/distance_min/while/body/eval_jaxpr/dot_general | solution.py:23
  90.3 3.0 %minimum_reduce_fusion = f32[3072]{0:T(1024)} fusion(f32[3072]{0:T(1024)S(1)} %fusion.20, f32[256]{0:T(256)S(1)} %fusion.24, f32[3072]{0:T(1024)S(1)} %fusion, bf16[256,1024]{1,0:T(8,128)(2,1)S(1)} %collective-permute-done.4, bf16[3072,1024]{1,0:T(8,128)(2,1)S(1)} %bitcast.73), kind=kOutput, calls=%fused_computation.25 | convolution fusion | flops 1615328256 | bytes 6853632 | tf_op jit(solution)/shard_map/distance_min/while/body/eval_jaxpr/dot_general | solution.py:23
  (33 shorter events, 1.0 us)
Async XLA Ops:
  3.6 11.9 %copy-start = (s32[1,256]{1,0:T(1,128)S(1)}, s32[1,256]{1,0:T(1,128)}, u32[]{:S(2)}) copy-start(s32[1,256]{1,0:T(1,128)} %param.6) | copy-start | bytes 3076
  3.6 11.9 %copy-start.1 = (s32[1,256]{1,0:T(1,128)S(1)}, s32[1,256]{1,0:T(1,128)}, u32[]{:S(2)}) copy-start(s32[1,256]{1,0:T(1,128)} %param.7) | copy-start | bytes 3076
  6.9 16.2 %all-to-all-start = ((bf16[32,2,1024]{2,1,0:T(2,128)(2,1)}), bf16[32,2,1024]{2,1,0:T(2,128)(2,1)S(1)}, u32[]{:S(2)}, u32[]{:S(2)}) async-start(bf16[32,2,1024]{2,1,0:T(2,128)(2,1)} %compact_centers.1), calls=%async_computation | async-start | bytes 262144 | tf_op jit(solution)/shard_map/compact_centers/all_to_all | solution.py:113
  24.7 25.9 %all-to-all-start.1 = ((bf16[32,8,1024]{2,1,0:T(8,128)(2,1)}), bf16[32,8,1024]{2,1,0:T(8,128)(2,1)S(1)}, u32[]{:S(2)}, u32[]{:S(2)}) async-start(bf16[32,8,1024]{2,1,0:T(8,128)(2,1)} %broadcast_in_dim.112), calls=%async_computation.1 | async-start | bytes 1048576 | tf_op jit(solution)/shard_map/spread_centers/all_to_all | solution.py:86
  34.0 20.4 %copy-start.2 = (f32[3072]{0:T(1024)S(1)}, f32[3072]{0:T(1024)}, u32[]{:S(2)}) copy-start(f32[3072]{0:T(1024)} %param.5) | copy-start | bytes 36868
  50.5 19.3 %collective-permute-start.6 = (bf16[256,1024]{1,0:T(8,128)(2,1)S(1)}, bf16[256,1024]{1,0:T(8,128)(2,1)S(1)}, u32[]{:S(2)}, u32[]{:S(2)}) collective-permute-start(bf16[256,1024]{1,0:T(8,128)(2,1)S(1)} %bitcast.74), channel_id=1, source_target_pairs={{0,1},{1,0},{2,3},{3,2},{4,5},{5,4},{6,7},{7,6},{8,9},{9,8},{10,11... | collective-permute-start | bytes 1572872 | tf_op jit(solution)/shard_map/spread_centers/ppermute | solution.py:126
  52.7 13.6 %collective-permute-start.2 = (bf16[256,1024]{1,0:T(8,128)(2,1)S(1)}, bf16[256,1024]{1,0:T(8,128)(2,1)S(1)}, u32[]{:S(2)}, u32[]{:S(2)}) collective-permute-start(bf16[256,1024]{1,0:T(8,128)(2,1)S(1)} %bitcast.75), channel_id=1, source_target_pairs={{0,24},{8,0},{16,8},{24,16},{1,25},{9,1},{17,9},{25,17},{2,26},{10... | collective-permute-start | bytes 1572872 | tf_op jit(solution)/shard_map/spread_centers/ppermute | solution.py:121
  53.6 14.9 %collective-permute-start = (bf16[256,1024]{1,0:T(8,128)(2,1)S(1)}, bf16[256,1024]{1,0:T(8,128)(2,1)S(1)}, u32[]{:S(2)}, u32[]{:S(2)}) collective-permute-start(bf16[256,1024]{1,0:T(8,128)(2,1)S(1)} %bitcast.76), channel_id=1, source_target_pairs={{0,8},{8,16},{16,24},{24,0},{1,9},{9,17},{17,25},{25,1},{2,10},{10... | collective-permute-start | bytes 1572872 | tf_op jit(solution)/shard_map/spread_centers/ppermute | solution.py:121
  54.2 15.8 %slice-start = ((s8[6291456]{0:T(1024)(128)(4,1)}), s8[4194304]{0:T(1024)(128)(4,1)S(1)}, s32[]{:S(2)}) async-start(s8[6291456]{0:T(1024)(128)(4,1)} %bitcast.72), calls=%async_computation.2 | async-start | bytes 8388608
  54.4 15.6 %slice-start.1 = ((s8[6291456]{0:T(1024)(128)(4,1)}), s8[2097152]{0:T(1024)(128)(4,1)S(1)}, s32[]{:S(2)}) async-start(s8[6291456]{0:T(1024)(128)(4,1)} %bitcast.72), calls=%async_computation.3 | async-start | bytes 4194304
  66.3 10.3 %collective-permute-start.3 = (bf16[128,1024]{1,0:T(8,128)(2,1)S(1)}, bf16[128,1024]{1,0:T(8,128)(2,1)S(1)}, u32[]{:S(2)}, u32[]{:S(2)}) collective-permute-start(bf16[128,1024]{1,0:T(8,128)(2,1)S(1)} %slice.11), channel_id=1, source_target_pairs={{0,24},{8,0},{16,8},{24,16},{1,25},{9,1},{17,9},{25,17},{2,26},{10... | collective-permute-start | bytes 786440 | tf_op jit(solution)/shard_map/spread_centers/ppermute | solution.py:121
  68.5 8.0 %collective-permute-start.1 = (bf16[128,1024]{1,0:T(8,128)(2,1)S(1)}, bf16[128,1024]{1,0:T(8,128)(2,1)S(1)}, u32[]{:S(2)}, u32[]{:S(2)}) collective-permute-start(bf16[128,1024]{1,0:T(8,128)(2,1)S(1)} %slice.10), channel_id=1, source_target_pairs={{0,8},{8,16},{16,24},{24,0},{1,9},{9,17},{17,25},{25,1},{2,10},{10... | collective-permute-start | bytes 786440 | tf_op jit(solution)/shard_map/spread_centers/ppermute | solution.py:121
  68.7 14.7 %collective-permute-start.5 = (bf16[512,1024]{1,0:T(8,128)(2,1)S(1)}, bf16[512,1024]{1,0:T(8,128)(2,1)S(1)}, u32[]{:S(2)}, u32[]{:S(2)}) collective-permute-start(bf16[512,1024]{1,0:T(8,128)(2,1)S(1)} %constant_dynamic-update-slice_fusion.2), channel_id=1, source_target_pairs={{0,1},{1,0},{2,3},{3,2},{4,5},{5,4},{6,7},{7,6},{8,9},{9,8},{10,11... | collective-permute-start | bytes 3145736 | tf_op jit(solution)/shard_map/spread_centers/ppermute | solution.py:126
  76.6 6.6 %collective-permute-start.4 = (bf16[256,1024]{1,0:T(8,128)(2,1)S(1)}, bf16[256,1024]{1,0:T(8,128)(2,1)S(1)}, u32[]{:S(2)}, u32[]{:S(2)}) collective-permute-start(bf16[256,1024]{1,0:T(8,128)(2,1)S(1)} %constant_dynamic-update-slice_fusion), channel_id=1, source_target_pairs={{0,1},{1,0},{2,3},{3,2},{4,5},{5,4},{6,7},{7,6},{8,9},{9,8},{10,11... | collective-permute-start | bytes 1572872 | tf_op jit(solution)/shard_map/spread_centers/ppermute | solution.py:126

commit v13 on v9

--- a/solution.py
+++ b/solution.py
@@ -103,8 +103,13 @@
     with jax.named_scope("compact_centers"):
         devices = jnp.arange(dev_count, dtype=jnp.int32)
         center_count = owners.shape[0]
-        key = owners * center_count + jnp.arange(center_count, dtype=jnp.int32)
-        position = jnp.sum((key[None, :] < key[:, None]).astype(jnp.int32), axis=1)
+        order = lax.broadcasted_iota(jnp.int32, (center_count, center_count), 1) < lax.broadcasted_iota(
+            jnp.int32, (center_count, center_count), 0
+        )
+        before = (owners[None, :] < owners[:, None]) | (
+            (owners[None, :] == owners[:, None]) & order
+        )
+        position = jnp.sum(before.astype(jnp.int32), axis=1)
         to_peer = ((owners == my_index)[None, :]) & (
             (position % dev_count)[None, :] == devices[:, None]
         )

time: 86.9 us -> 86 us (0.990)
    add x2 -> x0, other arithmetic: 1.43 us -> none  [shards(): key = owners * center_count + jnp.arange(center_count, dtype=jnp.int32)]
  transfers between devices with their start and end apart: 9 -> 9, of which waited for: 3 -> 3; matrix products, arithmetic and copies ran while one was open for 24% -> 25% of each run, Pallas kernels for 0% -> 0%
where the time goes in v13:
time: 86 us; the launch traced here: 85.6 us
  starting transfers between devices  30.1 us (35%)
  waiting for transfers between devices  21.7 us (25%)
  matrix products  19.6 us (23%)
  other arithmetic  9.28 us (11%)
  Pallas kernels  3.03 us (4%)
  local copies, waits for them, and re-layouts  1.64 us (2%)
    dot_general x6, matrix products, one_block(): lax.dot_general(block_rows, fragment, (((1,), (1,)), ((), ())), preferred...  19.6 us
    all_to_all x1, waiting for transfers between devices, replicate_gather(): got = lax.all_to_all(copies, axes, 0, 0, tiled=True)  12.5 us
    all_to_all x1, starting transfers between devices, replicate_gather(): got = lax.all_to_all(copies, axes, 0, 0, tiled=True)  8.91 us
    all_to_all x1, starting transfers between devices, shards(): landed = lax.all_to_all(send_rows, DEV_AXES, 0, 0, tiled=True)  8.88 us
    all_to_all x1, waiting for transfers between devices, shards(): landed = lax.all_to_all(send_rows, DEV_AXES, 0, 0, tiled=True)  7.37 us
    ppermute x3, starting transfers between devices, core_swap(): return lax.ppermute(x, 'c', [(0, 1), (1, 0)])  6.62 us
    ppermute x4, starting transfers between devices, y_send(): lax.ppermute(x, 'y', [(i, (i + s) % y_count) for i in range(y_count)])  5.67 us
    dot_general x1, other arithmetic, shards(): jnp.einsum('rd,rd->r', pool, pool, preferred_element_type=jnp.float32)  4.08 us
  transfers between devices with their start and end apart: 9, of which 3 were waited for; matrix products, arithmetic and copies ran while one was open for 25% of the time, Pallas kernels for 0%

profile of v13, /device:TPU:1, one launch (start us, length us, event | category | flops | bytes accessed | tf_op | source)
XLA Modules:
  0.0 85.6 jit_solution(11542828114250279424)
XLA Ops:
  0.0 1.0 %convert_reduce_fusion = s32[256]{0:T(256)S(1)} fusion(s32[256]{0:T(256)} %bitcast.68), kind=kLoop, calls=%fused_computation.37 | loop fusion | flops 458496 | bytes 2048 | tf_op jit(solution)/shard_map/compact_centers/reduce_sum | solution.py:112
  1.0 0.7 compare_reduce_fusion
  1.7 0.8 select_reduce_fusion
  2.5 0.5 fusion.32.index_ref
  3.0 3.0 %compact_centers.1 = bf16[32,2,1024]{2,1,0:T(2,128)(2,1)} custom-call(s32[32]{0:T(128)} %fusion.32.index_ref, bf16[3072,1024]{1,0:T(8,128)(2,1)} %table_ref.1), custom_call_target="tpu_custom_call" | custom-call | bytes 131072 | tf_op jit(solution)/shard_map/compact_centers/pallas_call | solution.py:72
  6.1 8.9 %all-to-all-start = ((bf16[32,2,1024]{2,1,0:T(2,128)(2,1)}), bf16[32,2,1024]{2,1,0:T(2,128)(2,1)S(1)}, u32[]{:S(2)}, u32[]{:S(2)}) async-start(bf16[32,2,1024]{2,1,0:T(2,128)(2,1)} %compact_centers.1), calls=%async_computation | async-start | bytes 262144 | tf_op jit(solution)/shard_map/compact_centers/all_to_all | solution.py:118
  15.0 0.2 fusion.24
  15.2 7.4 %all-to-all-done = bf16[32,2,1024]{2,1,0:T(2,128)(2,1)S(1)} async-done(((bf16[32,2,1024]{2,1,0:T(2,128)(2,1)}), bf16[32,2,1024]{2,1,0:T(2,128)(2,1)S(1)}, u32[]{:S(2)}, u32[]{:S(2)}) %all-to-all-start) | async-done | bytes 131104 | tf_op jit(solution)/shard_map/compact_centers/all_to_all | solution.py:118
  22.6 0.6 gather_fusion
  23.3 0.9 broadcast_in_dim.98
  24.1 8.9 %all-to-all-start.1 = ((bf16[32,8,1024]{2,1,0:T(8,128)(2,1)}), bf16[32,8,1024]{2,1,0:T(8,128)(2,1)S(1)}, u32[]{:S(2)}, u32[]{:S(2)}) async-start(bf16[32,8,1024]{2,1,0:T(8,128)(2,1)} %broadcast_in_dim.98), calls=%async_computation.1 | async-start | bytes 1048576 | tf_op jit(solution)/shard_map/spread_centers/all_to_all | solution.py:86
  33.1 4.1 %fusion = f32[3072]{0:T(1024)S(1)} fusion(bf16[3072,1024]{1,0:T(8,128)(2,1)} %table_ref.1), kind=kLoop, calls=%fused_computation.2 | loop fusion | flops 9434112 | bytes 6303744 | tf_op jit(solution)/shard_map/rd,rd->r/dot_general | solution.py:128
  37.1 12.5 %all-to-all-done.1 = bf16[32,8,1024]{2,1,0:T(8,128)(2,1)S(1)} async-done(((bf16[32,8,1024]{2,1,0:T(8,128)(2,1)}), bf16[32,8,1024]{2,1,0:T(8,128)(2,1)S(1)}, u32[]{:S(2)}, u32[]{:S(2)}) %all-to-all-start.1) | async-done | bytes 524320 | tf_op jit(solution)/shard_map/spread_centers/all_to_all | solution.py:86
  49.6 0.3 collective-permute-start.1
  50.0 2.3 %collective-permute-start.2 = (bf16[256,1024]{1,0:T(8,128)(2,1)S(1)}, bf16[256,1024]{1,0:T(8,128)(2,1)S(1)}, u32[]{:S(2)}, u32[]{:S(2)}) collective-permute-start(bf16[256,1024]{1,0:T(8,128)(2,1)S(1)} %bitcast.66), channel_id=1, source_target_pairs={{0,24},{8,0},{16,8},{24,16},{1,25},{9,1},{17,9},{25,17},{2,26},{10... | collective-permute-start | bytes 1572872 | tf_op jit(solution)/shard_map/spread_centers/ppermute | solution.py:126
  52.3 2.7 %collective-permute-start = (bf16[256,1024]{1,0:T(8,128)(2,1)S(1)}, bf16[256,1024]{1,0:T(8,128)(2,1)S(1)}, u32[]{:S(2)}, u32[]{:S(2)}) collective-permute-start(bf16[256,1024]{1,0:T(8,128)(2,1)S(1)} %bitcast.67), channel_id=1, source_target_pairs={{0,1},{1,0},{2,3},{3,2},{4,5},{5,4},{6,7},{7,6},{8,9},{9,8},{10,11... | collective-permute-start | bytes 1572872 | tf_op jit(solution)/shard_map/spread_centers/ppermute | solution.py:131
  55.0 0.2 fusion.20
  55.2 5.0 %fusion.16 = f32[3072]{0:T(1024)S(1)} fusion(bf16[3072,1024]{1,0:T(8,128)(2,1)} %table_ref.1, f32[256]{0:T(256)S(1)} %fusion.20, f32[3072]{0:T(1024)S(1)} %fusion, bf16[32,8,1024]{2,1,0:T(8,128)(2,1)S(1)} %all-to-all-done.1), kind=kOutput, calls=%fused_computation.28 | convolution fusion | flops 1614541824 | bytes 6841344 | tf_op jit(solution)/shard_map/distance_min/while/body/eval_jaxpr/dot_general | solution.py:23
  60.2 1.8 %collective-permute-done.1 = bf16[256,1024]{1,0:T(8,128)(2,1)S(1)} collective-permute-done((bf16[256,1024]{1,0:T(8,128)(2,1)S(1)}, bf16[256,1024]{1,0:T(8,128)(2,1)S(1)}, u32[]{:S(2)}, u32[]{:S(2)}) %collective-permute-start.1) | collective-permute-done | bytes 524320 | tf_op jit(solution)/shard_map/spread_centers/ppermute | solution.py:126
  62.2 3.2 %collective-permute-start.3 = (bf16[512,1024]{1,0:T(8,128)(2,1)S(1)}, bf16[512,1024]{1,0:T(8,128)(2,1)S(1)}, u32[]{:S(2)}, u32[]{:S(2)}) collective-permute-start(bf16[512,1024]{1,0:T(8,128)(2,1)S(1)} %constant_dynamic-update-slice_fusion), channel_id=1, source_target_pairs={{0,1},{1,0},{2,3},{3,2},{4,5},{5,4},{6,7},{7,6},{8,9},{9,8},{10,11... | collective-permute-start | bytes 3145736 | tf_op jit(solution)/shard_map/spread_centers/ppermute | solution.py:131
  65.4 0.3 fusion.14
  65.8 2.9 %collective-permute-start.5 = (bf16[128,1024]{1,0:T(8,128)(2,1)S(1)}, bf16[128,1024]{1,0:T(8,128)(2,1)S(1)}, u32[]{:S(2)}, u32[]{:S(2)}) collective-permute-start(bf16[128,1024]{1,0:T(8,128)(2,1)S(1)} %slice.11), channel_id=1, source_target_pairs={{0,24},{8,0},{16,8},{24,16},{1,25},{9,1},{17,9},{25,17},{2,26},{10... | collective-permute-start | bytes 786440 | tf_op jit(solution)/shard_map/spread_centers/ppermute | solution.py:126
  68.7 4.0 %fusion.4 = f32[3072]{0:T(1024)S(1)} fusion(bf16[512,1024]{1,0:T(8,128)(2,1)S(1)} %constant_dynamic-update-slice_fusion, bf16[3072,1024]{1,0:T(8,128)(2,1)S(1)} %bitcast.64, f32[512]{0:T(512)S(1)} %fusion.14, f32[3072]{0:T(1024)S(1)} %fusion), kind=kOutput, calls=%fused_computation.8 | convolution fusion | flops 3229086720 | bytes 7366656 | tf_op jit(solution)/shard_map/distance_min/while/body/eval_jaxpr/dot_general | solution.py:23
  72.7 0.2 fusion.19
  72.9 2.1 %maximum_reduce_fusion.1 = f32[3072]{0:T(1024)S(1)} fusion(f32[256]{0:T(256)S(1)} %fusion.19, f32[3072]{0:T(1024)S(1)} %fusion, bf16[256,1024]{1,0:T(8,128)(2,1)S(1)} %collective-permute-done, bf16[3072,1024]{1,0:T(8,128)(2,1)S(1)} %bitcast.64), kind=kOutput, calls=%fused_computation.22 | convolution fusion | flops 1614541824 | bytes 6841344 | tf_op jit(solution)/shard_map/distance_min/while/body/eval_jaxpr/dot_general | solution.py:23
  75.1 0.7 collective-permute-start.6
  76.0 2.2 %fusion.15 = f32[3072]{0:T(1024)S(1)} fusion(bf16[256,1024]{1,0:T(8,128)(2,1)S(1)} %constant_dynamic-update-slice_fusion.2, bf16[3072,1024]{1,0:T(8,128)(2,1)S(1)} %bitcast.64, f32[256]{0:T(256)S(1)} %fusion.18, f32[3072]{0:T(1024)S(1)} %fusion), kind=kOutput, calls=%fused_computation.27 | convolution fusion | flops 1614541824 | bytes 6841344 | tf_op jit(solution)/shard_map/distance_min/while/body/eval_jaxpr/dot_general | solution.py:23
  78.2 0.2 fusion.17
  78.4 2.2 %maximum_reduce_fusion = f32[3072]{0:T(1024)S(1)} fusion(f32[256]{0:T(256)S(1)} %fusion.17, f32[3072]{0:T(1024)S(1)} %fusion, bf16[256,1024]{1,0:T(8,128)(2,1)S(1)} %collective-permute-done.6, bf16[3072,1024]{1,0:T(8,128)(2,1)S(1)} %bitcast.64), kind=kOutput, calls=%fused_computation.21 | convolution fusion | flops 1614541824 | bytes 6841344 | tf_op jit(solution)/shard_map/distance_min/while/body/eval_jaxpr/dot_general | solution.py:23
  80.6 0.3 fusion.13
  80.9 4.0 %fusion.2 = f32[3072]{0:T(1024)S(1)} fusion(bf16[512,1024]{1,0:T(8,128)(2,1)S(1)} %collective-permute-done.3, bf16[3072,1024]{1,0:T(8,128)(2,1)S(1)} %bitcast.64, f32[512]{0:T(512)S(1)} %fusion.13, f32[3072]{0:T(1024)S(1)} %fusion), kind=kOutput, calls=%fused_computation.5 | convolution fusion | flops 3229086720 | bytes 7366656 | tf_op jit(solution)/shard_map/distance_min/while/body/eval_jaxpr/dot_general | solution.py:23
  84.9 0.6 minimum_minimum_fusion
  (32 shorter events, 0.6 us)
Async XLA Ops:
  0.0 15.0 %copy-start = (s32[1,256]{1,0:T(1,128)S(1)}, s32[1,256]{1,0:T(1,128)}, u32[]{:S(2)}) copy-start(s32[1,256]{1,0:T(1,128)} %param.6) | copy-start | bytes 3076
  0.0 15.0 %copy-start.2 = (s32[1,256]{1,0:T(1,128)S(1)}, s32[1,256]{1,0:T(1,128)}, u32[]{:S(2)}) copy-start(s32[1,256]{1,0:T(1,128)} %param.7) | copy-start | bytes 3076
  6.1 16.5 %all-to-all-start = ((bf16[32,2,1024]{2,1,0:T(2,128)(2,1)}), bf16[32,2,1024]{2,1,0:T(2,128)(2,1)S(1)}, u32[]{:S(2)}, u32[]{:S(2)}) async-start(bf16[32,2,1024]{2,1,0:T(2,128)(2,1)} %compact_centers.1), calls=%async_computation | async-start | bytes 262144 | tf_op jit(solution)/shard_map/compact_centers/all_to_all | solution.py:118
  24.1 25.5 %all-to-all-start.1 = ((bf16[32,8,1024]{2,1,0:T(8,128)(2,1)}), bf16[32,8,1024]{2,1,0:T(8,128)(2,1)S(1)}, u32[]{:S(2)}, u32[]{:S(2)}) async-start(bf16[32,8,1024]{2,1,0:T(8,128)(2,1)} %broadcast_in_dim.98), calls=%async_computation.1 | async-start | bytes 1048576 | tf_op jit(solution)/shard_map/spread_centers/all_to_all | solution.py:86
  49.6 12.4 %collective-permute-start.1 = (bf16[256,1024]{1,0:T(8,128)(2,1)S(1)}, bf16[256,1024]{1,0:T(8,128)(2,1)S(1)}, u32[]{:S(2)}, u32[]{:S(2)}) collective-permute-start(bf16[256,1024]{1,0:T(8,128)(2,1)S(1)} %bitcast.65), channel_id=1, source_target_pairs={{0,8},{8,16},{16,24},{24,0},{1,9},{9,17},{17,25},{25,1},{2,10},{10... | collective-permute-start | bytes 1572872 | tf_op jit(solution)/shard_map/spread_centers/ppermute | solution.py:126
  50.0 12.2 %collective-permute-start.2 = (bf16[256,1024]{1,0:T(8,128)(2,1)S(1)}, bf16[256,1024]{1,0:T(8,128)(2,1)S(1)}, u32[]{:S(2)}, u32[]{:S(2)}) collective-permute-start(bf16[256,1024]{1,0:T(8,128)(2,1)S(1)} %bitcast.66), channel_id=1, source_target_pairs={{0,24},{8,0},{16,8},{24,16},{1,25},{9,1},{17,9},{25,17},{2,26},{10... | collective-permute-start | bytes 1572872 | tf_op jit(solution)/shard_map/spread_centers/ppermute | solution.py:126
  52.3 20.4 %collective-permute-start = (bf16[256,1024]{1,0:T(8,128)(2,1)S(1)}, bf16[256,1024]{1,0:T(8,128)(2,1)S(1)}, u32[]{:S(2)}, u32[]{:S(2)}) collective-permute-start(bf16[256,1024]{1,0:T(8,128)(2,1)S(1)} %bitcast.67), channel_id=1, source_target_pairs={{0,1},{1,0},{2,3},{3,2},{4,5},{5,4},{6,7},{7,6},{8,9},{9,8},{10,11... | collective-permute-start | bytes 1572872 | tf_op jit(solution)/shard_map/spread_centers/ppermute | solution.py:131
  55.0 13.7 %slice-start = ((s8[6291456]{0:T(1024)(128)(4,1)}), s8[4194304]{0:T(1024)(128)(4,1)S(1)}, s32[]{:S(2)}) async-start(s8[6291456]{0:T(1024)(128)(4,1)} %bitcast.63), calls=%async_computation.2 | async-start | bytes 8388608
  55.2 13.5 %slice-start.1 = ((s8[6291456]{0:T(1024)(128)(4,1)}), s8[2097152]{0:T(1024)(128)(4,1)S(1)}, s32[]{:S(2)}) async-start(s8[6291456]{0:T(1024)(128)(4,1)} %bitcast.63), calls=%async_computation.3 | async-start | bytes 4194304
  62.2 18.4 %collective-permute-start.3 = (bf16[512,1024]{1,0:T(8,128)(2,1)S(1)}, bf16[512,1024]{1,0:T(8,128)(2,1)S(1)}, u32[]{:S(2)}, u32[]{:S(2)}) collective-permute-start(bf16[512,1024]{1,0:T(8,128)(2,1)S(1)} %constant_dynamic-update-slice_fusion), channel_id=1, source_target_pairs={{0,1},{1,0},{2,3},{3,2},{4,5},{5,4},{6,7},{7,6},{8,9},{9,8},{10,11... | collective-permute-start | bytes 3145736 | tf_op jit(solution)/shard_map/spread_centers/ppermute | solution.py:131
  65.7 9.4 %collective-permute-start.4 = (bf16[128,1024]{1,0:T(8,128)(2,1)S(1)}, bf16[128,1024]{1,0:T(8,128)(2,1)S(1)}, u32[]{:S(2)}, u32[]{:S(2)}) collective-permute-start(bf16[128,1024]{1,0:T(8,128)(2,1)S(1)} %slice.10), channel_id=1, source_target_pairs={{0,8},{8,16},{16,24},{24,0},{1,9},{9,17},{17,25},{25,1},{2,10},{10... | collective-permute-start | bytes 786440 | tf_op jit(solution)/shard_map/spread_centers/ppermute | solution.py:126
  65.8 9.3 %collective-permute-start.5 = (bf16[128,1024]{1,0:T(8,128)(2,1)S(1)}, bf16[128,1024]{1,0:T(8,128)(2,1)S(1)}, u32[]{:S(2)}, u32[]{:S(2)}) collective-permute-start(bf16[128,1024]{1,0:T(8,128)(2,1)S(1)} %slice.11), channel_id=1, source_target_pairs={{0,24},{8,0},{16,8},{24,16},{1,25},{9,1},{17,9},{25,17},{2,26},{10... | collective-permute-start | bytes 786440 | tf_op jit(solution)/shard_map/spread_centers/ppermute | solution.py:126
  75.1 3.1 %collective-permute-start.6 = (bf16[256,1024]{1,0:T(8,128)(2,1)S(1)}, bf16[256,1024]{1,0:T(8,128)(2,1)S(1)}, u32[]{:S(2)}, u32[]{:S(2)}) collective-permute-start(bf16[256,1024]{1,0:T(8,128)(2,1)S(1)} %constant_dynamic-update-slice_fusion.2), channel_id=1, source_target_pairs={{0,1},{1,0},{2,3},{3,2},{4,5},{5,4},{6,7},{7,6},{8,9},{9,8},{10,11... | collective-permute-start | bytes 1572872 | tf_op jit(solution)/shard_map/spread_centers/ppermute | solution.py:131
  80.9 4.0 %copy-start.1 = (f32[3072]{0:T(1024)S(1)}, f32[3072]{0:T(1024)}, u32[]{:S(2)}) copy-start(f32[3072]{0:T(1024)} %param.5) | copy-start | bytes 36868

commit v14 on v13

--- a/solution.py
+++ b/solution.py
@@ -12,27 +12,42 @@
 CORES = 2
 
 
+def _fold_kernel(frag_ref, center_norm_ref, rows_ref, row_norm_ref, running_ref, out_ref):
+    inner = lax.dot_general(
+        frag_ref[...], rows_ref[...], (((1,), (1,)), ((), ())), preferred_element_type=jnp.float32
+    )
+    distance = jnp.maximum(row_norm_ref[...] + center_norm_ref[...] - 2.0 * inner, 0.0)
+    out_ref[...] = jnp.minimum(running_ref[...], jnp.min(distance, axis=0, keepdims=True))
+
+
 def fold_chunk(pool_rows, row_norm, running, fragment):
     center_norm = jnp.einsum("cd,cd->c", fragment, fragment, preferred_element_type=jnp.float32)
-    total_rows = pool_rows.shape[0]
-    block = total_rows
-    blocks = total_rows // block
-
-    def one_block(args):
-        block_rows, block_norm, block_near = args
-        inner = lax.dot_general(
-            block_rows, fragment, (((1,), (1,)), ((), ())), preferred_element_type=jnp.float32
-        )
-        distance = jnp.maximum(block_norm[:, None] + center_norm[None, :] - 2.0 * inner, 0.0)
-        return jnp.minimum(block_near, jnp.min(distance, axis=1))
-
-    result = lax.map(
-        one_block,
-        (
-            pool_rows.reshape(blocks, block, pool_rows.shape[1]),
-            row_norm.reshape(blocks, block),
-            running.reshape(blocks, block),
+    total_rows, width = pool_rows.shape
+    count = fragment.shape[0]
+    block = math.gcd(total_rows, 1024)
+    result = pl.pallas_call(
+        _fold_kernel,
+        out_shape=jax.ShapeDtypeStruct((1, total_rows), jnp.float32),
+        grid=(total_rows // block,),
+        in_specs=[
+            pl.BlockSpec((count, width), lambda i: (0, 0)),
+            pl.BlockSpec((count, 1), lambda i: (0, 0)),
+            pl.BlockSpec((block, width), lambda i: (i, 0)),
+            pl.BlockSpec((1, block), lambda i: (0, i)),
+            pl.BlockSpec((1, block), lambda i: (0, i)),
+        ],
+        out_specs=pl.BlockSpec((1, block), lambda i: (0, i)),
+        cost_estimate=pl.CostEstimate(
+            flops=2 * count * total_rows * width,
+            bytes_accessed=2 * (total_rows + count) * width + 12 * total_rows,
+            transcendentals=0,
         ),
+    )(
+        fragment,
+        center_norm.reshape(count, 1),
+        pool_rows,
+        row_norm.reshape(1, total_rows),
+        running.reshape(1, total_rows),
     )
     return result.reshape(total_rows)
 

time: 86 us -> 115 us (1.34)
  Pallas kernels: 3.03 us -> 39 us
  blocking collectives: 0 us -> 25.4 us
  matrix products: 19.6 us -> 0 us
  starting transfers between devices: 30.1 us -> 16.9 us
  waiting for transfers between devices: 21.7 us -> 13.9 us
  local copies, waits for them, and re-layouts: 1.64 us -> 8.15 us
  other arithmetic: 9.28 us -> 10.5 us
    pallas_call x0 -> x6, Pallas kernels: none -> 35.9 us  [fold_chunk(): pl.pallas_call(_fold_kernel, out_shape=jax.ShapeDtypeStruct((1, total_row...]
    all_to_all x0 -> x1, blocking collectives: none -> 25.4 us  [replicate_gather(): got = lax.all_to_all(copies, axes, 0, 0, tiled=True)]
    dot_general x6 -> x0, matrix products: 19.6 us -> none  [one_block(): lax.dot_general(block_rows, fragment, (((1,), (1,)), ((), ())), preferred...]
    all_to_all x1 -> x0, waiting for transfers between devices: 12.5 us -> none  [replicate_gather(): got = lax.all_to_all(copies, axes, 0, 0, tiled=True)]
    all_to_all x1 -> x0, starting transfers between devices: 8.91 us -> none  [replicate_gather(): got = lax.all_to_all(copies, axes, 0, 0, tiled=True)]
    reshape x0 -> x6, local copies, waits for them, and re-layouts: none -> 4.92 us  [fold_chunk(): center_norm.reshape(count, 1)]
    ppermute x4, waiting for transfers between devices: 1.84 us -> 6.55 us  [y_send(): lax.ppermute(x, 'y', [(i, (i + s) % y_count) for i in range(y_count)])]
    ppermute x3, starting transfers between devices: 6.62 us -> 4.48 us  [core_swap(): return lax.ppermute(x, 'c', [(0, 1), (1, 0)])]
  transfers between devices with their start and end apart: 9 -> 8, of which waited for: 3 -> 2; matrix products, arithmetic and copies ran while one was open for 25% -> 11% of each run, Pallas kernels for 0% -> 16%
where the time goes in v14:
time: 115 us; the launch traced here: 114 us
  Pallas kernels  39 us (34%)
  blocking collectives  25.4 us (22%)
  starting transfers between devices  16.9 us (15%)
  waiting for transfers between devices  13.9 us (12%)
  other arithmetic  10.5 us (9%)
  local copies, waits for them, and re-layouts  8.15 us (7%)
    pallas_call x6, Pallas kernels, fold_chunk(): pl.pallas_call(_fold_kernel, out_shape=jax.ShapeDtypeStruct((1, total_row...  35.9 us
    all_to_all x1, blocking collectives, replicate_gather(): got = lax.all_to_all(copies, axes, 0, 0, tiled=True)  25.4 us
    all_to_all x1, starting transfers between devices, shards(): landed = lax.all_to_all(send_rows, DEV_AXES, 0, 0, tiled=True)  8.84 us
    all_to_all x1, waiting for transfers between devices, shards(): landed = lax.all_to_all(send_rows, DEV_AXES, 0, 0, tiled=True)  7.37 us
    ppermute x4, waiting for transfers between devices, y_send(): lax.ppermute(x, 'y', [(i, (i + s) % y_count) for i in range(y_count)])  6.55 us
    reshape x6, local copies, waits for them, and re-layouts, fold_chunk(): center_norm.reshape(count, 1)  4.92 us
    dot_general x1, other arithmetic, shards(): jnp.einsum('rd,rd->r', pool, pool, preferred_element_type=jnp.float32)  4.67 us
    ppermute x3, starting transfers between devices, core_swap(): return lax.ppermute(x, 'c', [(0, 1), (1, 0)])  4.48 us
  transfers between devices with their start and end apart: 8, of which 2 were waited for; matrix products, arithmetic and copies ran while one was open for 11% of the time, Pallas kernels for 16%

profile of v14, /device:TPU:1, one launch (start us, length us, event | category | flops | bytes accessed | tf_op | source)
XLA Modules:
  0.0 114.0 jit_solution(2270206002645868325)
XLA Ops:
  0.0 0.8 compare_reduce_fusion
  0.8 0.9 convert_reduce_fusion
  1.7 0.8 select_reduce_fusion
  2.5 0.5 fusion.18.index_ref
  3.1 3.1 %compact_centers.1 = bf16[32,2,1024]{2,1,0:T(2,128)(2,1)} custom-call(s32[32]{0:T(128)} %fusion.18.index_ref, bf16[3072,1024]{1,0:T(8,128)(2,1)} %rows_ref.11), custom_call_target="tpu_custom_call" | custom-call | bytes 131072 | tf_op jit(solution)/shard_map/compact_centers/pallas_call | solution.py:87
  6.2 8.8 %all-to-all-start = ((bf16[32,2,1024]{2,1,0:T(2,128)(2,1)}), bf16[32,2,1024]{2,1,0:T(2,128)(2,1)S(1)}, u32[]{:S(2)}, u32[]{:S(2)}) async-start(bf16[32,2,1024]{2,1,0:T(2,128)(2,1)} %compact_centers.1), calls=%async_computation | async-start | bytes 262144 | tf_op jit(solution)/shard_map/compact_centers/all_to_all | solution.py:133
  15.3 7.4 %all-to-all-done = bf16[32,2,1024]{2,1,0:T(2,128)(2,1)S(1)} async-done(((bf16[32,2,1024]{2,1,0:T(2,128)(2,1)}), bf16[32,2,1024]{2,1,0:T(2,128)(2,1)S(1)}, u32[]{:S(2)}, u32[]{:S(2)}) %all-to-all-start) | async-done | bytes 131104 | tf_op jit(solution)/shard_map/compact_centers/all_to_all | solution.py:133
  22.7 0.6 gather_fusion
  23.4 25.4 %all_to_all.10 = bf16[32,8,1024]{2,1,0:T(8,128)(2,1)S(1)} all-to-all(bf16[32,8,1024]{2,1,0:T(8,128)(2,1)S(1)} %broadcast_in_dim.61), channel_id=1, replica_groups=mesh['z'=8,'y'=4,'x'=4,'c'=2] {'z','x'}, dimensions={0} | all-to-all | bytes 1048576 | tf_op jit(solution)/shard_map/spread_centers/all_to_all | solution.py:101
  48.8 0.9 collective-permute-start.2
  49.7 0.6 collective-permute-start
  50.3 4.7 %fusion = f32[3072]{0:T(1024)} fusion(bf16[3072,1024]{1,0:T(8,128)(2,1)} %rows_ref.11), kind=kLoop, calls=%fused_computation.2 | loop fusion | flops 9434112 | bytes 6303744 | tf_op jit(solution)/shard_map/rd,rd->r/dot_general | solution.py:143
  54.9 2.7 %collective-permute-start.6 = (bf16[256,1024]{1,0:T(8,128)(2,1)S(1)}, bf16[256,1024]{1,0:T(8,128)(2,1)S(1)}, u32[]{:S(2)}, u32[]{:S(2)}) collective-permute-start(bf16[256,1024]{1,0:T(8,128)(2,1)S(1)} %bitcast.25), channel_id=1, source_target_pairs={{0,1},{1,0},{2,3},{3,2},{4,5},{5,4},{6,7},{7,6},{8,9},{9,8},{10,11... | collective-permute-start | bytes 1572872 | tf_op jit(solution)/shard_map/spread_centers/ppermute | solution.py:146
  57.9 0.8 copy.11.center_norm_ref
  58.7 5.5 %distance_min.6.running_ref = f32[1,3072]{1,0:T(1,128)} custom-call(bf16[256,1024]{1,0:T(8,128)(2,1)} %bitcast.26, f32[256,1]{1,0:T(8,128)} %copy.11.center_norm_ref, bf16[3072,1024]{1,0:T(8,128)(2,1)} %rows_ref.11, f32[1,3072]{1,0:T(1,128)} %bitcast.27, f32[1,3072]{1,0:T(1,128)} %bitcast.35), custom_call_target="tpu_custom_call" | custom-call | flops 1610612736 | bytes 6852608 | tf_op jit(solution)/shard_map/distance_min/pallas_call | solution.py:28
  64.2 0.7 slice.11
  65.0 2.1 %collective-permute-start.3 = (bf16[128,1024]{1,0:T(8,128)(2,1)}, bf16[128,1024]{1,0:T(8,128)(2,1)S(1)}, u32[]{:S(2)}, u32[]{:S(2)}) collective-permute-start(bf16[128,1024]{1,0:T(8,128)(2,1)} %slice.11), channel_id=1, source_target_pairs={{0,24},{8,0},{16,8},{24,16},{1,25},{9,1},{17,9},{25,17},{2,26},{10... | collective-permute-start | bytes 786440 | tf_op jit(solution)/shard_map/spread_centers/ppermute | solution.py:141
  67.1 0.7 slice.10
  68.7 0.8 copy.12.center_norm_ref
  69.5 0.9 copy.13.center_norm_ref
  70.4 6.5 %collective-permute-done.1 = bf16[128,1024]{1,0:T(8,128)(2,1)} collective-permute-done((bf16[128,1024]{1,0:T(8,128)(2,1)}, bf16[128,1024]{1,0:T(8,128)(2,1)}, u32[]{:S(2)}, u32[]{:S(2)}) %collective-permute-start.1) | collective-permute-done | bytes 262176 | tf_op jit(solution)/shard_map/spread_centers/ppermute | solution.py:141
  76.9 1.0 constant_dynamic-update-slice_fusion.1
  78.0 1.4 %collective-permute-start.4 = (bf16[256,1024]{1,0:T(8,128)(2,1)S(1)}, bf16[256,1024]{1,0:T(8,128)(2,1)S(1)}, u32[]{:S(2)}, u32[]{:S(2)}) collective-permute-start(bf16[256,1024]{1,0:T(8,128)(2,1)S(1)} %constant_dynamic-update-slice_fusion.frag_ref), channel_id=1, source_target_pairs={{0,1},{1,0},{2,3},{3,2},{4,5},{5,4},{6,7},{7,6},{8,9},{9,8},{10,11... | collective-permute-start | bytes 1572872 | tf_op jit(solution)/shard_map/spread_centers/ppermute | solution.py:146
  79.3 5.5 %distance_min.7.running_ref = f32[1,3072]{1,0:T(1,128)} custom-call(bf16[256,1024]{1,0:T(8,128)(2,1)} %copy-done.3, f32[256,1]{1,0:T(8,128)} %copy.12.center_norm_ref, bf16[3072,1024]{1,0:T(8,128)(2,1)} %rows_ref.11, f32[1,3072]{1,0:T(1,128)} %bitcast.28, f32[1,3072]{1,0:T(1,128)} %distance_min.6.running_ref), custom_call_target="tpu_custom_call" | custom-call | flops 1610612736 | bytes 6852608 | tf_op jit(solution)/shard_map/distance_min/pallas_call | solution.py:28
  84.9 6.9 %distance_min.8.running_ref = f32[1,3072]{1,0:T(1,128)} custom-call(bf16[512,1024]{1,0:T(8,128)(2,1)} %copy-done.2, f32[512,1]{1,0:T(8,128)} %copy.13.center_norm_ref, bf16[3072,1024]{1,0:T(8,128)(2,1)} %rows_ref.11, f32[1,3072]{1,0:T(1,128)} %bitcast.29, f32[1,3072]{1,0:T(1,128)} %distance_min.7.running_ref), custom_call_target="tpu_custom_call" | custom-call | flops 3221225472 | bytes 7376896 | tf_op jit(solution)/shard_map/distance_min/pallas_call | solution.py:28
  91.9 0.8 copy.15.center_norm_ref
  92.9 0.8 copy.16.center_norm_ref
  93.7 1.5 %fusion.2 = f32[512]{0:T(512)S(1)} fusion(bf16[512,1024]{1,0:T(8,128)(2,1)} %collective-permute-done.5.frag_ref), kind=kLoop, calls=%fused_computation.6 | loop fusion | flops 1572352 | bytes 1050624 | tf_op jit(solution)/shard_map/distance_min/cd,cd->c/dot_general | solution.py:24
  95.2 0.9 copy.14.center_norm_ref
  96.1 6.8 %distance_min.9.running_ref = f32[1,3072]{1,0:T(1,128)} custom-call(bf16[512,1024]{1,0:T(8,128)(2,1)} %collective-permute-done.5.frag_ref, f32[512,1]{1,0:T(8,128)} %copy.14.center_norm_ref, bf16[3072,1024]{1,0:T(8,128)(2,1)} %rows_ref.11, f32[1,3072]{1,0:T(1,128)} %bitcast.30, f32[1,3072]{1,0:T(1,128)} %distance_min.8.running_ref), custom_call_target="tpu_custom_call" | custom-call | flops 3221225472 | bytes 7376896 | tf_op jit(solution)/shard_map/distance_min/pallas_call | solution.py:28
  102.9 5.5 %distance_min.10.running_ref = f32[1,3072]{1,0:T(1,128)} custom-call(bf16[256,1024]{1,0:T(8,128)(2,1)} %copy-done.1, f32[256,1]{1,0:T(8,128)} %copy.15.center_norm_ref, bf16[3072,1024]{1,0:T(8,128)(2,1)} %rows_ref.11, f32[1,3072]{1,0:T(1,128)} %bitcast.31, f32[1,3072]{1,0:T(1,128)} %distance_min.9.running_ref), custom_call_target="tpu_custom_call" | custom-call | flops 1610612736 | bytes 6852608 | tf_op jit(solution)/shard_map/distance_min/pallas_call | solution.py:28
  108.4 5.5 %distance_min.11 = f32[1,3072]{1,0:T(1,128)} custom-call(bf16[256,1024]{1,0:T(8,128)(2,1)} %copy-done.4, f32[256,1]{1,0:T(8,128)} %copy.16.center_norm_ref, bf16[3072,1024]{1,0:T(8,128)(2,1)} %rows_ref.11, f32[1,3072]{1,0:T(1,128)} %bitcast.32, f32[1,3072]{1,0:T(1,128)} %distance_min.10.running_ref), custom_call_target="tpu_custom_call" | custom-call | flops 1610612736 | bytes 6852608 | tf_op jit(solution)/shard_map/distance_min/pallas_call | solution.py:28
  (39 shorter events, 1.9 us)
Async XLA Ops:
  0.0 15.1 %copy-start.5 = (s32[1,256]{1,0:T(1,128)S(1)}, s32[1,256]{1,0:T(1,128)}, u32[]{:S(2)}) copy-start(s32[1,256]{1,0:T(1,128)} %param.6) | copy-start | bytes 3076
  0.0 15.1 %copy-start.6 = (s32[1,256]{1,0:T(1,128)S(1)}, s32[1,256]{1,0:T(1,128)}, u32[]{:S(2)}) copy-start(s32[1,256]{1,0:T(1,128)} %param.7) | copy-start | bytes 3076
  6.2 16.5 %all-to-all-start = ((bf16[32,2,1024]{2,1,0:T(2,128)(2,1)}), bf16[32,2,1024]{2,1,0:T(2,128)(2,1)S(1)}, u32[]{:S(2)}, u32[]{:S(2)}) async-start(bf16[32,2,1024]{2,1,0:T(2,128)(2,1)} %compact_centers.1), calls=%async_computation | async-start | bytes 262144 | tf_op jit(solution)/shard_map/compact_centers/all_to_all | solution.py:133
  48.8 9.9 %copy-start = (bf16[32,8,1024]{2,1,0:T(8,128)(2,1)}, bf16[32,8,1024]{2,1,0:T(8,128)(2,1)S(1)}, u32[]{:S(2)}) copy-start(bf16[32,8,1024]{2,1,0:T(8,128)(2,1)S(1)} %all_to_all.10) | copy-start | bytes 1572868
  48.8 15.4 %collective-permute-start.2 = (bf16[256,1024]{1,0:T(8,128)(2,1)S(1)}, bf16[256,1024]{1,0:T(8,128)(2,1)S(1)}, u32[]{:S(2)}, u32[]{:S(2)}) collective-permute-start(bf16[256,1024]{1,0:T(8,128)(2,1)S(1)} %bitcast.23), channel_id=1, source_target_pairs={{0,24},{8,0},{16,8},{24,16},{1,25},{9,1},{17,9},{25,17},{2,26},{10... | collective-permute-start | bytes 1572872 | tf_op jit(solution)/shard_map/spread_centers/ppermute | solution.py:141
  49.7 17.4 %collective-permute-start = (bf16[256,1024]{1,0:T(8,128)(2,1)S(1)}, bf16[256,1024]{1,0:T(8,128)(2,1)S(1)}, u32[]{:S(2)}, u32[]{:S(2)}) collective-permute-start(bf16[256,1024]{1,0:T(8,128)(2,1)S(1)} %bitcast.24), channel_id=1, source_target_pairs={{0,8},{8,16},{16,24},{24,0},{1,9},{9,17},{17,25},{25,1},{2,10},{10... | collective-permute-start | bytes 1572872 | tf_op jit(solution)/shard_map/spread_centers/ppermute | solution.py:141
  54.9 13.6 %collective-permute-start.6 = (bf16[256,1024]{1,0:T(8,128)(2,1)S(1)}, bf16[256,1024]{1,0:T(8,128)(2,1)S(1)}, u32[]{:S(2)}, u32[]{:S(2)}) collective-permute-start(bf16[256,1024]{1,0:T(8,128)(2,1)S(1)} %bitcast.25), channel_id=1, source_target_pairs={{0,1},{1,0},{2,3},{3,2},{4,5},{5,4},{6,7},{7,6},{8,9},{9,8},{10,11... | collective-permute-start | bytes 1572872 | tf_op jit(solution)/shard_map/spread_centers/ppermute | solution.py:146
  65.0 12.9 %collective-permute-start.3 = (bf16[128,1024]{1,0:T(8,128)(2,1)}, bf16[128,1024]{1,0:T(8,128)(2,1)S(1)}, u32[]{:S(2)}, u32[]{:S(2)}) collective-permute-start(bf16[128,1024]{1,0:T(8,128)(2,1)} %slice.11), channel_id=1, source_target_pairs={{0,24},{8,0},{16,8},{24,16},{1,25},{9,1},{17,9},{25,17},{2,26},{10... | collective-permute-start | bytes 786440 | tf_op jit(solution)/shard_map/spread_centers/ppermute | solution.py:141
  67.8 9.1 %collective-permute-start.1 = (bf16[128,1024]{1,0:T(8,128)(2,1)}, bf16[128,1024]{1,0:T(8,128)(2,1)}, u32[]{:S(2)}, u32[]{:S(2)}) collective-permute-start(bf16[128,1024]{1,0:T(8,128)(2,1)} %slice.10), channel_id=1, source_target_pairs={{0,8},{8,16},{16,24},{24,0},{1,9},{9,17},{17,25},{25,1},{2,10},{10... | collective-permute-start | bytes 786440 | tf_op jit(solution)/shard_map/spread_centers/ppermute | solution.py:141
  67.9 17.0 %copy-start.2 = (bf16[512,1024]{1,0:T(8,128)(2,1)}, bf16[512,1024]{1,0:T(8,128)(2,1)S(1)}, u32[]{:S(2)}) copy-start(bf16[512,1024]{1,0:T(8,128)(2,1)S(1)} %constant_dynamic-update-slice_fusion.2.frag_ref) | copy-start | bytes 3145732
  67.9 25.8 %collective-permute-start.5 = (bf16[512,1024]{1,0:T(8,128)(2,1)S(1)}, bf16[512,1024]{1,0:T(8,128)(2,1)}, u32[]{:S(2)}, u32[]{:S(2)}) collective-permute-start(bf16[512,1024]{1,0:T(8,128)(2,1)S(1)} %constant_dynamic-update-slice_fusion.2.frag_ref), channel_id=1, source_target_pairs={{0,1},{1,0},{2,3},{3,2},{4,5},{5,4},{6,7},{7,6},{8,9},{9,8},{10,11... | collective-permute-start | bytes 3145736 | tf_op jit(solution)/shard_map/spread_centers/ppermute | solution.py:146
  68.5 10.8 %copy-start.3 = (bf16[256,1024]{1,0:T(8,128)(2,1)}, bf16[256,1024]{1,0:T(8,128)(2,1)S(1)}, u32[]{:S(2)}) copy-start(bf16[256,1024]{1,0:T(8,128)(2,1)S(1)} %collective-permute-done.6.frag_ref) | copy-start | bytes 1572868
  77.9 13.8 %copy-start.1 = (bf16[256,1024]{1,0:T(8,128)(2,1)}, bf16[256,1024]{1,0:T(8,128)(2,1)S(1)}, u32[]{:S(2)}) copy-start(bf16[256,1024]{1,0:T(8,128)(2,1)S(1)} %constant_dynamic-update-slice_fusion.frag_ref) | copy-start | bytes 1572868
  78.0 14.8 %collective-permute-start.4 = (bf16[256,1024]{1,0:T(8,128)(2,1)S(1)}, bf16[256,1024]{1,0:T(8,128)(2,1)S(1)}, u32[]{:S(2)}, u32[]{:S(2)}) collective-permute-start(bf16[256,1024]{1,0:T(8,128)(2,1)S(1)} %constant_dynamic-update-slice_fusion.frag_ref), channel_id=1, source_target_pairs={{0,1},{1,0},{2,3},{3,2},{4,5},{5,4},{6,7},{7,6},{8,9},{9,8},{10,11... | collective-permute-start | bytes 1572872 | tf_op jit(solution)/shard_map/spread_centers/ppermute | solution.py:146
  92.7 10.2 %copy-start.4 = (bf16[256,1024]{1,0:T(8,128)(2,1)}, bf16[256,1024]{1,0:T(8,128)(2,1)S(1)}, u32[]{:S(2)}) copy-start(bf16[256,1024]{1,0:T(8,128)(2,1)S(1)} %collective-permute-done.4.frag_ref) | copy-start | bytes 1572868

commit v15 on v13

--- a/solution.py
+++ b/solution.py
@@ -138,7 +138,9 @@
             [y_send(y_near[0][:split], 1), y_send(y_near[1][split:], -1)], axis=0
         )
         near = jnp.concatenate(y_near, axis=0)
-        pieces = [plane, core_swap(plane), near, core_swap(near), y_far, core_swap(y_far)]
+        both_near = jnp.concatenate([near, core_swap(near)], axis=0)
+        both_far = jnp.concatenate([y_far, core_swap(y_far)], axis=0)
+        pieces = [plane, core_swap(plane), both_near, both_far]
 
     with jax.named_scope("distance_min"):
         running = nearest

time: 86 us -> 89.2 us (1.037)
  starting transfers between devices: 30.1 us -> 33.8 us
    ppermute x3, starting transfers between devices: 6.62 us -> 10.6 us  [core_swap(): return lax.ppermute(x, 'c', [(0, 1), (1, 0)])]
    dot_general x6 -> x4, matrix products: 19.6 us -> 18.8 us  [one_block(): lax.dot_general(block_rows, fragment, (((1,), (1,)), ((), ())), preferred...]
  transfers between devices with their start and end apart: 9 -> 9, of which waited for: 3 -> 3; matrix products, arithmetic and copies ran while one was open for 25% -> 19% of each run, Pallas kernels for 0% -> 0%
where the time goes in v15:
time: 89.2 us; the launch traced here: 88.8 us
  starting transfers between devices  33.8 us (38%)
  waiting for transfers between devices  21.7 us (24%)
  matrix products  18.8 us (21%)
  other arithmetic  9.21 us (10%)
  Pallas kernels  3.24 us (4%)
  local copies, waits for them, and re-layouts  1.75 us (2%)
    dot_general x4, matrix products, one_block(): lax.dot_general(block_rows, fragment, (((1,), (1,)), ((), ())), preferred...  18.8 us
    all_to_all x1, waiting for transfers between devices, replicate_gather(): got = lax.all_to_all(copies, axes, 0, 0, tiled=True)  12.5 us
    ppermute x3, starting transfers between devices, core_swap(): return lax.ppermute(x, 'c', [(0, 1), (1, 0)])  10.6 us
    all_to_all x1, starting transfers between devices, replicate_gather(): got = lax.all_to_all(copies, axes, 0, 0, tiled=True)  9.2 us
    all_to_all x1, starting transfers between devices, shards(): landed = lax.all_to_all(send_rows, DEV_AXES, 0, 0, tiled=True)  8.49 us
    all_to_all x1, waiting for transfers between devices, shards(): landed = lax.all_to_all(send_rows, DEV_AXES, 0, 0, tiled=True)  7.37 us
    ppermute x4, starting transfers between devices, y_send(): lax.ppermute(x, 'y', [(i, (i + s) % y_count) for i in range(y_count)])  5.49 us
    dot_general x1, other arithmetic, shards(): jnp.einsum('rd,rd->r', pool, pool, preferred_element_type=jnp.float32)  4.08 us
  transfers between devices with their start and end apart: 9, of which 3 were waited for; matrix products, arithmetic and copies ran while one was open for 19% of the time, Pallas kernels for 0%

profile of v15, /device:TPU:1, one launch (start us, length us, event | category | flops | bytes accessed | tf_op | source)
XLA Modules:
  0.0 88.8 jit_solution(12398000438278666045)
XLA Ops:
  0.0 1.0 %convert_reduce_fusion = s32[256]{0:T(256)S(1)} fusion(s32[256]{0:T(256)} %bitcast.52), kind=kLoop, calls=%fused_computation.27 | loop fusion | flops 458496 | bytes 2048 | tf_op jit(solution)/shard_map/compact_centers/reduce_sum | solution.py:112
  1.0 0.7 compare_reduce_fusion
  1.7 0.8 select_reduce_fusion
  2.5 0.5 fusion.25.index_ref
  3.0 3.2 %compact_centers.1 = bf16[32,2,1024]{2,1,0:T(2,128)(2,1)} custom-call(s32[32]{0:T(128)} %fusion.25.index_ref, bf16[3072,1024]{1,0:T(8,128)(2,1)} %table_ref.1), custom_call_target="tpu_custom_call" | custom-call | bytes 131072 | tf_op jit(solution)/shard_map/compact_centers/pallas_call | solution.py:72
  6.3 8.5 %all-to-all-start = ((bf16[32,2,1024]{2,1,0:T(2,128)(2,1)}), bf16[32,2,1024]{2,1,0:T(2,128)(2,1)S(1)}, u32[]{:S(2)}, u32[]{:S(2)}) async-start(bf16[32,2,1024]{2,1,0:T(2,128)(2,1)} %compact_centers.1), calls=%async_computation | async-start | bytes 262144 | tf_op jit(solution)/shard_map/compact_centers/all_to_all | solution.py:118
  14.8 0.2 fusion.17
  15.0 7.4 %all-to-all-done = bf16[32,2,1024]{2,1,0:T(2,128)(2,1)S(1)} async-done(((bf16[32,2,1024]{2,1,0:T(2,128)(2,1)}), bf16[32,2,1024]{2,1,0:T(2,128)(2,1)S(1)}, u32[]{:S(2)}, u32[]{:S(2)}) %all-to-all-start) | async-done | bytes 131104 | tf_op jit(solution)/shard_map/compact_centers/all_to_all | solution.py:118
  22.5 0.6 gather_fusion
  23.0 0.1 broadcast_select_fusion
  23.1 0.9 broadcast_in_dim.86
  24.0 9.2 %all-to-all-start.1 = ((bf16[32,8,1024]{2,1,0:T(8,128)(2,1)}), bf16[32,8,1024]{2,1,0:T(8,128)(2,1)S(1)}, u32[]{:S(2)}, u32[]{:S(2)}) async-start(bf16[32,8,1024]{2,1,0:T(8,128)(2,1)} %broadcast_in_dim.86), calls=%async_computation.1 | async-start | bytes 1048576 | tf_op jit(solution)/shard_map/spread_centers/all_to_all | solution.py:86
  33.2 4.1 %fusion.2 = f32[3072]{0:T(1024)S(1)} fusion(bf16[3072,1024]{1,0:T(8,128)(2,1)} %table_ref.1), kind=kLoop, calls=%fused_computation.5 | loop fusion | flops 9434112 | bytes 6303744 | tf_op jit(solution)/shard_map/rd,rd->r/dot_general | solution.py:128
  37.2 12.5 %all-to-all-done.1 = bf16[32,8,1024]{2,1,0:T(8,128)(2,1)S(1)} async-done(((bf16[32,8,1024]{2,1,0:T(8,128)(2,1)}), bf16[32,8,1024]{2,1,0:T(8,128)(2,1)S(1)}, u32[]{:S(2)}, u32[]{:S(2)}) %all-to-all-start.1) | async-done | bytes 524320 | tf_op jit(solution)/shard_map/spread_centers/all_to_all | solution.py:86
  49.7 0.3 collective-permute-start.1
  50.1 2.3 %collective-permute-start.2 = (bf16[256,1024]{1,0:T(8,128)(2,1)S(1)}, bf16[256,1024]{1,0:T(8,128)(2,1)S(1)}, u32[]{:S(2)}, u32[]{:S(2)}) collective-permute-start(bf16[256,1024]{1,0:T(8,128)(2,1)S(1)} %bitcast.50), channel_id=1, source_target_pairs={{0,24},{8,0},{16,8},{24,16},{1,25},{9,1},{17,9},{25,17},{2,26},{10... | collective-permute-start | bytes 1572872 | tf_op jit(solution)/shard_map/spread_centers/ppermute | solution.py:126
  52.4 2.7 %collective-permute-start = (bf16[256,1024]{1,0:T(8,128)(2,1)S(1)}, bf16[256,1024]{1,0:T(8,128)(2,1)S(1)}, u32[]{:S(2)}, u32[]{:S(2)}) collective-permute-start(bf16[256,1024]{1,0:T(8,128)(2,1)S(1)} %bitcast.51), channel_id=1, source_target_pairs={{0,1},{1,0},{2,3},{3,2},{4,5},{5,4},{6,7},{7,6},{8,9},{9,8},{10,11... | collective-permute-start | bytes 1572872 | tf_op jit(solution)/shard_map/spread_centers/ppermute | solution.py:131
  55.2 0.2 fusion.13
  55.3 5.0 %fusion.11 = f32[3072]{0:T(1024)S(1)} fusion(bf16[3072,1024]{1,0:T(8,128)(2,1)} %table_ref.1, f32[256]{0:T(256)S(1)} %fusion.13, f32[3072]{0:T(1024)S(1)} %fusion.2, bf16[32,8,1024]{2,1,0:T(8,128)(2,1)S(1)} %all-to-all-done.1), kind=kOutput, calls=%fused_computation.20 | convolution fusion | flops 1614541824 | bytes 6841344 | tf_op jit(solution)/shard_map/distance_min/while/body/eval_jaxpr/dot_general | solution.py:23
  60.4 1.8 %collective-permute-done.1 = bf16[256,1024]{1,0:T(8,128)(2,1)S(1)} collective-permute-done((bf16[256,1024]{1,0:T(8,128)(2,1)S(1)}, bf16[256,1024]{1,0:T(8,128)(2,1)S(1)}, u32[]{:S(2)}, u32[]{:S(2)}) %collective-permute-start.1) | collective-permute-done | bytes 524320 | tf_op jit(solution)/shard_map/spread_centers/ppermute | solution.py:126
  62.2 0.1 collective-permute-start.4
  62.3 2.7 %collective-permute-start.5 = (bf16[128,1024]{1,0:T(8,128)(2,1)S(1)}, bf16[128,1024]{1,0:T(8,128)(2,1)S(1)}, u32[]{:S(2)}, u32[]{:S(2)}) collective-permute-start(bf16[128,1024]{1,0:T(8,128)(2,1)S(1)} %slice.11), channel_id=1, source_target_pairs={{0,24},{8,0},{16,8},{24,16},{1,25},{9,1},{17,9},{25,17},{2,26},{10... | collective-permute-start | bytes 786440 | tf_op jit(solution)/shard_map/spread_centers/ppermute | solution.py:126
  65.1 3.7 %collective-permute-start.3 = (bf16[512,1024]{1,0:T(8,128)(2,1)S(1)}, bf16[512,1024]{1,0:T(8,128)(2,1)S(1)}, u32[]{:S(2)}, u32[]{:S(2)}) collective-permute-start(bf16[512,1024]{1,0:T(8,128)(2,1)S(1)} %pad_maximum_fusion), channel_id=1, source_target_pairs={{0,1},{1,0},{2,3},{3,2},{4,5},{5,4},{6,7},{7,6},{8,9},{9,8},{10,11... | collective-permute-start | bytes 3145736 | tf_op jit(solution)/shard_map/spread_centers/ppermute | solution.py:131
  68.9 0.2 fusion.12
  69.1 4.1 %collective-permute-start.6 = (bf16[256,1024]{1,0:T(8,128)(2,1)S(1)}, bf16[256,1024]{1,0:T(8,128)(2,1)S(1)}, u32[]{:S(2)}, u32[]{:S(2)}) collective-permute-start(bf16[256,1024]{1,0:T(8,128)(2,1)S(1)} %pad_maximum_fusion.1), channel_id=1, source_target_pairs={{0,1},{1,0},{2,3},{3,2},{4,5},{5,4},{6,7},{7,6},{8,9},{9,8},{10,11... | collective-permute-start | bytes 1572872 | tf_op jit(solution)/shard_map/spread_centers/ppermute | solution.py:131
  73.3 2.2 %maximum_reduce_fusion = f32[3072]{0:T(1024)S(1)} fusion(f32[256]{0:T(256)S(1)} %fusion.12, f32[3072]{0:T(1024)S(1)} %fusion.2, bf16[256,1024]{1,0:T(8,128)(2,1)S(1)} %collective-permute-done, bf16[3072,1024]{1,0:T(8,128)(2,1)S(1)} %bitcast.48), kind=kOutput, calls=%fused_computation.17 | convolution fusion | flops 1614541824 | bytes 6841344 | tf_op jit(solution)/shard_map/distance_min/while/body/eval_jaxpr/dot_general | solution.py:23
  75.7 0.3 fusion.10
  75.9 4.0 %fusion.4 = f32[3072]{0:T(1024)S(1)} fusion(bf16[512,1024]{1,0:T(8,128)(2,1)S(1)} %constant_dynamic-update-slice_fusion.3, bf16[3072,1024]{1,0:T(8,128)(2,1)S(1)} %bitcast.48, f32[512]{0:T(512)S(1)} %fusion.10, f32[3072]{0:T(1024)S(1)} %fusion.2), kind=kOutput, calls=%fused_computation.8 | convolution fusion | flops 3229086720 | bytes 7366656 | tf_op jit(solution)/shard_map/distance_min/while/body/eval_jaxpr/dot_general | solution.py:23
  80.0 0.1 constant_dynamic-update-slice_fusion
  80.1 0.5 fusion.5
  80.6 7.6 %fusion.1 = f32[3072]{0:T(1024)S(1)} fusion(bf16[1024,1024]{1,0:T(8,128)(2,1)S(1)} %constant_dynamic-update-slice_fusion, bf16[3072,1024]{1,0:T(8,128)(2,1)S(1)} %bitcast.48, f32[1024]{0:T(1024)S(1)} %fusion.5, f32[3072]{0:T(1024)S(1)} %fusion.2), kind=kOutput, calls=%fused_computation.3 | convolution fusion | flops 6458176512 | bytes 8417280 | tf_op jit(solution)/shard_map/distance_min/while/body/eval_jaxpr/dot_general | solution.py:23
  88.2 0.6 minimum_minimum_fusion
  (32 shorter events, 0.4 us)
Async XLA Ops:
  0.0 14.8 %copy-start = (s32[1,256]{1,0:T(1,128)S(1)}, s32[1,256]{1,0:T(1,128)}, u32[]{:S(2)}) copy-start(s32[1,256]{1,0:T(1,128)} %param.6) | copy-start | bytes 3076
  0.0 14.8 %copy-start.2 = (s32[1,256]{1,0:T(1,128)S(1)}, s32[1,256]{1,0:T(1,128)}, u32[]{:S(2)}) copy-start(s32[1,256]{1,0:T(1,128)} %param.7) | copy-start | bytes 3076
  6.3 16.1 %all-to-all-start = ((bf16[32,2,1024]{2,1,0:T(2,128)(2,1)}), bf16[32,2,1024]{2,1,0:T(2,128)(2,1)S(1)}, u32[]{:S(2)}, u32[]{:S(2)}) async-start(bf16[32,2,1024]{2,1,0:T(2,128)(2,1)} %compact_centers.1), calls=%async_computation | async-start | bytes 262144 | tf_op jit(solution)/shard_map/compact_centers/all_to_all | solution.py:118
  24.0 25.8 %all-to-all-start.1 = ((bf16[32,8,1024]{2,1,0:T(8,128)(2,1)}), bf16[32,8,1024]{2,1,0:T(8,128)(2,1)S(1)}, u32[]{:S(2)}, u32[]{:S(2)}) async-start(bf16[32,8,1024]{2,1,0:T(8,128)(2,1)} %broadcast_in_dim.86), calls=%async_computation.1 | async-start | bytes 1048576 | tf_op jit(solution)/shard_map/spread_centers/all_to_all | solution.py:86
  49.7 12.4 %collective-permute-start.1 = (bf16[256,1024]{1,0:T(8,128)(2,1)S(1)}, bf16[256,1024]{1,0:T(8,128)(2,1)S(1)}, u32[]{:S(2)}, u32[]{:S(2)}) collective-permute-start(bf16[256,1024]{1,0:T(8,128)(2,1)S(1)} %bitcast.49), channel_id=1, source_target_pairs={{0,8},{8,16},{16,24},{24,0},{1,9},{9,17},{17,25},{25,1},{2,10},{10... | collective-permute-start | bytes 1572872 | tf_op jit(solution)/shard_map/spread_centers/ppermute | solution.py:126
  50.1 12.2 %collective-permute-start.2 = (bf16[256,1024]{1,0:T(8,128)(2,1)S(1)}, bf16[256,1024]{1,0:T(8,128)(2,1)S(1)}, u32[]{:S(2)}, u32[]{:S(2)}) collective-permute-start(bf16[256,1024]{1,0:T(8,128)(2,1)S(1)} %bitcast.50), channel_id=1, source_target_pairs={{0,24},{8,0},{16,8},{24,16},{1,25},{9,1},{17,9},{25,17},{2,26},{10... | collective-permute-start | bytes 1572872 | tf_op jit(solution)/shard_map/spread_centers/ppermute | solution.py:126
  52.4 16.5 %collective-permute-start = (bf16[256,1024]{1,0:T(8,128)(2,1)S(1)}, bf16[256,1024]{1,0:T(8,128)(2,1)S(1)}, u32[]{:S(2)}, u32[]{:S(2)}) collective-permute-start(bf16[256,1024]{1,0:T(8,128)(2,1)S(1)} %bitcast.51), channel_id=1, source_target_pairs={{0,1},{1,0},{2,3},{3,2},{4,5},{5,4},{6,7},{7,6},{8,9},{9,8},{10,11... | collective-permute-start | bytes 1572872 | tf_op jit(solution)/shard_map/spread_centers/ppermute | solution.py:131
  55.1 18.1 %slice-start = ((s8[6291456]{0:T(1024)(128)(4,1)}), s8[4194304]{0:T(1024)(128)(4,1)S(1)}, s32[]{:S(2)}) async-start(s8[6291456]{0:T(1024)(128)(4,1)} %bitcast.47), calls=%async_computation.2 | async-start | bytes 8388608
  55.3 17.9 %slice-start.1 = ((s8[6291456]{0:T(1024)(128)(4,1)}), s8[2097152]{0:T(1024)(128)(4,1)S(1)}, s32[]{:S(2)}) async-start(s8[6291456]{0:T(1024)(128)(4,1)} %bitcast.47), calls=%async_computation.3 | async-start | bytes 4194304
  62.2 6.9 %collective-permute-start.4 = (bf16[128,1024]{1,0:T(8,128)(2,1)S(1)}, bf16[128,1024]{1,0:T(8,128)(2,1)S(1)}, u32[]{:S(2)}, u32[]{:S(2)}) collective-permute-start(bf16[128,1024]{1,0:T(8,128)(2,1)S(1)} %slice.10), channel_id=1, source_target_pairs={{0,8},{8,16},{16,24},{24,0},{1,9},{9,17},{17,25},{25,1},{2,10},{10... | collective-permute-start | bytes 786440 | tf_op jit(solution)/shard_map/spread_centers/ppermute | solution.py:126
  62.3 6.7 %collective-permute-start.5 = (bf16[128,1024]{1,0:T(8,128)(2,1)S(1)}, bf16[128,1024]{1,0:T(8,128)(2,1)S(1)}, u32[]{:S(2)}, u32[]{:S(2)}) collective-permute-start(bf16[128,1024]{1,0:T(8,128)(2,1)S(1)} %slice.11), channel_id=1, source_target_pairs={{0,24},{8,0},{16,8},{24,16},{1,25},{9,1},{17,9},{25,17},{2,26},{10... | collective-permute-start | bytes 786440 | tf_op jit(solution)/shard_map/spread_centers/ppermute | solution.py:126
  65.1 14.8 %collective-permute-start.3 = (bf16[512,1024]{1,0:T(8,128)(2,1)S(1)}, bf16[512,1024]{1,0:T(8,128)(2,1)S(1)}, u32[]{:S(2)}, u32[]{:S(2)}) collective-permute-start(bf16[512,1024]{1,0:T(8,128)(2,1)S(1)} %pad_maximum_fusion), channel_id=1, source_target_pairs={{0,1},{1,0},{2,3},{3,2},{4,5},{5,4},{6,7},{7,6},{8,9},{9,8},{10,11... | collective-permute-start | bytes 3145736 | tf_op jit(solution)/shard_map/spread_centers/ppermute | solution.py:131
  69.1 6.5 %collective-permute-start.6 = (bf16[256,1024]{1,0:T(8,128)(2,1)S(1)}, bf16[256,1024]{1,0:T(8,128)(2,1)S(1)}, u32[]{:S(2)}, u32[]{:S(2)}) collective-permute-start(bf16[256,1024]{1,0:T(8,128)(2,1)S(1)} %pad_maximum_fusion.1), channel_id=1, source_target_pairs={{0,1},{1,0},{2,3},{3,2},{4,5},{5,4},{6,7},{7,6},{8,9},{9,8},{10,11... | collective-permute-start | bytes 1572872 | tf_op jit(solution)/shard_map/spread_centers/ppermute | solution.py:131
  80.5 7.6 %copy-start.1 = (f32[3072]{0:T(1024)S(1)}, f32[3072]{0:T(1024)}, u32[]{:S(2)}) copy-start(f32[3072]{0:T(1024)} %param.5) | copy-start | bytes 36868

commit v16 on v13

--- a/solution.py
+++ b/solution.py
@@ -137,8 +137,10 @@
         y_far = jnp.concatenate(
             [y_send(y_near[0][:split], 1), y_send(y_near[1][split:], -1)], axis=0
         )
-        near = jnp.concatenate(y_near, axis=0)
-        pieces = [plane, core_swap(plane), near, core_swap(near), y_far, core_swap(y_far)]
+        pieces = [plane, core_swap(plane)]
+        for part in y_near:
+            pieces += [part, core_swap(part)]
+        pieces += [y_far, core_swap(y_far)]
 
     with jax.named_scope("distance_min"):
         running = nearest

time: 86 us -> 88.6 us (1.030)
  waiting for transfers between devices: 21.7 us -> 26.8 us
  starting transfers between devices: 30.1 us -> 26.9 us
    ppermute x4, waiting for transfers between devices: 1.84 us -> 6.89 us  [y_send(): lax.ppermute(x, 'y', [(i, (i + s) % y_count) for i in range(y_count)])]
    ppermute x4, starting transfers between devices: 5.67 us -> 3.73 us  [y_send(): lax.ppermute(x, 'y', [(i, (i + s) % y_count) for i in range(y_count)])]
    ppermute x3 -> x4, starting transfers between devices: 6.62 us -> 5.38 us  [core_swap(): return lax.ppermute(x, 'c', [(0, 1), (1, 0)])]
    dot_general x6 -> x8, matrix products: 19.6 us -> 19.9 us  [one_block(): lax.dot_general(block_rows, fragment, (((1,), (1,)), ((), ())), preferred...]
  transfers between devices with their start and end apart: 9 -> 10, of which waited for: 3 -> 3; matrix products, arithmetic and copies ran while one was open for 25% -> 27% of each run, Pallas kernels for 0% -> 0%
where the time goes in v16:
time: 88.6 us; the launch traced here: 88.1 us
  starting transfers between devices  26.9 us (30%)
  waiting for transfers between devices  26.8 us (30%)
  matrix products  19.9 us (22%)
  other arithmetic  9.42 us (11%)
  Pallas kernels  3.16 us (4%)
  local copies, waits for them, and re-layouts  1.57 us (2%)
    dot_general x8, matrix products, one_block(): lax.dot_general(block_rows, fragment, (((1,), (1,)), ((), ())), preferred...  19.9 us
    all_to_all x1, waiting for transfers between devices, replicate_gather(): got = lax.all_to_all(copies, axes, 0, 0, tiled=True)  12.5 us
    all_to_all x1, starting transfers between devices, replicate_gather(): got = lax.all_to_all(copies, axes, 0, 0, tiled=True)  9.05 us
    all_to_all x1, starting transfers between devices, shards(): landed = lax.all_to_all(send_rows, DEV_AXES, 0, 0, tiled=True)  8.78 us
    all_to_all x1, waiting for transfers between devices, shards(): landed = lax.all_to_all(send_rows, DEV_AXES, 0, 0, tiled=True)  7.37 us
    ppermute x4, waiting for transfers between devices, y_send(): lax.ppermute(x, 'y', [(i, (i + s) % y_count) for i in range(y_count)])  6.89 us
    ppermute x4, starting transfers between devices, core_swap(): return lax.ppermute(x, 'c', [(0, 1), (1, 0)])  5.38 us
    dot_general x1, other arithmetic, shards(): jnp.einsum('rd,rd->r', pool, pool, preferred_element_type=jnp.float32)  4.08 us
  transfers between devices with their start and end apart: 10, of which 3 were waited for; matrix products, arithmetic and copies ran while one was open for 27% of the time, Pallas kernels for 0%

profile of v16, /device:TPU:1, one launch (start us, length us, event | category | flops | bytes accessed | tf_op | source)
XLA Modules:
  0.0 88.1 jit_solution(2856037062089225674)
XLA Ops:
  0.0 0.7 compare_reduce_fusion
  0.7 0.9 %convert_reduce_fusion = s32[256]{0:T(256)S(1)} fusion(s32[256]{0:T(256)} %bitcast.76), kind=kLoop, calls=%fused_computation.47 | loop fusion | flops 458496 | bytes 2048 | tf_op jit(solution)/shard_map/compact_centers/reduce_sum | solution.py:112
  1.7 0.8 select_reduce_fusion
  2.5 0.5 fusion.34.index_ref
  3.0 3.2 %compact_centers.1 = bf16[32,2,1024]{2,1,0:T(2,128)(2,1)} custom-call(s32[32]{0:T(128)} %fusion.34.index_ref, bf16[3072,1024]{1,0:T(8,128)(2,1)} %table_ref.1), custom_call_target="tpu_custom_call" | custom-call | bytes 131072 | tf_op jit(solution)/shard_map/compact_centers/pallas_call | solution.py:72
  6.2 8.8 %all-to-all-start = ((bf16[32,2,1024]{2,1,0:T(2,128)(2,1)}), bf16[32,2,1024]{2,1,0:T(2,128)(2,1)S(1)}, u32[]{:S(2)}, u32[]{:S(2)}) async-start(bf16[32,2,1024]{2,1,0:T(2,128)(2,1)} %compact_centers.1), calls=%async_computation | async-start | bytes 262144 | tf_op jit(solution)/shard_map/compact_centers/all_to_all | solution.py:118
  15.0 0.2 fusion.26
  15.2 7.4 %all-to-all-done = bf16[32,2,1024]{2,1,0:T(2,128)(2,1)S(1)} async-done(((bf16[32,2,1024]{2,1,0:T(2,128)(2,1)}), bf16[32,2,1024]{2,1,0:T(2,128)(2,1)S(1)}, u32[]{:S(2)}, u32[]{:S(2)}) %all-to-all-start) | async-done | bytes 131104 | tf_op jit(solution)/shard_map/compact_centers/all_to_all | solution.py:118
  22.6 0.6 gather_fusion
  23.3 0.9 broadcast_in_dim.110
  24.1 9.0 %all-to-all-start.1 = ((bf16[32,8,1024]{2,1,0:T(8,128)(2,1)}), bf16[32,8,1024]{2,1,0:T(8,128)(2,1)S(1)}, u32[]{:S(2)}, u32[]{:S(2)}) async-start(bf16[32,8,1024]{2,1,0:T(8,128)(2,1)} %broadcast_in_dim.110), calls=%async_computation.1 | async-start | bytes 1048576 | tf_op jit(solution)/shard_map/spread_centers/all_to_all | solution.py:86
  33.2 4.1 %fusion = f32[3072]{0:T(1024)S(1)} fusion(bf16[3072,1024]{1,0:T(8,128)(2,1)} %table_ref.1), kind=kLoop, calls=%fused_computation.2 | loop fusion | flops 9434112 | bytes 6303744 | tf_op jit(solution)/shard_map/rd,rd->r/dot_general | solution.py:128
  37.3 12.5 %all-to-all-done.1 = bf16[32,8,1024]{2,1,0:T(8,128)(2,1)S(1)} async-done(((bf16[32,8,1024]{2,1,0:T(8,128)(2,1)}), bf16[32,8,1024]{2,1,0:T(8,128)(2,1)S(1)}, u32[]{:S(2)}, u32[]{:S(2)}) %all-to-all-start.1) | async-done | bytes 524320 | tf_op jit(solution)/shard_map/spread_centers/all_to_all | solution.py:86
  49.8 2.2 %collective-permute-start = (bf16[256,1024]{1,0:T(8,128)(2,1)S(1)}, bf16[256,1024]{1,0:T(8,128)(2,1)S(1)}, u32[]{:S(2)}, u32[]{:S(2)}) collective-permute-start(bf16[256,1024]{1,0:T(8,128)(2,1)S(1)} %bitcast.73), channel_id=1, source_target_pairs={{0,1},{1,0},{2,3},{3,2},{4,5},{5,4},{6,7},{7,6},{8,9},{9,8},{10,11... | collective-permute-start | bytes 1572872 | tf_op jit(solution)/shard_map/spread_centers/ppermute | solution.py:131
  51.9 0.9 %collective-permute-start.3 = (bf16[256,1024]{1,0:T(8,128)(2,1)S(1)}, bf16[256,1024]{1,0:T(8,128)(2,1)S(1)}, u32[]{:S(2)}, u32[]{:S(2)}) collective-permute-start(bf16[256,1024]{1,0:T(8,128)(2,1)S(1)} %bitcast.74), channel_id=1, source_target_pairs={{0,24},{8,0},{16,8},{24,16},{1,25},{9,1},{17,9},{25,17},{2,26},{10... | collective-permute-start | bytes 1572872 | tf_op jit(solution)/shard_map/spread_centers/ppermute | solution.py:126
  52.8 0.6 collective-permute-start.1
  53.6 5.0 %fusion.14 = f32[3072]{0:T(1024)S(1)} fusion(bf16[3072,1024]{1,0:T(8,128)(2,1)} %table_ref.1, f32[256]{0:T(256)S(1)} %fusion.22, f32[3072]{0:T(1024)S(1)} %fusion, bf16[32,8,1024]{2,1,0:T(8,128)(2,1)S(1)} %all-to-all-done.1), kind=kOutput, calls=%fused_computation.30 | convolution fusion | flops 1614541824 | bytes 6841344 | tf_op jit(solution)/shard_map/distance_min/while/body/eval_jaxpr/dot_general | solution.py:23
  58.6 6.9 %collective-permute-done.3 = bf16[256,1024]{1,0:T(8,128)(2,1)S(1)} collective-permute-done((bf16[256,1024]{1,0:T(8,128)(2,1)S(1)}, bf16[256,1024]{1,0:T(8,128)(2,1)S(1)}, u32[]{:S(2)}, u32[]{:S(2)}) %collective-permute-start.3) | collective-permute-done | bytes 524320 | tf_op jit(solution)/shard_map/spread_centers/ppermute | solution.py:126
  65.5 2.2 %collective-permute-start.6 = (bf16[128,1024]{1,0:T(8,128)(2,1)S(1)}, bf16[128,1024]{1,0:T(8,128)(2,1)S(1)}, u32[]{:S(2)}, u32[]{:S(2)}) collective-permute-start(bf16[128,1024]{1,0:T(8,128)(2,1)S(1)} %slice.11), channel_id=1, source_target_pairs={{0,24},{8,0},{16,8},{24,16},{1,25},{9,1},{17,9},{25,17},{2,26},{10... | collective-permute-start | bytes 786440 | tf_op jit(solution)/shard_map/spread_centers/ppermute | solution.py:126
  67.8 1.2 %collective-permute-start.4 = (bf16[256,1024]{1,0:T(8,128)(2,1)S(1)}, bf16[256,1024]{1,0:T(8,128)(2,1)S(1)}, u32[]{:S(2)}, u32[]{:S(2)}) collective-permute-start(bf16[256,1024]{1,0:T(8,128)(2,1)S(1)} %collective-permute-done.3), channel_id=1, source_target_pairs={{0,1},{1,0},{2,3},{3,2},{4,5},{5,4},{6,7},{7,6},{8,9},{9,8},{10,11... | collective-permute-start | bytes 1572872 | tf_op jit(solution)/shard_map/spread_centers/ppermute | solution.py:131
  69.0 0.3 collective-permute-start.2
  69.6 0.2 fusion.21
  69.8 2.1 %maximum_reduce_fusion.5 = f32[3072]{0:T(1024)S(1)} fusion(f32[256]{0:T(256)S(1)} %fusion.21, f32[3072]{0:T(1024)S(1)} %fusion, bf16[256,1024]{1,0:T(8,128)(2,1)S(1)} %collective-permute-done, bf16[3072,1024]{1,0:T(8,128)(2,1)S(1)} %bitcast.72), kind=kOutput, calls=%fused_computation.28 | convolution fusion | flops 1614541824 | bytes 6841344 | tf_op jit(solution)/shard_map/distance_min/while/body/eval_jaxpr/dot_general | solution.py:23
  72.0 2.1 %maximum_reduce_fusion.2 = f32[3072]{0:T(1024)S(1)} fusion(f32[256]{0:T(256)S(1)} %fusion.18, f32[3072]{0:T(1024)S(1)} %fusion, bf16[256,1024]{1,0:T(8,128)(2,1)S(1)} %collective-permute-done.3, bf16[3072,1024]{1,0:T(8,128)(2,1)S(1)} %bitcast.72), kind=kOutput, calls=%fused_computation.25 | convolution fusion | flops 1614541824 | bytes 6841344 | tf_op jit(solution)/shard_map/distance_min/while/body/eval_jaxpr/dot_general | solution.py:23
  74.1 2.1 %maximum_reduce_fusion.4 = f32[3072]{0:T(1024)S(1)} fusion(f32[256]{0:T(256)S(1)} %fusion.20, f32[3072]{0:T(1024)S(1)} %fusion, bf16[256,1024]{1,0:T(8,128)(2,1)S(1)} %collective-permute-done.1, bf16[3072,1024]{1,0:T(8,128)(2,1)S(1)} %bitcast.72), kind=kOutput, calls=%fused_computation.27 | convolution fusion | flops 1614541824 | bytes 6841344 | tf_op jit(solution)/shard_map/distance_min/while/body/eval_jaxpr/dot_general | solution.py:23
  76.3 0.2 fusion.16
  76.5 1.8 %collective-permute-start.7 = (bf16[256,1024]{1,0:T(8,128)(2,1)S(1)}, bf16[256,1024]{1,0:T(8,128)(2,1)S(1)}, u32[]{:S(2)}, u32[]{:S(2)}) collective-permute-start(bf16[256,1024]{1,0:T(8,128)(2,1)S(1)} %constant_dynamic-update-slice_fusion), channel_id=1, source_target_pairs={{0,1},{1,0},{2,3},{3,2},{4,5},{5,4},{6,7},{7,6},{8,9},{9,8},{10,11... | collective-permute-start | bytes 1572872 | tf_op jit(solution)/shard_map/spread_centers/ppermute | solution.py:131
  78.3 2.1 %fusion.13 = f32[3072]{0:T(1024)S(1)} fusion(bf16[256,1024]{1,0:T(8,128)(2,1)S(1)} %constant_dynamic-update-slice_fusion, bf16[3072,1024]{1,0:T(8,128)(2,1)S(1)} %bitcast.72, f32[256]{0:T(256)S(1)} %fusion.16, f32[3072]{0:T(1024)S(1)} %fusion), kind=kOutput, calls=%fused_computation.29 | convolution fusion | flops 1614541824 | bytes 6841344 | tf_op jit(solution)/shard_map/distance_min/while/body/eval_jaxpr/dot_general | solution.py:23
  80.6 2.1 %maximum_reduce_fusion.1 = f32[3072]{0:T(1024)S(1)} fusion(f32[256]{0:T(256)S(1)} %fusion.17, f32[3072]{0:T(1024)S(1)} %fusion, bf16[256,1024]{1,0:T(8,128)(2,1)S(1)} %collective-permute-done.4, bf16[3072,1024]{1,0:T(8,128)(2,1)S(1)} %bitcast.72), kind=kOutput, calls=%fused_computation.24 | convolution fusion | flops 1614541824 | bytes 6841344 | tf_op jit(solution)/shard_map/distance_min/while/body/eval_jaxpr/dot_general | solution.py:23
  82.9 2.1 %maximum_reduce_fusion.3 = f32[3072]{0:T(1024)S(1)} fusion(f32[256]{0:T(256)S(1)} %fusion.19, f32[3072]{0:T(1024)S(1)} %fusion, bf16[256,1024]{1,0:T(8,128)(2,1)S(1)} %collective-permute-done.2, bf16[3072,1024]{1,0:T(8,128)(2,1)S(1)} %bitcast.72), kind=kOutput, calls=%fused_computation.26 | convolution fusion | flops 1614541824 | bytes 6841344 | tf_op jit(solution)/shard_map/distance_min/while/body/eval_jaxpr/dot_general | solution.py:23
  85.3 2.1 %maximum_reduce_fusion = f32[3072]{0:T(1024)S(1)} fusion(f32[256]{0:T(256)S(1)} %fusion.15, f32[3072]{0:T(1024)S(1)} %fusion, bf16[256,1024]{1,0:T(8,128)(2,1)S(1)} %collective-permute-done.7, bf16[3072,1024]{1,0:T(8,128)(2,1)S(1)} %bitcast.72), kind=kOutput, calls=%fused_computation.23 | convolution fusion | flops 1614541824 | bytes 6841344 | tf_op jit(solution)/shard_map/distance_min/while/body/eval_jaxpr/dot_general | solution.py:23
  87.4 0.6 minimum_minimum_fusion
  (36 shorter events, 1.5 us)
Async XLA Ops:
  3.0 12.0 %copy-start = (s32[1,256]{1,0:T(1,128)S(1)}, s32[1,256]{1,0:T(1,128)}, u32[]{:S(2)}) copy-start(s32[1,256]{1,0:T(1,128)} %param.6) | copy-start | bytes 3076
  3.0 12.0 %copy-start.2 = (s32[1,256]{1,0:T(1,128)S(1)}, s32[1,256]{1,0:T(1,128)}, u32[]{:S(2)}) copy-start(s32[1,256]{1,0:T(1,128)} %param.7) | copy-start | bytes 3076
  6.2 16.4 %all-to-all-start = ((bf16[32,2,1024]{2,1,0:T(2,128)(2,1)}), bf16[32,2,1024]{2,1,0:T(2,128)(2,1)S(1)}, u32[]{:S(2)}, u32[]{:S(2)}) async-start(bf16[32,2,1024]{2,1,0:T(2,128)(2,1)} %compact_centers.1), calls=%async_computation | async-start | bytes 262144 | tf_op jit(solution)/shard_map/compact_centers/all_to_all | solution.py:118
  24.1 25.6 %all-to-all-start.1 = ((bf16[32,8,1024]{2,1,0:T(8,128)(2,1)}), bf16[32,8,1024]{2,1,0:T(8,128)(2,1)S(1)}, u32[]{:S(2)}, u32[]{:S(2)}) async-start(bf16[32,8,1024]{2,1,0:T(8,128)(2,1)} %broadcast_in_dim.110), calls=%async_computation.1 | async-start | bytes 1048576 | tf_op jit(solution)/shard_map/spread_centers/all_to_all | solution.py:86
  49.8 19.8 %collective-permute-start = (bf16[256,1024]{1,0:T(8,128)(2,1)S(1)}, bf16[256,1024]{1,0:T(8,128)(2,1)S(1)}, u32[]{:S(2)}, u32[]{:S(2)}) collective-permute-start(bf16[256,1024]{1,0:T(8,128)(2,1)S(1)} %bitcast.73), channel_id=1, source_target_pairs={{0,1},{1,0},{2,3},{3,2},{4,5},{5,4},{6,7},{7,6},{8,9},{9,8},{10,11... | collective-permute-start | bytes 1572872 | tf_op jit(solution)/shard_map/spread_centers/ppermute | solution.py:131
  51.9 13.6 %collective-permute-start.3 = (bf16[256,1024]{1,0:T(8,128)(2,1)S(1)}, bf16[256,1024]{1,0:T(8,128)(2,1)S(1)}, u32[]{:S(2)}, u32[]{:S(2)}) collective-permute-start(bf16[256,1024]{1,0:T(8,128)(2,1)S(1)} %bitcast.74), channel_id=1, source_target_pairs={{0,24},{8,0},{16,8},{24,16},{1,25},{9,1},{17,9},{25,17},{2,26},{10... | collective-permute-start | bytes 1572872 | tf_op jit(solution)/shard_map/spread_centers/ppermute | solution.py:126
  52.8 14.9 %collective-permute-start.1 = (bf16[256,1024]{1,0:T(8,128)(2,1)S(1)}, bf16[256,1024]{1,0:T(8,128)(2,1)S(1)}, u32[]{:S(2)}, u32[]{:S(2)}) collective-permute-start(bf16[256,1024]{1,0:T(8,128)(2,1)S(1)} %bitcast.75), channel_id=1, source_target_pairs={{0,8},{8,16},{16,24},{24,0},{1,9},{9,17},{17,25},{25,1},{2,10},{10... | collective-permute-start | bytes 1572872 | tf_op jit(solution)/shard_map/spread_centers/ppermute | solution.py:126
  53.4 16.4 %slice-start = ((s8[6291456]{0:T(1024)(128)(4,1)}), s8[4194304]{0:T(1024)(128)(4,1)S(1)}, s32[]{:S(2)}) async-start(s8[6291456]{0:T(1024)(128)(4,1)} %bitcast.71), calls=%async_computation.2 | async-start | bytes 8388608
  53.6 16.2 %slice-start.1 = ((s8[6291456]{0:T(1024)(128)(4,1)}), s8[2097152]{0:T(1024)(128)(4,1)S(1)}, s32[]{:S(2)}) async-start(s8[6291456]{0:T(1024)(128)(4,1)} %bitcast.71), calls=%async_computation.3 | async-start | bytes 4194304
  65.5 10.8 %collective-permute-start.6 = (bf16[128,1024]{1,0:T(8,128)(2,1)S(1)}, bf16[128,1024]{1,0:T(8,128)(2,1)S(1)}, u32[]{:S(2)}, u32[]{:S(2)}) collective-permute-start(bf16[128,1024]{1,0:T(8,128)(2,1)S(1)} %slice.11), channel_id=1, source_target_pairs={{0,24},{8,0},{16,8},{24,16},{1,25},{9,1},{17,9},{25,17},{2,26},{10... | collective-permute-start | bytes 786440 | tf_op jit(solution)/shard_map/spread_centers/ppermute | solution.py:126
  67.7 8.5 %collective-permute-start.5 = (bf16[128,1024]{1,0:T(8,128)(2,1)S(1)}, bf16[128,1024]{1,0:T(8,128)(2,1)S(1)}, u32[]{:S(2)}, u32[]{:S(2)}) collective-permute-start(bf16[128,1024]{1,0:T(8,128)(2,1)S(1)} %slice.10), channel_id=1, source_target_pairs={{0,8},{8,16},{16,24},{24,0},{1,9},{9,17},{17,25},{25,1},{2,10},{10... | collective-permute-start | bytes 786440 | tf_op jit(solution)/shard_map/spread_centers/ppermute | solution.py:126
  67.8 12.6 %collective-permute-start.4 = (bf16[256,1024]{1,0:T(8,128)(2,1)S(1)}, bf16[256,1024]{1,0:T(8,128)(2,1)S(1)}, u32[]{:S(2)}, u32[]{:S(2)}) collective-permute-start(bf16[256,1024]{1,0:T(8,128)(2,1)S(1)} %collective-permute-done.3), channel_id=1, source_target_pairs={{0,1},{1,0},{2,3},{3,2},{4,5},{5,4},{6,7},{7,6},{8,9},{9,8},{10,11... | collective-permute-start | bytes 1572872 | tf_op jit(solution)/shard_map/spread_centers/ppermute | solution.py:131
  69.0 13.8 %collective-permute-start.2 = (bf16[256,1024]{1,0:T(8,128)(2,1)S(1)}, bf16[256,1024]{1,0:T(8,128)(2,1)S(1)}, u32[]{:S(2)}, u32[]{:S(2)}) collective-permute-start(bf16[256,1024]{1,0:T(8,128)(2,1)S(1)} %collective-permute-done.1), channel_id=1, source_target_pairs={{0,1},{1,0},{2,3},{3,2},{4,5},{5,4},{6,7},{7,6},{8,9},{9,8},{10,11... | collective-permute-start | bytes 1572872 | tf_op jit(solution)/shard_map/spread_centers/ppermute | solution.py:131
  76.5 8.6 %collective-permute-start.7 = (bf16[256,1024]{1,0:T(8,128)(2,1)S(1)}, bf16[256,1024]{1,0:T(8,128)(2,1)S(1)}, u32[]{:S(2)}, u32[]{:S(2)}) collective-permute-start(bf16[256,1024]{1,0:T(8,128)(2,1)S(1)} %constant_dynamic-update-slice_fusion), channel_id=1, source_target_pairs={{0,1},{1,0},{2,3},{3,2},{4,5},{5,4},{6,7},{7,6},{8,9},{9,8},{10,11... | collective-permute-start | bytes 1572872 | tf_op jit(solution)/shard_map/spread_centers/ppermute | solution.py:131
  85.3 2.1 %copy-start.1 = (f32[3072]{0:T(1024)S(1)}, f32[3072]{0:T(1024)}, u32[]{:S(2)}) copy-start(f32[3072]{0:T(1024)} %param.5) | copy-start | bytes 36868

commit v17 on v13

--- a/solution.py
+++ b/solution.py
@@ -131,7 +131,7 @@
         return lax.ppermute(x, "c", [(0, 1), (1, 0)])
 
     with jax.named_scope("spread_centers"):
-        plane = replicate_gather(compact, ("z", "x"), z_count * x_count)
+        plane = replicate_gather(compact, ("x", "z"), z_count * x_count)
         y_near = y_send(plane, 1), y_send(plane, -1)
         split = plane.shape[0] // 2
         y_far = jnp.concatenate(

time: 86 us -> 84.8 us (0.986); the launches traced: 85.6 us -> 83.3 us
  waiting for transfers between devices: 21.7 us -> 17.5 us
  starting transfers between devices: 30.1 us -> 31.9 us
    all_to_all x1, waiting for transfers between devices: 12.5 us -> 10.1 us  [replicate_gather(): got = lax.all_to_all(copies, axes, 0, 0, tiled=True)]
    ppermute x4, waiting for transfers between devices: 1.84 us -> 0.01 us  [y_send(): lax.ppermute(x, 'y', [(i, (i + s) % y_count) for i in range(y_count)])]
    ppermute x3, starting transfers between devices: 6.62 us -> 8.42 us  [core_swap(): return lax.ppermute(x, 'c', [(0, 1), (1, 0)])]
  transfers between devices with their start and end apart: 9 -> 9, of which waited for: 3 -> 2; matrix products, arithmetic and copies ran while one was open for 25% -> 25% of each run, Pallas kernels for 0% -> 0%
where the time goes in v17:
time: 84.8 us; the launch traced here: 83.3 us
  starting transfers between devices  31.9 us (38%)
  matrix products  19.6 us (23%)
  waiting for transfers between devices  17.5 us (21%)
  other arithmetic  9.28 us (11%)
  Pallas kernels  3.24 us (4%)
  local copies, waits for them, and re-layouts  1.64 us (2%)
    dot_general x6, matrix products, one_block(): lax.dot_general(block_rows, fragment, (((1,), (1,)), ((), ())), preferred...  19.6 us
    all_to_all x1, waiting for transfers between devices, replicate_gather(): got = lax.all_to_all(copies, axes, 0, 0, tiled=True)  10.1 us
    all_to_all x1, starting transfers between devices, replicate_gather(): got = lax.all_to_all(copies, axes, 0, 0, tiled=True)  9.3 us
    all_to_all x1, starting transfers between devices, shards(): landed = lax.all_to_all(send_rows, DEV_AXES, 0, 0, tiled=True)  8.46 us
    ppermute x3, starting transfers between devices, core_swap(): return lax.ppermute(x, 'c', [(0, 1), (1, 0)])  8.42 us
    all_to_all x1, waiting for transfers between devices, shards(): landed = lax.all_to_all(send_rows, DEV_AXES, 0, 0, tiled=True)  7.37 us
    ppermute x4, starting transfers between devices, y_send(): lax.ppermute(x, 'y', [(i, (i + s) % y_count) for i in range(y_count)])  5.67 us
    dot_general x1, other arithmetic, shards(): jnp.einsum('rd,rd->r', pool, pool, preferred_element_type=jnp.float32)  4.08 us
  transfers between devices with their start and end apart: 9, of which 2 were waited for; matrix products, arithmetic and copies ran while one was open for 25% of the time, Pallas kernels for 0%

profile of v17, /device:TPU:1, one launch (start us, length us, event | category | flops | bytes accessed | tf_op | source)
XLA Modules:
  0.0 83.3 jit_solution(7254708413218320891)
XLA Ops:
  0.0 1.0 %convert_reduce_fusion = s32[256]{0:T(256)S(1)} fusion(s32[256]{0:T(256)} %bitcast.68), kind=kLoop, calls=%fused_computation.37 | loop fusion | flops 458496 | bytes 2048 | tf_op jit(solution)/shard_map/compact_centers/reduce_sum | solution.py:112
  1.0 0.7 compare_reduce_fusion
  1.7 0.8 select_reduce_fusion
  2.5 0.5 fusion.32.index_ref
  3.0 3.2 %compact_centers.1 = bf16[32,2,1024]{2,1,0:T(2,128)(2,1)} custom-call(s32[32]{0:T(128)} %fusion.32.index_ref, bf16[3072,1024]{1,0:T(8,128)(2,1)} %table_ref.1), custom_call_target="tpu_custom_call" | custom-call | bytes 131072 | tf_op jit(solution)/shard_map/compact_centers/pallas_call | solution.py:72
  6.3 8.5 %all-to-all-start = ((bf16[32,2,1024]{2,1,0:T(2,128)(2,1)}), bf16[32,2,1024]{2,1,0:T(2,128)(2,1)S(1)}, u32[]{:S(2)}, u32[]{:S(2)}) async-start(bf16[32,2,1024]{2,1,0:T(2,128)(2,1)} %compact_centers.1), calls=%async_computation | async-start | bytes 262144 | tf_op jit(solution)/shard_map/compact_centers/all_to_all | solution.py:118
  14.8 0.2 fusion.24
  15.0 7.4 %all-to-all-done = bf16[32,2,1024]{2,1,0:T(2,128)(2,1)S(1)} async-done(((bf16[32,2,1024]{2,1,0:T(2,128)(2,1)}), bf16[32,2,1024]{2,1,0:T(2,128)(2,1)S(1)}, u32[]{:S(2)}, u32[]{:S(2)}) %all-to-all-start) | async-done | bytes 131104 | tf_op jit(solution)/shard_map/compact_centers/all_to_all | solution.py:118
  22.4 0.6 gather_fusion
  23.1 0.9 %broadcast_in_dim.98 = bf16[32,8,1024]{2,1,0:T(8,128)(2,1)} broadcast(bf16[8,1024]{1,0:T(8,128)(2,1)S(1)} %broadcast_select_fusion), dimensions={1,2} | broadcast | bytes 540672 | tf_op jit(solution)/shard_map/spread_centers/broadcast_in_dim | solution.py:85
  23.9 9.3 %all-to-all-start.1 = ((bf16[32,8,1024]{2,1,0:T(8,128)(2,1)}), bf16[32,8,1024]{2,1,0:T(8,128)(2,1)S(1)}, u32[]{:S(2)}, u32[]{:S(2)}) async-start(bf16[32,8,1024]{2,1,0:T(8,128)(2,1)} %broadcast_in_dim.98), calls=%async_computation.1 | async-start | bytes 1048576 | tf_op jit(solution)/shard_map/spread_centers/all_to_all | solution.py:86
  33.2 4.1 %fusion = f32[3072]{0:T(1024)S(1)} fusion(bf16[3072,1024]{1,0:T(8,128)(2,1)} %table_ref.1), kind=kLoop, calls=%fused_computation.2 | loop fusion | flops 9434112 | bytes 6303744 | tf_op jit(solution)/shard_map/rd,rd->r/dot_general | solution.py:128
  37.3 10.1 %all-to-all-done.1 = bf16[32,8,1024]{2,1,0:T(8,128)(2,1)S(1)} async-done(((bf16[32,8,1024]{2,1,0:T(8,128)(2,1)}), bf16[32,8,1024]{2,1,0:T(8,128)(2,1)S(1)}, u32[]{:S(2)}, u32[]{:S(2)}) %all-to-all-start.1) | async-done | bytes 524320 | tf_op jit(solution)/shard_map/spread_centers/all_to_all | solution.py:86
  47.4 0.3 collective-permute-start.1
  47.7 2.4 %collective-permute-start.2 = (bf16[256,1024]{1,0:T(8,128)(2,1)S(1)}, bf16[256,1024]{1,0:T(8,128)(2,1)S(1)}, u32[]{:S(2)}, u32[]{:S(2)}) collective-permute-start(bf16[256,1024]{1,0:T(8,128)(2,1)S(1)} %bitcast.66), channel_id=1, source_target_pairs={{0,24},{8,0},{16,8},{24,16},{1,25},{9,1},{17,9},{25,17},{2,26},{10... | collective-permute-start | bytes 1572872 | tf_op jit(solution)/shard_map/spread_centers/ppermute | solution.py:126
  50.1 4.0 %collective-permute-start = (bf16[256,1024]{1,0:T(8,128)(2,1)S(1)}, bf16[256,1024]{1,0:T(8,128)(2,1)S(1)}, u32[]{:S(2)}, u32[]{:S(2)}) collective-permute-start(bf16[256,1024]{1,0:T(8,128)(2,1)S(1)} %bitcast.67), channel_id=1, source_target_pairs={{0,1},{1,0},{2,3},{3,2},{4,5},{5,4},{6,7},{7,6},{8,9},{9,8},{10,11... | collective-permute-start | bytes 1572872 | tf_op jit(solution)/shard_map/spread_centers/ppermute | solution.py:131
  54.1 0.2 fusion.20
  54.3 5.0 %fusion.16 = f32[3072]{0:T(1024)S(1)} fusion(bf16[3072,1024]{1,0:T(8,128)(2,1)} %table_ref.1, f32[256]{0:T(256)S(1)} %fusion.20, f32[3072]{0:T(1024)S(1)} %fusion, bf16[32,8,1024]{2,1,0:T(8,128)(2,1)S(1)} %all-to-all-done.1), kind=kOutput, calls=%fused_computation.28 | convolution fusion | flops 1614541824 | bytes 6841344 | tf_op jit(solution)/shard_map/distance_min/while/body/eval_jaxpr/dot_general | solution.py:23
  59.4 3.7 %collective-permute-start.3 = (bf16[512,1024]{1,0:T(8,128)(2,1)S(1)}, bf16[512,1024]{1,0:T(8,128)(2,1)S(1)}, u32[]{:S(2)}, u32[]{:S(2)}) collective-permute-start(bf16[512,1024]{1,0:T(8,128)(2,1)S(1)} %constant_dynamic-update-slice_fusion), channel_id=1, source_target_pairs={{0,1},{1,0},{2,3},{3,2},{4,5},{5,4},{6,7},{7,6},{8,9},{9,8},{10,11... | collective-permute-start | bytes 3145736 | tf_op jit(solution)/shard_map/spread_centers/ppermute | solution.py:131
  63.1 0.3 fusion.14
  63.6 2.9 %collective-permute-start.5 = (bf16[128,1024]{1,0:T(8,128)(2,1)S(1)}, bf16[128,1024]{1,0:T(8,128)(2,1)S(1)}, u32[]{:S(2)}, u32[]{:S(2)}) collective-permute-start(bf16[128,1024]{1,0:T(8,128)(2,1)S(1)} %slice.11), channel_id=1, source_target_pairs={{0,24},{8,0},{16,8},{24,16},{1,25},{9,1},{17,9},{25,17},{2,26},{10... | collective-permute-start | bytes 786440 | tf_op jit(solution)/shard_map/spread_centers/ppermute | solution.py:126
  66.5 4.0 %fusion.4 = f32[3072]{0:T(1024)S(1)} fusion(bf16[512,1024]{1,0:T(8,128)(2,1)S(1)} %constant_dynamic-update-slice_fusion, bf16[3072,1024]{1,0:T(8,128)(2,1)S(1)} %bitcast.64, f32[512]{0:T(512)S(1)} %fusion.14, f32[3072]{0:T(1024)S(1)} %fusion), kind=kOutput, calls=%fused_computation.8 | convolution fusion | flops 3229086720 | bytes 7366656 | tf_op jit(solution)/shard_map/distance_min/while/body/eval_jaxpr/dot_general | solution.py:23
  70.5 0.2 fusion.19
  70.7 2.1 %maximum_reduce_fusion.1 = f32[3072]{0:T(1024)S(1)} fusion(f32[256]{0:T(256)S(1)} %fusion.19, f32[3072]{0:T(1024)S(1)} %fusion, bf16[256,1024]{1,0:T(8,128)(2,1)S(1)} %collective-permute-done, bf16[3072,1024]{1,0:T(8,128)(2,1)S(1)} %bitcast.64), kind=kOutput, calls=%fused_computation.22 | convolution fusion | flops 1614541824 | bytes 6841344 | tf_op jit(solution)/shard_map/distance_min/while/body/eval_jaxpr/dot_general | solution.py:23
  72.9 0.7 collective-permute-start.6
  73.6 0.2 fusion.18
  73.8 2.2 %fusion.15 = f32[3072]{0:T(1024)S(1)} fusion(bf16[256,1024]{1,0:T(8,128)(2,1)S(1)} %constant_dynamic-update-slice_fusion.2, bf16[3072,1024]{1,0:T(8,128)(2,1)S(1)} %bitcast.64, f32[256]{0:T(256)S(1)} %fusion.18, f32[3072]{0:T(1024)S(1)} %fusion), kind=kOutput, calls=%fused_computation.27 | convolution fusion | flops 1614541824 | bytes 6841344 | tf_op jit(solution)/shard_map/distance_min/while/body/eval_jaxpr/dot_general | solution.py:23
  76.0 0.2 fusion.17
  76.2 2.2 %maximum_reduce_fusion = f32[3072]{0:T(1024)S(1)} fusion(f32[256]{0:T(256)S(1)} %fusion.17, f32[3072]{0:T(1024)S(1)} %fusion, bf16[256,1024]{1,0:T(8,128)(2,1)S(1)} %collective-permute-done.6, bf16[3072,1024]{1,0:T(8,128)(2,1)S(1)} %bitcast.64), kind=kOutput, calls=%fused_computation.21 | convolution fusion | flops 1614541824 | bytes 6841344 | tf_op jit(solution)/shard_map/distance_min/while/body/eval_jaxpr/dot_general | solution.py:23
  78.4 0.3 fusion.13
  78.7 4.0 %fusion.2 = f32[3072]{0:T(1024)S(1)} fusion(bf16[512,1024]{1,0:T(8,128)(2,1)S(1)} %collective-permute-done.3, bf16[3072,1024]{1,0:T(8,128)(2,1)S(1)} %bitcast.64, f32[512]{0:T(512)S(1)} %fusion.13, f32[3072]{0:T(1024)S(1)} %fusion), kind=kOutput, calls=%fused_computation.5 | convolution fusion | flops 3229086720 | bytes 7366656 | tf_op jit(solution)/shard_map/distance_min/while/body/eval_jaxpr/dot_general | solution.py:23
  82.7 0.6 minimum_minimum_fusion
  (32 shorter events, 0.4 us)
Async XLA Ops:
  0.0 14.7 %copy-start = (s32[1,256]{1,0:T(1,128)S(1)}, s32[1,256]{1,0:T(1,128)}, u32[]{:S(2)}) copy-start(s32[1,256]{1,0:T(1,128)} %param.6) | copy-start | bytes 3076
  0.0 14.8 %copy-start.2 = (s32[1,256]{1,0:T(1,128)S(1)}, s32[1,256]{1,0:T(1,128)}, u32[]{:S(2)}) copy-start(s32[1,256]{1,0:T(1,128)} %param.7) | copy-start | bytes 3076
  6.3 16.1 %all-to-all-start = ((bf16[32,2,1024]{2,1,0:T(2,128)(2,1)}), bf16[32,2,1024]{2,1,0:T(2,128)(2,1)S(1)}, u32[]{:S(2)}, u32[]{:S(2)}) async-start(bf16[32,2,1024]{2,1,0:T(2,128)(2,1)} %compact_centers.1), calls=%async_computation | async-start | bytes 262144 | tf_op jit(solution)/shard_map/compact_centers/all_to_all | solution.py:118
  23.9 23.5 %all-to-all-start.1 = ((bf16[32,8,1024]{2,1,0:T(8,128)(2,1)}), bf16[32,8,1024]{2,1,0:T(8,128)(2,1)S(1)}, u32[]{:S(2)}, u32[]{:S(2)}) async-start(bf16[32,8,1024]{2,1,0:T(8,128)(2,1)} %broadcast_in_dim.98), calls=%async_computation.1 | async-start | bytes 1048576 | tf_op jit(solution)/shard_map/spread_centers/all_to_all | solution.py:86
  47.4 11.9 %collective-permute-start.1 = (bf16[256,1024]{1,0:T(8,128)(2,1)S(1)}, bf16[256,1024]{1,0:T(8,128)(2,1)S(1)}, u32[]{:S(2)}, u32[]{:S(2)}) collective-permute-start(bf16[256,1024]{1,0:T(8,128)(2,1)S(1)} %bitcast.65), channel_id=1, source_target_pairs={{0,8},{8,16},{16,24},{24,0},{1,9},{9,17},{17,25},{25,1},{2,10},{10... | collective-permute-start | bytes 1572872 | tf_op jit(solution)/shard_map/spread_centers/ppermute | solution.py:126
  47.7 11.7 %collective-permute-start.2 = (bf16[256,1024]{1,0:T(8,128)(2,1)S(1)}, bf16[256,1024]{1,0:T(8,128)(2,1)S(1)}, u32[]{:S(2)}, u32[]{:S(2)}) collective-permute-start(bf16[256,1024]{1,0:T(8,128)(2,1)S(1)} %bitcast.66), channel_id=1, source_target_pairs={{0,24},{8,0},{16,8},{24,16},{1,25},{9,1},{17,9},{25,17},{2,26},{10... | collective-permute-start | bytes 1572872 | tf_op jit(solution)/shard_map/spread_centers/ppermute | solution.py:126
  50.1 20.4 %collective-permute-start = (bf16[256,1024]{1,0:T(8,128)(2,1)S(1)}, bf16[256,1024]{1,0:T(8,128)(2,1)S(1)}, u32[]{:S(2)}, u32[]{:S(2)}) collective-permute-start(bf16[256,1024]{1,0:T(8,128)(2,1)S(1)} %bitcast.67), channel_id=1, source_target_pairs={{0,1},{1,0},{2,3},{3,2},{4,5},{5,4},{6,7},{7,6},{8,9},{9,8},{10,11... | collective-permute-start | bytes 1572872 | tf_op jit(solution)/shard_map/spread_centers/ppermute | solution.py:131
  54.1 12.3 %slice-start = ((s8[6291456]{0:T(1024)(128)(4,1)}), s8[4194304]{0:T(1024)(128)(4,1)S(1)}, s32[]{:S(2)}) async-start(s8[6291456]{0:T(1024)(128)(4,1)} %bitcast.63), calls=%async_computation.2 | async-start | bytes 8388608
  54.3 12.2 %slice-start.1 = ((s8[6291456]{0:T(1024)(128)(4,1)}), s8[2097152]{0:T(1024)(128)(4,1)S(1)}, s32[]{:S(2)}) async-start(s8[6291456]{0:T(1024)(128)(4,1)} %bitcast.63), calls=%async_computation.3 | async-start | bytes 4194304
  59.4 18.9 %collective-permute-start.3 = (bf16[512,1024]{1,0:T(8,128)(2,1)S(1)}, bf16[512,1024]{1,0:T(8,128)(2,1)S(1)}, u32[]{:S(2)}, u32[]{:S(2)}) collective-permute-start(bf16[512,1024]{1,0:T(8,128)(2,1)S(1)} %constant_dynamic-update-slice_fusion), channel_id=1, source_target_pairs={{0,1},{1,0},{2,3},{3,2},{4,5},{5,4},{6,7},{7,6},{8,9},{9,8},{10,11... | collective-permute-start | bytes 3145736 | tf_op jit(solution)/shard_map/spread_centers/ppermute | solution.py:131
  63.4 9.4 %collective-permute-start.4 = (bf16[128,1024]{1,0:T(8,128)(2,1)S(1)}, bf16[128,1024]{1,0:T(8,128)(2,1)S(1)}, u32[]{:S(2)}, u32[]{:S(2)}) collective-permute-start(bf16[128,1024]{1,0:T(8,128)(2,1)S(1)} %slice.10), channel_id=1, source_target_pairs={{0,8},{8,16},{16,24},{24,0},{1,9},{9,17},{17,25},{25,1},{2,10},{10... | collective-permute-start | bytes 786440 | tf_op jit(solution)/shard_map/spread_centers/ppermute | solution.py:126
  63.6 9.3 %collective-permute-start.5 = (bf16[128,1024]{1,0:T(8,128)(2,1)S(1)}, bf16[128,1024]{1,0:T(8,128)(2,1)S(1)}, u32[]{:S(2)}, u32[]{:S(2)}) collective-permute-start(bf16[128,1024]{1,0:T(8,128)(2,1)S(1)} %slice.11), channel_id=1, source_target_pairs={{0,24},{8,0},{16,8},{24,16},{1,25},{9,1},{17,9},{25,17},{2,26},{10... | collective-permute-start | bytes 786440 | tf_op jit(solution)/shard_map/spread_centers/ppermute | solution.py:126
  72.9 3.1 %collective-permute-start.6 = (bf16[256,1024]{1,0:T(8,128)(2,1)S(1)}, bf16[256,1024]{1,0:T(8,128)(2,1)S(1)}, u32[]{:S(2)}, u32[]{:S(2)}) collective-permute-start(bf16[256,1024]{1,0:T(8,128)(2,1)S(1)} %constant_dynamic-update-slice_fusion.2), channel_id=1, source_target_pairs={{0,1},{1,0},{2,3},{3,2},{4,5},{5,4},{6,7},{7,6},{8,9},{9,8},{10,11... | collective-permute-start | bytes 1572872 | tf_op jit(solution)/shard_map/spread_centers/ppermute | solution.py:131
  78.7 4.0 %copy-start.1 = (f32[3072]{0:T(1024)S(1)}, f32[3072]{0:T(1024)}, u32[]{:S(2)}) copy-start(f32[3072]{0:T(1024)} %param.5) | copy-start | bytes 36868

commit v18 on v17

--- a/solution.py
+++ b/solution.py
@@ -115,7 +115,12 @@
         )
         peer_offset = jnp.sum(jnp.where(to_peer, offsets[None, :], 0), axis=1)
         send_rows = gather_rows(pool, peer_offset)
-        landed = lax.all_to_all(send_rows, DEV_AXES, 0, 0, tiled=True)
+        grid = (y_count, x_count, dev_count // (y_count * x_count))
+        tail = send_rows.shape[1:]
+        flip = (2, 1, 0) + tuple(range(3, 3 + len(tail)))
+        reordered = send_rows.reshape(grid + tail).transpose(flip).reshape(send_rows.shape)
+        landed = lax.all_to_all(reordered, DEV_AXES[::-1], 0, 0, tiled=True)
+        landed = landed.reshape(grid[::-1] + tail).transpose(flip).reshape(send_rows.shape)
         wanted = my_index + dev_count * jnp.arange(per_device, dtype=jnp.int32)
         is_wanted = position[None, :] == wanted[:, None]
         source = jnp.sum(jnp.where(is_wanted, owners[None, :], 0), axis=1)

time: 84.8 us -> 86 us (1.014)
  local copies, waits for them, and re-layouts: 1.64 us -> 3.38 us
    reshape x0 -> x1, local copies, waits for them, and re-layouts: none -> 1.65 us  [shards(): send_rows.reshape(grid + tail).transpose(flip).reshape(send_rows.shape)]
where the time goes in v18:
time: 86 us; the launch traced here: 84.9 us
  starting transfers between devices  31.9 us (37%)
  matrix products  19.6 us (23%)
  waiting for transfers between devices  17.2 us (20%)
  other arithmetic  9.28 us (11%)
  local copies, waits for them, and re-layouts  3.38 us (4%)
  Pallas kernels  3.24 us (4%)
    dot_general x6, matrix products, one_block(): lax.dot_general(block_rows, fragment, (((1,), (1,)), ((), ())), preferred...  19.6 us
    all_to_all x1, waiting for transfers between devices, replicate_gather(): got = lax.all_to_all(copies, axes, 0, 0, tiled=True)  9.93 us
    all_to_all x1, starting transfers between devices, replicate_gather(): got = lax.all_to_all(copies, axes, 0, 0, tiled=True)  9.4 us
    all_to_all x1, starting transfers between devices, shards(): landed = lax.all_to_all(reordered, DEV_AXES[::-1], 0, 0, tiled=True)  8.45 us
    ppermute x3, starting transfers between devices, core_swap(): return lax.ppermute(x, 'c', [(0, 1), (1, 0)])  8.41 us
    all_to_all x1, waiting for transfers between devices, shards(): landed = lax.all_to_all(reordered, DEV_AXES[::-1], 0, 0, tiled=True)  7.27 us
    ppermute x4, starting transfers between devices, y_send(): lax.ppermute(x, 'y', [(i, (i + s) % y_count) for i in range(y_count)])  5.67 us
    dot_general x1, other arithmetic, shards(): jnp.einsum('rd,rd->r', pool, pool, preferred_element_type=jnp.float32)  4.08 us
  transfers between devices with their start and end apart: 9, of which 2 were waited for; matrix products, arithmetic and copies ran while one was open for 25% of the time, Pallas kernels for 0%

profile of v18, /device:TPU:1, one launch (start us, length us, event | category | flops | bytes accessed | tf_op | source)
XLA Modules:
  0.0 84.9 jit_solution(807479367717410776)
XLA Ops:
  0.0 1.0 %convert_reduce_fusion = s32[256]{0:T(256)S(1)} fusion(s32[256]{0:T(256)} %bitcast.77), kind=kLoop, calls=%fused_computation.37 | loop fusion | flops 458496 | bytes 2048 | tf_op jit(solution)/shard_map/compact_centers/reduce_sum | solution.py:112
  1.0 0.7 compare_reduce_fusion
  1.7 0.8 select_reduce_fusion
  2.5 0.5 fusion.32.index_ref
  3.0 3.2 %compact_centers.1 = bf16[32,2,1024]{2,1,0:T(2,128)(2,1)} custom-call(s32[32]{0:T(128)} %fusion.32.index_ref, bf16[3072,1024]{1,0:T(8,128)(2,1)} %table_ref.1), custom_call_target="tpu_custom_call" | custom-call | bytes 131072 | tf_op jit(solution)/shard_map/compact_centers/pallas_call | solution.py:72
  6.3 1.6 %copy.7 = bf16[4,4,2,2,1024]{4,3,0,1,2:T(2,128)(2,1)} copy(bf16[4,4,2,2,1024]{4,3,2,1,0:T(2,128)(2,1)} %bitcast.75) | data formatting | bytes 262144 | tf_op jit(solution)/shard_map/compact_centers/reshape | solution.py:121
  7.9 8.5 %all-to-all-start = ((bf16[32,2,1024]{2,1,0:T(2,128)(2,1)}), bf16[32,2,1024]{2,1,0:T(2,128)(2,1)S(1)}, u32[]{:S(2)}, u32[]{:S(2)}) async-start(bf16[32,2,1024]{2,1,0:T(2,128)(2,1)} %bitcast.4), calls=%async_computation | async-start | bytes 262144 | tf_op jit(solution)/shard_map/compact_centers/all_to_all | solution.py:122
  16.4 0.2 fusion.24
  16.6 7.3 %all-to-all-done = bf16[32,2,1024]{2,1,0:T(2,128)(2,1)S(1)} async-done(((bf16[32,2,1024]{2,1,0:T(2,128)(2,1)}), bf16[32,2,1024]{2,1,0:T(2,128)(2,1)S(1)}, u32[]{:S(2)}, u32[]{:S(2)}) %all-to-all-start) | async-done | bytes 131104 | tf_op jit(solution)/shard_map/compact_centers/all_to_all | solution.py:122
  24.1 0.6 gather_fusion
  24.7 0.9 %broadcast_in_dim.98 = bf16[32,8,1024]{2,1,0:T(8,128)(2,1)} broadcast(bf16[8,1024]{1,0:T(8,128)(2,1)S(1)} %broadcast_select_fusion), dimensions={1,2} | broadcast | bytes 540672 | tf_op jit(solution)/shard_map/spread_centers/broadcast_in_dim | solution.py:85
  25.6 9.4 %all-to-all-start.1 = ((bf16[32,8,1024]{2,1,0:T(8,128)(2,1)}), bf16[32,8,1024]{2,1,0:T(8,128)(2,1)S(1)}, u32[]{:S(2)}, u32[]{:S(2)}) async-start(bf16[32,8,1024]{2,1,0:T(8,128)(2,1)} %broadcast_in_dim.98), calls=%async_computation.1 | async-start | bytes 1048576 | tf_op jit(solution)/shard_map/spread_centers/all_to_all | solution.py:86
  35.0 4.1 %fusion = f32[3072]{0:T(1024)S(1)} fusion(bf16[3072,1024]{1,0:T(8,128)(2,1)} %table_ref.1), kind=kLoop, calls=%fused_computation.2 | loop fusion | flops 9434112 | bytes 6303744 | tf_op jit(solution)/shard_map/rd,rd->r/dot_general | solution.py:133
  39.1 9.9 %all-to-all-done.1 = bf16[32,8,1024]{2,1,0:T(8,128)(2,1)S(1)} async-done(((bf16[32,8,1024]{2,1,0:T(8,128)(2,1)}), bf16[32,8,1024]{2,1,0:T(8,128)(2,1)S(1)}, u32[]{:S(2)}, u32[]{:S(2)}) %all-to-all-start.1) | async-done | bytes 524320 | tf_op jit(solution)/shard_map/spread_centers/all_to_all | solution.py:86
  49.0 0.2 collective-permute-start.1
  49.2 2.4 %collective-permute-start.2 = (bf16[256,1024]{1,0:T(8,128)(2,1)S(1)}, bf16[256,1024]{1,0:T(8,128)(2,1)S(1)}, u32[]{:S(2)}, u32[]{:S(2)}) collective-permute-start(bf16[256,1024]{1,0:T(8,128)(2,1)S(1)} %bitcast.73), channel_id=1, source_target_pairs={{0,24},{8,0},{16,8},{24,16},{1,25},{9,1},{17,9},{25,17},{2,26},{10... | collective-permute-start | bytes 1572872 | tf_op jit(solution)/shard_map/spread_centers/ppermute | solution.py:131
  51.7 4.5 %collective-permute-start = (bf16[256,1024]{1,0:T(8,128)(2,1)S(1)}, bf16[256,1024]{1,0:T(8,128)(2,1)S(1)}, u32[]{:S(2)}, u32[]{:S(2)}) collective-permute-start(bf16[256,1024]{1,0:T(8,128)(2,1)S(1)} %bitcast.74), channel_id=1, source_target_pairs={{0,1},{1,0},{2,3},{3,2},{4,5},{5,4},{6,7},{7,6},{8,9},{9,8},{10,11... | collective-permute-start | bytes 1572872 | tf_op jit(solution)/shard_map/spread_centers/ppermute | solution.py:136
  56.1 0.2 fusion.20
  56.3 5.0 %fusion.16 = f32[3072]{0:T(1024)S(1)} fusion(bf16[3072,1024]{1,0:T(8,128)(2,1)} %table_ref.1, f32[256]{0:T(256)S(1)} %fusion.20, f32[3072]{0:T(1024)S(1)} %fusion, bf16[32,8,1024]{2,1,0:T(8,128)(2,1)S(1)} %all-to-all-done.1), kind=kOutput, calls=%fused_computation.28 | convolution fusion | flops 1614541824 | bytes 6841344 | tf_op jit(solution)/shard_map/distance_min/while/body/eval_jaxpr/dot_general | solution.py:23
  61.4 3.3 %collective-permute-start.3 = (bf16[512,1024]{1,0:T(8,128)(2,1)S(1)}, bf16[512,1024]{1,0:T(8,128)(2,1)S(1)}, u32[]{:S(2)}, u32[]{:S(2)}) collective-permute-start(bf16[512,1024]{1,0:T(8,128)(2,1)S(1)} %constant_dynamic-update-slice_fusion), channel_id=1, source_target_pairs={{0,1},{1,0},{2,3},{3,2},{4,5},{5,4},{6,7},{7,6},{8,9},{9,8},{10,11... | collective-permute-start | bytes 3145736 | tf_op jit(solution)/shard_map/spread_centers/ppermute | solution.py:136
  64.7 0.3 fusion.14
  65.1 2.9 %collective-permute-start.5 = (bf16[128,1024]{1,0:T(8,128)(2,1)S(1)}, bf16[128,1024]{1,0:T(8,128)(2,1)S(1)}, u32[]{:S(2)}, u32[]{:S(2)}) collective-permute-start(bf16[128,1024]{1,0:T(8,128)(2,1)S(1)} %slice.11), channel_id=1, source_target_pairs={{0,24},{8,0},{16,8},{24,16},{1,25},{9,1},{17,9},{25,17},{2,26},{10... | collective-permute-start | bytes 786440 | tf_op jit(solution)/shard_map/spread_centers/ppermute | solution.py:131
  68.1 4.0 %fusion.4 = f32[3072]{0:T(1024)S(1)} fusion(bf16[512,1024]{1,0:T(8,128)(2,1)S(1)} %constant_dynamic-update-slice_fusion, bf16[3072,1024]{1,0:T(8,128)(2,1)S(1)} %bitcast.71, f32[512]{0:T(512)S(1)} %fusion.14, f32[3072]{0:T(1024)S(1)} %fusion), kind=kOutput, calls=%fused_computation.8 | convolution fusion | flops 3229086720 | bytes 7366656 | tf_op jit(solution)/shard_map/distance_min/while/body/eval_jaxpr/dot_general | solution.py:23
  72.1 0.2 fusion.19
  72.3 2.2 %maximum_reduce_fusion.1 = f32[3072]{0:T(1024)S(1)} fusion(f32[256]{0:T(256)S(1)} %fusion.19, f32[3072]{0:T(1024)S(1)} %fusion, bf16[256,1024]{1,0:T(8,128)(2,1)S(1)} %collective-permute-done, bf16[3072,1024]{1,0:T(8,128)(2,1)S(1)} %bitcast.71), kind=kOutput, calls=%fused_computation.22 | convolution fusion | flops 1614541824 | bytes 6841344 | tf_op jit(solution)/shard_map/distance_min/while/body/eval_jaxpr/dot_general | solution.py:23
  74.5 0.7 collective-permute-start.6
  75.4 2.2 %fusion.15 = f32[3072]{0:T(1024)S(1)} fusion(bf16[256,1024]{1,0:T(8,128)(2,1)S(1)} %constant_dynamic-update-slice_fusion.2, bf16[3072,1024]{1,0:T(8,128)(2,1)S(1)} %bitcast.71, f32[256]{0:T(256)S(1)} %fusion.18, f32[3072]{0:T(1024)S(1)} %fusion), kind=kOutput, calls=%fused_computation.27 | convolution fusion | flops 1614541824 | bytes 6841344 | tf_op jit(solution)/shard_map/distance_min/while/body/eval_jaxpr/dot_general | solution.py:23
  77.6 0.2 fusion.17
  77.8 2.2 %maximum_reduce_fusion = f32[3072]{0:T(1024)S(1)} fusion(f32[256]{0:T(256)S(1)} %fusion.17, f32[3072]{0:T(1024)S(1)} %fusion, bf16[256,1024]{1,0:T(8,128)(2,1)S(1)} %collective-permute-done.6, bf16[3072,1024]{1,0:T(8,128)(2,1)S(1)} %bitcast.71), kind=kOutput, calls=%fused_computation.21 | convolution fusion | flops 1614541824 | bytes 6841344 | tf_op jit(solution)/shard_map/distance_min/while/body/eval_jaxpr/dot_general | solution.py:23
  80.0 0.3 fusion.13
  80.3 4.0 %fusion.2 = f32[3072]{0:T(1024)S(1)} fusion(bf16[512,1024]{1,0:T(8,128)(2,1)S(1)} %collective-permute-done.3, bf16[3072,1024]{1,0:T(8,128)(2,1)S(1)} %bitcast.71, f32[512]{0:T(512)S(1)} %fusion.13, f32[3072]{0:T(1024)S(1)} %fusion), kind=kOutput, calls=%fused_computation.5 | convolution fusion | flops 3229086720 | bytes 7366656 | tf_op jit(solution)/shard_map/distance_min/while/body/eval_jaxpr/dot_general | solution.py:23
  84.3 0.6 minimum_minimum_fusion
  (34 shorter events, 0.7 us)
Async XLA Ops:
  0.0 16.4 %copy-start = (s32[1,256]{1,0:T(1,128)S(1)}, s32[1,256]{1,0:T(1,128)}, u32[]{:S(2)}) copy-start(s32[1,256]{1,0:T(1,128)} %param.6) | copy-start | bytes 3076
  0.0 16.4 %copy-start.2 = (s32[1,256]{1,0:T(1,128)S(1)}, s32[1,256]{1,0:T(1,128)}, u32[]{:S(2)}) copy-start(s32[1,256]{1,0:T(1,128)} %param.7) | copy-start | bytes 3076
  7.9 16.0 %all-to-all-start = ((bf16[32,2,1024]{2,1,0:T(2,128)(2,1)}), bf16[32,2,1024]{2,1,0:T(2,128)(2,1)S(1)}, u32[]{:S(2)}, u32[]{:S(2)}) async-start(bf16[32,2,1024]{2,1,0:T(2,128)(2,1)} %bitcast.4), calls=%async_computation | async-start | bytes 262144 | tf_op jit(solution)/shard_map/compact_centers/all_to_all | solution.py:122
  25.6 23.4 %all-to-all-start.1 = ((bf16[32,8,1024]{2,1,0:T(8,128)(2,1)}), bf16[32,8,1024]{2,1,0:T(8,128)(2,1)S(1)}, u32[]{:S(2)}, u32[]{:S(2)}) async-start(bf16[32,8,1024]{2,1,0:T(8,128)(2,1)} %broadcast_in_dim.98), calls=%async_computation.1 | async-start | bytes 1048576 | tf_op jit(solution)/shard_map/spread_centers/all_to_all | solution.py:86
  49.0 12.3 %collective-permute-start.1 = (bf16[256,1024]{1,0:T(8,128)(2,1)S(1)}, bf16[256,1024]{1,0:T(8,128)(2,1)S(1)}, u32[]{:S(2)}, u32[]{:S(2)}) collective-permute-start(bf16[256,1024]{1,0:T(8,128)(2,1)S(1)} %bitcast.72), channel_id=1, source_target_pairs={{0,8},{8,16},{16,24},{24,0},{1,9},{9,17},{17,25},{25,1},{2,10},{10... | collective-permute-start | bytes 1572872 | tf_op jit(solution)/shard_map/spread_centers/ppermute | solution.py:131
  49.2 12.2 %collective-permute-start.2 = (bf16[256,1024]{1,0:T(8,128)(2,1)S(1)}, bf16[256,1024]{1,0:T(8,128)(2,1)S(1)}, u32[]{:S(2)}, u32[]{:S(2)}) collective-permute-start(bf16[256,1024]{1,0:T(8,128)(2,1)S(1)} %bitcast.73), channel_id=1, source_target_pairs={{0,24},{8,0},{16,8},{24,16},{1,25},{9,1},{17,9},{25,17},{2,26},{10... | collective-permute-start | bytes 1572872 | tf_op jit(solution)/shard_map/spread_centers/ppermute | solution.py:131
  51.7 20.4 %collective-permute-start = (bf16[256,1024]{1,0:T(8,128)(2,1)S(1)}, bf16[256,1024]{1,0:T(8,128)(2,1)S(1)}, u32[]{:S(2)}, u32[]{:S(2)}) collective-permute-start(bf16[256,1024]{1,0:T(8,128)(2,1)S(1)} %bitcast.74), channel_id=1, source_target_pairs={{0,1},{1,0},{2,3},{3,2},{4,5},{5,4},{6,7},{7,6},{8,9},{9,8},{10,11... | collective-permute-start | bytes 1572872 | tf_op jit(solution)/shard_map/spread_centers/ppermute | solution.py:136
  56.1 11.9 %slice-start = ((s8[6291456]{0:T(1024)(128)(4,1)}), s8[4194304]{0:T(1024)(128)(4,1)S(1)}, s32[]{:S(2)}) async-start(s8[6291456]{0:T(1024)(128)(4,1)} %bitcast.70), calls=%async_computation.2 | async-start | bytes 8388608
  56.3 11.8 %slice-start.1 = ((s8[6291456]{0:T(1024)(128)(4,1)}), s8[2097152]{0:T(1024)(128)(4,1)S(1)}, s32[]{:S(2)}) async-start(s8[6291456]{0:T(1024)(128)(4,1)} %bitcast.70), calls=%async_computation.3 | async-start | bytes 4194304
  61.4 18.5 %collective-permute-start.3 = (bf16[512,1024]{1,0:T(8,128)(2,1)S(1)}, bf16[512,1024]{1,0:T(8,128)(2,1)S(1)}, u32[]{:S(2)}, u32[]{:S(2)}) collective-permute-start(bf16[512,1024]{1,0:T(8,128)(2,1)S(1)} %constant_dynamic-update-slice_fusion), channel_id=1, source_target_pairs={{0,1},{1,0},{2,3},{3,2},{4,5},{5,4},{6,7},{7,6},{8,9},{9,8},{10,11... | collective-permute-start | bytes 3145736 | tf_op jit(solution)/shard_map/spread_centers/ppermute | solution.py:136
  65.0 9.4 %collective-permute-start.4 = (bf16[128,1024]{1,0:T(8,128)(2,1)S(1)}, bf16[128,1024]{1,0:T(8,128)(2,1)S(1)}, u32[]{:S(2)}, u32[]{:S(2)}) collective-permute-start(bf16[128,1024]{1,0:T(8,128)(2,1)S(1)} %slice.10), channel_id=1, source_target_pairs={{0,8},{8,16},{16,24},{24,0},{1,9},{9,17},{17,25},{25,1},{2,10},{10... | collective-permute-start | bytes 786440 | tf_op jit(solution)/shard_map/spread_centers/ppermute | solution.py:131
  65.1 9.3 %collective-permute-start.5 = (bf16[128,1024]{1,0:T(8,128)(2,1)S(1)}, bf16[128,1024]{1,0:T(8,128)(2,1)S(1)}, u32[]{:S(2)}, u32[]{:S(2)}) collective-permute-start(bf16[128,1024]{1,0:T(8,128)(2,1)S(1)} %slice.11), channel_id=1, source_target_pairs={{0,24},{8,0},{16,8},{24,16},{1,25},{9,1},{17,9},{25,17},{2,26},{10... | collective-permute-start | bytes 786440 | tf_op jit(solution)/shard_map/spread_centers/ppermute | solution.py:131
  74.5 3.1 %collective-permute-start.6 = (bf16[256,1024]{1,0:T(8,128)(2,1)S(1)}, bf16[256,1024]{1,0:T(8,128)(2,1)S(1)}, u32[]{:S(2)}, u32[]{:S(2)}) collective-permute-start(bf16[256,1024]{1,0:T(8,128)(2,1)S(1)} %constant_dynamic-update-slice_fusion.2), channel_id=1, source_target_pairs={{0,1},{1,0},{2,3},{3,2},{4,5},{5,4},{6,7},{7,6},{8,9},{9,8},{10,11... | collective-permute-start | bytes 1572872 | tf_op jit(solution)/shard_map/spread_centers/ppermute | solution.py:136
  80.3 4.0 %copy-start.1 = (f32[3072]{0:T(1024)S(1)}, f32[3072]{0:T(1024)}, u32[]{:S(2)}) copy-start(f32[3072]{0:T(1024)} %param.5) | copy-start | bytes 36868

commit v19 on v17

--- a/solution.py
+++ b/solution.py
@@ -115,12 +115,17 @@
         )
         peer_offset = jnp.sum(jnp.where(to_peer, offsets[None, :], 0), axis=1)
         send_rows = gather_rows(pool, peer_offset)
-        landed = lax.all_to_all(send_rows, DEV_AXES, 0, 0, tiled=True)
-        wanted = my_index + dev_count * jnp.arange(per_device, dtype=jnp.int32)
+        peer_axes = DEV_AXES[::-1]
+        landed = lax.all_to_all(send_rows, peer_axes, 0, 0, tiled=True)
+        wanted = lax.axis_index(peer_axes) + dev_count * jnp.arange(per_device, dtype=jnp.int32)
         is_wanted = position[None, :] == wanted[:, None]
         source = jnp.sum(jnp.where(is_wanted, owners[None, :], 0), axis=1)
         parity = jnp.sum(jnp.where(is_wanted, offsets[None, :], 0), axis=1) % 2
-        compact = jnp.take(landed.reshape(-1, landed.shape[-1]), source * 2 + parity, axis=0)
+        cores = dev_count // (y_count * x_count)
+        source_peer = ((source % cores) * x_count + (source // cores) % x_count) * y_count + source // (
+            cores * x_count
+        )
+        compact = jnp.take(landed.reshape(-1, landed.shape[-1]), source_peer * 2 + parity, axis=0)
 
     def y_send(x, s):
         return lax.ppermute(x, "y", [(i, (i + s) % y_count) for i in range(y_count)])

time: 84.8 us -> 84.3 us (level)
  no operation moved by 1% of the time
where the time goes in v19:
time: 84.3 us; the launch traced here: 83.2 us
  starting transfers between devices  32 us (38%)
  matrix products  19.6 us (23%)
  waiting for transfers between devices  17.2 us (20%)
  other arithmetic  9.3 us (11%)
  Pallas kernels  3.2 us (4%)
  local copies, waits for them, and re-layouts  1.64 us (2%)
    dot_general x6, matrix products, one_block(): lax.dot_general(block_rows, fragment, (((1,), (1,)), ((), ())), preferred...  19.6 us
    all_to_all x1, waiting for transfers between devices, replicate_gather(): got = lax.all_to_all(copies, axes, 0, 0, tiled=True)  9.93 us
    all_to_all x1, starting transfers between devices, replicate_gather(): got = lax.all_to_all(copies, axes, 0, 0, tiled=True)  9.27 us
    all_to_all x1, starting transfers between devices, shards(): landed = lax.all_to_all(send_rows, peer_axes, 0, 0, tiled=True)  8.64 us
    ppermute x3, starting transfers between devices, core_swap(): return lax.ppermute(x, 'c', [(0, 1), (1, 0)])  8.41 us
    all_to_all x1, waiting for transfers between devices, shards(): landed = lax.all_to_all(send_rows, peer_axes, 0, 0, tiled=True)  7.23 us
    ppermute x4, starting transfers between devices, y_send(): lax.ppermute(x, 'y', [(i, (i + s) % y_count) for i in range(y_count)])  5.67 us
    dot_general x1, other arithmetic, shards(): jnp.einsum('rd,rd->r', pool, pool, preferred_element_type=jnp.float32)  4.08 us
  transfers between devices with their start and end apart: 9, of which 2 were waited for; matrix products, arithmetic and copies ran while one was open for 25% of the time, Pallas kernels for 0%

profile of v19, /device:TPU:1, one launch (start us, length us, event | category | flops | bytes accessed | tf_op | source)
XLA Modules:
  0.0 83.2 jit_solution(12038824513449599641)
XLA Ops:
  0.0 1.0 %convert_reduce_fusion = s32[256]{0:T(256)S(1)} fusion(s32[256]{0:T(256)} %bitcast.82), kind=kLoop, calls=%fused_computation.37 | loop fusion | flops 458496 | bytes 2048 | tf_op jit(solution)/shard_map/compact_centers/reduce_sum | solution.py:112
  1.0 0.7 compare_reduce_fusion
  1.7 0.8 select_reduce_fusion
  2.5 0.5 fusion.38.index_ref
  3.0 3.2 %compact_centers.1 = bf16[32,2,1024]{2,1,0:T(2,128)(2,1)} custom-call(s32[32]{0:T(128)} %fusion.38.index_ref, bf16[3072,1024]{1,0:T(8,128)(2,1)} %table_ref.1), custom_call_target="tpu_custom_call" | custom-call | bytes 131072 | tf_op jit(solution)/shard_map/compact_centers/pallas_call | solution.py:72
  6.2 8.6 %all-to-all-start = ((bf16[32,2,1024]{2,1,0:T(2,128)(2,1)}), bf16[32,2,1024]{2,1,0:T(2,128)(2,1)S(1)}, u32[]{:S(2)}, u32[]{:S(2)}) async-start(bf16[32,2,1024]{2,1,0:T(2,128)(2,1)} %compact_centers.1), calls=%async_computation | async-start | bytes 262144 | tf_op jit(solution)/shard_map/compact_centers/all_to_all | solution.py:119
  14.9 0.2 fusion.24
  15.2 7.2 %all-to-all-done = bf16[32,2,1024]{2,1,0:T(2,128)(2,1)S(1)} async-done(((bf16[32,2,1024]{2,1,0:T(2,128)(2,1)}), bf16[32,2,1024]{2,1,0:T(2,128)(2,1)S(1)}, u32[]{:S(2)}, u32[]{:S(2)}) %all-to-all-start) | async-done | bytes 131104 | tf_op jit(solution)/shard_map/compact_centers/all_to_all | solution.py:119
  22.5 0.6 gather_fusion
  23.1 0.9 %broadcast_in_dim.98 = bf16[32,8,1024]{2,1,0:T(8,128)(2,1)} broadcast(bf16[8,1024]{1,0:T(8,128)(2,1)S(1)} %broadcast_select_fusion), dimensions={1,2} | broadcast | bytes 540672 | tf_op jit(solution)/shard_map/spread_centers/broadcast_in_dim | solution.py:85
  24.0 9.3 %all-to-all-start.1 = ((bf16[32,8,1024]{2,1,0:T(8,128)(2,1)}), bf16[32,8,1024]{2,1,0:T(8,128)(2,1)S(1)}, u32[]{:S(2)}, u32[]{:S(2)}) async-start(bf16[32,8,1024]{2,1,0:T(8,128)(2,1)} %broadcast_in_dim.98), calls=%async_computation.1 | async-start | bytes 1048576 | tf_op jit(solution)/shard_map/spread_centers/all_to_all | solution.py:86
  33.3 4.1 %fusion = f32[3072]{0:T(1024)S(1)} fusion(bf16[3072,1024]{1,0:T(8,128)(2,1)} %table_ref.1), kind=kLoop, calls=%fused_computation.2 | loop fusion | flops 9434112 | bytes 6303744 | tf_op jit(solution)/shard_map/rd,rd->r/dot_general | solution.py:133
  37.3 9.9 %all-to-all-done.1 = bf16[32,8,1024]{2,1,0:T(8,128)(2,1)S(1)} async-done(((bf16[32,8,1024]{2,1,0:T(8,128)(2,1)}), bf16[32,8,1024]{2,1,0:T(8,128)(2,1)S(1)}, u32[]{:S(2)}, u32[]{:S(2)}) %all-to-all-start.1) | async-done | bytes 524320 | tf_op jit(solution)/shard_map/spread_centers/all_to_all | solution.py:86
  47.3 0.2 collective-permute-start.1
  47.5 2.4 %collective-permute-start.2 = (bf16[256,1024]{1,0:T(8,128)(2,1)S(1)}, bf16[256,1024]{1,0:T(8,128)(2,1)S(1)}, u32[]{:S(2)}, u32[]{:S(2)}) collective-permute-start(bf16[256,1024]{1,0:T(8,128)(2,1)S(1)} %bitcast.80), channel_id=1, source_target_pairs={{0,24},{8,0},{16,8},{24,16},{1,25},{9,1},{17,9},{25,17},{2,26},{10... | collective-permute-start | bytes 1572872 | tf_op jit(solution)/shard_map/spread_centers/ppermute | solution.py:131
  49.9 4.5 %collective-permute-start = (bf16[256,1024]{1,0:T(8,128)(2,1)S(1)}, bf16[256,1024]{1,0:T(8,128)(2,1)S(1)}, u32[]{:S(2)}, u32[]{:S(2)}) collective-permute-start(bf16[256,1024]{1,0:T(8,128)(2,1)S(1)} %bitcast.81), channel_id=1, source_target_pairs={{0,1},{1,0},{2,3},{3,2},{4,5},{5,4},{6,7},{7,6},{8,9},{9,8},{10,11... | collective-permute-start | bytes 1572872 | tf_op jit(solution)/shard_map/spread_centers/ppermute | solution.py:136
  54.4 0.2 fusion.20
  54.6 5.0 %fusion.16 = f32[3072]{0:T(1024)S(1)} fusion(bf16[3072,1024]{1,0:T(8,128)(2,1)} %table_ref.1, f32[256]{0:T(256)S(1)} %fusion.20, f32[3072]{0:T(1024)S(1)} %fusion, bf16[32,8,1024]{2,1,0:T(8,128)(2,1)S(1)} %all-to-all-done.1), kind=kOutput, calls=%fused_computation.28 | convolution fusion | flops 1614541824 | bytes 6841344 | tf_op jit(solution)/shard_map/distance_min/while/body/eval_jaxpr/dot_general | solution.py:23
  59.7 3.3 %collective-permute-start.3 = (bf16[512,1024]{1,0:T(8,128)(2,1)S(1)}, bf16[512,1024]{1,0:T(8,128)(2,1)S(1)}, u32[]{:S(2)}, u32[]{:S(2)}) collective-permute-start(bf16[512,1024]{1,0:T(8,128)(2,1)S(1)} %constant_dynamic-update-slice_fusion), channel_id=1, source_target_pairs={{0,1},{1,0},{2,3},{3,2},{4,5},{5,4},{6,7},{7,6},{8,9},{9,8},{10,11... | collective-permute-start | bytes 3145736 | tf_op jit(solution)/shard_map/spread_centers/ppermute | solution.py:136
  63.0 0.3 fusion.14
  63.4 2.9 %collective-permute-start.5 = (bf16[128,1024]{1,0:T(8,128)(2,1)S(1)}, bf16[128,1024]{1,0:T(8,128)(2,1)S(1)}, u32[]{:S(2)}, u32[]{:S(2)}) collective-permute-start(bf16[128,1024]{1,0:T(8,128)(2,1)S(1)} %slice.11), channel_id=1, source_target_pairs={{0,24},{8,0},{16,8},{24,16},{1,25},{9,1},{17,9},{25,17},{2,26},{10... | collective-permute-start | bytes 786440 | tf_op jit(solution)/shard_map/spread_centers/ppermute | solution.py:131
  66.3 4.0 %fusion.4 = f32[3072]{0:T(1024)S(1)} fusion(bf16[512,1024]{1,0:T(8,128)(2,1)S(1)} %constant_dynamic-update-slice_fusion, bf16[3072,1024]{1,0:T(8,128)(2,1)S(1)} %bitcast.78, f32[512]{0:T(512)S(1)} %fusion.14, f32[3072]{0:T(1024)S(1)} %fusion), kind=kOutput, calls=%fused_computation.8 | convolution fusion | flops 3229086720 | bytes 7366656 | tf_op jit(solution)/shard_map/distance_min/while/body/eval_jaxpr/dot_general | solution.py:23
  70.4 0.2 fusion.19
  70.6 2.1 %maximum_reduce_fusion.1 = f32[3072]{0:T(1024)S(1)} fusion(f32[256]{0:T(256)S(1)} %fusion.19, f32[3072]{0:T(1024)S(1)} %fusion, bf16[256,1024]{1,0:T(8,128)(2,1)S(1)} %collective-permute-done, bf16[3072,1024]{1,0:T(8,128)(2,1)S(1)} %bitcast.78), kind=kOutput, calls=%fused_computation.22 | convolution fusion | flops 1614541824 | bytes 6841344 | tf_op jit(solution)/shard_map/distance_min/while/body/eval_jaxpr/dot_general | solution.py:23
  72.8 0.7 collective-permute-start.6
  73.5 0.2 fusion.18
  73.6 2.2 %fusion.15 = f32[3072]{0:T(1024)S(1)} fusion(bf16[256,1024]{1,0:T(8,128)(2,1)S(1)} %constant_dynamic-update-slice_fusion.2, bf16[3072,1024]{1,0:T(8,128)(2,1)S(1)} %bitcast.78, f32[256]{0:T(256)S(1)} %fusion.18, f32[3072]{0:T(1024)S(1)} %fusion), kind=kOutput, calls=%fused_computation.27 | convolution fusion | flops 1614541824 | bytes 6841344 | tf_op jit(solution)/shard_map/distance_min/while/body/eval_jaxpr/dot_general | solution.py:23
  75.9 0.2 fusion.17
  76.0 2.2 %maximum_reduce_fusion = f32[3072]{0:T(1024)S(1)} fusion(f32[256]{0:T(256)S(1)} %fusion.17, f32[3072]{0:T(1024)S(1)} %fusion, bf16[256,1024]{1,0:T(8,128)(2,1)S(1)} %collective-permute-done.6, bf16[3072,1024]{1,0:T(8,128)(2,1)S(1)} %bitcast.78), kind=kOutput, calls=%fused_computation.21 | convolution fusion | flops 1614541824 | bytes 6841344 | tf_op jit(solution)/shard_map/distance_min/while/body/eval_jaxpr/dot_general | solution.py:23
  78.3 0.3 fusion.13
  78.5 4.0 %fusion.2 = f32[3072]{0:T(1024)S(1)} fusion(bf16[512,1024]{1,0:T(8,128)(2,1)S(1)} %collective-permute-done.3, bf16[3072,1024]{1,0:T(8,128)(2,1)S(1)} %bitcast.78, f32[512]{0:T(512)S(1)} %fusion.13, f32[3072]{0:T(1024)S(1)} %fusion), kind=kOutput, calls=%fused_computation.5 | convolution fusion | flops 3229086720 | bytes 7366656 | tf_op jit(solution)/shard_map/distance_min/while/body/eval_jaxpr/dot_general | solution.py:23
  82.6 0.6 minimum_minimum_fusion
  (32 shorter events, 0.5 us)
Async XLA Ops:
  0.0 14.9 %copy-start = (s32[1,256]{1,0:T(1,128)S(1)}, s32[1,256]{1,0:T(1,128)}, u32[]{:S(2)}) copy-start(s32[1,256]{1,0:T(1,128)} %param.6) | copy-start | bytes 3076
  0.0 14.9 %copy-start.2 = (s32[1,256]{1,0:T(1,128)S(1)}, s32[1,256]{1,0:T(1,128)}, u32[]{:S(2)}) copy-start(s32[1,256]{1,0:T(1,128)} %param.7) | copy-start | bytes 3076
  6.2 16.2 %all-to-all-start = ((bf16[32,2,1024]{2,1,0:T(2,128)(2,1)}), bf16[32,2,1024]{2,1,0:T(2,128)(2,1)S(1)}, u32[]{:S(2)}, u32[]{:S(2)}) async-start(bf16[32,2,1024]{2,1,0:T(2,128)(2,1)} %compact_centers.1), calls=%async_computation | async-start | bytes 262144 | tf_op jit(solution)/shard_map/compact_centers/all_to_all | solution.py:119
  24.0 23.3 %all-to-all-start.1 = ((bf16[32,8,1024]{2,1,0:T(8,128)(2,1)}), bf16[32,8,1024]{2,1,0:T(8,128)(2,1)S(1)}, u32[]{:S(2)}, u32[]{:S(2)}) async-start(bf16[32,8,1024]{2,1,0:T(8,128)(2,1)} %broadcast_in_dim.98), calls=%async_computation.1 | async-start | bytes 1048576 | tf_op jit(solution)/shard_map/spread_centers/all_to_all | solution.py:86
  47.3 12.3 %collective-permute-start.1 = (bf16[256,1024]{1,0:T(8,128)(2,1)S(1)}, bf16[256,1024]{1,0:T(8,128)(2,1)S(1)}, u32[]{:S(2)}, u32[]{:S(2)}) collective-permute-start(bf16[256,1024]{1,0:T(8,128)(2,1)S(1)} %bitcast.79), channel_id=1, source_target_pairs={{0,8},{8,16},{16,24},{24,0},{1,9},{9,17},{17,25},{25,1},{2,10},{10... | collective-permute-start | bytes 1572872 | tf_op jit(solution)/shard_map/spread_centers/ppermute | solution.py:131
  47.5 12.2 %collective-permute-start.2 = (bf16[256,1024]{1,0:T(8,128)(2,1)S(1)}, bf16[256,1024]{1,0:T(8,128)(2,1)S(1)}, u32[]{:S(2)}, u32[]{:S(2)}) collective-permute-start(bf16[256,1024]{1,0:T(8,128)(2,1)S(1)} %bitcast.80), channel_id=1, source_target_pairs={{0,24},{8,0},{16,8},{24,16},{1,25},{9,1},{17,9},{25,17},{2,26},{10... | collective-permute-start | bytes 1572872 | tf_op jit(solution)/shard_map/spread_centers/ppermute | solution.py:131
  49.9 20.4 %collective-permute-start = (bf16[256,1024]{1,0:T(8,128)(2,1)S(1)}, bf16[256,1024]{1,0:T(8,128)(2,1)S(1)}, u32[]{:S(2)}, u32[]{:S(2)}) collective-permute-start(bf16[256,1024]{1,0:T(8,128)(2,1)S(1)} %bitcast.81), channel_id=1, source_target_pairs={{0,1},{1,0},{2,3},{3,2},{4,5},{5,4},{6,7},{7,6},{8,9},{9,8},{10,11... | collective-permute-start | bytes 1572872 | tf_op jit(solution)/shard_map/spread_centers/ppermute | solution.py:136
  54.4 11.9 %slice-start = ((s8[6291456]{0:T(1024)(128)(4,1)}), s8[4194304]{0:T(1024)(128)(4,1)S(1)}, s32[]{:S(2)}) async-start(s8[6291456]{0:T(1024)(128)(4,1)} %bitcast.77), calls=%async_computation.2 | async-start | bytes 8388608
  54.6 11.8 %slice-start.1 = ((s8[6291456]{0:T(1024)(128)(4,1)}), s8[2097152]{0:T(1024)(128)(4,1)S(1)}, s32[]{:S(2)}) async-start(s8[6291456]{0:T(1024)(128)(4,1)} %bitcast.77), calls=%async_computation.3 | async-start | bytes 4194304
  59.7 18.5 %collective-permute-start.3 = (bf16[512,1024]{1,0:T(8,128)(2,1)S(1)}, bf16[512,1024]{1,0:T(8,128)(2,1)S(1)}, u32[]{:S(2)}, u32[]{:S(2)}) collective-permute-start(bf16[512,1024]{1,0:T(8,128)(2,1)S(1)} %constant_dynamic-update-slice_fusion), channel_id=1, source_target_pairs={{0,1},{1,0},{2,3},{3,2},{4,5},{5,4},{6,7},{7,6},{8,9},{9,8},{10,11... | collective-permute-start | bytes 3145736 | tf_op jit(solution)/shard_map/spread_centers/ppermute | solution.py:136
  63.3 9.4 %collective-permute-start.4 = (bf16[128,1024]{1,0:T(8,128)(2,1)S(1)}, bf16[128,1024]{1,0:T(8,128)(2,1)S(1)}, u32[]{:S(2)}, u32[]{:S(2)}) collective-permute-start(bf16[128,1024]{1,0:T(8,128)(2,1)S(1)} %slice.10), channel_id=1, source_target_pairs={{0,8},{8,16},{16,24},{24,0},{1,9},{9,17},{17,25},{25,1},{2,10},{10... | collective-permute-start | bytes 786440 | tf_op jit(solution)/shard_map/spread_centers/ppermute | solution.py:131
  63.4 9.3 %collective-permute-start.5 = (bf16[128,1024]{1,0:T(8,128)(2,1)S(1)}, bf16[128,1024]{1,0:T(8,128)(2,1)S(1)}, u32[]{:S(2)}, u32[]{:S(2)}) collective-permute-start(bf16[128,1024]{1,0:T(8,128)(2,1)S(1)} %slice.11), channel_id=1, source_target_pairs={{0,24},{8,0},{16,8},{24,16},{1,25},{9,1},{17,9},{25,17},{2,26},{10... | collective-permute-start | bytes 786440 | tf_op jit(solution)/shard_map/spread_centers/ppermute | solution.py:131
  72.8 3.1 %collective-permute-start.6 = (bf16[256,1024]{1,0:T(8,128)(2,1)S(1)}, bf16[256,1024]{1,0:T(8,128)(2,1)S(1)}, u32[]{:S(2)}, u32[]{:S(2)}) collective-permute-start(bf16[256,1024]{1,0:T(8,128)(2,1)S(1)} %constant_dynamic-update-slice_fusion.2), channel_id=1, source_target_pairs={{0,1},{1,0},{2,3},{3,2},{4,5},{5,4},{6,7},{7,6},{8,9},{9,8},{10,11... | collective-permute-start | bytes 1572872 | tf_op jit(solution)/shard_map/spread_centers/ppermute | solution.py:136
  78.5 4.0 %copy-start.1 = (f32[3072]{0:T(1024)S(1)}, f32[3072]{0:T(1024)}, u32[]{:S(2)}) copy-start(f32[3072]{0:T(1024)} %param.5) | copy-start | bytes 36868
